TPU v7x, 32 devices: a whole 2x2x4 slice. The times are simulated.
32 devices in a mesh: tm: 4 (over x, core), space: 8 (over z, y).
Axes of the slice: x: 2, y: 2, z: 4, core: 2. Of those that a mesh axis runs over, the one named last changes fastest.
Arguments:
- initial: float32 [4, 2, 64, 32, 128], P('tm', None, 'space'), may hold values from 0 to 1.5
- decay_rate: float32 [2, 64, 32, 128], P(None, 'space'), may hold values from 0.2 to 2
- source: float32 [2, 64, 32, 128], P(None, 'space'), may hold values from -2.5 to 2.5
- diffusivity: float32 [2], replicated, may hold values from 0.4 to 0.9
Outputs:
- end_state: float32 [4, 2, 64, 32, 128], P('tm', None, 'space')
All inputs are finite; a program needn't handle non-finite values.
Results may differ from a plain program's by a relative error of at most 0.00002.
Values sent between devices are 32-bit elements; how exact they have to be, the bound alone decides.
No kernel may reach another device: no remote copies, remote signals or barrier semaphores. Data moves between devices by JAX's collectives and lax.ppermute only.
A program may use at most 64 MiB of HBM per device.

v0:
```python
import math

import jax
import jax.numpy as jnp
from jax import lax
from jax.sharding import PartitionSpec as P

ROUNDS = 3

START_HALO = 5

step_length = 0.5


def lagrange_integral(nodes, j, upper_end):
    coeffs = [1.0]
    scale_down = 1.0
    for i in range(len(nodes)):
        if i != j:
            grown = [0.0] * (len(coeffs) + 1)
            for p in range(len(coeffs)):
                grown[p + 1] = grown[p + 1] + coeffs[p]
                grown[p] = grown[p] - nodes[i] * coeffs[p]
            coeffs = grown
            scale_down = scale_down * (nodes[j] - nodes[i])
    summed_up = 0.0
    for p in range(len(coeffs)):
        summed_up = summed_up + coeffs[p] * upper_end ** (p + 1) / (p + 1)
    return summed_up / scale_down


def node_tables():
    radical = math.sqrt(3.0 / 7.0)
    fine_nodes = [0.0, 0.5 * (1.0 - radical), 0.5, 0.5 * (1.0 + radical), 1.0]
    coarse_nodes = [0.0, 0.5, 1.0]
    integrals = [
        [lagrange_integral(fine_nodes, j, fine_nodes[m]) for j in range(5)] for m in range(5)
    ]
    spread_table = [
        [float(step_length * (integrals[m + 1][j] - integrals[m][j])) for j in range(5)]
        for m in range(4)
    ]
    grouped_table = [
        [spread_table[2 * c][j] + spread_table[2 * c + 1][j] for j in range(5)] for c in range(2)
    ]
    interp_table = []
    for m in range(5):
        weights_row = []
        for k in range(3):
            factor = 1.0
            for i in range(3):
                if i != k:
                    factor = (
                        factor
                        * (fine_nodes[m] - coarse_nodes[i])
                        / (coarse_nodes[k] - coarse_nodes[i])
                    )
            weights_row.append(factor)
        interp_table.append(weights_row)
    widths = [step_length * (fine_nodes[m + 1] - fine_nodes[m]) for m in range(4)]
    return (spread_table, grouped_table, interp_table, widths)


def to_even_odd(a):
    return jnp.concatenate([a[..., 0::2, :], a[..., 1::2, :]], axis=-2)


def from_even_odd(a):
    half = a.shape[-2] // 2
    woven = jnp.stack([a[..., :half, :], a[..., half:, :]], axis=-2)
    return woven.reshape(a.shape)


def crop(field, h):
    a, have = field
    d = have - h
    assert d >= 0
    if d == 0:
        return a
    return lax.slice_in_dim(a, d, a.shape[-3] - d, axis=a.ndim - 3)


def space_halo(a, h):
    if h == 0:
        return a
    size = lax.axis_size("space")
    rows = a.shape[-3]
    assert h <= rows
    up = [(i, (i + 1) % size) for i in range(size)]
    down = [((i + 1) % size, i) for i in range(size)]
    before = lax.ppermute(lax.slice_in_dim(a, rows - h, rows, axis=a.ndim - 3), "space", up)
    after = lax.ppermute(lax.slice_in_dim(a, 0, h, axis=a.ndim - 3), "space", down)
    return jnp.concatenate([before, a, after], axis=a.ndim - 3)


def from_previous_slice(a, h):
    slices = lax.axis_size("tm")
    size = lax.axis_size("space")
    rows = a.shape[-3]
    axes = ("tm", "space")

    def moved(piece, shift):
        pairs = [
            (t * size + s, (t + 1) * size + (s + shift) % size)
            for t in range(slices - 1)
            for s in range(size)
        ]
        return lax.ppermute(piece, axes, pairs)

    centre = moved(a, 0)
    if h == 0:
        return centre
    before = moved(lax.slice_in_dim(a, rows - h, rows, axis=a.ndim - 3), 1)
    after = moved(lax.slice_in_dim(a, 0, h, axis=a.ndim - 3), -1)
    return jnp.concatenate([before, centre, after], axis=a.ndim - 3)


def react_terms(field, laplace, diffusivity, source):
    first_part = field[0]
    second_part = field[1]
    product = first_part * second_part * second_part
    return jnp.stack(
        [
            diffusivity[0] * laplace[0] - product + source[0],
            diffusivity[1] * laplace[1] + product + source[1],
        ],
        axis=0,
    )


def fine_laplace(a):
    centre = a[..., 1:-1, :, :]
    pair_x = a[..., 2:, :, :] + a[..., :-2, :, :]
    half = centre.shape[-2] // 2
    even = centre[..., :half, :]
    odd = centre[..., half:, :]
    pair_y = jnp.concatenate(
        [odd + jnp.roll(odd, 1, -2), jnp.roll(even, -1, -2) + even], axis=-2
    )
    pair_z = jnp.roll(centre, -1, -1) + jnp.roll(centre, 1, -1)
    return pair_x + pair_y + pair_z - 6.0 * centre


def coarse_laplace(a):
    centre = a[..., 1:-1, :, :]
    pair_x = a[..., 2:, :, :] + a[..., :-2, :, :]
    pair_y = jnp.roll(centre, -1, -2) + jnp.roll(centre, 1, -2)
    pair_z = jnp.roll(centre, -1, -1) + jnp.roll(centre, 1, -1)
    return (pair_x - 2.0 * centre) * 0.25 + (pair_y - 2.0 * centre) * 0.25 + (
        pair_z - 2.0 * centre
    )


def restrict(field):
    a, h = field
    h2 = h - h % 2
    a = crop(field, h2)
    rows = a.shape[-3]
    half = a.shape[-2] // 2
    pairs = a.reshape(a.shape[:-3] + (rows // 2, 2) + a.shape[-2:])
    even = pairs[..., :half, :]
    odd = pairs[..., half:, :]
    upper = even[..., 0, :, :] + even[..., 1, :, :]
    lower = odd[..., 0, :, :] + odd[..., 1, :, :]
    return (upper + lower) * 0.25, h2 // 2


def prolong(a):
    rows = jnp.repeat(a, 2, axis=a.ndim - 3)
    return jnp.concatenate([rows, rows], axis=-2)


def packed_halo(fields):
    size = lax.axis_size("space")
    rows = fields[0][0].shape[-3]
    axis = fields[0][0].ndim - 3
    up = [(i, (i + 1) % size) for i in range(size)]
    down = [((i + 1) % size, i) for i in range(size)]
    lasts = jnp.concatenate(
        [lax.slice_in_dim(a, rows - w, rows, axis=axis) for a, w in fields], axis=axis
    )
    firsts = jnp.concatenate([lax.slice_in_dim(a, 0, w, axis=axis) for a, w in fields], axis=axis)
    before = lax.ppermute(lasts, "space", up)
    after = lax.ppermute(firsts, "space", down)
    out = []
    offset = 0
    for a, w in fields:
        out.append(
            (
                jnp.concatenate(
                    [
                        lax.slice_in_dim(before, offset, offset + w, axis=axis),
                        a,
                        lax.slice_in_dim(after, offset, offset + w, axis=axis),
                    ],
                    axis=axis,
                ),
                w,
            )
        )
        offset += w
    return out


def per_device(initial, decay_rate, source, diffusivity):
    spread_table, grouped_table, interp_table, widths = node_tables()
    first_slice = lax.axis_index("tm") == 0
    hs = START_HALO
    assert hs == 5 and initial.shape[-3] >= hs
    hfix = hs - 1

    own_start = to_even_odd(initial[0])
    fixed = space_halo(jnp.stack([to_even_odd(decay_rate), to_even_odd(source)]), hfix)
    decay = (fixed[0], hfix)
    src = (fixed[1], hfix)
    rate_c = restrict(decay)
    source_c = restrict(src)

    def fine_E(field):
        a, h = field
        laplace = fine_laplace(a)
        return react_terms(a[..., 1:-1, :, :], laplace, diffusivity, crop(src, h - 1)), h - 1

    def coarse_E(field):
        a, h = field
        laplace = coarse_laplace(a)
        return react_terms(a[..., 1:-1, :, :], laplace, diffusivity, crop(source_c, h - 1)), h - 1

    def full(field, field_E):
        h = min(field[1], field_E[1])
        return crop(field_E, h) - crop(decay, h) * crop(field, h), h

    def step_terms(states, terms):
        fulls = [full(states[j], terms[j]) for j in range(5)]
        hf = min(f[1] for f in fulls)
        out = []
        for m in range(4):
            h = min(hf, terms[m][1], states[m + 1][1])
            summed = spread_table[m][0] * crop(fulls[0], h)
            for j in range(1, 5):
                summed = summed + spread_table[m][j] * crop(fulls[j], h)
            own = (
                widths[m] * crop(decay, h) * crop(states[m + 1], h)
                - widths[m] * crop(terms[m], h)
            ) + summed
            out.append((own, h))
        return out

    def advance(begin, step_parts, last):
        swept = [begin]
        new_terms = [fine_E(begin)]
        for m in range(4):
            h = min(new_terms[m][1], step_parts[m][1])
            numerator = (
                crop(swept[m], h) + widths[m] * crop(new_terms[m], h)
            ) + crop(step_parts[m], h)
            swept.append((numerator / (1.0 + widths[m] * crop(decay, h)), h))
            new_terms.append(fine_E(swept[m + 1]))
        assert new_terms[4][1] >= 0
        new_full = [full(swept[j], new_terms[j]) for j in range(5)]
        hf = min(f[1] for f in new_full)
        coarse_vals = [restrict(swept[0]), restrict(swept[2]), restrict(swept[4])]
        integrated = []
        for c in range(2):
            summed = grouped_table[c][0] * crop(new_full[0], hf)
            for j in range(1, 5):
                summed = summed + grouped_table[c][j] * crop(new_full[j], hf)
            integrated.append(restrict((summed, hf)))
        half_step = 0.5 * step_length
        rc = crop(rate_c, 0)
        coarse_one = (
            crop(coarse_vals[0], 0)
            + half_step * rc * crop(coarse_vals[1], 0)
            + crop(integrated[0], 0)
        ) / (1.0 + half_step * rc)
        if last:
            ho = 0
            one, mid = packed_halo([(coarse_one, 1), (crop(coarse_vals[1], 0), 1)])
            low, late = coarse_vals[2], integrated[1]
        else:
            ho = 1
            one, mid, low, late = packed_halo(
                [
                    (coarse_one, 2),
                    (crop(coarse_vals[1], 0), 2),
                    (crop(coarse_vals[2], 0), 1),
                    (crop(integrated[1], 0), 1),
                ]
            )
        one_terms = coarse_E((crop(one, ho + 1), ho + 1))
        mid_terms = coarse_E((crop(mid, ho + 1), ho + 1))
        rc = crop(rate_c, ho)
        coarse_two = (
            crop(one, ho)
            + half_step * (one_terms[0] - mid_terms[0])
            + half_step * rc * crop(low, ho)
            + crop(late, ho)
        ) / (1.0 + half_step * rc)
        delta_one = crop(one, ho) - crop(mid, ho)
        delta_two = coarse_two - crop(low, ho)
        result = [swept[0]]
        for m in range(1, 5):
            if last and m < 4:
                result.append(None)
                continue
            fine = prolong(interp_table[m][1] * delta_one + interp_table[m][2] * delta_two)
            result.append((crop(swept[m], ho) + crop((fine, 2 * ho), ho), ho))
        return result, new_terms[0]

    own_ext = space_halo(own_start, hs)
    begin = (jnp.where(first_slice, own_ext, from_previous_slice(own_start, hs)), hs)
    state = (own_ext, hs)
    state_terms = fine_E(state)
    step_parts = step_terms([state] * 5, [state_terms] * 5)
    for k in range(ROUNDS):
        last = k + 1 == ROUNDS
        states, begin_terms = advance(begin, step_parts, last)
        if not last:
            terms = [begin_terms] + [fine_E(states[m]) for m in range(1, 5)]
            own_parts = step_terms(states, terms)
            step_parts = packed_halo(
                [(crop(own_parts[m], 0), hs - 1 - m) for m in range(4)]
            )
            prior = from_previous_slice(crop(states[4], 0), hs)
            begin = (jnp.where(first_slice, own_ext, prior), hs)
    return from_even_odd(crop(states[4], 0))[None]


def solution(mesh):
    placed = (
        P("tm", None, "space", None, None),
        P(None, "space", None, None),
        P(None, "space", None, None),
        P(),
    )
    return jax.shard_map(
        per_device,
        mesh=mesh,
        in_specs=placed,
        out_specs=P("tm", None, "space", None, None),
        check_vma=False,
    )
```

profile of v0, /device:TPU:0, one launch (start us, length us, event | category | flops | bytes accessed | tf_op | source)
XLA Modules:
  0.0 165.5 jit_solution(14766304964945698099)
XLA Ops:
  1.2 4.3 %collective-permute-start.2 = (f32[2,5,32,128]{3,2,1,0:T(8,128)S(1)}, f32[2,5,32,128]{3,2,1,0:T(8,128)S(1)}, u32[]{:S(2)}, u32[]{:S(2)}) collective-permute-start(f32[2,5,32,128]{3,2,1,0:T(8,128)S(1)} %get-tuple-element.430), channel_id=1, source_target_pairs={{0,9},{1,10},{2,11},{3,12},{4,13},{5,14},{6,15},{7,8},{8,17},{9,18... | collective-permute-start | bytes 491528 | tf_op jit(solution)/shard_map/ppermute | solution.py:108
  5.5 1.6 collective-permute-start
  7.1 6.2 %collective-permute-start.4 = (f32[2,5,32,128]{3,2,1,0:T(8,128)S(1)}, f32[2,5,32,128]{3,2,1,0:T(8,128)S(1)}, u32[]{:S(2)}, u32[]{:S(2)}) collective-permute-start(f32[2,5,32,128]{3,2,1,0:T(8,128)S(1)} %get-tuple-element.431), channel_id=1, source_target_pairs={{0,15},{1,8},{2,9},{3,10},{4,11},{5,12},{6,13},{7,14},{8,23},{9,16... | collective-permute-start | bytes 491528 | tf_op jit(solution)/shard_map/ppermute | solution.py:108
  14.0 2.1 %collective-permute-start.3 = (f32[2,8,32,128]{3,2,1,0:T(8,128)S(1)}, f32[2,8,32,128]{3,2,1,0:T(8,128)S(1)}, u32[]{:S(2)}, u32[]{:S(2)}) collective-permute-start(f32[2,8,32,128]{3,2,1,0:T(8,128)S(1)} %pad_maximum_fusion.15), channel_id=1, source_target_pairs={{0,8},{1,9},{2,10},{3,11},{4,12},{5,13},{6,14},{7,15},{8,16},{9,17... | collective-permute-start | bytes 786440 | tf_op jit(solution)/shard_map/ppermute | solution.py:108
  17.8 1.2 collective-permute-start.5
  19.0 3.6 %collective-permute-start.6 = (f32[2,2,4,32,128]{4,3,2,1,0:T(8,128)S(1)}, f32[2,2,4,32,128]{4,3,2,1,0:T(8,128)S(1)}, u32[]{:S(2)}, u32[]{:S(2)}) collective-permute-start(f32[2,2,4,32,128]{4,3,2,1,0:T(8,128)S(1)} %get-tuple-element.207), channel_id=1, source_target_pairs={{1,0},{2,1},{3,2},{4,3},{5,4},{6,5},{7,6},{0,7},{9,8},{10,9},{11,1... | collective-permute-start | bytes 786440 | tf_op jit(solution)/shard_map/ppermute | solution.py:92
  23.8 7.4 %collective-permute-done.5 = f32[2,2,4,32,128]{4,3,2,1,0:T(8,128)S(1)} collective-permute-done((f32[2,2,4,32,128]{4,3,2,1,0:T(8,128)S(1)}, f32[2,2,4,32,128]{4,3,2,1,0:T(8,128)S(1)}, u32[]{:S(2)}, u32[]{:S(2)}) %collective-permute-start.5) | collective-permute-done | bytes 262176 | tf_op jit(solution)/shard_map/ppermute | solution.py:91
  31.2 1.8 %collective-permute-done.6 = f32[2,2,4,32,128]{4,3,2,1,0:T(8,128)S(1)} collective-permute-done((f32[2,2,4,32,128]{4,3,2,1,0:T(8,128)S(1)}, f32[2,2,4,32,128]{4,3,2,1,0:T(8,128)S(1)}, u32[]{:S(2)}, u32[]{:S(2)}) %collective-permute-start.6) | collective-permute-done | bytes 262176 | tf_op jit(solution)/shard_map/ppermute | solution.py:92
  34.3 1.5 fusion.167
  37.8 1.3 fusion.183
  40.5 1.3 fusion.195
  43.0 1.3 fusion.209
  45.4 1.3 fusion.266
  47.5 4.2 %collective-permute-start.8 = (f32[2,6,16,128]{3,2,1,0:T(8,128)S(1)}, f32[2,6,16,128]{3,2,1,0:T(8,128)S(1)}, u32[]{:S(2)}, u32[]{:S(2)}) collective-permute-start(f32[2,6,16,128]{3,2,1,0:T(8,128)S(1)} %pad_maximum_fusion.57), channel_id=1, source_target_pairs={{1,0},{2,1},{3,2},{4,3},{5,4},{6,5},{7,6},{0,7},{9,8},{10,9},{11,1... | collective-permute-start | bytes 294920 | tf_op jit(solution)/shard_map/ppermute | solution.py:184
  51.8 2.2 %collective-permute-done.8 = f32[2,6,16,128]{3,2,1,0:T(8,128)S(1)} collective-permute-done((f32[2,6,16,128]{3,2,1,0:T(8,128)S(1)}, f32[2,6,16,128]{3,2,1,0:T(8,128)S(1)}, u32[]{:S(2)}, u32[]{:S(2)}) %collective-permute-start.8) | collective-permute-done | bytes 98336 | tf_op jit(solution)/shard_map/ppermute | solution.py:184
  54.0 5.1 %collective-permute-done.7 = f32[2,6,16,128]{3,2,1,0:T(8,128)S(1)} collective-permute-done((f32[2,6,16,128]{3,2,1,0:T(8,128)S(1)}, f32[2,6,16,128]{3,2,1,0:T(8,128)S(1)}, u32[]{:S(2)}, u32[]{:S(2)}) %collective-permute-start.7) | collective-permute-done | bytes 98336 | tf_op jit(solution)/shard_map/ppermute | solution.py:183
  59.8 1.2 fusion.425
  62.9 1.3 collective-permute-start.9
  64.2 6.8 %collective-permute-start.11 = (f32[2,5,32,128]{3,2,1,0:T(8,128)S(1)}, f32[2,5,32,128]{3,2,1,0:T(8,128)S(1)}, u32[]{:S(2)}, u32[]{:S(2)}) collective-permute-start(f32[2,5,32,128]{3,2,1,0:T(8,128)S(1)} %get-tuple-element.395), channel_id=1, source_target_pairs={{0,15},{1,8},{2,9},{3,10},{4,11},{5,12},{6,13},{7,14},{8,23},{9,16... | collective-permute-start | bytes 491528 | tf_op jit(solution)/shard_map/ppermute | solution.py:108
  71.5 1.3 fusion.247
  73.4 1.3 fusion.251
  75.6 1.4 collective-permute-start.10
  78.1 1.1 collective-permute-start.12
  80.3 1.4 fusion.159
  81.7 12.0 %collective-permute-done.13 = f32[2,10,32,128]{3,2,1,0:T(8,128)S(1)} collective-permute-done((f32[2,10,32,128]{3,2,1,0:T(8,128)S(1)}, f32[2,10,32,128]{3,2,1,0:T(8,128)S(1)}, u32[]{:S(2)}, u32[]{:S(2)}) %collective-permute-start.13) | collective-permute-done | bytes 327712 | tf_op jit(solution)/shard_map/ppermute | solution.py:184
  94.9 1.4 fusion.179
  98.2 1.3 fusion.191
  101.3 1.3 fusion.205
  104.2 1.3 fusion.238
  106.3 1.1 collective-permute-start.15
  108.5 2.5 %collective-permute-done.15 = f32[2,6,16,128]{3,2,1,0:T(8,128)S(1)} collective-permute-done((f32[2,6,16,128]{3,2,1,0:T(8,128)S(1)}, f32[2,6,16,128]{3,2,1,0:T(8,128)S(1)}, u32[]{:S(2)}, u32[]{:S(2)}) %collective-permute-start.15) | collective-permute-done | bytes 98336 | tf_op jit(solution)/shard_map/ppermute | solution.py:184
  111.0 3.8 %collective-permute-done.14 = f32[2,6,16,128]{3,2,1,0:T(8,128)S(1)} collective-permute-done((f32[2,6,16,128]{3,2,1,0:T(8,128)S(1)}, f32[2,6,16,128]{3,2,1,0:T(8,128)S(1)}, u32[]{:S(2)}, u32[]{:S(2)}) %collective-permute-start.14) | collective-permute-done | bytes 98336 | tf_op jit(solution)/shard_map/ppermute | solution.py:183
  115.5 1.2 fusion.417
  118.5 1.3 collective-permute-start.16
  119.8 2.6 %collective-permute-start.18 = (f32[2,5,32,128]{3,2,1,0:T(8,128)S(1)}, f32[2,5,32,128]{3,2,1,0:T(8,128)S(1)}, u32[]{:S(2)}, u32[]{:S(2)}) collective-permute-start(f32[2,5,32,128]{3,2,1,0:T(8,128)S(1)} %get-tuple-element.341), channel_id=1, source_target_pairs={{0,15},{1,8},{2,9},{3,10},{4,11},{5,12},{6,13},{7,14},{8,23},{9,16... | collective-permute-start | bytes 491528 | tf_op jit(solution)/shard_map/ppermute | solution.py:108
  123.0 1.3 fusion.222
  124.9 1.3 fusion.226
  127.1 1.3 collective-permute-start.17
  128.5 1.6 collective-permute-start.20
  131.7 1.4 fusion.139
  133.1 10.5 %collective-permute-done.20 = f32[2,10,32,128]{3,2,1,0:T(8,128)S(1)} collective-permute-done((f32[2,10,32,128]{3,2,1,0:T(8,128)S(1)}, f32[2,10,32,128]{3,2,1,0:T(8,128)S(1)}, u32[]{:S(2)}, u32[]{:S(2)}) %collective-permute-start.20) | collective-permute-done | bytes 327712 | tf_op jit(solution)/shard_map/ppermute | solution.py:184
  144.8 1.3 fusion.175
  148.1 1.3 fusion.187
  151.4 1.3 fusion.201
  154.3 1.3 fusion.213
  157.3 4.0 %collective-permute-start.21 = (f32[2,2,16,128]{3,2,1,0:T(8,128)S(1)}, f32[2,2,16,128]{3,2,1,0:T(8,128)S(1)}, u32[]{:S(2)}, u32[]{:S(2)}) collective-permute-start(f32[2,2,16,128]{3,2,1,0:T(8,128)S(1)} %pad_maximum_fusion.66), channel_id=1, source_target_pairs={{1,0},{2,1},{3,2},{4,3},{5,4},{6,5},{7,6},{0,7},{9,8},{10,9},{11,1... | collective-permute-start | bytes 98312 | tf_op jit(solution)/shard_map/ppermute | solution.py:184
  161.3 1.6 collective-permute-done.22
  163.2 1.2 fusion.429
  (347 shorter events, 41.7 us)
Async XLA Ops:
  0.0 1.1 copy-start.2
  1.2 16.6 %collective-permute-start.2 = (f32[2,5,32,128]{3,2,1,0:T(8,128)S(1)}, f32[2,5,32,128]{3,2,1,0:T(8,128)S(1)}, u32[]{:S(2)}, u32[]{:S(2)}) collective-permute-start(f32[2,5,32,128]{3,2,1,0:T(8,128)S(1)} %get-tuple-element.430), channel_id=1, source_target_pairs={{0,9},{1,10},{2,11},{3,12},{4,13},{5,14},{6,15},{7,8},{8,17},{9,18... | collective-permute-start | bytes 491528 | tf_op jit(solution)/shard_map/ppermute | solution.py:108
  5.5 13.5 %collective-permute-start = (f32[2,5,32,128]{3,2,1,0:T(8,128)S(1)}, f32[2,5,32,128]{3,2,1,0:T(8,128)S(1)}, u32[]{:S(2)}, u32[]{:S(2)}) collective-permute-start(f32[2,5,32,128]{3,2,1,0:T(8,128)S(1)} %get-tuple-element.430), channel_id=1, source_target_pairs={{0,1},{1,2},{2,3},{3,4},{4,5},{5,6},{6,7},{7,0},{8,9},{9,10},{10,1... | collective-permute-start | bytes 491528 | tf_op jit(solution)/shard_map/ppermute | solution.py:91
  7.1 9.1 %copy-start.3 = (f32[2,8,32,128]{3,2,1,0:T(8,128)S(1)}, f32[2,8,32,128]{3,2,1,0:T(8,128)}, u32[]{:S(2)}) copy-start(f32[2,8,32,128]{3,2,1,0:T(8,128)} %param.5) | copy-start | bytes 786436
  7.1 15.5 %collective-permute-start.4 = (f32[2,5,32,128]{3,2,1,0:T(8,128)S(1)}, f32[2,5,32,128]{3,2,1,0:T(8,128)S(1)}, u32[]{:S(2)}, u32[]{:S(2)}) collective-permute-start(f32[2,5,32,128]{3,2,1,0:T(8,128)S(1)} %get-tuple-element.431), channel_id=1, source_target_pairs={{0,15},{1,8},{2,9},{3,10},{4,11},{5,12},{6,13},{7,14},{8,23},{9,16... | collective-permute-start | bytes 491528 | tf_op jit(solution)/shard_map/ppermute | solution.py:108
  13.3 9.4 %collective-permute-start.1 = (f32[2,5,32,128]{3,2,1,0:T(8,128)S(1)}, f32[2,5,32,128]{3,2,1,0:T(8,128)S(1)}, u32[]{:S(2)}, u32[]{:S(2)}) collective-permute-start(f32[2,5,32,128]{3,2,1,0:T(8,128)S(1)} %get-tuple-element.431), channel_id=1, source_target_pairs={{1,0},{2,1},{3,2},{4,3},{5,4},{6,5},{7,6},{0,7},{9,8},{10,9},{11,1... | collective-permute-start | bytes 491528 | tf_op jit(solution)/shard_map/ppermute | solution.py:92
  14.0 2.3 %copy-start.4 = (f32[2,8,32,128]{3,2,1,0:T(8,128)S(1)}, f32[2,8,32,128]{3,2,1,0:T(8,128)}, u32[]{:S(2)}) copy-start(f32[2,8,32,128]{3,2,1,0:T(8,128)} %param.6) | copy-start | bytes 786436
  14.0 8.6 %collective-permute-start.3 = (f32[2,8,32,128]{3,2,1,0:T(8,128)S(1)}, f32[2,8,32,128]{3,2,1,0:T(8,128)S(1)}, u32[]{:S(2)}, u32[]{:S(2)}) collective-permute-start(f32[2,8,32,128]{3,2,1,0:T(8,128)S(1)} %pad_maximum_fusion.15), channel_id=1, source_target_pairs={{0,8},{1,9},{2,10},{3,11},{4,12},{5,13},{6,14},{7,15},{8,16},{9,17... | collective-permute-start | bytes 786440 | tf_op jit(solution)/shard_map/ppermute | solution.py:108
  16.6 0.7 copy-start.5
  17.8 13.4 %collective-permute-start.5 = (f32[2,2,4,32,128]{4,3,2,1,0:T(8,128)S(1)}, f32[2,2,4,32,128]{4,3,2,1,0:T(8,128)S(1)}, u32[]{:S(2)}, u32[]{:S(2)}) collective-permute-start(f32[2,2,4,32,128]{4,3,2,1,0:T(8,128)S(1)} %get-tuple-element.206), channel_id=1, source_target_pairs={{0,1},{1,2},{2,3},{3,4},{4,5},{5,6},{6,7},{7,0},{8,9},{9,10},{10,1... | collective-permute-start | bytes 786440 | tf_op jit(solution)/shard_map/ppermute | solution.py:91
  19.0 14.0 %collective-permute-start.6 = (f32[2,2,4,32,128]{4,3,2,1,0:T(8,128)S(1)}, f32[2,2,4,32,128]{4,3,2,1,0:T(8,128)S(1)}, u32[]{:S(2)}, u32[]{:S(2)}) collective-permute-start(f32[2,2,4,32,128]{4,3,2,1,0:T(8,128)S(1)} %get-tuple-element.207), channel_id=1, source_target_pairs={{1,0},{2,1},{3,2},{4,3},{5,4},{6,5},{7,6},{0,7},{9,8},{10,9},{11,1... | collective-permute-start | bytes 786440 | tf_op jit(solution)/shard_map/ppermute | solution.py:92
  47.5 6.5 %collective-permute-start.8 = (f32[2,6,16,128]{3,2,1,0:T(8,128)S(1)}, f32[2,6,16,128]{3,2,1,0:T(8,128)S(1)}, u32[]{:S(2)}, u32[]{:S(2)}) collective-permute-start(f32[2,6,16,128]{3,2,1,0:T(8,128)S(1)} %pad_maximum_fusion.57), channel_id=1, source_target_pairs={{1,0},{2,1},{3,2},{4,3},{5,4},{6,5},{7,6},{0,7},{9,8},{10,9},{11,1... | collective-permute-start | bytes 294920 | tf_op jit(solution)/shard_map/ppermute | solution.py:184
  51.7 7.4 %collective-permute-start.7 = (f32[2,6,16,128]{3,2,1,0:T(8,128)S(1)}, f32[2,6,16,128]{3,2,1,0:T(8,128)S(1)}, u32[]{:S(2)}, u32[]{:S(2)}) collective-permute-start(f32[2,6,16,128]{3,2,1,0:T(8,128)S(1)} %pad_maximum_fusion.56), channel_id=1, source_target_pairs={{0,1},{1,2},{2,3},{3,4},{4,5},{5,6},{6,7},{7,0},{8,9},{9,10},{10,1... | collective-permute-start | bytes 294920 | tf_op jit(solution)/shard_map/ppermute | solution.py:183
  62.9 16.3 %collective-permute-start.9 = (f32[2,5,32,128]{3,2,1,0:T(8,128)S(1)}, f32[2,5,32,128]{3,2,1,0:T(8,128)S(1)}, u32[]{:S(2)}, u32[]{:S(2)}) collective-permute-start(f32[2,5,32,128]{3,2,1,0:T(8,128)S(1)} %get-tuple-element.394), channel_id=1, source_target_pairs={{0,9},{1,10},{2,11},{3,12},{4,13},{5,14},{6,15},{7,8},{8,17},{9,18... | collective-permute-start | bytes 491528 | tf_op jit(solution)/shard_map/ppermute | solution.py:108
  64.2 15.0 %collective-permute-start.11 = (f32[2,5,32,128]{3,2,1,0:T(8,128)S(1)}, f32[2,5,32,128]{3,2,1,0:T(8,128)S(1)}, u32[]{:S(2)}, u32[]{:S(2)}) collective-permute-start(f32[2,5,32,128]{3,2,1,0:T(8,128)S(1)} %get-tuple-element.395), channel_id=1, source_target_pairs={{0,15},{1,8},{2,9},{3,10},{4,11},{5,12},{6,13},{7,14},{8,23},{9,16... | collective-permute-start | bytes 491528 | tf_op jit(solution)/shard_map/ppermute | solution.py:108
  75.6 3.6 %collective-permute-start.10 = (f32[2,8,32,128]{3,2,1,0:T(8,128)S(1)}, f32[2,8,32,128]{3,2,1,0:T(8,128)S(1)}, u32[]{:S(2)}, u32[]{:S(2)}) collective-permute-start(f32[2,8,32,128]{3,2,1,0:T(8,128)S(1)} %get-tuple-element.286), channel_id=1, source_target_pairs={{0,8},{1,9},{2,10},{3,11},{4,12},{5,13},{6,14},{7,15},{8,16},{9,17... | collective-permute-start | bytes 786440 | tf_op jit(solution)/shard_map/ppermute | solution.py:108
  77.0 16.7 %collective-permute-start.13 = (f32[2,10,32,128]{3,2,1,0:T(8,128)S(1)}, f32[2,10,32,128]{3,2,1,0:T(8,128)S(1)}, u32[]{:S(2)}, u32[]{:S(2)}) collective-permute-start(f32[2,10,32,128]{3,2,1,0:T(8,128)S(1)} %pad_maximum_fusion.25), channel_id=1, source_target_pairs={{1,0},{2,1},{3,2},{4,3},{5,4},{6,5},{7,6},{0,7},{9,8},{10,9},{11,1... | collective-permute-start | bytes 983048 | tf_op jit(solution)/shard_map/ppermute | solution.py:184
  78.1 15.7 %collective-permute-start.12 = (f32[2,10,32,128]{3,2,1,0:T(8,128)S(1)}, f32[2,10,32,128]{3,2,1,0:T(8,128)S(1)}, u32[]{:S(2)}, u32[]{:S(2)}) collective-permute-start(f32[2,10,32,128]{3,2,1,0:T(8,128)S(1)} %pad_maximum_fusion.24), channel_id=1, source_target_pairs={{0,1},{1,2},{2,3},{3,4},{4,5},{5,6},{6,7},{7,0},{8,9},{9,10},{10,1... | collective-permute-start | bytes 983048 | tf_op jit(solution)/shard_map/ppermute | solution.py:183
  93.7 2.6 %copy-start.1 = (f32[2,10,32,128]{3,2,1,0:T(8,128)}, f32[2,10,32,128]{3,2,1,0:T(8,128)S(1)}, u32[]{:S(2)}) copy-start(f32[2,10,32,128]{3,2,1,0:T(8,128)S(1)} %collective-permute-done.13) | copy-start | bytes 983044
  96.3 0.9 slice-start.3
  99.5 0.8 slice-start.4
  102.6 0.8 slice-start.5
  106.3 4.7 %collective-permute-start.15 = (f32[2,6,16,128]{3,2,1,0:T(8,128)S(1)}, f32[2,6,16,128]{3,2,1,0:T(8,128)S(1)}, u32[]{:S(2)}, u32[]{:S(2)}) collective-permute-start(f32[2,6,16,128]{3,2,1,0:T(8,128)S(1)} %pad_maximum_fusion.60), channel_id=1, source_target_pairs={{1,0},{2,1},{3,2},{4,3},{5,4},{6,5},{7,6},{0,7},{9,8},{10,9},{11,1... | collective-permute-start | bytes 294920 | tf_op jit(solution)/shard_map/ppermute | solution.py:184
  107.4 7.4 %collective-permute-start.14 = (f32[2,6,16,128]{3,2,1,0:T(8,128)S(1)}, f32[2,6,16,128]{3,2,1,0:T(8,128)S(1)}, u32[]{:S(2)}, u32[]{:S(2)}) collective-permute-start(f32[2,6,16,128]{3,2,1,0:T(8,128)S(1)} %pad_maximum_fusion.59), channel_id=1, source_target_pairs={{0,1},{1,2},{2,3},{3,4},{4,5},{5,6},{6,7},{7,0},{8,9},{9,10},{10,1... | collective-permute-start | bytes 294920 | tf_op jit(solution)/shard_map/ppermute | solution.py:183
  118.5 12.1 %collective-permute-start.16 = (f32[2,5,32,128]{3,2,1,0:T(8,128)S(1)}, f32[2,5,32,128]{3,2,1,0:T(8,128)S(1)}, u32[]{:S(2)}, u32[]{:S(2)}) collective-permute-start(f32[2,5,32,128]{3,2,1,0:T(8,128)S(1)} %get-tuple-element.340), channel_id=1, source_target_pairs={{0,9},{1,10},{2,11},{3,12},{4,13},{5,14},{6,15},{7,8},{8,17},{9,18... | collective-permute-start | bytes 491528 | tf_op jit(solution)/shard_map/ppermute | solution.py:108
  119.8 10.8 %collective-permute-start.18 = (f32[2,5,32,128]{3,2,1,0:T(8,128)S(1)}, f32[2,5,32,128]{3,2,1,0:T(8,128)S(1)}, u32[]{:S(2)}, u32[]{:S(2)}) collective-permute-start(f32[2,5,32,128]{3,2,1,0:T(8,128)S(1)} %get-tuple-element.341), channel_id=1, source_target_pairs={{0,15},{1,8},{2,9},{3,10},{4,11},{5,12},{6,13},{7,14},{8,23},{9,16... | collective-permute-start | bytes 491528 | tf_op jit(solution)/shard_map/ppermute | solution.py:108
  127.1 3.5 %collective-permute-start.17 = (f32[2,8,32,128]{3,2,1,0:T(8,128)S(1)}, f32[2,8,32,128]{3,2,1,0:T(8,128)S(1)}, u32[]{:S(2)}, u32[]{:S(2)}) collective-permute-start(f32[2,8,32,128]{3,2,1,0:T(8,128)S(1)} %get-tuple-element.287), channel_id=1, source_target_pairs={{0,8},{1,9},{2,10},{3,11},{4,12},{5,13},{6,14},{7,15},{8,16},{9,17... | collective-permute-start | bytes 786440 | tf_op jit(solution)/shard_map/ppermute | solution.py:108
  128.5 15.1 %collective-permute-start.20 = (f32[2,10,32,128]{3,2,1,0:T(8,128)S(1)}, f32[2,10,32,128]{3,2,1,0:T(8,128)S(1)}, u32[]{:S(2)}, u32[]{:S(2)}) collective-permute-start(f32[2,10,32,128]{3,2,1,0:T(8,128)S(1)} %pad_maximum_fusion.27), channel_id=1, source_target_pairs={{1,0},{2,1},{3,2},{4,3},{5,4},{6,5},{7,6},{0,7},{9,8},{10,9},{11,1... | collective-permute-start | bytes 983048 | tf_op jit(solution)/shard_map/ppermute | solution.py:184
  130.1 13.5 %collective-permute-start.19 = (f32[2,10,32,128]{3,2,1,0:T(8,128)S(1)}, f32[2,10,32,128]{3,2,1,0:T(8,128)S(1)}, u32[]{:S(2)}, u32[]{:S(2)}) collective-permute-start(f32[2,10,32,128]{3,2,1,0:T(8,128)S(1)} %pad_maximum_fusion.26), channel_id=1, source_target_pairs={{0,1},{1,2},{2,3},{3,4},{4,5},{5,6},{6,7},{7,0},{8,9},{9,10},{10,1... | collective-permute-start | bytes 983048 | tf_op jit(solution)/shard_map/ppermute | solution.py:183
  143.6 2.5 %copy-start = (f32[2,10,32,128]{3,2,1,0:T(8,128)}, f32[2,10,32,128]{3,2,1,0:T(8,128)S(1)}, u32[]{:S(2)}) copy-start(f32[2,10,32,128]{3,2,1,0:T(8,128)S(1)} %collective-permute-done.20) | copy-start | bytes 983044
  146.1 0.9 slice-start
  149.4 0.8 slice-start.1
  152.7 0.8 slice-start.2
  156.3 6.7 %collective-permute-start.22 = (f32[2,2,16,128]{3,2,1,0:T(8,128)S(1)}, f32[2,2,16,128]{3,2,1,0:T(8,128)S(1)}, u32[]{:S(2)}, u32[]{:S(2)}) collective-permute-start(f32[2,2,16,128]{3,2,1,0:T(8,128)S(1)} %pad_maximum_fusion.67), channel_id=1, source_target_pairs={{0,1},{1,2},{2,3},{3,4},{4,5},{5,6},{6,7},{7,0},{8,9},{9,10},{10,1... | collective-permute-start | bytes 98312 | tf_op jit(solution)/shard_map/ppermute | solution.py:183
  157.3 5.7 %collective-permute-start.21 = (f32[2,2,16,128]{3,2,1,0:T(8,128)S(1)}, f32[2,2,16,128]{3,2,1,0:T(8,128)S(1)}, u32[]{:S(2)}, u32[]{:S(2)}) collective-permute-start(f32[2,2,16,128]{3,2,1,0:T(8,128)S(1)} %pad_maximum_fusion.66), channel_id=1, source_target_pairs={{1,0},{2,1},{3,2},{4,3},{5,4},{6,5},{7,6},{0,7},{9,8},{10,9},{11,1... | collective-permute-start | bytes 98312 | tf_op jit(solution)/shard_map/ppermute | solution.py:184
where the time goes:
time: 167 us; the launch traced here: 165 us
  starting transfers between devices  49.9 us (30%)
  other arithmetic  47.3 us (28%)
  waiting for transfers between devices  47 us (28%)
  local copies, waits for them, and re-layouts  19.4 us (12%)
  between operations  1.95 us (1%)
    add x22, other arithmetic, react_terms(): diffusivity[0] * laplace[0] - product + source[0]  29.1 us
    ppermute x9, starting transfers between devices, moved(): return lax.ppermute(piece, axes, pairs)  27.3 us
    ppermute x5, waiting for transfers between devices, packed_halo(): after = lax.ppermute(firsts, 'space', down)  27.3 us
    ppermute x5, starting transfers between devices, packed_halo(): after = lax.ppermute(firsts, 'space', down)  11.9 us
    ppermute x5, waiting for transfers between devices, packed_halo(): before = lax.ppermute(lasts, 'space', up)  10.5 us
    slice x48, local copies, waits for them, and re-layouts, fine_laplace(): pair_z = jnp.roll(centre, -1, -1) + jnp.roll(centre, 1, -1)  7.9 us
    ppermute x2, waiting for transfers between devices, space_halo(): lax.ppermute(lax.slice_in_dim(a, rows - h, rows, axis=a.ndim - 3), 'space...  7.44 us
    sub x23, other arithmetic, fine_laplace(): return pair_x + pair_y + pair_z - 6.0 * centre  6.57 us
  transfers between devices with their start and end apart: 23, of which 9 were waited for; matrix products, arithmetic and copies ran while one was open for 10% of the time, Pallas kernels for 0%

commit v1 on v0

--- a/solution.py
+++ b/solution.py
@@ -3,6 +3,8 @@
 import jax
 import jax.numpy as jnp
 from jax import lax
+from jax.experimental import pallas as pl
+from jax.experimental.pallas import tpu as pltpu
 from jax.sharding import PartitionSpec as P
 
 ROUNDS = 3
@@ -170,6 +172,81 @@
     return jnp.concatenate([rows, rows], axis=-2)
 
 
+def kernel_laplace(f):
+    centre = f[:, 1:-1]
+    pair_x = f[:, 2:] + f[:, :-2]
+    half = centre.shape[2] // 2
+    even = centre[:, :, :half]
+    odd = centre[:, :, half:]
+    pair_y = jnp.concatenate(
+        [odd + pltpu.roll(odd, 1, 2), pltpu.roll(even, half - 1, 2) + even], axis=2
+    )
+    lanes = centre.shape[3]
+    pair_z = pltpu.roll(centre, lanes - 1, 3) + pltpu.roll(centre, 1, 3)
+    return pair_x + pair_y + pair_z - 6.0 * centre
+
+
+def sweep_kernel(diff_ref, b_ref, a0_ref, a1_ref, a2_ref, a3_ref, dec_ref, src_ref,
+                 n1_ref, n2_ref, n3_ref, n4_ref, e0_ref, s0_ref, s1_ref):
+    spread_table, grouped_table, interp_table, widths = node_tables()
+    rows = e0_ref.shape[1]
+    hs = (b_ref.shape[1] - rows) // 2
+    hd = (dec_ref.shape[1] - rows) // 2
+    d0 = diff_ref[0]
+    d1 = diff_ref[1]
+
+    def at(ref, h):
+        off = hd - h
+        return ref[:, off:off + rows + 2 * h]
+
+    def cut(v, have, h):
+        d = have - h
+        return v[:, d:v.shape[1] - d]
+
+    def terms(f, h):
+        laplace = kernel_laplace(f)
+        centre = f[:, 1:-1]
+        s = at(src_ref, h - 1)
+        product = centre[0] * centre[1] * centre[1]
+        return jnp.stack([d0 * laplace[0] - product + s[0], d1 * laplace[1] + product + s[1]])
+
+    parts = [a0_ref, a1_ref, a2_ref, a3_ref]
+    swept = [b_ref[...]]
+    found = []
+    for m in range(4):
+        have = hs - m
+        e = terms(swept[m], have)
+        found.append(e)
+        h = have - 1
+        numerator = (cut(swept[m], have, h) + widths[m] * e) + parts[m][...]
+        swept.append(numerator / (1.0 + widths[m] * at(dec_ref, h)))
+    found.append(terms(swept[4], hs - 4))
+    dec0 = at(dec_ref, 0)
+    fulls = [cut(found[j], hs - 1 - j, 0) - dec0 * cut(swept[j], hs - j, 0) for j in range(5)]
+    for c, out in ((0, s0_ref), (1, s1_ref)):
+        summed = grouped_table[c][0] * fulls[0]
+        for j in range(1, 5):
+            summed = summed + grouped_table[c][j] * fulls[j]
+        out[...] = summed
+    for m, out in ((1, n1_ref), (2, n2_ref), (3, n3_ref), (4, n4_ref)):
+        out[...] = cut(swept[m], hs - m, 1)
+    e0_ref[...] = cut(found[0], hs - 1, 0)
+
+
+def fine_sweep(diffusivity, begin, parts, decay, src):
+    rows = begin.shape[1] - 2 * START_HALO
+    shape = begin.shape
+    wide = jax.ShapeDtypeStruct((shape[0], rows + 2) + shape[2:], jnp.float32)
+    own = jax.ShapeDtypeStruct((shape[0], rows) + shape[2:], jnp.float32)
+    vmem = pl.BlockSpec(memory_space=pltpu.VMEM)
+    return pl.pallas_call(
+        sweep_kernel,
+        out_shape=(wide, wide, wide, wide, own, own, own),
+        in_specs=[pl.BlockSpec(memory_space=pltpu.SMEM)] + [vmem] * 7,
+        out_specs=(vmem,) * 7,
+    )(diffusivity, begin, *parts, decay, src)
+
+
 def packed_halo(fields):
     size = lax.axis_size("space")
     rows = fields[0][0].shape[-3]
@@ -247,25 +324,14 @@
         return out
 
     def advance(begin, step_parts, last):
-        swept = [begin]
-        new_terms = [fine_E(begin)]
-        for m in range(4):
-            h = min(new_terms[m][1], step_parts[m][1])
-            numerator = (
-                crop(swept[m], h) + widths[m] * crop(new_terms[m], h)
-            ) + crop(step_parts[m], h)
-            swept.append((numerator / (1.0 + widths[m] * crop(decay, h)), h))
-            new_terms.append(fine_E(swept[m + 1]))
-        assert new_terms[4][1] >= 0
-        new_full = [full(swept[j], new_terms[j]) for j in range(5)]
-        hf = min(f[1] for f in new_full)
+        parts = [crop(step_parts[m], hs - 1 - m) for m in range(4)]
+        n1, n2, n3, n4, e0, s0, s1 = fine_sweep(
+            diffusivity, begin[0], parts, decay[0], src[0]
+        )
+        swept = [begin, (n1, 1), (n2, 1), (n3, 1), (n4, 1)]
+        begin_terms = (e0, 0)
+        integrated = [restrict((s0, 0)), restrict((s1, 0))]
         coarse_vals = [restrict(swept[0]), restrict(swept[2]), restrict(swept[4])]
-        integrated = []
-        for c in range(2):
-            summed = grouped_table[c][0] * crop(new_full[0], hf)
-            for j in range(1, 5):
-                summed = summed + grouped_table[c][j] * crop(new_full[j], hf)
-            integrated.append(restrict((summed, hf)))
         half_step = 0.5 * step_length
         rc = crop(rate_c, 0)
         coarse_one = (
@@ -305,7 +371,7 @@
                 continue
             fine = prolong(interp_table[m][1] * delta_one + interp_table[m][2] * delta_two)
             result.append((crop(swept[m], ho) + crop((fine, 2 * ho), ho), ho))
-        return result, new_terms[0]
+        return result, begin_terms
 
     own_ext = space_halo(own_start, hs)
     begin = (jnp.where(first_slice, own_ext, from_previous_slice(own_start, hs)), hs)

time: 167 us -> 178 us (1.066)
  other arithmetic: 47.3 us -> 33.2 us
  Pallas kernels: 0 us -> 13.7 us
  local copies, waits for them, and re-layouts: 19.4 us -> 26.6 us
  waiting for transfers between devices: 47 us -> 52.3 us
    add x22 -> x8, other arithmetic: 29.1 us -> 11.5 us  [react_terms(): diffusivity[0] * laplace[0] - product + source[0]]
    ppermute x9, waiting for transfers between devices: 0.02 us -> 14.3 us  [moved(): return lax.ppermute(piece, axes, pairs)]
    pallas_call x0 -> x3, Pallas kernels: none -> 13.7 us  [fine_sweep(): pl.pallas_call(sweep_kernel, out_shape=(wide, wide, wide, wide, own, own,...]
    ppermute x5, waiting for transfers between devices: 27.3 us -> 15.9 us  [packed_halo(): after = lax.ppermute(firsts, 'space', down)]
    unnamed x12 -> x56, local copies, waits for them, and re-layouts: 0.66 us -> 11.8 us
    ppermute x2, waiting for transfers between devices: 1.79 us -> 9.93 us  [space_halo(): lax.ppermute(lax.slice_in_dim(a, 0, h, axis=a.ndim - 3), 'space', down)]
    ppermute x9, starting transfers between devices: 27.3 us -> 19.6 us  [moved(): return lax.ppermute(piece, axes, pairs)]
    ppermute x2, waiting for transfers between devices: 7.44 us -> 0.01 us  [space_halo(): lax.ppermute(lax.slice_in_dim(a, rows - h, rows, axis=a.ndim - 3), 'space...]
  transfers between devices with their start and end apart: 23 -> 23, of which waited for: 9 -> 10; matrix products, arithmetic and copies ran while one was open for 10% -> 8% of each run, Pallas kernels for 0% -> 0%
where the time goes in v1:
time: 178 us; the launch traced here: 177 us
  waiting for transfers between devices  52.3 us (29%)
  starting transfers between devices  49.7 us (28%)
  other arithmetic  33.2 us (19%)
  local copies, waits for them, and re-layouts  26.6 us (15%)
  Pallas kernels  13.7 us (8%)
    ppermute x9, starting transfers between devices, moved(): return lax.ppermute(piece, axes, pairs)  19.6 us
    ppermute x5, starting transfers between devices, packed_halo(): after = lax.ppermute(firsts, 'space', down)  17 us
    ppermute x5, waiting for transfers between devices, packed_halo(): after = lax.ppermute(firsts, 'space', down)  15.9 us
    ppermute x9, waiting for transfers between devices, moved(): return lax.ppermute(piece, axes, pairs)  14.3 us
    pallas_call x3, Pallas kernels, fine_sweep(): pl.pallas_call(sweep_kernel, out_shape=(wide, wide, wide, wide, own, own,...  13.7 us
    ppermute x5, waiting for transfers between devices, packed_halo(): before = lax.ppermute(lasts, 'space', up)  12.2 us
    unnamed x56, local copies, waits for them, and re-layouts  11.8 us
    add x8, other arithmetic, react_terms(): diffusivity[0] * laplace[0] - product + source[0]  11.5 us
  transfers between devices with their start and end apart: 23, of which 10 were waited for; matrix products, arithmetic and copies ran while one was open for 8% of the time, Pallas kernels for 0%

profile of v1, /device:TPU:0, one launch (start us, length us, event | category | flops | bytes accessed | tf_op | source)
XLA Modules:
  0.0 177.1 jit_solution(15599814559437947518)
XLA Ops:
  0.0 1.0 slice.1743
  1.2 6.1 %collective-permute-start.1 = (f32[2,5,32,128]{3,2,1,0:T(8,128)S(1)}, f32[2,5,32,128]{3,2,1,0:T(8,128)S(1)}, u32[]{:S(2)}, u32[]{:S(2)}) collective-permute-start(f32[2,5,32,128]{3,2,1,0:T(8,128)S(1)} %get-tuple-element.248), channel_id=1, source_target_pairs={{1,0},{2,1},{3,2},{4,3},{5,4},{6,5},{7,6},{0,7},{9,8},{10,9},{11,1... | collective-permute-start | bytes 491528 | tf_op jit(solution)/shard_map/ppermute | solution.py:94
  7.3 1.6 collective-permute-start.4
  8.8 1.6 collective-permute-start
  10.4 3.4 %collective-permute-start.2 = (f32[2,5,32,128]{3,2,1,0:T(8,128)S(1)}, f32[2,5,32,128]{3,2,1,0:T(8,128)S(1)}, u32[]{:S(2)}, u32[]{:S(2)}) collective-permute-start(f32[2,5,32,128]{3,2,1,0:T(8,128)S(1)} %get-tuple-element.247), channel_id=1, source_target_pairs={{0,9},{1,10},{2,11},{3,12},{4,13},{5,14},{6,15},{7,8},{8,17},{9,18... | collective-permute-start | bytes 491528 | tf_op jit(solution)/shard_map/ppermute | solution.py:110
  13.9 2.1 %collective-permute-start.3 = (f32[2,8,32,128]{3,2,1,0:T(8,128)S(1)}, f32[2,8,32,128]{3,2,1,0:T(8,128)S(1)}, u32[]{:S(2)}, u32[]{:S(2)}) collective-permute-start(f32[2,8,32,128]{3,2,1,0:T(8,128)S(1)} %pad_maximum_fusion.9), channel_id=1, source_target_pairs={{0,8},{1,9},{2,10},{3,11},{4,12},{5,13},{6,14},{7,15},{8,16},{9,17... | collective-permute-start | bytes 786440 | tf_op jit(solution)/shard_map/ppermute | solution.py:110
  17.8 4.2 %collective-permute-start.6 = (f32[2,2,4,32,128]{4,3,2,1,0:T(8,128)S(1)}, f32[2,2,4,32,128]{4,3,2,1,0:T(8,128)S(1)}, u32[]{:S(2)}, u32[]{:S(2)}) collective-permute-start(f32[2,2,4,32,128]{4,3,2,1,0:T(8,128)S(1)} %get-tuple-element.130), channel_id=1, source_target_pairs={{1,0},{2,1},{3,2},{4,3},{5,4},{6,5},{7,6},{0,7},{9,8},{10,9},{11,1... | collective-permute-start | bytes 786440 | tf_op jit(solution)/shard_map/ppermute | solution.py:94
  23.1 9.9 %collective-permute-done.6 = f32[2,2,4,32,128]{4,3,2,1,0:T(8,128)S(1)} collective-permute-done((f32[2,2,4,32,128]{4,3,2,1,0:T(8,128)S(1)}, f32[2,2,4,32,128]{4,3,2,1,0:T(8,128)S(1)}, u32[]{:S(2)}, u32[]{:S(2)}) %collective-permute-start.6) | collective-permute-done | bytes 262176 | tf_op jit(solution)/shard_map/ppermute | solution.py:94
  33.2 1.5 fusion.40
  34.9 1.6 broadcast_multiply_fusion.6
  36.5 1.1 slice_add_fusion.1.a1_ref
  37.5 1.0 slice_add_fusion.6.a2_ref
  38.6 1.2 fusion.263
  40.7 4.6 %shard_map.46 = (f32[2,10,32,128]{3,2,1,0:T(8,128)}, f32[2,10,32,128]{3,2,1,0:T(8,128)}, f32[2,10,32,128]{3,2,1,0:T(8,128)}, f32[2,10,32,128]{3,2,1,0:T(8,128)},...) custom-call(f32[2]{0:T(128)} %diff_ref.5, f32[2,18,32,128]{3,2,1,0:T(8,128)} %copy-done.4, ...), custom_call_target="tpu_custom_call" | custom-call | tf_op jit(solution)/shard_map/pallas_call | solution.py:242
  45.3 1.0 fusion.206
  48.5 3.4 %collective-permute-start.8 = (f32[2,6,16,128]{3,2,1,0:T(8,128)S(1)}, f32[2,6,16,128]{3,2,1,0:T(8,128)S(1)}, u32[]{:S(2)}, u32[]{:S(2)}) collective-permute-start(f32[2,6,16,128]{3,2,1,0:T(8,128)S(1)} %pad_maximum_fusion.53), channel_id=1, source_target_pairs={{1,0},{2,1},{3,2},{4,3},{5,4},{6,5},{7,6},{0,7},{9,8},{10,9},{11,1... | collective-permute-start | bytes 294920 | tf_op jit(solution)/shard_map/ppermute | solution.py:261
  52.0 2.1 %collective-permute-done.8 = f32[2,6,16,128]{3,2,1,0:T(8,128)S(1)} collective-permute-done((f32[2,6,16,128]{3,2,1,0:T(8,128)S(1)}, f32[2,6,16,128]{3,2,1,0:T(8,128)S(1)}, u32[]{:S(2)}, u32[]{:S(2)}) %collective-permute-start.8) | collective-permute-done | bytes 98336 | tf_op jit(solution)/shard_map/ppermute | solution.py:261
  54.1 5.1 %collective-permute-done.7 = f32[2,6,16,128]{3,2,1,0:T(8,128)S(1)} collective-permute-done((f32[2,6,16,128]{3,2,1,0:T(8,128)S(1)}, f32[2,6,16,128]{3,2,1,0:T(8,128)S(1)}, u32[]{:S(2)}, u32[]{:S(2)}) %collective-permute-start.7) | collective-permute-done | bytes 98336 | tf_op jit(solution)/shard_map/ppermute | solution.py:260
  60.0 1.3 fusion.246
  64.7 1.3 collective-permute-start.11
  67.4 1.5 fusion.73
  69.4 1.5 fusion.77
  71.0 1.3 add_add_fusion.8
  72.7 3.7 %collective-permute-start.10 = (f32[2,8,32,128]{3,2,1,0:T(8,128)S(1)}, f32[2,8,32,128]{3,2,1,0:T(8,128)S(1)}, u32[]{:S(2)}, u32[]{:S(2)}) collective-permute-start(f32[2,8,32,128]{3,2,1,0:T(8,128)S(1)} %get-tuple-element.139), channel_id=1, source_target_pairs={{0,8},{1,9},{2,10},{3,11},{4,12},{5,13},{6,14},{7,15},{8,16},{9,17... | collective-permute-start | bytes 786440 | tf_op jit(solution)/shard_map/ppermute | solution.py:110
  76.4 3.6 %collective-permute-start.9 = (f32[2,5,32,128]{3,2,1,0:T(8,128)S(1)}, f32[2,5,32,128]{3,2,1,0:T(8,128)S(1)}, u32[]{:S(2)}, u32[]{:S(2)}) collective-permute-start(f32[2,5,32,128]{3,2,1,0:T(8,128)S(1)} %get-tuple-element.223), channel_id=1, source_target_pairs={{0,9},{1,10},{2,11},{3,12},{4,13},{5,14},{6,15},{7,8},{8,17},{9,18... | collective-permute-start | bytes 491528 | tf_op jit(solution)/shard_map/ppermute | solution.py:110
  80.1 3.3 %collective-permute-start.13 = (f32[2,10,32,128]{3,2,1,0:T(8,128)S(1)}, f32[2,10,32,128]{3,2,1,0:T(8,128)S(1)}, u32[]{:S(2)}, u32[]{:S(2)}) collective-permute-start(f32[2,10,32,128]{3,2,1,0:T(8,128)S(1)} %pad_maximum_fusion.19), channel_id=1, source_target_pairs={{1,0},{2,1},{3,2},{4,3},{5,4},{6,5},{7,6},{0,7},{9,8},{10,9},{11,1... | collective-permute-start | bytes 983048 | tf_op jit(solution)/shard_map/ppermute | solution.py:261
  83.7 7.2 %collective-permute-done.9 = f32[2,5,32,128]{3,2,1,0:T(8,128)S(1)} collective-permute-done((f32[2,5,32,128]{3,2,1,0:T(8,128)S(1)}, f32[2,5,32,128]{3,2,1,0:T(8,128)S(1)}, u32[]{:S(2)}, u32[]{:S(2)}) %collective-permute-start.9) | collective-permute-done | bytes 163872 | tf_op jit(solution)/shard_map/ppermute | solution.py:110
  91.8 5.7 %collective-permute-done.13 = f32[2,10,32,128]{3,2,1,0:T(8,128)S(1)} collective-permute-done((f32[2,10,32,128]{3,2,1,0:T(8,128)S(1)}, f32[2,10,32,128]{3,2,1,0:T(8,128)S(1)}, u32[]{:S(2)}, u32[]{:S(2)}) %collective-permute-start.13) | collective-permute-done | bytes 327712 | tf_op jit(solution)/shard_map/ppermute | solution.py:261
  103.2 4.6 %shard_map.47 = (f32[2,10,32,128]{3,2,1,0:T(8,128)}, f32[2,10,32,128]{3,2,1,0:T(8,128)}, f32[2,10,32,128]{3,2,1,0:T(8,128)}, f32[2,10,32,128]{3,2,1,0:T(8,128)},...) custom-call(f32[2]{0:T(128)} %diff_ref.5, f32[2,18,32,128]{3,2,1,0:T(8,128)} %copy-done.5, ...), custom_call_target="tpu_custom_call" | custom-call | tf_op jit(solution)/shard_map/pallas_call | solution.py:242
  107.8 1.0 fusion.184
  111.0 2.7 %collective-permute-start.15 = (f32[2,6,16,128]{3,2,1,0:T(8,128)S(1)}, f32[2,6,16,128]{3,2,1,0:T(8,128)S(1)}, u32[]{:S(2)}, u32[]{:S(2)}) collective-permute-start(f32[2,6,16,128]{3,2,1,0:T(8,128)S(1)} %pad_maximum_fusion.56), channel_id=1, source_target_pairs={{1,0},{2,1},{3,2},{4,3},{5,4},{6,5},{7,6},{0,7},{9,8},{10,9},{11,1... | collective-permute-start | bytes 294920 | tf_op jit(solution)/shard_map/ppermute | solution.py:261
  113.7 2.1 %collective-permute-done.15 = f32[2,6,16,128]{3,2,1,0:T(8,128)S(1)} collective-permute-done((f32[2,6,16,128]{3,2,1,0:T(8,128)S(1)}, f32[2,6,16,128]{3,2,1,0:T(8,128)S(1)}, u32[]{:S(2)}, u32[]{:S(2)}) %collective-permute-start.15) | collective-permute-done | bytes 98336 | tf_op jit(solution)/shard_map/ppermute | solution.py:261
  115.9 5.1 %collective-permute-done.14 = f32[2,6,16,128]{3,2,1,0:T(8,128)S(1)} collective-permute-done((f32[2,6,16,128]{3,2,1,0:T(8,128)S(1)}, f32[2,6,16,128]{3,2,1,0:T(8,128)S(1)}, u32[]{:S(2)}, u32[]{:S(2)}) %collective-permute-start.14) | collective-permute-done | bytes 98336 | tf_op jit(solution)/shard_map/ppermute | solution.py:260
  121.7 1.3 fusion.238
  126.6 1.3 collective-permute-start.18
  129.3 1.5 fusion.56
  131.3 1.5 fusion.52
  132.8 1.3 add_add_fusion.4
  134.6 1.3 collective-permute-start.17
  135.9 1.3 collective-permute-start.16
  137.3 3.8 %collective-permute-start.20 = (f32[2,10,32,128]{3,2,1,0:T(8,128)S(1)}, f32[2,10,32,128]{3,2,1,0:T(8,128)S(1)}, u32[]{:S(2)}, u32[]{:S(2)}) collective-permute-start(f32[2,10,32,128]{3,2,1,0:T(8,128)S(1)} %pad_maximum_fusion.22), channel_id=1, source_target_pairs={{1,0},{2,1},{3,2},{4,3},{5,4},{6,5},{7,6},{0,7},{9,8},{10,9},{11,1... | collective-permute-start | bytes 983048 | tf_op jit(solution)/shard_map/ppermute | solution.py:261
  141.2 7.1 %collective-permute-done.16 = f32[2,5,32,128]{3,2,1,0:T(8,128)S(1)} collective-permute-done((f32[2,5,32,128]{3,2,1,0:T(8,128)S(1)}, f32[2,5,32,128]{3,2,1,0:T(8,128)S(1)}, u32[]{:S(2)}, u32[]{:S(2)}) %collective-permute-start.16) | collective-permute-done | bytes 163872 | tf_op jit(solution)/shard_map/ppermute | solution.py:110
  149.2 6.0 %collective-permute-done.20 = f32[2,10,32,128]{3,2,1,0:T(8,128)S(1)} collective-permute-done((f32[2,10,32,128]{3,2,1,0:T(8,128)S(1)}, f32[2,10,32,128]{3,2,1,0:T(8,128)S(1)}, u32[]{:S(2)}, u32[]{:S(2)}) %collective-permute-start.20) | collective-permute-done | bytes 327712 | tf_op jit(solution)/shard_map/ppermute | solution.py:261
  160.9 4.6 %shard_map.48 = (f32[2,10,32,128]{3,2,1,0:T(8,128)}, f32[2,10,32,128]{3,2,1,0:T(8,128)}, f32[2,10,32,128]{3,2,1,0:T(8,128)}, f32[2,10,32,128]{3,2,1,0:T(8,128)},...) custom-call(f32[2]{0:T(128)} %diff_ref.5, f32[2,18,32,128]{3,2,1,0:T(8,128)} %copy-done.6, ...), custom_call_target="tpu_custom_call" | custom-call | tf_op jit(solution)/shard_map/pallas_call | solution.py:242
  165.4 1.0 slice.2115
  168.7 3.8 %collective-permute-start.21 = (f32[2,2,16,128]{3,2,1,0:T(8,128)S(1)}, f32[2,2,16,128]{3,2,1,0:T(8,128)S(1)}, u32[]{:S(2)}, u32[]{:S(2)}) collective-permute-start(f32[2,2,16,128]{3,2,1,0:T(8,128)S(1)} %pad_maximum_fusion.62), channel_id=1, source_target_pairs={{1,0},{2,1},{3,2},{4,3},{5,4},{6,5},{7,6},{0,7},{9,8},{10,9},{11,1... | collective-permute-start | bytes 98312 | tf_op jit(solution)/shard_map/ppermute | solution.py:261
  172.5 1.9 %collective-permute-done.22 = f32[2,2,16,128]{3,2,1,0:T(8,128)S(1)} collective-permute-done((f32[2,2,16,128]{3,2,1,0:T(8,128)S(1)}, f32[2,2,16,128]{3,2,1,0:T(8,128)S(1)}, u32[]{:S(2)}, u32[]{:S(2)}) %collective-permute-start.22) | collective-permute-done | bytes 32800 | tf_op jit(solution)/shard_map/ppermute | solution.py:260
  174.6 1.4 fusion.250
  (294 shorter events, 38.1 us)
Async XLA Ops:
  0.0 1.1 copy-start.23
  1.2 16.6 %collective-permute-start.1 = (f32[2,5,32,128]{3,2,1,0:T(8,128)S(1)}, f32[2,5,32,128]{3,2,1,0:T(8,128)S(1)}, u32[]{:S(2)}, u32[]{:S(2)}) collective-permute-start(f32[2,5,32,128]{3,2,1,0:T(8,128)S(1)} %get-tuple-element.248), channel_id=1, source_target_pairs={{1,0},{2,1},{3,2},{4,3},{5,4},{6,5},{7,6},{0,7},{9,8},{10,9},{11,1... | collective-permute-start | bytes 491528 | tf_op jit(solution)/shard_map/ppermute | solution.py:94
  7.3 14.7 %collective-permute-start.4 = (f32[2,5,32,128]{3,2,1,0:T(8,128)S(1)}, f32[2,5,32,128]{3,2,1,0:T(8,128)S(1)}, u32[]{:S(2)}, u32[]{:S(2)}) collective-permute-start(f32[2,5,32,128]{3,2,1,0:T(8,128)S(1)} %get-tuple-element.248), channel_id=1, source_target_pairs={{0,15},{1,8},{2,9},{3,10},{4,11},{5,12},{6,13},{7,14},{8,23},{9,16... | collective-permute-start | bytes 491528 | tf_op jit(solution)/shard_map/ppermute | solution.py:110
  8.8 7.2 %copy-start.24 = (f32[2,8,32,128]{3,2,1,0:T(8,128)S(1)}, f32[2,8,32,128]{3,2,1,0:T(8,128)}, u32[]{:S(2)}) copy-start(f32[2,8,32,128]{3,2,1,0:T(8,128)} %param.5) | copy-start | bytes 786436
  8.8 13.1 %collective-permute-start = (f32[2,5,32,128]{3,2,1,0:T(8,128)S(1)}, f32[2,5,32,128]{3,2,1,0:T(8,128)S(1)}, u32[]{:S(2)}, u32[]{:S(2)}) collective-permute-start(f32[2,5,32,128]{3,2,1,0:T(8,128)S(1)} %get-tuple-element.247), channel_id=1, source_target_pairs={{0,1},{1,2},{2,3},{3,4},{4,5},{5,6},{6,7},{7,0},{8,9},{9,10},{10,1... | collective-permute-start | bytes 491528 | tf_op jit(solution)/shard_map/ppermute | solution.py:93
  10.4 11.6 %collective-permute-start.2 = (f32[2,5,32,128]{3,2,1,0:T(8,128)S(1)}, f32[2,5,32,128]{3,2,1,0:T(8,128)S(1)}, u32[]{:S(2)}, u32[]{:S(2)}) collective-permute-start(f32[2,5,32,128]{3,2,1,0:T(8,128)S(1)} %get-tuple-element.247), channel_id=1, source_target_pairs={{0,9},{1,10},{2,11},{3,12},{4,13},{5,14},{6,15},{7,8},{8,17},{9,18... | collective-permute-start | bytes 491528 | tf_op jit(solution)/shard_map/ppermute | solution.py:110
  13.9 2.4 %copy-start.25 = (f32[2,8,32,128]{3,2,1,0:T(8,128)S(1)}, f32[2,8,32,128]{3,2,1,0:T(8,128)}, u32[]{:S(2)}) copy-start(f32[2,8,32,128]{3,2,1,0:T(8,128)} %param.6) | copy-start | bytes 786436
  13.9 8.1 %collective-permute-start.3 = (f32[2,8,32,128]{3,2,1,0:T(8,128)S(1)}, f32[2,8,32,128]{3,2,1,0:T(8,128)S(1)}, u32[]{:S(2)}, u32[]{:S(2)}) collective-permute-start(f32[2,8,32,128]{3,2,1,0:T(8,128)S(1)} %pad_maximum_fusion.9), channel_id=1, source_target_pairs={{0,8},{1,9},{2,10},{3,11},{4,12},{5,13},{6,14},{7,15},{8,16},{9,17... | collective-permute-start | bytes 786440 | tf_op jit(solution)/shard_map/ppermute | solution.py:110
  17.8 15.3 %collective-permute-start.6 = (f32[2,2,4,32,128]{4,3,2,1,0:T(8,128)S(1)}, f32[2,2,4,32,128]{4,3,2,1,0:T(8,128)S(1)}, u32[]{:S(2)}, u32[]{:S(2)}) collective-permute-start(f32[2,2,4,32,128]{4,3,2,1,0:T(8,128)S(1)} %get-tuple-element.130), channel_id=1, source_target_pairs={{1,0},{2,1},{3,2},{4,3},{5,4},{6,5},{7,6},{0,7},{9,8},{10,9},{11,1... | collective-permute-start | bytes 786440 | tf_op jit(solution)/shard_map/ppermute | solution.py:94
  22.0 11.1 %collective-permute-start.5 = (f32[2,2,4,32,128]{4,3,2,1,0:T(8,128)S(1)}, f32[2,2,4,32,128]{4,3,2,1,0:T(8,128)S(1)}, u32[]{:S(2)}, u32[]{:S(2)}) collective-permute-start(f32[2,2,4,32,128]{4,3,2,1,0:T(8,128)S(1)} %get-tuple-element.129), channel_id=1, source_target_pairs={{0,1},{1,2},{2,3},{3,4},{4,5},{5,6},{6,7},{7,0},{8,9},{9,10},{10,1... | collective-permute-start | bytes 786440 | tf_op jit(solution)/shard_map/ppermute | solution.py:93
  22.1 17.7 %copy-start.4 = (f32[2,18,32,128]{3,2,1,0:T(8,128)}, f32[2,18,32,128]{3,2,1,0:T(8,128)S(1)}, u32[]{:S(2)}) copy-start(f32[2,18,32,128]{3,2,1,0:T(8,128)S(1)} %get-tuple-element.109.b_ref) | copy-start | bytes 1769476
  45.3 1.1 copy-start.10
  46.5 1.0 copy-start.8
  47.5 0.9 copy-start.21
  48.5 5.6 %collective-permute-start.8 = (f32[2,6,16,128]{3,2,1,0:T(8,128)S(1)}, f32[2,6,16,128]{3,2,1,0:T(8,128)S(1)}, u32[]{:S(2)}, u32[]{:S(2)}) collective-permute-start(f32[2,6,16,128]{3,2,1,0:T(8,128)S(1)} %pad_maximum_fusion.53), channel_id=1, source_target_pairs={{1,0},{2,1},{3,2},{4,3},{5,4},{6,5},{7,6},{0,7},{9,8},{10,9},{11,1... | collective-permute-start | bytes 294920 | tf_op jit(solution)/shard_map/ppermute | solution.py:261
  51.9 7.4 %collective-permute-start.7 = (f32[2,6,16,128]{3,2,1,0:T(8,128)S(1)}, f32[2,6,16,128]{3,2,1,0:T(8,128)S(1)}, u32[]{:S(2)}, u32[]{:S(2)}) collective-permute-start(f32[2,6,16,128]{3,2,1,0:T(8,128)S(1)} %pad_maximum_fusion.52), channel_id=1, source_target_pairs={{0,1},{1,2},{2,3},{3,4},{4,5},{5,6},{6,7},{7,0},{8,9},{9,10},{10,1... | collective-permute-start | bytes 294920 | tf_op jit(solution)/shard_map/ppermute | solution.py:260
  62.2 1.0 copy-start.16
  63.4 1.0 copy-start.14
  64.7 19.0 %collective-permute-start.11 = (f32[2,5,32,128]{3,2,1,0:T(8,128)S(1)}, f32[2,5,32,128]{3,2,1,0:T(8,128)S(1)}, u32[]{:S(2)}, u32[]{:S(2)}) collective-permute-start(f32[2,5,32,128]{3,2,1,0:T(8,128)S(1)} %get-tuple-element.224), channel_id=1, source_target_pairs={{0,15},{1,8},{2,9},{3,10},{4,11},{5,12},{6,13},{7,14},{8,23},{9,16... | collective-permute-start | bytes 491528 | tf_op jit(solution)/shard_map/ppermute | solution.py:110
  66.4 1.0 copy-start.2
  69.4 1.6 copy-start
  69.4 1.6 copy-start.18
  72.7 18.2 %collective-permute-start.10 = (f32[2,8,32,128]{3,2,1,0:T(8,128)S(1)}, f32[2,8,32,128]{3,2,1,0:T(8,128)S(1)}, u32[]{:S(2)}, u32[]{:S(2)}) collective-permute-start(f32[2,8,32,128]{3,2,1,0:T(8,128)S(1)} %get-tuple-element.139), channel_id=1, source_target_pairs={{0,8},{1,9},{2,10},{3,11},{4,12},{5,13},{6,14},{7,15},{8,16},{9,17... | collective-permute-start | bytes 786440 | tf_op jit(solution)/shard_map/ppermute | solution.py:110
  76.4 14.5 %collective-permute-start.9 = (f32[2,5,32,128]{3,2,1,0:T(8,128)S(1)}, f32[2,5,32,128]{3,2,1,0:T(8,128)S(1)}, u32[]{:S(2)}, u32[]{:S(2)}) collective-permute-start(f32[2,5,32,128]{3,2,1,0:T(8,128)S(1)} %get-tuple-element.223), channel_id=1, source_target_pairs={{0,9},{1,10},{2,11},{3,12},{4,13},{5,14},{6,15},{7,8},{8,17},{9,18... | collective-permute-start | bytes 491528 | tf_op jit(solution)/shard_map/ppermute | solution.py:110
  80.1 17.4 %collective-permute-start.13 = (f32[2,10,32,128]{3,2,1,0:T(8,128)S(1)}, f32[2,10,32,128]{3,2,1,0:T(8,128)S(1)}, u32[]{:S(2)}, u32[]{:S(2)}) collective-permute-start(f32[2,10,32,128]{3,2,1,0:T(8,128)S(1)} %pad_maximum_fusion.19), channel_id=1, source_target_pairs={{1,0},{2,1},{3,2},{4,3},{5,4},{6,5},{7,6},{0,7},{9,8},{10,9},{11,1... | collective-permute-start | bytes 983048 | tf_op jit(solution)/shard_map/ppermute | solution.py:261
  83.5 14.1 %collective-permute-start.12 = (f32[2,10,32,128]{3,2,1,0:T(8,128)S(1)}, f32[2,10,32,128]{3,2,1,0:T(8,128)S(1)}, u32[]{:S(2)}, u32[]{:S(2)}) collective-permute-start(f32[2,10,32,128]{3,2,1,0:T(8,128)S(1)} %pad_maximum_fusion.18), channel_id=1, source_target_pairs={{0,1},{1,2},{2,3},{3,4},{4,5},{5,6},{6,7},{7,0},{8,9},{9,10},{10,1... | collective-permute-start | bytes 983048 | tf_op jit(solution)/shard_map/ppermute | solution.py:260
  97.5 0.9 copy-start.12
  107.8 1.1 copy-start.7
  108.9 1.0 copy-start.9
  109.9 0.9 copy-start.22
  111.0 4.9 %collective-permute-start.15 = (f32[2,6,16,128]{3,2,1,0:T(8,128)S(1)}, f32[2,6,16,128]{3,2,1,0:T(8,128)S(1)}, u32[]{:S(2)}, u32[]{:S(2)}) collective-permute-start(f32[2,6,16,128]{3,2,1,0:T(8,128)S(1)} %pad_maximum_fusion.56), channel_id=1, source_target_pairs={{1,0},{2,1},{3,2},{4,3},{5,4},{6,5},{7,6},{0,7},{9,8},{10,9},{11,1... | collective-permute-start | bytes 294920 | tf_op jit(solution)/shard_map/ppermute | solution.py:261
  113.6 7.4 %collective-permute-start.14 = (f32[2,6,16,128]{3,2,1,0:T(8,128)S(1)}, f32[2,6,16,128]{3,2,1,0:T(8,128)S(1)}, u32[]{:S(2)}, u32[]{:S(2)}) collective-permute-start(f32[2,6,16,128]{3,2,1,0:T(8,128)S(1)} %pad_maximum_fusion.55), channel_id=1, source_target_pairs={{0,1},{1,2},{2,3},{3,4},{4,5},{5,6},{6,7},{7,0},{8,9},{9,10},{10,1... | collective-permute-start | bytes 294920 | tf_op jit(solution)/shard_map/ppermute | solution.py:260
  123.2 1.0 copy-start.17
  125.2 1.0 copy-start.15
  126.6 14.6 %collective-permute-start.18 = (f32[2,5,32,128]{3,2,1,0:T(8,128)S(1)}, f32[2,5,32,128]{3,2,1,0:T(8,128)S(1)}, u32[]{:S(2)}, u32[]{:S(2)}) collective-permute-start(f32[2,5,32,128]{3,2,1,0:T(8,128)S(1)} %get-tuple-element.182), channel_id=1, source_target_pairs={{0,15},{1,8},{2,9},{3,10},{4,11},{5,12},{6,13},{7,14},{8,23},{9,16... | collective-permute-start | bytes 491528 | tf_op jit(solution)/shard_map/ppermute | solution.py:110
  128.2 1.0 copy-start.3
  131.3 1.6 copy-start.1
  131.3 1.6 copy-start.19
  134.6 13.7 %collective-permute-start.17 = (f32[2,8,32,128]{3,2,1,0:T(8,128)S(1)}, f32[2,8,32,128]{3,2,1,0:T(8,128)S(1)}, u32[]{:S(2)}, u32[]{:S(2)}) collective-permute-start(f32[2,8,32,128]{3,2,1,0:T(8,128)S(1)} %get-tuple-element.140), channel_id=1, source_target_pairs={{0,8},{1,9},{2,10},{3,11},{4,12},{5,13},{6,14},{7,15},{8,16},{9,17... | collective-permute-start | bytes 786440 | tf_op jit(solution)/shard_map/ppermute | solution.py:110
  135.9 12.4 %collective-permute-start.16 = (f32[2,5,32,128]{3,2,1,0:T(8,128)S(1)}, f32[2,5,32,128]{3,2,1,0:T(8,128)S(1)}, u32[]{:S(2)}, u32[]{:S(2)}) collective-permute-start(f32[2,5,32,128]{3,2,1,0:T(8,128)S(1)} %get-tuple-element.181), channel_id=1, source_target_pairs={{0,9},{1,10},{2,11},{3,12},{4,13},{5,14},{6,15},{7,8},{8,17},{9,18... | collective-permute-start | bytes 491528 | tf_op jit(solution)/shard_map/ppermute | solution.py:110
  137.3 17.8 %collective-permute-start.20 = (f32[2,10,32,128]{3,2,1,0:T(8,128)S(1)}, f32[2,10,32,128]{3,2,1,0:T(8,128)S(1)}, u32[]{:S(2)}, u32[]{:S(2)}) collective-permute-start(f32[2,10,32,128]{3,2,1,0:T(8,128)S(1)} %pad_maximum_fusion.22), channel_id=1, source_target_pairs={{1,0},{2,1},{3,2},{4,3},{5,4},{6,5},{7,6},{0,7},{9,8},{10,9},{11,1... | collective-permute-start | bytes 983048 | tf_op jit(solution)/shard_map/ppermute | solution.py:261
  141.1 14.1 %collective-permute-start.19 = (f32[2,10,32,128]{3,2,1,0:T(8,128)S(1)}, f32[2,10,32,128]{3,2,1,0:T(8,128)S(1)}, u32[]{:S(2)}, u32[]{:S(2)}) collective-permute-start(f32[2,10,32,128]{3,2,1,0:T(8,128)S(1)} %pad_maximum_fusion.21), channel_id=1, source_target_pairs={{0,1},{1,2},{2,3},{3,4},{4,5},{5,6},{6,7},{7,0},{8,9},{9,10},{10,1... | collective-permute-start | bytes 983048 | tf_op jit(solution)/shard_map/ppermute | solution.py:260
  155.1 0.9 copy-start.13
  166.5 1.0 copy-start.26
  167.5 5.0 %copy-start.11 = (f32[2,10,32,128]{3,2,1,0:T(8,128)S(1)}, f32[2,10,32,128]{3,2,1,0:T(8,128)}, u32[]{:S(2)}) copy-start(f32[2,10,32,128]{3,2,1,0:T(8,128)} %get-tuple-element.37) | copy-start | bytes 983044
  167.7 6.7 %collective-permute-start.22 = (f32[2,2,16,128]{3,2,1,0:T(8,128)S(1)}, f32[2,2,16,128]{3,2,1,0:T(8,128)S(1)}, u32[]{:S(2)}, u32[]{:S(2)}) collective-permute-start(f32[2,2,16,128]{3,2,1,0:T(8,128)S(1)} %pad_maximum_fusion.63), channel_id=1, source_target_pairs={{0,1},{1,2},{2,3},{3,4},{4,5},{5,6},{6,7},{7,0},{8,9},{9,10},{10,1... | collective-permute-start | bytes 98312 | tf_op jit(solution)/shard_map/ppermute | solution.py:260
  168.7 5.7 %collective-permute-start.21 = (f32[2,2,16,128]{3,2,1,0:T(8,128)S(1)}, f32[2,2,16,128]{3,2,1,0:T(8,128)S(1)}, u32[]{:S(2)}, u32[]{:S(2)}) collective-permute-start(f32[2,2,16,128]{3,2,1,0:T(8,128)S(1)} %pad_maximum_fusion.62), channel_id=1, source_target_pairs={{1,0},{2,1},{3,2},{4,3},{5,4},{6,5},{7,6},{0,7},{9,8},{10,9},{11,1... | collective-permute-start | bytes 98312 | tf_op jit(solution)/shard_map/ppermute | solution.py:261
  174.6 1.4 copy-start.20
  (9 other events, 7.3 us)

commit v2 on v1

--- a/solution.py
+++ b/solution.py
@@ -186,7 +186,7 @@
     return pair_x + pair_y + pair_z - 6.0 * centre
 
 
-def sweep_kernel(diff_ref, b_ref, a0_ref, a1_ref, a2_ref, a3_ref, dec_ref, src_ref,
+def sweep_kernel(diff_ref, b_ref, own_ref, before_ref, after_ref, dec_ref, src_ref,
                  n1_ref, n2_ref, n3_ref, n4_ref, e0_ref, s0_ref, s1_ref):
     spread_table, grouped_table, interp_table, widths = node_tables()
     rows = e0_ref.shape[1]
@@ -210,7 +210,17 @@
         product = centre[0] * centre[1] * centre[1]
         return jnp.stack([d0 * laplace[0] - product + s[0], d1 * laplace[1] + product + s[1]])
 
-    parts = [a0_ref, a1_ref, a2_ref, a3_ref]
+    parts = []
+    offset = 0
+    for m in range(4):
+        w = hs - 1 - m
+        parts.append(
+            jnp.concatenate(
+                [before_ref[:, offset:offset + w], own_ref[m], after_ref[:, offset:offset + w]],
+                axis=1,
+            )
+        )
+        offset += w
     swept = [b_ref[...]]
     found = []
     for m in range(4):
@@ -218,7 +228,7 @@
         e = terms(swept[m], have)
         found.append(e)
         h = have - 1
-        numerator = (cut(swept[m], have, h) + widths[m] * e) + parts[m][...]
+        numerator = (cut(swept[m], have, h) + widths[m] * e) + parts[m]
         swept.append(numerator / (1.0 + widths[m] * at(dec_ref, h)))
     found.append(terms(swept[4], hs - 4))
     dec0 = at(dec_ref, 0)
@@ -242,9 +252,120 @@
     return pl.pallas_call(
         sweep_kernel,
         out_shape=(wide, wide, wide, wide, own, own, own),
-        in_specs=[pl.BlockSpec(memory_space=pltpu.SMEM)] + [vmem] * 7,
+        in_specs=[pl.BlockSpec(memory_space=pltpu.SMEM)] + [vmem] * 6,
         out_specs=(vmem,) * 7,
     )(diffusivity, begin, *parts, decay, src)
+
+
+def coarse_kernel_laplace(f):
+    centre = f[:, 1:-1]
+    pair_x = f[:, 2:] + f[:, :-2]
+    ny = centre.shape[2]
+    lanes = centre.shape[3]
+    pair_y = pltpu.roll(centre, ny - 1, 2) + pltpu.roll(centre, 1, 2)
+    pair_z = pltpu.roll(centre, lanes - 1, 3) + pltpu.roll(centre, 1, 3)
+    return (pair_x - 2.0 * centre) * 0.25 + (pair_y - 2.0 * centre) * 0.25 + (
+        pair_z - 2.0 * centre
+    )
+
+
+def finish_kernel(diff_ref, one_ref, mid_ref, low_ref, late_ref, rate_ref, csrc_ref,
+                  n1_ref, n2_ref, n3_ref, n4_ref, b_ref, e0_ref, dec_ref, src_ref, *outs):
+    spread_table, grouped_table, interp_table, widths = node_tables()
+    last = len(outs) == 1
+    rows = e0_ref.shape[1]
+    crows = rows // 2
+    ho = (low_ref.shape[1] - crows) // 2
+    hcr = (rate_ref.shape[1] - crows) // 2
+    hd = (dec_ref.shape[1] - rows) // 2
+    hs = (b_ref.shape[1] - rows) // 2
+    d0 = diff_ref[0]
+    d1 = diff_ref[1]
+
+    def at(ref, h, size, have):
+        off = have - h
+        return ref[:, off:off + size + 2 * h]
+
+    def cut(v, have, h):
+        d = have - h
+        return v[:, d:v.shape[1] - d]
+
+    def react(centre, laplace, s):
+        product = centre[0] * centre[1] * centre[1]
+        return jnp.stack([d0 * laplace[0] - product + s[0], d1 * laplace[1] + product + s[1]])
+
+    def coarse_terms(v):
+        return react(v[:, 1:-1], coarse_kernel_laplace(v), at(csrc_ref, ho, crows, hcr))
+
+    half_step = 0.5 * step_length
+    one = one_ref[...]
+    mid = mid_ref[...]
+    rc = at(rate_ref, ho, crows, hcr)
+    coarse_two = (
+        cut(one, ho + 1, ho)
+        + half_step * (coarse_terms(one) - coarse_terms(mid))
+        + half_step * rc * low_ref[...]
+        + late_ref[...]
+    ) / (1.0 + half_step * rc)
+    delta_one = cut(one, ho + 1, ho) - cut(mid, ho + 1, ho)
+    delta_two = coarse_two - low_ref[...]
+
+    def prolonged(c):
+        shape = c.shape
+        doubled = jnp.broadcast_to(c[:, :, None], (shape[0], shape[1], 2) + shape[2:])
+        doubled = doubled.reshape((shape[0], 2 * shape[1]) + shape[2:])
+        return jnp.concatenate([doubled, doubled], axis=2)
+
+    news = {}
+    for m, ref in ((1, n1_ref), (2, n2_ref), (3, n3_ref), (4, n4_ref)):
+        if last and m < 4:
+            continue
+        fine = prolonged(interp_table[m][1] * delta_one + interp_table[m][2] * delta_two)
+        news[m] = cut(ref[...], 1, ho) + cut(fine, 2 * ho, ho)
+    if last:
+        outs[0][...] = news[4]
+        return
+    own_out, lasts_out, firsts_out, u4_out = outs
+    src1 = at(src_ref, 0, rows, hd)
+    dec0 = at(dec_ref, 0, rows, hd)
+    states = [at(b_ref, 0, rows, hs)] + [cut(news[m], 1, 0) for m in range(1, 5)]
+    terms = [e0_ref[...]] + [
+        react(cut(news[m], 1, 0), kernel_laplace(news[m]), src1) for m in range(1, 5)
+    ]
+    fulls = [terms[j] - dec0 * states[j] for j in range(5)]
+    offset = 0
+    for m in range(4):
+        summed = spread_table[m][0] * fulls[0]
+        for j in range(1, 5):
+            summed = summed + spread_table[m][j] * fulls[j]
+        part = (widths[m] * dec0 * states[m + 1] - widths[m] * terms[m]) + summed
+        own_out[m] = part
+        w = hs - 1 - m
+        lasts_out[:, offset:offset + w] = part[:, rows - w:]
+        firsts_out[:, offset:offset + w] = part[:, :w]
+        offset += w
+    u4_out[...] = states[4]
+
+
+def finish_round(diffusivity, coarse, rate_c, source_c, swept, e0, decay, src, last):
+    begin = swept[0]
+    shape = begin.shape
+    rows = e0.shape[1]
+    field = jax.ShapeDtypeStruct((shape[0], rows) + shape[2:], jnp.float32)
+    if last:
+        out_shape = (field,)
+    else:
+        sent = sum(START_HALO - 1 - m for m in range(4))
+        edge = jax.ShapeDtypeStruct((shape[0], sent) + shape[2:], jnp.float32)
+        out_shape = (jax.ShapeDtypeStruct((4,) + field.shape, jnp.float32), edge, edge, field)
+    vmem = pl.BlockSpec(memory_space=pltpu.VMEM)
+    args = (diffusivity, *coarse, rate_c, source_c, *swept[1:], begin, e0, decay, src)
+    return pl.pallas_call(
+        finish_kernel,
+        out_shape=out_shape,
+        in_specs=[pl.BlockSpec(memory_space=pltpu.SMEM)] + [vmem] * (len(args) - 1),
+        out_specs=(vmem,) * len(out_shape),
+    )(*args)
 
 
 def packed_halo(fields):
@@ -323,73 +444,63 @@
             out.append((own, h))
         return out
 
-    def advance(begin, step_parts, last):
-        parts = [crop(step_parts[m], hs - 1 - m) for m in range(4)]
-        n1, n2, n3, n4, e0, s0, s1 = fine_sweep(
-            diffusivity, begin[0], parts, decay[0], src[0]
-        )
-        swept = [begin, (n1, 1), (n2, 1), (n3, 1), (n4, 1)]
-        begin_terms = (e0, 0)
-        integrated = [restrict((s0, 0)), restrict((s1, 0))]
-        coarse_vals = [restrict(swept[0]), restrict(swept[2]), restrict(swept[4])]
+    def advance(begin, pieces, last):
+        n1, n2, n3, n4, e0, s0, s1 = fine_sweep(diffusivity, begin[0], pieces, decay[0], src[0])
+        coarse_vals = [restrict(begin), restrict((n2, 1)), restrict((n4, 1))]
+        coarse_vals = [crop(v, 0) for v in coarse_vals]
+        integrated = [crop(restrict((s0, 0)), 0), crop(restrict((s1, 0)), 0)]
         half_step = 0.5 * step_length
         rc = crop(rate_c, 0)
         coarse_one = (
-            crop(coarse_vals[0], 0)
-            + half_step * rc * crop(coarse_vals[1], 0)
-            + crop(integrated[0], 0)
+            coarse_vals[0] + half_step * rc * coarse_vals[1] + integrated[0]
         ) / (1.0 + half_step * rc)
         if last:
-            ho = 0
-            one, mid = packed_halo([(coarse_one, 1), (crop(coarse_vals[1], 0), 1)])
-            low, late = coarse_vals[2], integrated[1]
+            one, mid = packed_halo([(coarse_one, 1), (coarse_vals[1], 1)])
+            coarse = (one[0], mid[0], coarse_vals[2], integrated[1])
         else:
-            ho = 1
             one, mid, low, late = packed_halo(
-                [
-                    (coarse_one, 2),
-                    (crop(coarse_vals[1], 0), 2),
-                    (crop(coarse_vals[2], 0), 1),
-                    (crop(integrated[1], 0), 1),
-                ]
+                [(coarse_one, 2), (coarse_vals[1], 2), (coarse_vals[2], 1), (integrated[1], 1)]
             )
-        one_terms = coarse_E((crop(one, ho + 1), ho + 1))
-        mid_terms = coarse_E((crop(mid, ho + 1), ho + 1))
-        rc = crop(rate_c, ho)
-        coarse_two = (
-            crop(one, ho)
-            + half_step * (one_terms[0] - mid_terms[0])
-            + half_step * rc * crop(low, ho)
-            + crop(late, ho)
-        ) / (1.0 + half_step * rc)
-        delta_one = crop(one, ho) - crop(mid, ho)
-        delta_two = coarse_two - crop(low, ho)
-        result = [swept[0]]
-        for m in range(1, 5):
-            if last and m < 4:
-                result.append(None)
-                continue
-            fine = prolong(interp_table[m][1] * delta_one + interp_table[m][2] * delta_two)
-            result.append((crop(swept[m], ho) + crop((fine, 2 * ho), ho), ho))
-        return result, begin_terms
-
+            coarse = (one[0], mid[0], low[0], late[0])
+        return finish_round(
+            diffusivity, coarse, rate_c[0], source_c[0],
+            (begin[0], n1, n2, n3, n4), e0, decay[0], src[0], last,
+        )
+
+    size = lax.axis_size("space")
+    up = [(i, (i + 1) % size) for i in range(size)]
+    down = [((i + 1) % size, i) for i in range(size)]
+    rows = own_start.shape[-3]
     own_ext = space_halo(own_start, hs)
     begin = (jnp.where(first_slice, own_ext, from_previous_slice(own_start, hs)), hs)
     state = (own_ext, hs)
     state_terms = fine_E(state)
-    step_parts = step_terms([state] * 5, [state_terms] * 5)
+    parts = step_terms([state] * 5, [state_terms] * 5)
+    wide = [crop(parts[m], hs - 1) for m in range(4)]
+    edge = hs - 1
+    pieces = (
+        jnp.stack([lax.slice_in_dim(p, edge, edge + rows, axis=1) for p in wide]),
+        jnp.concatenate(
+            [lax.slice_in_dim(p, m, edge, axis=1) for m, p in enumerate(wide)], axis=1
+        ),
+        jnp.concatenate(
+            [lax.slice_in_dim(p, edge + rows, edge + rows + edge - m, axis=1)
+             for m, p in enumerate(wide)], axis=1
+        ),
+    )
     for k in range(ROUNDS):
         last = k + 1 == ROUNDS
-        states, begin_terms = advance(begin, step_parts, last)
+        outs = advance(begin, pieces, last)
         if not last:
-            terms = [begin_terms] + [fine_E(states[m]) for m in range(1, 5)]
-            own_parts = step_terms(states, terms)
-            step_parts = packed_halo(
-                [(crop(own_parts[m], 0), hs - 1 - m) for m in range(4)]
+            own4, lasts, firsts, u4 = outs
+            pieces = (
+                own4,
+                lax.ppermute(lasts, "space", up),
+                lax.ppermute(firsts, "space", down),
             )
-            prior = from_previous_slice(crop(states[4], 0), hs)
+            prior = from_previous_slice(u4, hs)
             begin = (jnp.where(first_slice, own_ext, prior), hs)
-    return from_even_odd(crop(states[4], 0))[None]
+    return from_even_odd(outs[0])[None]
 
 
 def solution(mesh):

time: 178 us -> 171 us (0.961)
  other arithmetic: 33.2 us -> 17.7 us
  Pallas kernels: 13.7 us -> 25.9 us
  local copies, waits for them, and re-layouts: 26.6 us -> 16.9 us
  starting transfers between devices: 49.7 us -> 56.7 us
    ppermute x0 -> x4, waiting for transfers between devices: none -> 22.4 us  [the longest x2 14.9 us: per_device(): lax.ppermute(lasts, 'space', up)]
    ppermute x9, waiting for transfers between devices: 14.3 us -> 0.02 us  [moved(): return lax.ppermute(piece, axes, pairs)]
    pallas_call x0 -> x3, Pallas kernels: none -> 12.2 us  [finish_round(): pl.pallas_call(finish_kernel, out_shape=out_shape, in_specs=[pl.BlockSpec...]
    ppermute x9, starting transfers between devices: 19.6 us -> 31.4 us  [moved(): return lax.ppermute(piece, axes, pairs)]
    add x8 -> x1, other arithmetic: 11.5 us -> 1.46 us  [react_terms(): diffusivity[0] * laplace[0] - product + source[0]]
    ppermute x5 -> x3, waiting for transfers between devices: 15.9 us -> 6.36 us  [packed_halo(): after = lax.ppermute(firsts, 'space', down)]
    ppermute x0 -> x4, starting transfers between devices: none -> 9.52 us  [the longest x2 9.4 us: per_device(): lax.ppermute(firsts, 'space', down)]
    ppermute x5 -> x3, starting transfers between devices: 17 us -> 8.43 us  [packed_halo(): after = lax.ppermute(firsts, 'space', down)]
  transfers between devices with their start and end apart: 23 -> 23, of which waited for: 10 -> 12; matrix products, arithmetic and copies ran while one was open for 8% -> 3% of each run, Pallas kernels for 0% -> 0%
where the time goes in v2:
time: 171 us
  starting transfers between devices  56.7 us (33%)
  waiting for transfers between devices  52.8 us (31%)
  Pallas kernels  25.9 us (15%)
  other arithmetic  17.7 us (10%)
  local copies, waits for them, and re-layouts  16.9 us (10%)
    ppermute x9, starting transfers between devices, moved(): return lax.ppermute(piece, axes, pairs)  31.4 us
    ppermute x2, waiting for transfers between devices, per_device(): lax.ppermute(lasts, 'space', up)  14.9 us
    ppermute x3, waiting for transfers between devices, packed_halo(): before = lax.ppermute(lasts, 'space', up)  14.8 us
    pallas_call x3, Pallas kernels, fine_sweep(): pl.pallas_call(sweep_kernel, out_shape=(wide, wide, wide, wide, own, own,...  13.7 us
    pallas_call x3, Pallas kernels, finish_round(): pl.pallas_call(finish_kernel, out_shape=out_shape, in_specs=[pl.BlockSpec...  12.2 us
    ppermute x2, starting transfers between devices, per_device(): lax.ppermute(firsts, 'space', down)  9.4 us
    unnamed x54, local copies, waits for them, and re-layouts  8.69 us
    ppermute x3, starting transfers between devices, packed_halo(): after = lax.ppermute(firsts, 'space', down)  8.43 us
  transfers between devices with their start and end apart: 23, of which 12 were waited for; matrix products, arithmetic and copies ran while one was open for 3% of the time, Pallas kernels for 0%

profile of v2, /device:TPU:0, one launch (start us, length us, event | category | flops | bytes accessed | tf_op | source)
XLA Modules:
  0.0 170.7 jit_solution(9042099758122558251)
XLA Ops:
  0.0 1.0 slice.657
  1.2 4.3 %collective-permute-start.2 = (f32[2,5,32,128]{3,2,1,0:T(8,128)S(1)}, f32[2,5,32,128]{3,2,1,0:T(8,128)S(1)}, u32[]{:S(2)}, u32[]{:S(2)}) collective-permute-start(f32[2,5,32,128]{3,2,1,0:T(8,128)S(1)} %get-tuple-element.108), channel_id=1, source_target_pairs={{0,9},{1,10},{2,11},{3,12},{4,13},{5,14},{6,15},{7,8},{8,17},{9,18... | collective-permute-start | bytes 491528 | tf_op jit(solution)/shard_map/ppermute | solution.py:110
  5.5 1.6 collective-permute-start
  7.1 6.2 %collective-permute-start.4 = (f32[2,5,32,128]{3,2,1,0:T(8,128)S(1)}, f32[2,5,32,128]{3,2,1,0:T(8,128)S(1)}, u32[]{:S(2)}, u32[]{:S(2)}) collective-permute-start(f32[2,5,32,128]{3,2,1,0:T(8,128)S(1)} %get-tuple-element.109), channel_id=1, source_target_pairs={{0,15},{1,8},{2,9},{3,10},{4,11},{5,12},{6,13},{7,14},{8,23},{9,16... | collective-permute-start | bytes 491528 | tf_op jit(solution)/shard_map/ppermute | solution.py:110
  14.0 2.1 %collective-permute-start.3 = (f32[2,8,32,128]{3,2,1,0:T(8,128)S(1)}, f32[2,8,32,128]{3,2,1,0:T(8,128)S(1)}, u32[]{:S(2)}, u32[]{:S(2)}) collective-permute-start(f32[2,8,32,128]{3,2,1,0:T(8,128)S(1)} %pad_maximum_fusion.4), channel_id=1, source_target_pairs={{0,8},{1,9},{2,10},{3,11},{4,12},{5,13},{6,14},{7,15},{8,16},{9,17... | collective-permute-start | bytes 786440 | tf_op jit(solution)/shard_map/ppermute | solution.py:110
  17.9 1.2 collective-permute-start.5
  19.1 3.6 %collective-permute-start.6 = (f32[2,2,4,32,128]{4,3,2,1,0:T(8,128)S(1)}, f32[2,2,4,32,128]{4,3,2,1,0:T(8,128)S(1)}, u32[]{:S(2)}, u32[]{:S(2)}) collective-permute-start(f32[2,2,4,32,128]{4,3,2,1,0:T(8,128)S(1)} %get-tuple-element.101), channel_id=1, source_target_pairs={{1,0},{2,1},{3,2},{4,3},{5,4},{6,5},{7,6},{0,7},{9,8},{10,9},{11,1... | collective-permute-start | bytes 786440 | tf_op jit(solution)/shard_map/ppermute | solution.py:94
  23.8 7.4 %collective-permute-done.5 = f32[2,2,4,32,128]{4,3,2,1,0:T(8,128)S(1)} collective-permute-done((f32[2,2,4,32,128]{4,3,2,1,0:T(8,128)S(1)}, f32[2,2,4,32,128]{4,3,2,1,0:T(8,128)S(1)}, u32[]{:S(2)}, u32[]{:S(2)}) %collective-permute-start.5) | collective-permute-done | bytes 262176 | tf_op jit(solution)/shard_map/ppermute | solution.py:93
  31.2 1.8 %collective-permute-done.6 = f32[2,2,4,32,128]{4,3,2,1,0:T(8,128)S(1)} collective-permute-done((f32[2,2,4,32,128]{4,3,2,1,0:T(8,128)S(1)}, f32[2,2,4,32,128]{4,3,2,1,0:T(8,128)S(1)}, u32[]{:S(2)}, u32[]{:S(2)}) %collective-permute-start.6) | collective-permute-done | bytes 262176 | tf_op jit(solution)/shard_map/ppermute | solution.py:94
  33.1 1.5 fusion.6
  35.6 1.3 fusion.104
  38.5 1.1 pad_maximum_fusion.1.own_ref
  40.3 4.6 %shard_map.46 = (f32[2,10,32,128]{3,2,1,0:T(8,128)}, f32[2,10,32,128]{3,2,1,0:T(8,128)}, f32[2,10,32,128]{3,2,1,0:T(8,128)}, f32[2,10,32,128]{3,2,1,0:T(8,128)},...) custom-call(f32[2]{0:T(128)} %diff_ref.11, f32[2,18,32,128]{3,2,1,0:T(8,128)} %copy-done, ...), custom_call_target="tpu_custom_call" | custom-call | tf_op jit(solution)/shard_map/pallas_call | solution.py:252
  44.9 1.0 fusion.82
  46.0 0.9 copy-done.17
  48.0 4.2 %collective-permute-start.8 = (f32[2,6,16,128]{3,2,1,0:T(8,128)S(1)}, f32[2,6,16,128]{3,2,1,0:T(8,128)S(1)}, u32[]{:S(2)}, u32[]{:S(2)}) collective-permute-start(f32[2,6,16,128]{3,2,1,0:T(8,128)S(1)} %pad_maximum_fusion.14), channel_id=1, source_target_pairs={{1,0},{2,1},{3,2},{4,3},{5,4},{6,5},{7,6},{0,7},{9,8},{10,9},{11,1... | collective-permute-start | bytes 294920 | tf_op jit(solution)/shard_map/ppermute | solution.py:382
  52.3 2.2 %collective-permute-done.8 = f32[2,6,16,128]{3,2,1,0:T(8,128)S(1)} collective-permute-done((f32[2,6,16,128]{3,2,1,0:T(8,128)S(1)}, f32[2,6,16,128]{3,2,1,0:T(8,128)S(1)}, u32[]{:S(2)}, u32[]{:S(2)}) %collective-permute-start.8) | collective-permute-done | bytes 98336 | tf_op jit(solution)/shard_map/ppermute | solution.py:382
  54.5 5.1 %collective-permute-done.7 = f32[2,6,16,128]{3,2,1,0:T(8,128)S(1)} collective-permute-done((f32[2,6,16,128]{3,2,1,0:T(8,128)S(1)}, f32[2,6,16,128]{3,2,1,0:T(8,128)S(1)}, u32[]{:S(2)}, u32[]{:S(2)}) %collective-permute-start.7) | collective-permute-done | bytes 98336 | tf_op jit(solution)/shard_map/ppermute | solution.py:381
  62.2 4.6 %shard_map.47 = (f32[4,2,8,32,128]{4,3,2,1,0:T(8,128)}, f32[2,10,32,128]{3,2,1,0:T(8,128)}, f32[2,10,32,128]{3,2,1,0:T(8,128)}, f32[2,8,32,128]{3,2,1,0:T(8,128)}) custom-call(f32[2]{0:T(128)} %diff_ref.11, f32[2,8,16,128]{3,2,1,0:T(8,128)} %pad_maximum_fusion.9.one_ref, f32[2,8,16,128]{3,2,1,0:T(8,128)} %pad_maximum_fusion.10.mid_ref, ...), custom_call_target="tpu_custom_call" | custom-call | tf_op jit(solution)/shard_map/pallas_call | solution.py:363
  66.8 1.4 collective-permute-start.10
  68.3 1.0 fusion.114
  69.3 1.3 collective-permute-start.9
  70.6 7.2 %collective-permute-start.11 = (f32[2,5,32,128]{3,2,1,0:T(8,128)S(1)}, f32[2,5,32,128]{3,2,1,0:T(8,128)S(1)}, u32[]{:S(2)}, u32[]{:S(2)}) collective-permute-start(f32[2,5,32,128]{3,2,1,0:T(8,128)S(1)} %get-tuple-element.107), channel_id=1, source_target_pairs={{0,15},{1,8},{2,9},{3,10},{4,11},{5,12},{6,13},{7,14},{8,23},{9,16... | collective-permute-start | bytes 491528 | tf_op jit(solution)/shard_map/ppermute | solution.py:110
  77.9 4.7 %collective-permute-start.13 = (f32[2,10,32,128]{3,2,1,0:T(8,128)S(1)}, f32[2,10,32,128]{3,2,1,0:T(8,128)S(1)}, u32[]{:S(2)}, u32[]{:S(2)}) collective-permute-start(f32[2,10,32,128]{3,2,1,0:T(8,128)S(1)} %copy-done.25), channel_id=1, source_target_pairs={{1,0},{2,1},{3,2},{4,3},{5,4},{6,5},{7,6},{0,7},{9,8},{10,9},{11,1... | collective-permute-start | bytes 983048 | tf_op jit(solution)/shard_map/ppermute | solution.py:499
  83.6 7.2 %collective-permute-done.12.before_ref = f32[2,10,32,128]{3,2,1,0:T(8,128)S(1)} collective-permute-done((f32[2,10,32,128]{3,2,1,0:T(8,128)S(1)}, f32[2,10,32,128]{3,2,1,0:T(8,128)S(1)}, u32[]{:S(2)}, u32[]{:S(2)}) %collective-permute-start.12) | collective-permute-done | bytes 327712 | tf_op jit(solution)/shard_map/ppermute | solution.py:498
  90.7 4.0 %collective-permute-done.13.after_ref = f32[2,10,32,128]{3,2,1,0:T(8,128)S(1)} collective-permute-done((f32[2,10,32,128]{3,2,1,0:T(8,128)S(1)}, f32[2,10,32,128]{3,2,1,0:T(8,128)S(1)}, u32[]{:S(2)}, u32[]{:S(2)}) %collective-permute-start.13) | collective-permute-done | bytes 327712 | tf_op jit(solution)/shard_map/ppermute | solution.py:499
  95.5 4.6 %shard_map.48 = (f32[2,10,32,128]{3,2,1,0:T(8,128)}, f32[2,10,32,128]{3,2,1,0:T(8,128)}, f32[2,10,32,128]{3,2,1,0:T(8,128)}, f32[2,10,32,128]{3,2,1,0:T(8,128)},...) custom-call(f32[2]{0:T(128)} %diff_ref.11, f32[2,18,32,128]{3,2,1,0:T(8,128)} %copy-done.1, ...), custom_call_target="tpu_custom_call" | custom-call | tf_op jit(solution)/shard_map/pallas_call | solution.py:252
  100.1 1.0 fusion.60
  102.1 0.9 copy-done.16
  103.2 2.1 %collective-permute-start.15 = (f32[2,6,16,128]{3,2,1,0:T(8,128)S(1)}, f32[2,6,16,128]{3,2,1,0:T(8,128)S(1)}, u32[]{:S(2)}, u32[]{:S(2)}) collective-permute-start(f32[2,6,16,128]{3,2,1,0:T(8,128)S(1)} %pad_maximum_fusion.18), channel_id=1, source_target_pairs={{1,0},{2,1},{3,2},{4,3},{5,4},{6,5},{7,6},{0,7},{9,8},{10,9},{11,1... | collective-permute-start | bytes 294920 | tf_op jit(solution)/shard_map/ppermute | solution.py:382
  105.5 2.3 %collective-permute-done.15 = f32[2,6,16,128]{3,2,1,0:T(8,128)S(1)} collective-permute-done((f32[2,6,16,128]{3,2,1,0:T(8,128)S(1)}, f32[2,6,16,128]{3,2,1,0:T(8,128)S(1)}, u32[]{:S(2)}, u32[]{:S(2)}) %collective-permute-start.15) | collective-permute-done | bytes 98336 | tf_op jit(solution)/shard_map/ppermute | solution.py:382
  107.8 5.0 %collective-permute-done.14 = f32[2,6,16,128]{3,2,1,0:T(8,128)S(1)} collective-permute-done((f32[2,6,16,128]{3,2,1,0:T(8,128)S(1)}, f32[2,6,16,128]{3,2,1,0:T(8,128)S(1)}, u32[]{:S(2)}, u32[]{:S(2)}) %collective-permute-start.14) | collective-permute-done | bytes 98336 | tf_op jit(solution)/shard_map/ppermute | solution.py:381
  115.4 4.6 %shard_map.49 = (f32[4,2,8,32,128]{4,3,2,1,0:T(8,128)}, f32[2,10,32,128]{3,2,1,0:T(8,128)}, f32[2,10,32,128]{3,2,1,0:T(8,128)}, f32[2,8,32,128]{3,2,1,0:T(8,128)}) custom-call(f32[2]{0:T(128)} %diff_ref.11, f32[2,8,16,128]{3,2,1,0:T(8,128)} %pad_maximum_fusion.11.one_ref, f32[2,8,16,128]{3,2,1,0:T(8,128)} %pad_maximum_fusion.12.mid_ref, ...), custom_call_target="tpu_custom_call" | custom-call | tf_op jit(solution)/shard_map/pallas_call | solution.py:363
  120.0 1.4 collective-permute-start.17
  121.5 1.0 fusion.113
  122.5 1.3 collective-permute-start.16
  123.8 6.1 %collective-permute-start.18 = (f32[2,5,32,128]{3,2,1,0:T(8,128)S(1)}, f32[2,5,32,128]{3,2,1,0:T(8,128)S(1)}, u32[]{:S(2)}, u32[]{:S(2)}) collective-permute-start(f32[2,5,32,128]{3,2,1,0:T(8,128)S(1)} %get-tuple-element.105), channel_id=1, source_target_pairs={{0,15},{1,8},{2,9},{3,10},{4,11},{5,12},{6,13},{7,14},{8,23},{9,16... | collective-permute-start | bytes 491528 | tf_op jit(solution)/shard_map/ppermute | solution.py:110
  130.0 4.7 %collective-permute-start.20 = (f32[2,10,32,128]{3,2,1,0:T(8,128)S(1)}, f32[2,10,32,128]{3,2,1,0:T(8,128)S(1)}, u32[]{:S(2)}, u32[]{:S(2)}) collective-permute-start(f32[2,10,32,128]{3,2,1,0:T(8,128)S(1)} %copy-done.23), channel_id=1, source_target_pairs={{1,0},{2,1},{3,2},{4,3},{5,4},{6,5},{7,6},{0,7},{9,8},{10,9},{11,1... | collective-permute-start | bytes 983048 | tf_op jit(solution)/shard_map/ppermute | solution.py:499
  135.6 7.7 %collective-permute-done.19.before_ref = f32[2,10,32,128]{3,2,1,0:T(8,128)S(1)} collective-permute-done((f32[2,10,32,128]{3,2,1,0:T(8,128)S(1)}, f32[2,10,32,128]{3,2,1,0:T(8,128)S(1)}, u32[]{:S(2)}, u32[]{:S(2)}) %collective-permute-start.19) | collective-permute-done | bytes 327712 | tf_op jit(solution)/shard_map/ppermute | solution.py:498
  143.4 3.5 %collective-permute-done.20.after_ref = f32[2,10,32,128]{3,2,1,0:T(8,128)S(1)} collective-permute-done((f32[2,10,32,128]{3,2,1,0:T(8,128)S(1)}, f32[2,10,32,128]{3,2,1,0:T(8,128)S(1)}, u32[]{:S(2)}, u32[]{:S(2)}) %collective-permute-start.20) | collective-permute-done | bytes 327712 | tf_op jit(solution)/shard_map/ppermute | solution.py:499
  147.6 4.6 %shard_map.50 = (f32[2,10,32,128]{3,2,1,0:T(8,128)}, f32[2,10,32,128]{3,2,1,0:T(8,128)}, f32[2,10,32,128]{3,2,1,0:T(8,128)}, f32[2,10,32,128]{3,2,1,0:T(8,128)},...) custom-call(f32[2]{0:T(128)} %diff_ref.11, f32[2,18,32,128]{3,2,1,0:T(8,128)} %copy-done.2, ...), custom_call_target="tpu_custom_call" | custom-call | tf_op jit(solution)/shard_map/pallas_call | solution.py:252
  152.2 1.6 fusion.38.late_ref
  153.8 0.9 copy-done.11
  155.8 2.1 %collective-permute-start.22 = (f32[2,2,16,128]{3,2,1,0:T(8,128)S(1)}, f32[2,2,16,128]{3,2,1,0:T(8,128)S(1)}, u32[]{:S(2)}, u32[]{:S(2)}) collective-permute-start(f32[2,2,16,128]{3,2,1,0:T(8,128)S(1)} %pad_maximum_fusion.24), channel_id=1, source_target_pairs={{1,0},{2,1},{3,2},{4,3},{5,4},{6,5},{7,6},{0,7},{9,8},{10,9},{11,1... | collective-permute-start | bytes 98312 | tf_op jit(solution)/shard_map/ppermute | solution.py:382
  158.0 1.9 %collective-permute-done.22 = f32[2,2,16,128]{3,2,1,0:T(8,128)S(1)} collective-permute-done((f32[2,2,16,128]{3,2,1,0:T(8,128)S(1)}, f32[2,2,16,128]{3,2,1,0:T(8,128)S(1)}, u32[]{:S(2)}, u32[]{:S(2)}) %collective-permute-start.22) | collective-permute-done | bytes 32800 | tf_op jit(solution)/shard_map/ppermute | solution.py:382
  159.8 4.7 %collective-permute-done.21 = f32[2,2,16,128]{3,2,1,0:T(8,128)S(1)} collective-permute-done((f32[2,2,16,128]{3,2,1,0:T(8,128)S(1)}, f32[2,2,16,128]{3,2,1,0:T(8,128)S(1)}, u32[]{:S(2)}, u32[]{:S(2)}) %collective-permute-start.21) | collective-permute-done | bytes 32800 | tf_op jit(solution)/shard_map/ppermute | solution.py:381
  165.9 3.0 %shard_map.51 = f32[2,8,32,128]{3,2,1,0:T(8,128)} custom-call(f32[2]{0:T(128)} %diff_ref.11, f32[2,6,16,128]{3,2,1,0:T(8,128)} %pad_maximum_fusion.21.one_ref, f32[2,6,16,128]{3,2,1,0:T(8,128)} %pad_maximum_fusion.22.mid_ref, f32[2,4,16,128]{3,2,1,0:T(8,128)} %fusion.43.low_ref, f32[2,4,16,128]{3,2,1,0:T(8,128)} %fusion.38.late_ref, ...), custom_call_target="tpu_custom_call" | custom-call | tf_op jit(solution)/shard_map/pallas_call | solution.py:363
  168.9 1.0 slice_bitcast_fusion.7
  (159 shorter events, 21.5 us)
Async XLA Ops:
  0.0 1.1 copy-start.19
  1.2 16.7 %collective-permute-start.2 = (f32[2,5,32,128]{3,2,1,0:T(8,128)S(1)}, f32[2,5,32,128]{3,2,1,0:T(8,128)S(1)}, u32[]{:S(2)}, u32[]{:S(2)}) collective-permute-start(f32[2,5,32,128]{3,2,1,0:T(8,128)S(1)} %get-tuple-element.108), channel_id=1, source_target_pairs={{0,9},{1,10},{2,11},{3,12},{4,13},{5,14},{6,15},{7,8},{8,17},{9,18... | collective-permute-start | bytes 491528 | tf_op jit(solution)/shard_map/ppermute | solution.py:110
  5.5 13.6 %collective-permute-start = (f32[2,5,32,128]{3,2,1,0:T(8,128)S(1)}, f32[2,5,32,128]{3,2,1,0:T(8,128)S(1)}, u32[]{:S(2)}, u32[]{:S(2)}) collective-permute-start(f32[2,5,32,128]{3,2,1,0:T(8,128)S(1)} %get-tuple-element.108), channel_id=1, source_target_pairs={{0,1},{1,2},{2,3},{3,4},{4,5},{5,6},{6,7},{7,0},{8,9},{9,10},{10,1... | collective-permute-start | bytes 491528 | tf_op jit(solution)/shard_map/ppermute | solution.py:93
  7.1 9.1 %copy-start.20 = (f32[2,8,32,128]{3,2,1,0:T(8,128)S(1)}, f32[2,8,32,128]{3,2,1,0:T(8,128)}, u32[]{:S(2)}) copy-start(f32[2,8,32,128]{3,2,1,0:T(8,128)} %param.5) | copy-start | bytes 786436
  7.1 15.6 %collective-permute-start.4 = (f32[2,5,32,128]{3,2,1,0:T(8,128)S(1)}, f32[2,5,32,128]{3,2,1,0:T(8,128)S(1)}, u32[]{:S(2)}, u32[]{:S(2)}) collective-permute-start(f32[2,5,32,128]{3,2,1,0:T(8,128)S(1)} %get-tuple-element.109), channel_id=1, source_target_pairs={{0,15},{1,8},{2,9},{3,10},{4,11},{5,12},{6,13},{7,14},{8,23},{9,16... | collective-permute-start | bytes 491528 | tf_op jit(solution)/shard_map/ppermute | solution.py:110
  13.3 9.4 %collective-permute-start.1 = (f32[2,5,32,128]{3,2,1,0:T(8,128)S(1)}, f32[2,5,32,128]{3,2,1,0:T(8,128)S(1)}, u32[]{:S(2)}, u32[]{:S(2)}) collective-permute-start(f32[2,5,32,128]{3,2,1,0:T(8,128)S(1)} %get-tuple-element.109), channel_id=1, source_target_pairs={{1,0},{2,1},{3,2},{4,3},{5,4},{6,5},{7,6},{0,7},{9,8},{10,9},{11,1... | collective-permute-start | bytes 491528 | tf_op jit(solution)/shard_map/ppermute | solution.py:94
  14.0 2.3 %copy-start.21 = (f32[2,8,32,128]{3,2,1,0:T(8,128)S(1)}, f32[2,8,32,128]{3,2,1,0:T(8,128)}, u32[]{:S(2)}) copy-start(f32[2,8,32,128]{3,2,1,0:T(8,128)} %param.6) | copy-start | bytes 786436
  14.0 8.7 %collective-permute-start.3 = (f32[2,8,32,128]{3,2,1,0:T(8,128)S(1)}, f32[2,8,32,128]{3,2,1,0:T(8,128)S(1)}, u32[]{:S(2)}, u32[]{:S(2)}) collective-permute-start(f32[2,8,32,128]{3,2,1,0:T(8,128)S(1)} %pad_maximum_fusion.4), channel_id=1, source_target_pairs={{0,8},{1,9},{2,10},{3,11},{4,12},{5,13},{6,14},{7,15},{8,16},{9,17... | collective-permute-start | bytes 786440 | tf_op jit(solution)/shard_map/ppermute | solution.py:110
  17.9 13.3 %collective-permute-start.5 = (f32[2,2,4,32,128]{4,3,2,1,0:T(8,128)S(1)}, f32[2,2,4,32,128]{4,3,2,1,0:T(8,128)S(1)}, u32[]{:S(2)}, u32[]{:S(2)}) collective-permute-start(f32[2,2,4,32,128]{4,3,2,1,0:T(8,128)S(1)} %get-tuple-element.100), channel_id=1, source_target_pairs={{0,1},{1,2},{2,3},{3,4},{4,5},{5,6},{6,7},{7,0},{8,9},{9,10},{10,1... | collective-permute-start | bytes 786440 | tf_op jit(solution)/shard_map/ppermute | solution.py:93
  19.1 13.9 %collective-permute-start.6 = (f32[2,2,4,32,128]{4,3,2,1,0:T(8,128)S(1)}, f32[2,2,4,32,128]{4,3,2,1,0:T(8,128)S(1)}, u32[]{:S(2)}, u32[]{:S(2)}) collective-permute-start(f32[2,2,4,32,128]{4,3,2,1,0:T(8,128)S(1)} %get-tuple-element.101), channel_id=1, source_target_pairs={{1,0},{2,1},{3,2},{4,3},{5,4},{6,5},{7,6},{0,7},{9,8},{10,9},{11,1... | collective-permute-start | bytes 786440 | tf_op jit(solution)/shard_map/ppermute | solution.py:94
  22.8 14.1 %copy-start = (f32[2,18,32,128]{3,2,1,0:T(8,128)}, f32[2,18,32,128]{3,2,1,0:T(8,128)S(1)}, u32[]{:S(2)}) copy-start(f32[2,18,32,128]{3,2,1,0:T(8,128)S(1)} %get-tuple-element.91.b_ref) | copy-start | bytes 1769476
  37.7 8.3 %copy-start.3 = (f32[2,8,16,128]{3,2,1,0:T(8,128)}, f32[2,8,16,128]{3,2,1,0:T(8,128)S(1)}, u32[]{:S(2)}) copy-start(f32[2,8,16,128]{3,2,1,0:T(8,128)S(1)} %fusion.28.rate_ref) | copy-start | bytes 393220
  44.9 1.1 copy-start.6
  46.0 0.9 copy-start.17
  47.0 1.0 copy-start.7
  48.0 6.5 %collective-permute-start.8 = (f32[2,6,16,128]{3,2,1,0:T(8,128)S(1)}, f32[2,6,16,128]{3,2,1,0:T(8,128)S(1)}, u32[]{:S(2)}, u32[]{:S(2)}) collective-permute-start(f32[2,6,16,128]{3,2,1,0:T(8,128)S(1)} %pad_maximum_fusion.14), channel_id=1, source_target_pairs={{1,0},{2,1},{3,2},{4,3},{5,4},{6,5},{7,6},{0,7},{9,8},{10,9},{11,1... | collective-permute-start | bytes 294920 | tf_op jit(solution)/shard_map/ppermute | solution.py:382
  52.3 7.4 %collective-permute-start.7 = (f32[2,6,16,128]{3,2,1,0:T(8,128)S(1)}, f32[2,6,16,128]{3,2,1,0:T(8,128)S(1)}, u32[]{:S(2)}, u32[]{:S(2)}) collective-permute-start(f32[2,6,16,128]{3,2,1,0:T(8,128)S(1)} %pad_maximum_fusion.13), channel_id=1, source_target_pairs={{0,1},{1,2},{2,3},{3,4},{4,5},{5,6},{6,7},{7,0},{8,9},{9,10},{10,1... | collective-permute-start | bytes 294920 | tf_op jit(solution)/shard_map/ppermute | solution.py:381
  66.8 11.0 %copy-start.26 = (f32[2,10,32,128]{3,2,1,0:T(8,128)S(1)}, f32[2,10,32,128]{3,2,1,0:T(8,128)}, u32[]{:S(2)}) copy-start(f32[2,10,32,128]{3,2,1,0:T(8,128)} %get-tuple-element.43) | copy-start | bytes 983044
  66.8 11.1 %copy-start.25 = (f32[2,10,32,128]{3,2,1,0:T(8,128)S(1)}, f32[2,10,32,128]{3,2,1,0:T(8,128)}, u32[]{:S(2)}) copy-start(f32[2,10,32,128]{3,2,1,0:T(8,128)} %get-tuple-element.44) | copy-start | bytes 983044
  66.8 15.8 %collective-permute-start.10 = (f32[2,8,32,128]{3,2,1,0:T(8,128)}, f32[2,8,32,128]{3,2,1,0:T(8,128)S(1)}, u32[]{:S(2)}, u32[]{:S(2)}) collective-permute-start(f32[2,8,32,128]{3,2,1,0:T(8,128)} %get-tuple-element.41), channel_id=1, source_target_pairs={{0,8},{1,9},{2,10},{3,11},{4,12},{5,13},{6,14},{7,15},{8,16},{9,17... | collective-permute-start | bytes 786440 | tf_op jit(solution)/shard_map/ppermute | solution.py:110
  69.3 13.3 %collective-permute-start.9 = (f32[2,5,32,128]{3,2,1,0:T(8,128)S(1)}, f32[2,5,32,128]{3,2,1,0:T(8,128)S(1)}, u32[]{:S(2)}, u32[]{:S(2)}) collective-permute-start(f32[2,5,32,128]{3,2,1,0:T(8,128)S(1)} %get-tuple-element.106), channel_id=1, source_target_pairs={{0,9},{1,10},{2,11},{3,12},{4,13},{5,14},{6,15},{7,8},{8,17},{9,18... | collective-permute-start | bytes 491528 | tf_op jit(solution)/shard_map/ppermute | solution.py:110
  70.6 12.0 %collective-permute-start.11 = (f32[2,5,32,128]{3,2,1,0:T(8,128)S(1)}, f32[2,5,32,128]{3,2,1,0:T(8,128)S(1)}, u32[]{:S(2)}, u32[]{:S(2)}) collective-permute-start(f32[2,5,32,128]{3,2,1,0:T(8,128)S(1)} %get-tuple-element.107), channel_id=1, source_target_pairs={{0,15},{1,8},{2,9},{3,10},{4,11},{5,12},{6,13},{7,14},{8,23},{9,16... | collective-permute-start | bytes 491528 | tf_op jit(solution)/shard_map/ppermute | solution.py:110
  77.8 12.9 %collective-permute-start.12 = (f32[2,10,32,128]{3,2,1,0:T(8,128)S(1)}, f32[2,10,32,128]{3,2,1,0:T(8,128)S(1)}, u32[]{:S(2)}, u32[]{:S(2)}) collective-permute-start(f32[2,10,32,128]{3,2,1,0:T(8,128)S(1)} %copy-done.26), channel_id=1, source_target_pairs={{0,1},{1,2},{2,3},{3,4},{4,5},{5,6},{6,7},{7,0},{8,9},{9,10},{10,1... | collective-permute-start | bytes 983048 | tf_op jit(solution)/shard_map/ppermute | solution.py:498
  77.9 16.8 %collective-permute-start.13 = (f32[2,10,32,128]{3,2,1,0:T(8,128)S(1)}, f32[2,10,32,128]{3,2,1,0:T(8,128)S(1)}, u32[]{:S(2)}, u32[]{:S(2)}) collective-permute-start(f32[2,10,32,128]{3,2,1,0:T(8,128)S(1)} %copy-done.25), channel_id=1, source_target_pairs={{1,0},{2,1},{3,2},{4,3},{5,4},{6,5},{7,6},{0,7},{9,8},{10,9},{11,1... | collective-permute-start | bytes 983048 | tf_op jit(solution)/shard_map/ppermute | solution.py:499
  82.7 0.8 copy-start.1
  90.7 4.0 %copy-start.14 = (f32[2,10,32,128]{3,2,1,0:T(8,128)}, f32[2,10,32,128]{3,2,1,0:T(8,128)S(1)}, u32[]{:S(2)}) copy-start(f32[2,10,32,128]{3,2,1,0:T(8,128)S(1)} %collective-permute-done.12.before_ref) | copy-start | bytes 983044
  94.8 0.7 copy-start.15
  100.1 1.1 copy-start.8
  101.1 1.0 copy-start.9
  102.1 1.0 copy-start.16
  102.1 1.0 copy-start.4
  103.2 4.7 %collective-permute-start.15 = (f32[2,6,16,128]{3,2,1,0:T(8,128)S(1)}, f32[2,6,16,128]{3,2,1,0:T(8,128)S(1)}, u32[]{:S(2)}, u32[]{:S(2)}) collective-permute-start(f32[2,6,16,128]{3,2,1,0:T(8,128)S(1)} %pad_maximum_fusion.18), channel_id=1, source_target_pairs={{1,0},{2,1},{3,2},{4,3},{5,4},{6,5},{7,6},{0,7},{9,8},{10,9},{11,1... | collective-permute-start | bytes 294920 | tf_op jit(solution)/shard_map/ppermute | solution.py:382
  105.3 7.5 %collective-permute-start.14 = (f32[2,6,16,128]{3,2,1,0:T(8,128)S(1)}, f32[2,6,16,128]{3,2,1,0:T(8,128)S(1)}, u32[]{:S(2)}, u32[]{:S(2)}) collective-permute-start(f32[2,6,16,128]{3,2,1,0:T(8,128)S(1)} %pad_maximum_fusion.17), channel_id=1, source_target_pairs={{0,1},{1,2},{2,3},{3,4},{4,5},{5,6},{6,7},{7,0},{8,9},{9,10},{10,1... | collective-permute-start | bytes 294920 | tf_op jit(solution)/shard_map/ppermute | solution.py:381
  120.0 9.9 %copy-start.24 = (f32[2,10,32,128]{3,2,1,0:T(8,128)S(1)}, f32[2,10,32,128]{3,2,1,0:T(8,128)}, u32[]{:S(2)}) copy-start(f32[2,10,32,128]{3,2,1,0:T(8,128)} %get-tuple-element.54) | copy-start | bytes 983044
  120.0 10.0 %copy-start.23 = (f32[2,10,32,128]{3,2,1,0:T(8,128)S(1)}, f32[2,10,32,128]{3,2,1,0:T(8,128)}, u32[]{:S(2)}) copy-start(f32[2,10,32,128]{3,2,1,0:T(8,128)} %get-tuple-element.55) | copy-start | bytes 983044
  120.0 14.7 %collective-permute-start.17 = (f32[2,8,32,128]{3,2,1,0:T(8,128)}, f32[2,8,32,128]{3,2,1,0:T(8,128)S(1)}, u32[]{:S(2)}, u32[]{:S(2)}) collective-permute-start(f32[2,8,32,128]{3,2,1,0:T(8,128)} %get-tuple-element.52), channel_id=1, source_target_pairs={{0,8},{1,9},{2,10},{3,11},{4,12},{5,13},{6,14},{7,15},{8,16},{9,17... | collective-permute-start | bytes 786440 | tf_op jit(solution)/shard_map/ppermute | solution.py:110
  122.5 12.2 %collective-permute-start.16 = (f32[2,5,32,128]{3,2,1,0:T(8,128)S(1)}, f32[2,5,32,128]{3,2,1,0:T(8,128)S(1)}, u32[]{:S(2)}, u32[]{:S(2)}) collective-permute-start(f32[2,5,32,128]{3,2,1,0:T(8,128)S(1)} %get-tuple-element.104), channel_id=1, source_target_pairs={{0,9},{1,10},{2,11},{3,12},{4,13},{5,14},{6,15},{7,8},{8,17},{9,18... | collective-permute-start | bytes 491528 | tf_op jit(solution)/shard_map/ppermute | solution.py:110
  123.8 10.9 %collective-permute-start.18 = (f32[2,5,32,128]{3,2,1,0:T(8,128)S(1)}, f32[2,5,32,128]{3,2,1,0:T(8,128)S(1)}, u32[]{:S(2)}, u32[]{:S(2)}) collective-permute-start(f32[2,5,32,128]{3,2,1,0:T(8,128)S(1)} %get-tuple-element.105), channel_id=1, source_target_pairs={{0,15},{1,8},{2,9},{3,10},{4,11},{5,12},{6,13},{7,14},{8,23},{9,16... | collective-permute-start | bytes 491528 | tf_op jit(solution)/shard_map/ppermute | solution.py:110
  129.9 13.5 %collective-permute-start.19 = (f32[2,10,32,128]{3,2,1,0:T(8,128)S(1)}, f32[2,10,32,128]{3,2,1,0:T(8,128)S(1)}, u32[]{:S(2)}, u32[]{:S(2)}) collective-permute-start(f32[2,10,32,128]{3,2,1,0:T(8,128)S(1)} %copy-done.24), channel_id=1, source_target_pairs={{0,1},{1,2},{2,3},{3,4},{4,5},{5,6},{6,7},{7,0},{8,9},{9,10},{10,1... | collective-permute-start | bytes 983048 | tf_op jit(solution)/shard_map/ppermute | solution.py:498
  130.0 16.8 %collective-permute-start.20 = (f32[2,10,32,128]{3,2,1,0:T(8,128)S(1)}, f32[2,10,32,128]{3,2,1,0:T(8,128)S(1)}, u32[]{:S(2)}, u32[]{:S(2)}) collective-permute-start(f32[2,10,32,128]{3,2,1,0:T(8,128)S(1)} %copy-done.23), channel_id=1, source_target_pairs={{1,0},{2,1},{3,2},{4,3},{5,4},{6,5},{7,6},{0,7},{9,8},{10,9},{11,1... | collective-permute-start | bytes 983048 | tf_op jit(solution)/shard_map/ppermute | solution.py:499
  134.8 0.8 copy-start.2
  143.4 3.5 %copy-start.12 = (f32[2,10,32,128]{3,2,1,0:T(8,128)}, f32[2,10,32,128]{3,2,1,0:T(8,128)S(1)}, u32[]{:S(2)}) copy-start(f32[2,10,32,128]{3,2,1,0:T(8,128)S(1)} %collective-permute-done.19.before_ref) | copy-start | bytes 983044
  152.2 1.6 copy-start.10
  153.8 1.0 copy-start.11
  154.8 1.0 copy-start.18
  154.8 1.0 copy-start.5
  155.8 4.0 %collective-permute-start.22 = (f32[2,2,16,128]{3,2,1,0:T(8,128)S(1)}, f32[2,2,16,128]{3,2,1,0:T(8,128)S(1)}, u32[]{:S(2)}, u32[]{:S(2)}) collective-permute-start(f32[2,2,16,128]{3,2,1,0:T(8,128)S(1)} %pad_maximum_fusion.24), channel_id=1, source_target_pairs={{1,0},{2,1},{3,2},{4,3},{5,4},{6,5},{7,6},{0,7},{9,8},{10,9},{11,1... | collective-permute-start | bytes 98312 | tf_op jit(solution)/shard_map/ppermute | solution.py:382
  157.9 6.6 %collective-permute-start.21 = (f32[2,2,16,128]{3,2,1,0:T(8,128)S(1)}, f32[2,2,16,128]{3,2,1,0:T(8,128)S(1)}, u32[]{:S(2)}, u32[]{:S(2)}) collective-permute-start(f32[2,2,16,128]{3,2,1,0:T(8,128)S(1)} %pad_maximum_fusion.23), channel_id=1, source_target_pairs={{0,1},{1,2},{2,3},{3,4},{4,5},{5,6},{6,7},{7,0},{8,9},{9,10},{10,1... | collective-permute-start | bytes 98312 | tf_op jit(solution)/shard_map/ppermute | solution.py:381
  (2 other events, 1.4 us)

commit v3 on v2

--- a/solution.py
+++ b/solution.py
@@ -1,3 +1,4 @@
+import functools
 import math
 
 import jax
@@ -186,8 +187,20 @@
     return pair_x + pair_y + pair_z - 6.0 * centre
 
 
-def sweep_kernel(diff_ref, b_ref, own_ref, before_ref, after_ref, dec_ref, src_ref,
-                 n1_ref, n2_ref, n3_ref, n4_ref, e0_ref, s0_ref, s1_ref):
+def kernel_restrict(v):
+    shape = v.shape
+    pairs = v.reshape((shape[0], shape[1] // 2, 2) + shape[2:])
+    half = shape[2] // 2
+    even = pairs[:, :, :, :half]
+    odd = pairs[:, :, :, half:]
+    upper = even[:, :, 0] + even[:, :, 1]
+    lower = odd[:, :, 0] + odd[:, :, 1]
+    return (upper + lower) * 0.25
+
+
+def sweep_kernel(widths_sent, diff_ref, b_ref, own_ref, before_ref, after_ref, dec_ref, src_ref,
+                 rate_ref, n1_ref, n2_ref, n3_ref, n4_ref, e0_ref, cown_ref, clasts_ref,
+                 cfirsts_ref):
     spread_table, grouped_table, interp_table, widths = node_tables()
     rows = e0_ref.shape[1]
     hs = (b_ref.shape[1] - rows) // 2
@@ -233,28 +246,49 @@
     found.append(terms(swept[4], hs - 4))
     dec0 = at(dec_ref, 0)
     fulls = [cut(found[j], hs - 1 - j, 0) - dec0 * cut(swept[j], hs - j, 0) for j in range(5)]
-    for c, out in ((0, s0_ref), (1, s1_ref)):
+    integrated = []
+    for c in range(2):
         summed = grouped_table[c][0] * fulls[0]
         for j in range(1, 5):
             summed = summed + grouped_table[c][j] * fulls[j]
-        out[...] = summed
+        integrated.append(kernel_restrict(summed))
+    crows = rows // 2
+    hcr = (rate_ref.shape[1] - crows) // 2
+    rc = rate_ref[:, hcr:hcr + crows]
+    coarse_vals = [kernel_restrict(cut(swept[j], hs - j, 0)) for j in (0, 2, 4)]
+    half_step = 0.5 * step_length
+    coarse_one = (
+        coarse_vals[0] + half_step * rc * coarse_vals[1] + integrated[0]
+    ) / (1.0 + half_step * rc)
+    sent = [coarse_one, coarse_vals[1], coarse_vals[2], integrated[1]]
+    offset = 0
+    for i, piece in enumerate(sent):
+        cown_ref[i] = piece
+        w = widths_sent[i]
+        if w:
+            clasts_ref[:, offset:offset + w] = piece[:, crows - w:]
+            cfirsts_ref[:, offset:offset + w] = piece[:, :w]
+        offset += w
     for m, out in ((1, n1_ref), (2, n2_ref), (3, n3_ref), (4, n4_ref)):
         out[...] = cut(swept[m], hs - m, 1)
     e0_ref[...] = cut(found[0], hs - 1, 0)
 
 
-def fine_sweep(diffusivity, begin, parts, decay, src):
+def fine_sweep(diffusivity, begin, parts, decay, src, rate_c, widths_sent):
     rows = begin.shape[1] - 2 * START_HALO
     shape = begin.shape
     wide = jax.ShapeDtypeStruct((shape[0], rows + 2) + shape[2:], jnp.float32)
     own = jax.ShapeDtypeStruct((shape[0], rows) + shape[2:], jnp.float32)
+    cshape = (shape[0], rows // 2, shape[2] // 2, shape[3])
+    cown = jax.ShapeDtypeStruct((4,) + cshape, jnp.float32)
+    cedge = jax.ShapeDtypeStruct((shape[0], sum(widths_sent)) + cshape[2:], jnp.float32)
     vmem = pl.BlockSpec(memory_space=pltpu.VMEM)
     return pl.pallas_call(
-        sweep_kernel,
-        out_shape=(wide, wide, wide, wide, own, own, own),
-        in_specs=[pl.BlockSpec(memory_space=pltpu.SMEM)] + [vmem] * 6,
-        out_specs=(vmem,) * 7,
-    )(diffusivity, begin, *parts, decay, src)
+        functools.partial(sweep_kernel, widths_sent),
+        out_shape=(wide, wide, wide, wide, own, cown, cedge, cedge),
+        in_specs=[pl.BlockSpec(memory_space=pltpu.SMEM)] + [vmem] * 7,
+        out_specs=(vmem,) * 8,
+    )(diffusivity, begin, *parts, decay, src, rate_c)
 
 
 def coarse_kernel_laplace(f):
@@ -269,13 +303,28 @@
     )
 
 
-def finish_kernel(diff_ref, one_ref, mid_ref, low_ref, late_ref, rate_ref, csrc_ref,
+def finish_kernel(widths_sent, diff_ref, cown_ref, cbefore_ref, cafter_ref, rate_ref, csrc_ref,
                   n1_ref, n2_ref, n3_ref, n4_ref, b_ref, e0_ref, dec_ref, src_ref, *outs):
     spread_table, grouped_table, interp_table, widths = node_tables()
     last = len(outs) == 1
     rows = e0_ref.shape[1]
     crows = rows // 2
-    ho = (low_ref.shape[1] - crows) // 2
+    ho = widths_sent[2]
+    joined = []
+    offset = 0
+    for i in range(4):
+        w = widths_sent[i]
+        if w:
+            joined.append(
+                jnp.concatenate(
+                    [cbefore_ref[:, offset:offset + w], cown_ref[i], cafter_ref[:, offset:offset + w]],
+                    axis=1,
+                )
+            )
+        else:
+            joined.append(cown_ref[i])
+        offset += w
+    one, mid, low, late = joined
     hcr = (rate_ref.shape[1] - crows) // 2
     hd = (dec_ref.shape[1] - rows) // 2
     hs = (b_ref.shape[1] - rows) // 2
@@ -298,17 +347,15 @@
         return react(v[:, 1:-1], coarse_kernel_laplace(v), at(csrc_ref, ho, crows, hcr))
 
     half_step = 0.5 * step_length
-    one = one_ref[...]
-    mid = mid_ref[...]
     rc = at(rate_ref, ho, crows, hcr)
     coarse_two = (
         cut(one, ho + 1, ho)
         + half_step * (coarse_terms(one) - coarse_terms(mid))
-        + half_step * rc * low_ref[...]
-        + late_ref[...]
+        + half_step * rc * low
+        + late
     ) / (1.0 + half_step * rc)
     delta_one = cut(one, ho + 1, ho) - cut(mid, ho + 1, ho)
-    delta_two = coarse_two - low_ref[...]
+    delta_two = coarse_two - low
 
     def prolonged(c):
         shape = c.shape
@@ -347,7 +394,7 @@
     u4_out[...] = states[4]
 
 
-def finish_round(diffusivity, coarse, rate_c, source_c, swept, e0, decay, src, last):
+def finish_round(diffusivity, coarse, rate_c, source_c, swept, e0, decay, src, last, widths_sent):
     begin = swept[0]
     shape = begin.shape
     rows = e0.shape[1]
@@ -361,7 +408,7 @@
     vmem = pl.BlockSpec(memory_space=pltpu.VMEM)
     args = (diffusivity, *coarse, rate_c, source_c, *swept[1:], begin, e0, decay, src)
     return pl.pallas_call(
-        finish_kernel,
+        functools.partial(finish_kernel, widths_sent),
         out_shape=out_shape,
         in_specs=[pl.BlockSpec(memory_space=pltpu.SMEM)] + [vmem] * (len(args) - 1),
         out_specs=(vmem,) * len(out_shape),
@@ -445,26 +492,18 @@
         return out
 
     def advance(begin, pieces, last):
-        n1, n2, n3, n4, e0, s0, s1 = fine_sweep(diffusivity, begin[0], pieces, decay[0], src[0])
-        coarse_vals = [restrict(begin), restrict((n2, 1)), restrict((n4, 1))]
-        coarse_vals = [crop(v, 0) for v in coarse_vals]
-        integrated = [crop(restrict((s0, 0)), 0), crop(restrict((s1, 0)), 0)]
-        half_step = 0.5 * step_length
-        rc = crop(rate_c, 0)
-        coarse_one = (
-            coarse_vals[0] + half_step * rc * coarse_vals[1] + integrated[0]
-        ) / (1.0 + half_step * rc)
-        if last:
-            one, mid = packed_halo([(coarse_one, 1), (coarse_vals[1], 1)])
-            coarse = (one[0], mid[0], coarse_vals[2], integrated[1])
-        else:
-            one, mid, low, late = packed_halo(
-                [(coarse_one, 2), (coarse_vals[1], 2), (coarse_vals[2], 1), (integrated[1], 1)]
-            )
-            coarse = (one[0], mid[0], low[0], late[0])
+        widths_sent = (1, 1, 0, 0) if last else (2, 2, 1, 1)
+        n1, n2, n3, n4, e0, cown, clasts, cfirsts = fine_sweep(
+            diffusivity, begin[0], pieces, decay[0], src[0], rate_c[0], widths_sent
+        )
+        coarse = (
+            cown,
+            lax.ppermute(clasts, "space", up),
+            lax.ppermute(cfirsts, "space", down),
+        )
         return finish_round(
             diffusivity, coarse, rate_c[0], source_c[0],
-            (begin[0], n1, n2, n3, n4), e0, decay[0], src[0], last,
+            (begin[0], n1, n2, n3, n4), e0, decay[0], src[0], last, widths_sent,
         )
 
     size = lax.axis_size("space")

time: 171 us -> 144 us (0.84)
  the two profiles are of different devices: /device:TPU:0 before, /device:TPU:2 now
where the time goes in v3:
time: 144 us; the launch traced here: 143 us
  starting transfers between devices  53.5 us (37%)
  waiting for transfers between devices  41.3 us (29%)
  Pallas kernels  26 us (18%)
  local copies, waits for them, and re-layouts  12 us (8%)
  other arithmetic  9.82 us (7%)
    ppermute x9, waiting for transfers between devices, moved(): return lax.ppermute(piece, axes, pairs)  22.7 us
    ppermute x9, starting transfers between devices, moved(): return lax.ppermute(piece, axes, pairs)  19.7 us
    pallas_call x3, Pallas kernels, fine_sweep(): pl.pallas_call(functools.partial(sweep_kernel, widths_sent), out_shape=(w...  13.7 us
    pallas_call x3, Pallas kernels, finish_round(): pl.pallas_call(functools.partial(finish_kernel, widths_sent), out_shape=o...  12.3 us
    ppermute x3, starting transfers between devices, advance(): lax.ppermute(cfirsts, 'space', down)  10.7 us
    ppermute x2, starting transfers between devices, per_device(): lax.ppermute(firsts, 'space', down)  9.45 us
    ppermute x2, starting transfers between devices, space_halo(): lax.ppermute(lax.slice_in_dim(a, 0, h, axis=a.ndim - 3), 'space', down)  7.85 us
    ppermute x3, waiting for transfers between devices, advance(): lax.ppermute(clasts, 'space', up)  7.01 us
  transfers between devices with their start and end apart: 23, of which 11 were waited for; matrix products, arithmetic and copies ran while one was open for 5% of the time, Pallas kernels for 0%

profile of v3, /device:TPU:2, one launch (start us, length us, event | category | flops | bytes accessed | tf_op | source)
XLA Modules:
  0.0 143.0 jit_solution(7920010062503263835)
XLA Ops:
  0.0 1.0 slice.226
  1.2 2.9 %collective-permute-start.2 = (f32[2,5,32,128]{3,2,1,0:T(8,128)S(1)}, f32[2,5,32,128]{3,2,1,0:T(8,128)S(1)}, u32[]{:S(2)}, u32[]{:S(2)}) collective-permute-start(f32[2,5,32,128]{3,2,1,0:T(8,128)S(1)} %get-tuple-element.108), channel_id=1, source_target_pairs={{0,9},{1,10},{2,11},{3,12},{4,13},{5,14},{6,15},{7,8},{8,17},{9,18... | collective-permute-start | bytes 491528 | tf_op jit(solution)/shard_map/ppermute | solution.py:111
  4.1 1.6 %collective-permute-start = (f32[2,5,32,128]{3,2,1,0:T(8,128)S(1)}, f32[2,5,32,128]{3,2,1,0:T(8,128)S(1)}, u32[]{:S(2)}, u32[]{:S(2)}) collective-permute-start(f32[2,5,32,128]{3,2,1,0:T(8,128)S(1)} %get-tuple-element.108), channel_id=1, source_target_pairs={{0,1},{1,2},{2,3},{3,4},{4,5},{5,6},{6,7},{7,0},{8,9},{9,10},{10,1... | collective-permute-start | bytes 491528 | tf_op jit(solution)/shard_map/ppermute | solution.py:94
  5.6 3.0 %collective-permute-start.4 = (f32[2,5,32,128]{3,2,1,0:T(8,128)S(1)}, f32[2,5,32,128]{3,2,1,0:T(8,128)S(1)}, u32[]{:S(2)}, u32[]{:S(2)}) collective-permute-start(f32[2,5,32,128]{3,2,1,0:T(8,128)S(1)} %get-tuple-element.109), channel_id=1, source_target_pairs={{0,15},{1,8},{2,9},{3,10},{4,11},{5,12},{6,13},{7,14},{8,23},{9,16... | collective-permute-start | bytes 491528 | tf_op jit(solution)/shard_map/ppermute | solution.py:111
  8.6 2.3 %collective-permute-start.1 = (f32[2,5,32,128]{3,2,1,0:T(8,128)S(1)}, f32[2,5,32,128]{3,2,1,0:T(8,128)S(1)}, u32[]{:S(2)}, u32[]{:S(2)}) collective-permute-start(f32[2,5,32,128]{3,2,1,0:T(8,128)S(1)} %get-tuple-element.109), channel_id=1, source_target_pairs={{1,0},{2,1},{3,2},{4,3},{5,4},{6,5},{7,6},{0,7},{9,8},{10,9},{11,1... | collective-permute-start | bytes 491528 | tf_op jit(solution)/shard_map/ppermute | solution.py:95
  11.0 2.1 %collective-permute-start.3 = (f32[2,8,32,128]{3,2,1,0:T(8,128)S(1)}, f32[2,8,32,128]{3,2,1,0:T(8,128)S(1)}, u32[]{:S(2)}, u32[]{:S(2)}) collective-permute-start(f32[2,8,32,128]{3,2,1,0:T(8,128)S(1)} %pad_maximum_fusion.4), channel_id=1, source_target_pairs={{0,8},{1,9},{2,10},{3,11},{4,12},{5,13},{6,14},{7,15},{8,16},{9,17... | collective-permute-start | bytes 786440 | tf_op jit(solution)/shard_map/ppermute | solution.py:111
  14.8 1.5 %collective-permute-done.2 = f32[2,5,32,128]{3,2,1,0:T(8,128)S(1)} collective-permute-done((f32[2,5,32,128]{3,2,1,0:T(8,128)S(1)}, f32[2,5,32,128]{3,2,1,0:T(8,128)S(1)}, u32[]{:S(2)}, u32[]{:S(2)}) %collective-permute-start.2) | collective-permute-done | bytes 163872 | tf_op jit(solution)/shard_map/ppermute | solution.py:111
  16.3 1.8 %collective-permute-done = f32[2,5,32,128]{3,2,1,0:T(8,128)S(1)} collective-permute-done((f32[2,5,32,128]{3,2,1,0:T(8,128)S(1)}, f32[2,5,32,128]{3,2,1,0:T(8,128)S(1)}, u32[]{:S(2)}, u32[]{:S(2)}) %collective-permute-start) | collective-permute-done | bytes 163872 | tf_op jit(solution)/shard_map/ppermute | solution.py:94
  18.1 5.5 %collective-permute-start.6 = (f32[2,2,4,32,128]{4,3,2,1,0:T(8,128)S(1)}, f32[2,2,4,32,128]{4,3,2,1,0:T(8,128)S(1)}, u32[]{:S(2)}, u32[]{:S(2)}) collective-permute-start(f32[2,2,4,32,128]{4,3,2,1,0:T(8,128)S(1)} %get-tuple-element.101), channel_id=1, source_target_pairs={{1,0},{2,1},{3,2},{4,3},{5,4},{6,5},{7,6},{0,7},{9,8},{10,9},{11,1... | collective-permute-start | bytes 786440 | tf_op jit(solution)/shard_map/ppermute | solution.py:95
  23.6 0.9 pad_maximum_fusion.2
  25.5 2.8 %collective-permute-done.5 = f32[2,2,4,32,128]{4,3,2,1,0:T(8,128)S(1)} collective-permute-done((f32[2,2,4,32,128]{4,3,2,1,0:T(8,128)S(1)}, f32[2,2,4,32,128]{4,3,2,1,0:T(8,128)S(1)}, u32[]{:S(2)}, u32[]{:S(2)}) %collective-permute-start.5) | collective-permute-done | bytes 262176 | tf_op jit(solution)/shard_map/ppermute | solution.py:94
  28.3 4.7 %collective-permute-done.6 = f32[2,2,4,32,128]{4,3,2,1,0:T(8,128)S(1)} collective-permute-done((f32[2,2,4,32,128]{4,3,2,1,0:T(8,128)S(1)}, f32[2,2,4,32,128]{4,3,2,1,0:T(8,128)S(1)}, u32[]{:S(2)}, u32[]{:S(2)}) %collective-permute-start.6) | collective-permute-done | bytes 262176 | tf_op jit(solution)/shard_map/ppermute | solution.py:95
  33.1 1.5 %fusion.6 = (f32[1,16,32,128]{3,2,1,0:T(8,128)S(1)}, f32[1,16,32,128]{3,2,1,0:T(8,128)S(1)}) fusion(f32[2,2,16,32,128]{4,3,2,1,0:T(8,128)S(1)} %pad_maximum_fusion, f32[2,16,32,128]{3,2,1,0:T(8,128)S(1)} %fusion.2, f32[]{:T(128)} %bitcast.4, f32[2,18,32,128]{3,2,1,0:T(8,128)S(1)} %get-tuple-element.90, f32[]{:T(128)} %bitcast.6), kind=kLoop, calls=%fused_computation.39 | loop fusion | flops 524288 | bytes 2097160 | tf_op jit(solution)/shard_map/add | solution.py:127
  35.6 1.3 fusion.20
  37.7 0.8 pad_maximum_fusion.6.after_ref
  38.4 1.2 pad_maximum_fusion.1.own_ref
  39.6 0.8 pad_maximum_fusion.5.before_ref
  40.3 4.6 %shard_map.46 = (f32[2,10,32,128]{3,2,1,0:T(8,128)}, f32[2,10,32,128]{3,2,1,0:T(8,128)}, f32[2,10,32,128]{3,2,1,0:T(8,128)}, f32[2,10,32,128]{3,2,1,0:T(8,128)},...) custom-call(f32[2]{0:T(128)} %diff_ref.11, ...), custom_call_target="tpu_custom_call" | custom-call | tf_op jit(solution)/shard_map/pallas_call | solution.py:286
  44.9 4.7 %collective-permute-start.8 = (f32[2,6,16,128]{3,2,1,0:T(8,128)}, f32[2,6,16,128]{3,2,1,0:T(8,128)S(1)}, u32[]{:S(2)}, u32[]{:S(2)}) collective-permute-start(f32[2,6,16,128]{3,2,1,0:T(8,128)} %get-tuple-element.39), channel_id=1, source_target_pairs={{1,0},{2,1},{3,2},{4,3},{5,4},{6,5},{7,6},{0,7},{9,8},{10,9},{11,1... | collective-permute-start | bytes 294920 | tf_op jit(solution)/shard_map/ppermute | solution.py:502
  50.3 2.1 %collective-permute-done.7.cbefore_ref = f32[2,6,16,128]{3,2,1,0:T(8,128)S(1)} collective-permute-done((f32[2,6,16,128]{3,2,1,0:T(8,128)}, f32[2,6,16,128]{3,2,1,0:T(8,128)S(1)}, u32[]{:S(2)}, u32[]{:S(2)}) %collective-permute-start.7) | collective-permute-done | bytes 98336 | tf_op jit(solution)/shard_map/ppermute | solution.py:501
  53.1 4.7 %shard_map.47 = (f32[4,2,8,32,128]{4,3,2,1,0:T(8,128)}, f32[2,10,32,128]{3,2,1,0:T(8,128)}, f32[2,10,32,128]{3,2,1,0:T(8,128)}, f32[2,8,32,128]{3,2,1,0:T(8,128)}) custom-call(f32[2]{0:T(128)} %diff_ref.11, f32[4,2,4,16,128]{4,3,2,1,0:T(8,128)} %get-tuple-element.37.cown_ref, f32[2,6,16,128]{3,2,1,0:T(8,128)} %copy-done.7, f32[2,6,16,128]{3,2,1,0:T(8,128)} %copy-done.8, ...), custom_call_target="tpu_custom_call" | custom-call | tf_op jit(solution)/shard_map/pallas_call | solution.py:410
  57.8 1.9 %collective-permute-start.10 = (f32[2,8,32,128]{3,2,1,0:T(8,128)}, f32[2,8,32,128]{3,2,1,0:T(8,128)S(1)}, u32[]{:S(2)}, u32[]{:S(2)}) collective-permute-start(f32[2,8,32,128]{3,2,1,0:T(8,128)} %get-tuple-element.45), channel_id=1, source_target_pairs={{0,8},{1,9},{2,10},{3,11},{4,12},{5,13},{6,14},{7,15},{8,16},{9,17... | collective-permute-start | bytes 786440 | tf_op jit(solution)/shard_map/ppermute | solution.py:111
  59.7 4.7 %collective-permute-start.13 = (f32[2,10,32,128]{3,2,1,0:T(8,128)}, f32[2,10,32,128]{3,2,1,0:T(8,128)S(1)}, u32[]{:S(2)}, u32[]{:S(2)}) collective-permute-start(f32[2,10,32,128]{3,2,1,0:T(8,128)} %get-tuple-element.48), channel_id=1, source_target_pairs={{1,0},{2,1},{3,2},{4,3},{5,4},{6,5},{7,6},{0,7},{9,8},{10,9},{11,1... | collective-permute-start | bytes 983048 | tf_op jit(solution)/shard_map/ppermute | solution.py:538
  64.5 1.0 fusion.30
  65.5 1.9 %collective-permute-start.9 = (f32[2,5,32,128]{3,2,1,0:T(8,128)S(1)}, f32[2,5,32,128]{3,2,1,0:T(8,128)S(1)}, u32[]{:S(2)}, u32[]{:S(2)}) collective-permute-start(f32[2,5,32,128]{3,2,1,0:T(8,128)S(1)} %get-tuple-element.106), channel_id=1, source_target_pairs={{0,9},{1,10},{2,11},{3,12},{4,13},{5,14},{6,15},{7,8},{8,17},{9,18... | collective-permute-start | bytes 491528 | tf_op jit(solution)/shard_map/ppermute | solution.py:111
  67.4 1.9 %collective-permute-start.11 = (f32[2,5,32,128]{3,2,1,0:T(8,128)S(1)}, f32[2,5,32,128]{3,2,1,0:T(8,128)S(1)}, u32[]{:S(2)}, u32[]{:S(2)}) collective-permute-start(f32[2,5,32,128]{3,2,1,0:T(8,128)S(1)} %get-tuple-element.107), channel_id=1, source_target_pairs={{0,15},{1,8},{2,9},{3,10},{4,11},{5,12},{6,13},{7,14},{8,23},{9,16... | collective-permute-start | bytes 491528 | tf_op jit(solution)/shard_map/ppermute | solution.py:111
  69.4 9.9 %collective-permute-done.9 = f32[2,5,32,128]{3,2,1,0:T(8,128)S(1)} collective-permute-done((f32[2,5,32,128]{3,2,1,0:T(8,128)S(1)}, f32[2,5,32,128]{3,2,1,0:T(8,128)S(1)}, u32[]{:S(2)}, u32[]{:S(2)}) %collective-permute-start.9) | collective-permute-done | bytes 163872 | tf_op jit(solution)/shard_map/ppermute | solution.py:111
  79.3 0.9 maximum_select_fusion.1.b_ref
  81.2 4.6 %shard_map.48 = (f32[2,10,32,128]{3,2,1,0:T(8,128)}, f32[2,10,32,128]{3,2,1,0:T(8,128)}, f32[2,10,32,128]{3,2,1,0:T(8,128)}, f32[2,10,32,128]{3,2,1,0:T(8,128)},...) custom-call(f32[2]{0:T(128)} %diff_ref.11, ...), custom_call_target="tpu_custom_call" | custom-call | tf_op jit(solution)/shard_map/pallas_call | solution.py:286
  85.7 2.3 %collective-permute-start.14 = (f32[2,6,16,128]{3,2,1,0:T(8,128)}, f32[2,6,16,128]{3,2,1,0:T(8,128)S(1)}, u32[]{:S(2)}, u32[]{:S(2)}) collective-permute-start(f32[2,6,16,128]{3,2,1,0:T(8,128)} %get-tuple-element.50), channel_id=1, source_target_pairs={{0,1},{1,2},{2,3},{3,4},{4,5},{5,6},{6,7},{7,0},{8,9},{9,10},{10,1... | collective-permute-start | bytes 294920 | tf_op jit(solution)/shard_map/ppermute | solution.py:501
  88.1 2.9 %collective-permute-start.15 = (f32[2,6,16,128]{3,2,1,0:T(8,128)}, f32[2,6,16,128]{3,2,1,0:T(8,128)S(1)}, u32[]{:S(2)}, u32[]{:S(2)}) collective-permute-start(f32[2,6,16,128]{3,2,1,0:T(8,128)} %get-tuple-element.51), channel_id=1, source_target_pairs={{1,0},{2,1},{3,2},{4,3},{5,4},{6,5},{7,6},{0,7},{9,8},{10,9},{11,1... | collective-permute-start | bytes 294920 | tf_op jit(solution)/shard_map/ppermute | solution.py:502
  90.9 2.9 %collective-permute-done.14.cbefore_ref = f32[2,6,16,128]{3,2,1,0:T(8,128)S(1)} collective-permute-done((f32[2,6,16,128]{3,2,1,0:T(8,128)}, f32[2,6,16,128]{3,2,1,0:T(8,128)S(1)}, u32[]{:S(2)}, u32[]{:S(2)}) %collective-permute-start.14) | collective-permute-done | bytes 98336 | tf_op jit(solution)/shard_map/ppermute | solution.py:501
  93.8 2.0 %collective-permute-done.15.cafter_ref = f32[2,6,16,128]{3,2,1,0:T(8,128)S(1)} collective-permute-done((f32[2,6,16,128]{3,2,1,0:T(8,128)}, f32[2,6,16,128]{3,2,1,0:T(8,128)S(1)}, u32[]{:S(2)}, u32[]{:S(2)}) %collective-permute-start.15) | collective-permute-done | bytes 98336 | tf_op jit(solution)/shard_map/ppermute | solution.py:502
  96.5 4.7 %shard_map.49 = (f32[4,2,8,32,128]{4,3,2,1,0:T(8,128)}, f32[2,10,32,128]{3,2,1,0:T(8,128)}, f32[2,10,32,128]{3,2,1,0:T(8,128)}, f32[2,8,32,128]{3,2,1,0:T(8,128)}) custom-call(f32[2]{0:T(128)} %diff_ref.11, f32[4,2,4,16,128]{4,3,2,1,0:T(8,128)} %get-tuple-element.49.cown_ref, f32[2,6,16,128]{3,2,1,0:T(8,128)} %copy-done.9, f32[2,6,16,128]{3,2,1,0:T(8,128)} %copy-done.10, ...), custom_call_target="tpu_custom_call" | custom-call | tf_op jit(solution)/shard_map/pallas_call | solution.py:410
  101.1 2.0 %collective-permute-start.17 = (f32[2,8,32,128]{3,2,1,0:T(8,128)}, f32[2,8,32,128]{3,2,1,0:T(8,128)S(1)}, u32[]{:S(2)}, u32[]{:S(2)}) collective-permute-start(f32[2,8,32,128]{3,2,1,0:T(8,128)} %get-tuple-element.57), channel_id=1, source_target_pairs={{0,8},{1,9},{2,10},{3,11},{4,12},{5,13},{6,14},{7,15},{8,16},{9,17... | collective-permute-start | bytes 786440 | tf_op jit(solution)/shard_map/ppermute | solution.py:111
  103.2 4.7 %collective-permute-start.20 = (f32[2,10,32,128]{3,2,1,0:T(8,128)}, f32[2,10,32,128]{3,2,1,0:T(8,128)S(1)}, u32[]{:S(2)}, u32[]{:S(2)}) collective-permute-start(f32[2,10,32,128]{3,2,1,0:T(8,128)} %get-tuple-element.60), channel_id=1, source_target_pairs={{1,0},{2,1},{3,2},{4,3},{5,4},{6,5},{7,6},{0,7},{9,8},{10,9},{11,1... | collective-permute-start | bytes 983048 | tf_op jit(solution)/shard_map/ppermute | solution.py:538
  107.9 1.0 fusion.29
  109.0 1.9 %collective-permute-start.16 = (f32[2,5,32,128]{3,2,1,0:T(8,128)S(1)}, f32[2,5,32,128]{3,2,1,0:T(8,128)S(1)}, u32[]{:S(2)}, u32[]{:S(2)}) collective-permute-start(f32[2,5,32,128]{3,2,1,0:T(8,128)S(1)} %get-tuple-element.104), channel_id=1, source_target_pairs={{0,9},{1,10},{2,11},{3,12},{4,13},{5,14},{6,15},{7,8},{8,17},{9,18... | collective-permute-start | bytes 491528 | tf_op jit(solution)/shard_map/ppermute | solution.py:111
  110.9 2.1 %collective-permute-start.18 = (f32[2,5,32,128]{3,2,1,0:T(8,128)S(1)}, f32[2,5,32,128]{3,2,1,0:T(8,128)S(1)}, u32[]{:S(2)}, u32[]{:S(2)}) collective-permute-start(f32[2,5,32,128]{3,2,1,0:T(8,128)S(1)} %get-tuple-element.105), channel_id=1, source_target_pairs={{0,15},{1,8},{2,9},{3,10},{4,11},{5,12},{6,13},{7,14},{8,23},{9,16... | collective-permute-start | bytes 491528 | tf_op jit(solution)/shard_map/ppermute | solution.py:111
  113.0 11.3 %collective-permute-done.16 = f32[2,5,32,128]{3,2,1,0:T(8,128)S(1)} collective-permute-done((f32[2,5,32,128]{3,2,1,0:T(8,128)S(1)}, f32[2,5,32,128]{3,2,1,0:T(8,128)S(1)}, u32[]{:S(2)}, u32[]{:S(2)}) %collective-permute-start.16) | collective-permute-done | bytes 163872 | tf_op jit(solution)/shard_map/ppermute | solution.py:111
  124.3 0.9 maximum_select_fusion.2.b_ref
  126.0 4.6 %shard_map.50 = (f32[2,10,32,128]{3,2,1,0:T(8,128)}, f32[2,10,32,128]{3,2,1,0:T(8,128)}, f32[2,10,32,128]{3,2,1,0:T(8,128)}, f32[2,10,32,128]{3,2,1,0:T(8,128)},...) custom-call(f32[2]{0:T(128)} %diff_ref.11, ...), custom_call_target="tpu_custom_call" | custom-call | tf_op jit(solution)/shard_map/pallas_call | solution.py:286
  130.6 1.8 %collective-permute-start.21 = (f32[2,2,16,128]{3,2,1,0:T(8,128)}, f32[2,2,16,128]{3,2,1,0:T(8,128)S(1)}, u32[]{:S(2)}, u32[]{:S(2)}) collective-permute-start(f32[2,2,16,128]{3,2,1,0:T(8,128)} %get-tuple-element.62), channel_id=1, source_target_pairs={{0,1},{1,2},{2,3},{3,4},{4,5},{5,6},{6,7},{7,0},{8,9},{9,10},{10,1... | collective-permute-start | bytes 98312 | tf_op jit(solution)/shard_map/ppermute | solution.py:501
  132.4 3.1 %collective-permute-start.22 = (f32[2,2,16,128]{3,2,1,0:T(8,128)}, f32[2,2,16,128]{3,2,1,0:T(8,128)S(1)}, u32[]{:S(2)}, u32[]{:S(2)}) collective-permute-start(f32[2,2,16,128]{3,2,1,0:T(8,128)} %get-tuple-element.63), channel_id=1, source_target_pairs={{1,0},{2,1},{3,2},{4,3},{5,4},{6,5},{7,6},{0,7},{9,8},{10,9},{11,1... | collective-permute-start | bytes 98312 | tf_op jit(solution)/shard_map/ppermute | solution.py:502
  135.5 2.0 %collective-permute-done.21.cbefore_ref = f32[2,2,16,128]{3,2,1,0:T(8,128)S(1)} collective-permute-done((f32[2,2,16,128]{3,2,1,0:T(8,128)}, f32[2,2,16,128]{3,2,1,0:T(8,128)S(1)}, u32[]{:S(2)}, u32[]{:S(2)}) %collective-permute-start.21) | collective-permute-done | bytes 32800 | tf_op jit(solution)/shard_map/ppermute | solution.py:501
  138.2 3.0 %shard_map.51 = f32[2,8,32,128]{3,2,1,0:T(8,128)} custom-call(f32[2]{0:T(128)} %diff_ref.11, f32[4,2,4,16,128]{4,3,2,1,0:T(8,128)} %get-tuple-element.61.cown_ref, f32[2,2,16,128]{3,2,1,0:T(8,128)} %copy-done.11, f32[2,2,16,128]{3,2,1,0:T(8,128)} %copy-done.12, f32[2,8,16,128]{3,2,1,0:T(8,128)} %fusion.18.rate_ref, f32[2,8,16,128]{3,2,1,0:T(8,128)} %fusion.13.csrc_ref, ...), custom_call_target="tpu_custom_call" | custom-call | tf_op jit(solution)/shard_map/pallas_call | solution.py:410
  141.1 1.0 slice_bitcast_fusion.7
  142.2 0.8 copy.22
  (76 shorter events, 9.2 us)
Async XLA Ops:
  0.0 1.1 copy-start.4
  1.2 15.1 %collective-permute-start.2 = (f32[2,5,32,128]{3,2,1,0:T(8,128)S(1)}, f32[2,5,32,128]{3,2,1,0:T(8,128)S(1)}, u32[]{:S(2)}, u32[]{:S(2)}) collective-permute-start(f32[2,5,32,128]{3,2,1,0:T(8,128)S(1)} %get-tuple-element.108), channel_id=1, source_target_pairs={{0,9},{1,10},{2,11},{3,12},{4,13},{5,14},{6,15},{7,8},{8,17},{9,18... | collective-permute-start | bytes 491528 | tf_op jit(solution)/shard_map/ppermute | solution.py:111
  4.1 14.0 %collective-permute-start = (f32[2,5,32,128]{3,2,1,0:T(8,128)S(1)}, f32[2,5,32,128]{3,2,1,0:T(8,128)S(1)}, u32[]{:S(2)}, u32[]{:S(2)}) collective-permute-start(f32[2,5,32,128]{3,2,1,0:T(8,128)S(1)} %get-tuple-element.108), channel_id=1, source_target_pairs={{0,1},{1,2},{2,3},{3,4},{4,5},{5,6},{6,7},{7,0},{8,9},{9,10},{10,1... | collective-permute-start | bytes 491528 | tf_op jit(solution)/shard_map/ppermute | solution.py:94
  5.6 7.4 %copy-start.5 = (f32[2,8,32,128]{3,2,1,0:T(8,128)S(1)}, f32[2,8,32,128]{3,2,1,0:T(8,128)}, u32[]{:S(2)}) copy-start(f32[2,8,32,128]{3,2,1,0:T(8,128)} %param.5) | copy-start | bytes 786436
  5.6 17.9 %collective-permute-start.4 = (f32[2,5,32,128]{3,2,1,0:T(8,128)S(1)}, f32[2,5,32,128]{3,2,1,0:T(8,128)S(1)}, u32[]{:S(2)}, u32[]{:S(2)}) collective-permute-start(f32[2,5,32,128]{3,2,1,0:T(8,128)S(1)} %get-tuple-element.109), channel_id=1, source_target_pairs={{0,15},{1,8},{2,9},{3,10},{4,11},{5,12},{6,13},{7,14},{8,23},{9,16... | collective-permute-start | bytes 491528 | tf_op jit(solution)/shard_map/ppermute | solution.py:111
  8.6 15.0 %collective-permute-start.1 = (f32[2,5,32,128]{3,2,1,0:T(8,128)S(1)}, f32[2,5,32,128]{3,2,1,0:T(8,128)S(1)}, u32[]{:S(2)}, u32[]{:S(2)}) collective-permute-start(f32[2,5,32,128]{3,2,1,0:T(8,128)S(1)} %get-tuple-element.109), channel_id=1, source_target_pairs={{1,0},{2,1},{3,2},{4,3},{5,4},{6,5},{7,6},{0,7},{9,8},{10,9},{11,1... | collective-permute-start | bytes 491528 | tf_op jit(solution)/shard_map/ppermute | solution.py:95
  11.0 2.3 %copy-start.6 = (f32[2,8,32,128]{3,2,1,0:T(8,128)S(1)}, f32[2,8,32,128]{3,2,1,0:T(8,128)}, u32[]{:S(2)}) copy-start(f32[2,8,32,128]{3,2,1,0:T(8,128)} %param.6) | copy-start | bytes 786436
  11.0 12.6 %collective-permute-start.3 = (f32[2,8,32,128]{3,2,1,0:T(8,128)S(1)}, f32[2,8,32,128]{3,2,1,0:T(8,128)S(1)}, u32[]{:S(2)}, u32[]{:S(2)}) collective-permute-start(f32[2,8,32,128]{3,2,1,0:T(8,128)S(1)} %pad_maximum_fusion.4), channel_id=1, source_target_pairs={{0,8},{1,9},{2,10},{3,11},{4,12},{5,13},{6,14},{7,15},{8,16},{9,17... | collective-permute-start | bytes 786440 | tf_op jit(solution)/shard_map/ppermute | solution.py:111
  13.4 0.7 copy-start.13
  16.3 12.0 %collective-permute-start.5 = (f32[2,2,4,32,128]{4,3,2,1,0:T(8,128)S(1)}, f32[2,2,4,32,128]{4,3,2,1,0:T(8,128)S(1)}, u32[]{:S(2)}, u32[]{:S(2)}) collective-permute-start(f32[2,2,4,32,128]{4,3,2,1,0:T(8,128)S(1)} %get-tuple-element.100), channel_id=1, source_target_pairs={{0,1},{1,2},{2,3},{3,4},{4,5},{5,6},{6,7},{7,0},{8,9},{9,10},{10,1... | collective-permute-start | bytes 786440 | tf_op jit(solution)/shard_map/ppermute | solution.py:94
  18.1 14.9 %collective-permute-start.6 = (f32[2,2,4,32,128]{4,3,2,1,0:T(8,128)S(1)}, f32[2,2,4,32,128]{4,3,2,1,0:T(8,128)S(1)}, u32[]{:S(2)}, u32[]{:S(2)}) collective-permute-start(f32[2,2,4,32,128]{4,3,2,1,0:T(8,128)S(1)} %get-tuple-element.101), channel_id=1, source_target_pairs={{1,0},{2,1},{3,2},{4,3},{5,4},{6,5},{7,6},{0,7},{9,8},{10,9},{11,1... | collective-permute-start | bytes 786440 | tf_op jit(solution)/shard_map/ppermute | solution.py:95
  44.9 7.5 %collective-permute-start.7 = (f32[2,6,16,128]{3,2,1,0:T(8,128)}, f32[2,6,16,128]{3,2,1,0:T(8,128)S(1)}, u32[]{:S(2)}, u32[]{:S(2)}) collective-permute-start(f32[2,6,16,128]{3,2,1,0:T(8,128)} %get-tuple-element.38), channel_id=1, source_target_pairs={{0,1},{1,2},{2,3},{3,4},{4,5},{5,6},{6,7},{7,0},{8,9},{9,10},{10,1... | collective-permute-start | bytes 294920 | tf_op jit(solution)/shard_map/ppermute | solution.py:501
  44.9 7.5 %collective-permute-start.8 = (f32[2,6,16,128]{3,2,1,0:T(8,128)}, f32[2,6,16,128]{3,2,1,0:T(8,128)S(1)}, u32[]{:S(2)}, u32[]{:S(2)}) collective-permute-start(f32[2,6,16,128]{3,2,1,0:T(8,128)} %get-tuple-element.39), channel_id=1, source_target_pairs={{1,0},{2,1},{3,2},{4,3},{5,4},{6,5},{7,6},{0,7},{9,8},{10,9},{11,1... | collective-permute-start | bytes 294920 | tf_op jit(solution)/shard_map/ppermute | solution.py:502
  52.4 0.7 copy-start.7
  52.4 0.7 copy-start.8
  57.8 21.5 %collective-permute-start.10 = (f32[2,8,32,128]{3,2,1,0:T(8,128)}, f32[2,8,32,128]{3,2,1,0:T(8,128)S(1)}, u32[]{:S(2)}, u32[]{:S(2)}) collective-permute-start(f32[2,8,32,128]{3,2,1,0:T(8,128)} %get-tuple-element.45), channel_id=1, source_target_pairs={{0,8},{1,9},{2,10},{3,11},{4,12},{5,13},{6,14},{7,15},{8,16},{9,17... | collective-permute-start | bytes 786440 | tf_op jit(solution)/shard_map/ppermute | solution.py:111
  59.7 20.5 %collective-permute-start.12 = (f32[2,10,32,128]{3,2,1,0:T(8,128)}, f32[2,10,32,128]{3,2,1,0:T(8,128)S(1)}, u32[]{:S(2)}, u32[]{:S(2)}) collective-permute-start(f32[2,10,32,128]{3,2,1,0:T(8,128)} %get-tuple-element.47), channel_id=1, source_target_pairs={{0,1},{1,2},{2,3},{3,4},{4,5},{5,6},{6,7},{7,0},{8,9},{9,10},{10,1... | collective-permute-start | bytes 983048 | tf_op jit(solution)/shard_map/ppermute | solution.py:537
  59.7 20.7 %collective-permute-start.13 = (f32[2,10,32,128]{3,2,1,0:T(8,128)}, f32[2,10,32,128]{3,2,1,0:T(8,128)S(1)}, u32[]{:S(2)}, u32[]{:S(2)}) collective-permute-start(f32[2,10,32,128]{3,2,1,0:T(8,128)} %get-tuple-element.48), channel_id=1, source_target_pairs={{1,0},{2,1},{3,2},{4,3},{5,4},{6,5},{7,6},{0,7},{9,8},{10,9},{11,1... | collective-permute-start | bytes 983048 | tf_op jit(solution)/shard_map/ppermute | solution.py:538
  65.5 13.8 %collective-permute-start.9 = (f32[2,5,32,128]{3,2,1,0:T(8,128)S(1)}, f32[2,5,32,128]{3,2,1,0:T(8,128)S(1)}, u32[]{:S(2)}, u32[]{:S(2)}) collective-permute-start(f32[2,5,32,128]{3,2,1,0:T(8,128)S(1)} %get-tuple-element.106), channel_id=1, source_target_pairs={{0,9},{1,10},{2,11},{3,12},{4,13},{5,14},{6,15},{7,8},{8,17},{9,18... | collective-permute-start | bytes 491528 | tf_op jit(solution)/shard_map/ppermute | solution.py:111
  67.4 11.9 %collective-permute-start.11 = (f32[2,5,32,128]{3,2,1,0:T(8,128)S(1)}, f32[2,5,32,128]{3,2,1,0:T(8,128)S(1)}, u32[]{:S(2)}, u32[]{:S(2)}) collective-permute-start(f32[2,5,32,128]{3,2,1,0:T(8,128)S(1)} %get-tuple-element.107), channel_id=1, source_target_pairs={{0,15},{1,8},{2,9},{3,10},{4,11},{5,12},{6,13},{7,14},{8,23},{9,16... | collective-permute-start | bytes 491528 | tf_op jit(solution)/shard_map/ppermute | solution.py:111
  80.2 0.7 copy-start.2
  80.4 0.7 copy-start.3
  85.7 8.1 %collective-permute-start.14 = (f32[2,6,16,128]{3,2,1,0:T(8,128)}, f32[2,6,16,128]{3,2,1,0:T(8,128)S(1)}, u32[]{:S(2)}, u32[]{:S(2)}) collective-permute-start(f32[2,6,16,128]{3,2,1,0:T(8,128)} %get-tuple-element.50), channel_id=1, source_target_pairs={{0,1},{1,2},{2,3},{3,4},{4,5},{5,6},{6,7},{7,0},{8,9},{9,10},{10,1... | collective-permute-start | bytes 294920 | tf_op jit(solution)/shard_map/ppermute | solution.py:501
  88.1 7.8 %collective-permute-start.15 = (f32[2,6,16,128]{3,2,1,0:T(8,128)}, f32[2,6,16,128]{3,2,1,0:T(8,128)S(1)}, u32[]{:S(2)}, u32[]{:S(2)}) collective-permute-start(f32[2,6,16,128]{3,2,1,0:T(8,128)} %get-tuple-element.51), channel_id=1, source_target_pairs={{1,0},{2,1},{3,2},{4,3},{5,4},{6,5},{7,6},{0,7},{9,8},{10,9},{11,1... | collective-permute-start | bytes 294920 | tf_op jit(solution)/shard_map/ppermute | solution.py:502
  93.8 2.1 %copy-start.9 = (f32[2,6,16,128]{3,2,1,0:T(8,128)}, f32[2,6,16,128]{3,2,1,0:T(8,128)S(1)}, u32[]{:S(2)}) copy-start(f32[2,6,16,128]{3,2,1,0:T(8,128)S(1)} %collective-permute-done.14.cbefore_ref) | copy-start | bytes 294916
  95.9 0.6 copy-start.10
  101.1 23.1 %collective-permute-start.17 = (f32[2,8,32,128]{3,2,1,0:T(8,128)}, f32[2,8,32,128]{3,2,1,0:T(8,128)S(1)}, u32[]{:S(2)}, u32[]{:S(2)}) collective-permute-start(f32[2,8,32,128]{3,2,1,0:T(8,128)} %get-tuple-element.57), channel_id=1, source_target_pairs={{0,8},{1,9},{2,10},{3,11},{4,12},{5,13},{6,14},{7,15},{8,16},{9,17... | collective-permute-start | bytes 786440 | tf_op jit(solution)/shard_map/ppermute | solution.py:111
  103.2 22.0 %collective-permute-start.19 = (f32[2,10,32,128]{3,2,1,0:T(8,128)}, f32[2,10,32,128]{3,2,1,0:T(8,128)S(1)}, u32[]{:S(2)}, u32[]{:S(2)}) collective-permute-start(f32[2,10,32,128]{3,2,1,0:T(8,128)} %get-tuple-element.59), channel_id=1, source_target_pairs={{0,1},{1,2},{2,3},{3,4},{4,5},{5,6},{6,7},{7,0},{8,9},{9,10},{10,1... | collective-permute-start | bytes 983048 | tf_op jit(solution)/shard_map/ppermute | solution.py:537
  103.2 22.0 %collective-permute-start.20 = (f32[2,10,32,128]{3,2,1,0:T(8,128)}, f32[2,10,32,128]{3,2,1,0:T(8,128)S(1)}, u32[]{:S(2)}, u32[]{:S(2)}) collective-permute-start(f32[2,10,32,128]{3,2,1,0:T(8,128)} %get-tuple-element.60), channel_id=1, source_target_pairs={{1,0},{2,1},{3,2},{4,3},{5,4},{6,5},{7,6},{0,7},{9,8},{10,9},{11,1... | collective-permute-start | bytes 983048 | tf_op jit(solution)/shard_map/ppermute | solution.py:538
  109.0 15.3 %collective-permute-start.16 = (f32[2,5,32,128]{3,2,1,0:T(8,128)S(1)}, f32[2,5,32,128]{3,2,1,0:T(8,128)S(1)}, u32[]{:S(2)}, u32[]{:S(2)}) collective-permute-start(f32[2,5,32,128]{3,2,1,0:T(8,128)S(1)} %get-tuple-element.104), channel_id=1, source_target_pairs={{0,9},{1,10},{2,11},{3,12},{4,13},{5,14},{6,15},{7,8},{8,17},{9,18... | collective-permute-start | bytes 491528 | tf_op jit(solution)/shard_map/ppermute | solution.py:111
  110.9 13.4 %collective-permute-start.18 = (f32[2,5,32,128]{3,2,1,0:T(8,128)S(1)}, f32[2,5,32,128]{3,2,1,0:T(8,128)S(1)}, u32[]{:S(2)}, u32[]{:S(2)}) collective-permute-start(f32[2,5,32,128]{3,2,1,0:T(8,128)S(1)} %get-tuple-element.105), channel_id=1, source_target_pairs={{0,15},{1,8},{2,9},{3,10},{4,11},{5,12},{6,13},{7,14},{8,23},{9,16... | collective-permute-start | bytes 491528 | tf_op jit(solution)/shard_map/ppermute | solution.py:111
  125.2 0.7 copy-start
  125.2 0.8 copy-start.1
  130.6 6.9 %collective-permute-start.21 = (f32[2,2,16,128]{3,2,1,0:T(8,128)}, f32[2,2,16,128]{3,2,1,0:T(8,128)S(1)}, u32[]{:S(2)}, u32[]{:S(2)}) collective-permute-start(f32[2,2,16,128]{3,2,1,0:T(8,128)} %get-tuple-element.62), channel_id=1, source_target_pairs={{0,1},{1,2},{2,3},{3,4},{4,5},{5,6},{6,7},{7,0},{8,9},{9,10},{10,1... | collective-permute-start | bytes 98312 | tf_op jit(solution)/shard_map/ppermute | solution.py:501
  132.4 5.1 %collective-permute-start.22 = (f32[2,2,16,128]{3,2,1,0:T(8,128)}, f32[2,2,16,128]{3,2,1,0:T(8,128)S(1)}, u32[]{:S(2)}, u32[]{:S(2)}) collective-permute-start(f32[2,2,16,128]{3,2,1,0:T(8,128)} %get-tuple-element.63), channel_id=1, source_target_pairs={{1,0},{2,1},{3,2},{4,3},{5,4},{6,5},{7,6},{0,7},{9,8},{10,9},{11,1... | collective-permute-start | bytes 98312 | tf_op jit(solution)/shard_map/ppermute | solution.py:502
  137.5 0.6 copy-start.11
  137.5 0.6 copy-start.12

commit v4 on v3

--- a/solution.py
+++ b/solution.py
@@ -96,10 +96,9 @@
     return jnp.concatenate([before, a, after], axis=a.ndim - 3)
 
 
-def from_previous_slice(a, h):
+def from_previous_slice(pieces):
     slices = lax.axis_size("tm")
     size = lax.axis_size("space")
-    rows = a.shape[-3]
     axes = ("tm", "space")
 
     def moved(piece, shift):
@@ -110,12 +109,8 @@
         ]
         return lax.ppermute(piece, axes, pairs)
 
-    centre = moved(a, 0)
-    if h == 0:
-        return centre
-    before = moved(lax.slice_in_dim(a, rows - h, rows, axis=a.ndim - 3), 1)
-    after = moved(lax.slice_in_dim(a, 0, h, axis=a.ndim - 3), -1)
-    return jnp.concatenate([before, centre, after], axis=a.ndim - 3)
+    own, lasts, firsts = pieces
+    return moved(own, 0), moved(lasts, 1), moved(firsts, -1)
 
 
 def react_terms(field, laplace, diffusivity, source):
@@ -198,12 +193,13 @@
     return (upper + lower) * 0.25
 
 
-def sweep_kernel(widths_sent, diff_ref, b_ref, own_ref, before_ref, after_ref, dec_ref, src_ref,
-                 rate_ref, n1_ref, n2_ref, n3_ref, n4_ref, e0_ref, cown_ref, clasts_ref,
+def sweep_kernel(widths_sent, diff_ref, flag_ref, start_ref, centre_ref, bbefore_ref, bafter_ref,
+                 own_ref, before_ref, after_ref, dec_ref, src_ref,
+                 rate_ref, n1_ref, n2_ref, n3_ref, n4_ref, e0_ref, b0_ref, cown_ref, clasts_ref,
                  cfirsts_ref):
     spread_table, grouped_table, interp_table, widths = node_tables()
     rows = e0_ref.shape[1]
-    hs = (b_ref.shape[1] - rows) // 2
+    hs = (start_ref.shape[1] - rows) // 2
     hd = (dec_ref.shape[1] - rows) // 2
     d0 = diff_ref[0]
     d1 = diff_ref[1]
@@ -234,7 +230,8 @@
             )
         )
         offset += w
-    swept = [b_ref[...]]
+    joined = jnp.concatenate([bbefore_ref[...], centre_ref[...], bafter_ref[...]], axis=1)
+    swept = [jnp.where(flag_ref[0] == 1, start_ref[...], joined)]
     found = []
     for m in range(4):
         have = hs - m
@@ -272,11 +269,12 @@
     for m, out in ((1, n1_ref), (2, n2_ref), (3, n3_ref), (4, n4_ref)):
         out[...] = cut(swept[m], hs - m, 1)
     e0_ref[...] = cut(found[0], hs - 1, 0)
-
-
-def fine_sweep(diffusivity, begin, parts, decay, src, rate_c, widths_sent):
-    rows = begin.shape[1] - 2 * START_HALO
-    shape = begin.shape
+    b0_ref[...] = cut(swept[0], hs, 0)
+
+
+def fine_sweep(diffusivity, flag, start, prior, parts, decay, src, rate_c, widths_sent):
+    rows = start.shape[1] - 2 * START_HALO
+    shape = start.shape
     wide = jax.ShapeDtypeStruct((shape[0], rows + 2) + shape[2:], jnp.float32)
     own = jax.ShapeDtypeStruct((shape[0], rows) + shape[2:], jnp.float32)
     cshape = (shape[0], rows // 2, shape[2] // 2, shape[3])
@@ -285,10 +283,10 @@
     vmem = pl.BlockSpec(memory_space=pltpu.VMEM)
     return pl.pallas_call(
         functools.partial(sweep_kernel, widths_sent),
-        out_shape=(wide, wide, wide, wide, own, cown, cedge, cedge),
-        in_specs=[pl.BlockSpec(memory_space=pltpu.SMEM)] + [vmem] * 7,
-        out_specs=(vmem,) * 8,
-    )(diffusivity, begin, *parts, decay, src, rate_c)
+        out_shape=(wide, wide, wide, wide, own, own, cown, cedge, cedge),
+        in_specs=[pl.BlockSpec(memory_space=pltpu.SMEM)] * 2 + [vmem] * 10,
+        out_specs=(vmem,) * 9,
+    )(diffusivity, flag, start, *prior, *parts, decay, src, rate_c)
 
 
 def coarse_kernel_laplace(f):
@@ -327,7 +325,7 @@
     one, mid, low, late = joined
     hcr = (rate_ref.shape[1] - crows) // 2
     hd = (dec_ref.shape[1] - rows) // 2
-    hs = (b_ref.shape[1] - rows) // 2
+    hs = START_HALO
     d0 = diff_ref[0]
     d1 = diff_ref[1]
 
@@ -372,10 +370,10 @@
     if last:
         outs[0][...] = news[4]
         return
-    own_out, lasts_out, firsts_out, u4_out = outs
+    own_out, lasts_out, firsts_out, u4_out, u4_last_out, u4_first_out = outs
     src1 = at(src_ref, 0, rows, hd)
     dec0 = at(dec_ref, 0, rows, hd)
-    states = [at(b_ref, 0, rows, hs)] + [cut(news[m], 1, 0) for m in range(1, 5)]
+    states = [b_ref[...]] + [cut(news[m], 1, 0) for m in range(1, 5)]
     terms = [e0_ref[...]] + [
         react(cut(news[m], 1, 0), kernel_laplace(news[m]), src1) for m in range(1, 5)
     ]
@@ -392,6 +390,8 @@
         firsts_out[:, offset:offset + w] = part[:, :w]
         offset += w
     u4_out[...] = states[4]
+    u4_last_out[...] = states[4][:, rows - hs:]
+    u4_first_out[...] = states[4][:, :hs]
 
 
 def finish_round(diffusivity, coarse, rate_c, source_c, swept, e0, decay, src, last, widths_sent):
@@ -404,7 +404,8 @@
     else:
         sent = sum(START_HALO - 1 - m for m in range(4))
         edge = jax.ShapeDtypeStruct((shape[0], sent) + shape[2:], jnp.float32)
-        out_shape = (jax.ShapeDtypeStruct((4,) + field.shape, jnp.float32), edge, edge, field)
+        rim = jax.ShapeDtypeStruct((shape[0], START_HALO) + shape[2:], jnp.float32)
+        out_shape = (jax.ShapeDtypeStruct((4,) + field.shape, jnp.float32), edge, edge, field, rim, rim)
     vmem = pl.BlockSpec(memory_space=pltpu.VMEM)
     args = (diffusivity, *coarse, rate_c, source_c, *swept[1:], begin, e0, decay, src)
     return pl.pallas_call(
@@ -452,12 +453,14 @@
     first_slice = lax.axis_index("tm") == 0
     hs = START_HALO
     assert hs == 5 and initial.shape[-3] >= hs
-    hfix = hs - 1
 
     own_start = to_even_odd(initial[0])
-    fixed = space_halo(jnp.stack([to_even_odd(decay_rate), to_even_odd(source)]), hfix)
-    decay = (fixed[0], hfix)
-    src = (fixed[1], hfix)
+    fixed = space_halo(
+        jnp.stack([own_start, to_even_odd(decay_rate), to_even_odd(source)]), hs
+    )
+    own_ext = fixed[0]
+    decay = (fixed[1], hs)
+    src = (fixed[2], hs)
     rate_c = restrict(decay)
     source_c = restrict(src)
 
@@ -491,10 +494,10 @@
             out.append((own, h))
         return out
 
-    def advance(begin, pieces, last):
+    def advance(prior, pieces, last):
         widths_sent = (1, 1, 0, 0) if last else (2, 2, 1, 1)
-        n1, n2, n3, n4, e0, cown, clasts, cfirsts = fine_sweep(
-            diffusivity, begin[0], pieces, decay[0], src[0], rate_c[0], widths_sent
+        n1, n2, n3, n4, e0, b0, cown, clasts, cfirsts = fine_sweep(
+            diffusivity, flag, own_ext, prior, pieces, decay[0], src[0], rate_c[0], widths_sent
         )
         coarse = (
             cown,
@@ -503,15 +506,14 @@
         )
         return finish_round(
             diffusivity, coarse, rate_c[0], source_c[0],
-            (begin[0], n1, n2, n3, n4), e0, decay[0], src[0], last, widths_sent,
+            (b0, n1, n2, n3, n4), e0, decay[0], src[0], last, widths_sent,
         )
 
     size = lax.axis_size("space")
     up = [(i, (i + 1) % size) for i in range(size)]
     down = [((i + 1) % size, i) for i in range(size)]
     rows = own_start.shape[-3]
-    own_ext = space_halo(own_start, hs)
-    begin = (jnp.where(first_slice, own_ext, from_previous_slice(own_start, hs)), hs)
+    flag = jnp.where(first_slice, 1, 0).astype(jnp.int32).reshape(1)
     state = (own_ext, hs)
     state_terms = fine_E(state)
     parts = step_terms([state] * 5, [state_terms] * 5)
@@ -527,18 +529,20 @@
              for m, p in enumerate(wide)], axis=1
         ),
     )
+    prior = from_previous_slice(
+        (own_start, own_start[:, rows - hs:], own_start[:, :hs])
+    )
     for k in range(ROUNDS):
         last = k + 1 == ROUNDS
-        outs = advance(begin, pieces, last)
+        outs = advance(prior, pieces, last)
         if not last:
-            own4, lasts, firsts, u4 = outs
+            own4, lasts, firsts, u4, u4_last, u4_first = outs
             pieces = (
                 own4,
                 lax.ppermute(lasts, "space", up),
                 lax.ppermute(firsts, "space", down),
             )
-            prior = from_previous_slice(u4, hs)
-            begin = (jnp.where(first_slice, own_ext, prior), hs)
+            prior = from_previous_slice((u4, u4_last, u4_first))
     return from_even_odd(outs[0])[None]
 
 

time: 144 us -> 147 us (1.021)
  waiting for transfers between devices: 41.3 us -> 50.8 us
  starting transfers between devices: 53.5 us -> 46.6 us
  other arithmetic: 9.82 us -> 7.81 us
    ppermute x2 -> x1, waiting for transfers between devices: 4.57 us -> 15.2 us  [space_halo(): lax.ppermute(lax.slice_in_dim(a, rows - h, rows, axis=a.ndim - 3), 'space...]
    ppermute x2 -> x1, starting transfers between devices: 7.85 us -> 3.2 us  [space_halo(): lax.ppermute(lax.slice_in_dim(a, 0, h, axis=a.ndim - 3), 'space', down)]
    slice x6, local copies, waits for them, and re-layouts: 1.44 us -> 5.84 us  [to_even_odd(): return jnp.concatenate([a[..., 0::2, :], a[..., 1::2, :]], axis=-2)]
    slice x3 -> x2, local copies, waits for them, and re-layouts: 3.36 us -> 0.14 us  [the longest x1 0.1 us: space_halo(): lax.slice_in_dim(a, rows - h, rows, axis=a.ndim - 3)]
    ppermute x2 -> x1, waiting for transfers between devices: 4.7 us -> 2.2 us  [space_halo(): lax.ppermute(lax.slice_in_dim(a, 0, h, axis=a.ndim - 3), 'space', down)]
    ppermute x2, waiting for transfers between devices: 0.23 us -> 2.67 us  [per_device(): lax.ppermute(firsts, 'space', down)]
    select_n x2 -> x0, other arithmetic: 1.8 us -> none  [per_device(): begin = (jnp.where(first_slice, own_ext, prior), hs)]
    ppermute x9, starting transfers between devices: 19.7 us -> 18.2 us  [moved(): return lax.ppermute(piece, axes, pairs)]
  transfers between devices with their start and end apart: 23 -> 21, of which waited for: 11 -> 11; matrix products, arithmetic and copies ran while one was open for 5% -> 6% of each run, Pallas kernels for 0% -> 0%
where the time goes in v4:
time: 147 us; the launch traced here: 146 us
  waiting for transfers between devices  50.8 us (35%)
  starting transfers between devices  46.6 us (32%)
  Pallas kernels  26.8 us (18%)
  local copies, waits for them, and re-layouts  13.4 us (9%)
  other arithmetic  7.81 us (5%)
    ppermute x9, waiting for transfers between devices, moved(): return lax.ppermute(piece, axes, pairs)  21.5 us
    ppermute x9, starting transfers between devices, moved(): return lax.ppermute(piece, axes, pairs)  18.2 us
    ppermute x1, waiting for transfers between devices, space_halo(): lax.ppermute(lax.slice_in_dim(a, rows - h, rows, axis=a.ndim - 3), 'space...  15.2 us
    pallas_call x3, Pallas kernels, fine_sweep(): pl.pallas_call(functools.partial(sweep_kernel, widths_sent), out_shape=(w...  14.7 us
    pallas_call x3, Pallas kernels, finish_round(): pl.pallas_call(functools.partial(finish_kernel, widths_sent), out_shape=o...  12 us
    ppermute x3, starting transfers between devices, advance(): lax.ppermute(cfirsts, 'space', down)  10.6 us
    ppermute x2, starting transfers between devices, per_device(): lax.ppermute(firsts, 'space', down)  8.72 us
    ppermute x3, waiting for transfers between devices, advance(): lax.ppermute(clasts, 'space', up)  7.45 us
  transfers between devices with their start and end apart: 21, of which 11 were waited for; matrix products, arithmetic and copies ran while one was open for 6% of the time, Pallas kernels for 0%

profile of v4, /device:TPU:2, one launch (start us, length us, event | category | flops | bytes accessed | tf_op | source)
XLA Modules:
  0.0 145.9 jit_solution(9907871873080838349)
XLA Ops:
  0.0 1.0 slice.229
  1.0 1.0 slice.228
  1.9 1.0 slice.231
  2.9 1.0 slice.230
  3.9 1.0 slice.233
  4.9 1.0 slice.232
  6.1 1.6 %collective-permute-start = (f32[3,2,5,32,128]{4,3,2,1,0:T(8,128)S(1)}, f32[3,2,5,32,128]{4,3,2,1,0:T(8,128)S(1)}, u32[]{:S(2)}, u32[]{:S(2)}) collective-permute-start(f32[3,2,5,32,128]{4,3,2,1,0:T(8,128)S(1)} %get-tuple-element.93), channel_id=1, source_target_pairs={{0,1},{1,2},{2,3},{3,4},{4,5},{5,6},{6,7},{7,0},{8,9},{9,10},{10,1... | collective-permute-start | bytes 1474568 | tf_op jit(solution)/shard_map/ppermute | solution.py:94
  7.7 3.2 %collective-permute-start.1 = (f32[3,2,5,32,128]{4,3,2,1,0:T(8,128)S(1)}, f32[3,2,5,32,128]{4,3,2,1,0:T(8,128)S(1)}, u32[]{:S(2)}, u32[]{:S(2)}) collective-permute-start(f32[3,2,5,32,128]{4,3,2,1,0:T(8,128)S(1)} %get-tuple-element.94), channel_id=1, source_target_pairs={{1,0},{2,1},{3,2},{4,3},{5,4},{6,5},{7,6},{0,7},{9,8},{10,9},{11,1... | collective-permute-start | bytes 1474568 | tf_op jit(solution)/shard_map/ppermute | solution.py:95
  10.9 0.8 fusion.6
  11.7 2.6 %collective-permute-start.4 = (f32[2,5,32,128]{3,2,1,0:T(8,128)}, f32[2,5,32,128]{3,2,1,0:T(8,128)S(1)}, u32[]{:S(2)}, u32[]{:S(2)}) collective-permute-start(f32[2,5,32,128]{3,2,1,0:T(8,128)} %get-tuple-element.116), channel_id=1, source_target_pairs={{0,15},{1,8},{2,9},{3,10},{4,11},{5,12},{6,13},{7,14},{8,23},{9,16... | collective-permute-start | bytes 491528 | tf_op jit(solution)/shard_map/ppermute | solution.py:110
  14.3 1.9 %collective-permute-start.3 = (f32[2,5,32,128]{3,2,1,0:T(8,128)}, f32[2,5,32,128]{3,2,1,0:T(8,128)}, u32[]{:S(2)}, u32[]{:S(2)}) collective-permute-start(f32[2,5,32,128]{3,2,1,0:T(8,128)} %get-tuple-element.117), channel_id=1, source_target_pairs={{0,9},{1,10},{2,11},{3,12},{4,13},{5,14},{6,15},{7,8},{8,17},{9,18... | collective-permute-start | bytes 491528 | tf_op jit(solution)/shard_map/ppermute | solution.py:110
  16.3 1.9 %collective-permute-start.2 = (f32[2,8,32,128]{3,2,1,0:T(8,128)S(1)}, f32[2,8,32,128]{3,2,1,0:T(8,128)S(1)}, u32[]{:S(2)}, u32[]{:S(2)}) collective-permute-start(f32[2,8,32,128]{3,2,1,0:T(8,128)S(1)} %get-tuple-element.118), channel_id=1, source_target_pairs={{0,8},{1,9},{2,10},{3,11},{4,12},{5,13},{6,14},{7,15},{8,16},{9,17... | collective-permute-start | bytes 786440 | tf_op jit(solution)/shard_map/ppermute | solution.py:110
  18.8 15.2 %collective-permute-done = f32[3,2,5,32,128]{4,3,2,1,0:T(8,128)S(1)} collective-permute-done((f32[3,2,5,32,128]{4,3,2,1,0:T(8,128)S(1)}, f32[3,2,5,32,128]{4,3,2,1,0:T(8,128)S(1)}, u32[]{:S(2)}, u32[]{:S(2)}) %collective-permute-start) | collective-permute-done | bytes 491552 | tf_op jit(solution)/shard_map/ppermute | solution.py:94
  34.0 2.2 %collective-permute-done.1 = f32[3,2,5,32,128]{4,3,2,1,0:T(8,128)S(1)} collective-permute-done((f32[3,2,5,32,128]{4,3,2,1,0:T(8,128)S(1)}, f32[3,2,5,32,128]{4,3,2,1,0:T(8,128)S(1)}, u32[]{:S(2)}, u32[]{:S(2)}) %collective-permute-start.1) | collective-permute-done | bytes 491552 | tf_op jit(solution)/shard_map/ppermute | solution.py:95
  37.6 1.4 slice_add_fusion.2
  40.8 0.8 pad_maximum_fusion.6.after_ref
  41.5 0.8 pad_maximum_fusion.5.before_ref
  42.3 1.1 pad_maximum_fusion.1.own_ref
  44.2 4.9 %shard_map.46 = (f32[2,10,32,128]{3,2,1,0:T(8,128)}, f32[2,10,32,128]{3,2,1,0:T(8,128)}, f32[2,10,32,128]{3,2,1,0:T(8,128)}, f32[2,10,32,128]{3,2,1,0:T(8,128)},...) custom-call(f32[2]{0:T(128)} %diff_ref.11, ...), custom_call_target="tpu_custom_call" | custom-call | tf_op jit(solution)/shard_map/pallas_call | solution.py:284
  49.4 4.4 %collective-permute-start.6 = (f32[2,6,16,128]{3,2,1,0:T(8,128)}, f32[2,6,16,128]{3,2,1,0:T(8,128)S(1)}, u32[]{:S(2)}, u32[]{:S(2)}) collective-permute-start(f32[2,6,16,128]{3,2,1,0:T(8,128)} %get-tuple-element.46), channel_id=1, source_target_pairs={{1,0},{2,1},{3,2},{4,3},{5,4},{6,5},{7,6},{0,7},{9,8},{10,9},{11,1... | collective-permute-start | bytes 294920 | tf_op jit(solution)/shard_map/ppermute | solution.py:505
  54.5 2.2 %collective-permute-done.5.cbefore_ref = f32[2,6,16,128]{3,2,1,0:T(8,128)S(1)} collective-permute-done((f32[2,6,16,128]{3,2,1,0:T(8,128)}, f32[2,6,16,128]{3,2,1,0:T(8,128)S(1)}, u32[]{:S(2)}, u32[]{:S(2)}) %collective-permute-start.5) | collective-permute-done | bytes 98336 | tf_op jit(solution)/shard_map/ppermute | solution.py:504
  57.5 4.6 %shard_map.47 = (f32[4,2,8,32,128]{4,3,2,1,0:T(8,128)}, f32[2,10,32,128]{3,2,1,0:T(8,128)}, f32[2,10,32,128]{3,2,1,0:T(8,128)}, f32[2,8,32,128]{3,2,1,0:T(8,128)...) custom-call(f32[2]{0:T(128)} %diff_ref.11, f32[4,2,4,16,128]{4,3,2,1,0:T(8,128)} %get-tuple-element.44.cown_ref, ...), custom_call_target="tpu_custom_call" | custom-call | tf_op jit(solution)/shard_map/pallas_call | solution.py:411
  62.0 0.8 collective-permute-start.10
  62.8 4.0 %collective-permute-start.11 = (f32[2,10,32,128]{3,2,1,0:T(8,128)}, f32[2,10,32,128]{3,2,1,0:T(8,128)S(1)}, u32[]{:S(2)}, u32[]{:S(2)}) collective-permute-start(f32[2,10,32,128]{3,2,1,0:T(8,128)} %get-tuple-element.58), channel_id=1, source_target_pairs={{1,0},{2,1},{3,2},{4,3},{5,4},{6,5},{7,6},{0,7},{9,8},{10,9},{11,1... | collective-permute-start | bytes 983048 | tf_op jit(solution)/shard_map/ppermute | solution.py:543
  66.8 1.9 %collective-permute-start.7 = (f32[2,8,32,128]{3,2,1,0:T(8,128)}, f32[2,8,32,128]{3,2,1,0:T(8,128)S(1)}, u32[]{:S(2)}, u32[]{:S(2)}) collective-permute-start(f32[2,8,32,128]{3,2,1,0:T(8,128)} %get-tuple-element.53), channel_id=1, source_target_pairs={{0,8},{1,9},{2,10},{3,11},{4,12},{5,13},{6,14},{7,15},{8,16},{9,17... | collective-permute-start | bytes 786440 | tf_op jit(solution)/shard_map/ppermute | solution.py:110
  68.7 1.9 %collective-permute-start.8 = (f32[2,5,32,128]{3,2,1,0:T(8,128)}, f32[2,5,32,128]{3,2,1,0:T(8,128)S(1)}, u32[]{:S(2)}, u32[]{:S(2)}) collective-permute-start(f32[2,5,32,128]{3,2,1,0:T(8,128)} %get-tuple-element.54), channel_id=1, source_target_pairs={{0,9},{1,10},{2,11},{3,12},{4,13},{5,14},{6,15},{7,8},{8,17},{9,18... | collective-permute-start | bytes 491528 | tf_op jit(solution)/shard_map/ppermute | solution.py:110
  70.6 1.9 %collective-permute-start.9 = (f32[2,5,32,128]{3,2,1,0:T(8,128)}, f32[2,5,32,128]{3,2,1,0:T(8,128)S(1)}, u32[]{:S(2)}, u32[]{:S(2)}) collective-permute-start(f32[2,5,32,128]{3,2,1,0:T(8,128)} %get-tuple-element.55), channel_id=1, source_target_pairs={{0,15},{1,8},{2,9},{3,10},{4,11},{5,12},{6,13},{7,14},{8,23},{9,16... | collective-permute-start | bytes 491528 | tf_op jit(solution)/shard_map/ppermute | solution.py:110
  72.6 10.3 %collective-permute-done.8.bbefore_ref = f32[2,5,32,128]{3,2,1,0:T(8,128)S(1)} collective-permute-done((f32[2,5,32,128]{3,2,1,0:T(8,128)}, f32[2,5,32,128]{3,2,1,0:T(8,128)S(1)}, u32[]{:S(2)}, u32[]{:S(2)}) %collective-permute-start.8) | collective-permute-done | bytes 163872 | tf_op jit(solution)/shard_map/ppermute | solution.py:110
  82.9 2.2 %collective-permute-done.11.after_ref = f32[2,10,32,128]{3,2,1,0:T(8,128)S(1)} collective-permute-done((f32[2,10,32,128]{3,2,1,0:T(8,128)}, f32[2,10,32,128]{3,2,1,0:T(8,128)S(1)}, u32[]{:S(2)}, u32[]{:S(2)}) %collective-permute-start.11) | collective-permute-done | bytes 327712 | tf_op jit(solution)/shard_map/ppermute | solution.py:543
  85.1 0.7 copy-done.6
  85.9 4.9 %shard_map.48 = (f32[2,10,32,128]{3,2,1,0:T(8,128)}, f32[2,10,32,128]{3,2,1,0:T(8,128)}, f32[2,10,32,128]{3,2,1,0:T(8,128)}, f32[2,10,32,128]{3,2,1,0:T(8,128)},...) custom-call(f32[2]{0:T(128)} %diff_ref.11, ...), custom_call_target="tpu_custom_call" | custom-call | tf_op jit(solution)/shard_map/pallas_call | solution.py:284
  90.7 1.7 %collective-permute-start.12 = (f32[2,6,16,128]{3,2,1,0:T(8,128)}, f32[2,6,16,128]{3,2,1,0:T(8,128)S(1)}, u32[]{:S(2)}, u32[]{:S(2)}) collective-permute-start(f32[2,6,16,128]{3,2,1,0:T(8,128)} %get-tuple-element.60), channel_id=1, source_target_pairs={{0,1},{1,2},{2,3},{3,4},{4,5},{5,6},{6,7},{7,0},{8,9},{9,10},{10,1... | collective-permute-start | bytes 294920 | tf_op jit(solution)/shard_map/ppermute | solution.py:504
  92.4 3.1 %collective-permute-start.13 = (f32[2,6,16,128]{3,2,1,0:T(8,128)}, f32[2,6,16,128]{3,2,1,0:T(8,128)S(1)}, u32[]{:S(2)}, u32[]{:S(2)}) collective-permute-start(f32[2,6,16,128]{3,2,1,0:T(8,128)} %get-tuple-element.61), channel_id=1, source_target_pairs={{1,0},{2,1},{3,2},{4,3},{5,4},{6,5},{7,6},{0,7},{9,8},{10,9},{11,1... | collective-permute-start | bytes 294920 | tf_op jit(solution)/shard_map/ppermute | solution.py:505
  95.5 3.1 %collective-permute-done.12.cbefore_ref = f32[2,6,16,128]{3,2,1,0:T(8,128)S(1)} collective-permute-done((f32[2,6,16,128]{3,2,1,0:T(8,128)}, f32[2,6,16,128]{3,2,1,0:T(8,128)S(1)}, u32[]{:S(2)}, u32[]{:S(2)}) %collective-permute-start.12) | collective-permute-done | bytes 98336 | tf_op jit(solution)/shard_map/ppermute | solution.py:504
  98.6 1.7 %collective-permute-done.13.cafter_ref = f32[2,6,16,128]{3,2,1,0:T(8,128)S(1)} collective-permute-done((f32[2,6,16,128]{3,2,1,0:T(8,128)}, f32[2,6,16,128]{3,2,1,0:T(8,128)S(1)}, u32[]{:S(2)}, u32[]{:S(2)}) %collective-permute-start.13) | collective-permute-done | bytes 98336 | tf_op jit(solution)/shard_map/ppermute | solution.py:505
  100.9 4.6 %shard_map.49 = (f32[4,2,8,32,128]{4,3,2,1,0:T(8,128)}, f32[2,10,32,128]{3,2,1,0:T(8,128)}, f32[2,10,32,128]{3,2,1,0:T(8,128)}, f32[2,8,32,128]{3,2,1,0:T(8,128)...) custom-call(f32[2]{0:T(128)} %diff_ref.11, f32[4,2,4,16,128]{4,3,2,1,0:T(8,128)} %get-tuple-element.59.cown_ref, ...), custom_call_target="tpu_custom_call" | custom-call | tf_op jit(solution)/shard_map/pallas_call | solution.py:411
  105.6 4.7 %collective-permute-start.18 = (f32[2,10,32,128]{3,2,1,0:T(8,128)}, f32[2,10,32,128]{3,2,1,0:T(8,128)S(1)}, u32[]{:S(2)}, u32[]{:S(2)}) collective-permute-start(f32[2,10,32,128]{3,2,1,0:T(8,128)} %get-tuple-element.73), channel_id=1, source_target_pairs={{1,0},{2,1},{3,2},{4,3},{5,4},{6,5},{7,6},{0,7},{9,8},{10,9},{11,1... | collective-permute-start | bytes 983048 | tf_op jit(solution)/shard_map/ppermute | solution.py:543
  110.3 1.9 %collective-permute-start.14 = (f32[2,8,32,128]{3,2,1,0:T(8,128)}, f32[2,8,32,128]{3,2,1,0:T(8,128)S(1)}, u32[]{:S(2)}, u32[]{:S(2)}) collective-permute-start(f32[2,8,32,128]{3,2,1,0:T(8,128)} %get-tuple-element.68), channel_id=1, source_target_pairs={{0,8},{1,9},{2,10},{3,11},{4,12},{5,13},{6,14},{7,15},{8,16},{9,17... | collective-permute-start | bytes 786440 | tf_op jit(solution)/shard_map/ppermute | solution.py:110
  112.2 1.9 %collective-permute-start.15 = (f32[2,5,32,128]{3,2,1,0:T(8,128)}, f32[2,5,32,128]{3,2,1,0:T(8,128)S(1)}, u32[]{:S(2)}, u32[]{:S(2)}) collective-permute-start(f32[2,5,32,128]{3,2,1,0:T(8,128)} %get-tuple-element.69), channel_id=1, source_target_pairs={{0,9},{1,10},{2,11},{3,12},{4,13},{5,14},{6,15},{7,8},{8,17},{9,18... | collective-permute-start | bytes 491528 | tf_op jit(solution)/shard_map/ppermute | solution.py:110
  114.1 2.1 %collective-permute-start.16 = (f32[2,5,32,128]{3,2,1,0:T(8,128)}, f32[2,5,32,128]{3,2,1,0:T(8,128)S(1)}, u32[]{:S(2)}, u32[]{:S(2)}) collective-permute-start(f32[2,5,32,128]{3,2,1,0:T(8,128)} %get-tuple-element.70), channel_id=1, source_target_pairs={{0,15},{1,8},{2,9},{3,10},{4,11},{5,12},{6,13},{7,14},{8,23},{9,16... | collective-permute-start | bytes 491528 | tf_op jit(solution)/shard_map/ppermute | solution.py:110
  116.2 11.2 %collective-permute-done.15.bbefore_ref = f32[2,5,32,128]{3,2,1,0:T(8,128)S(1)} collective-permute-done((f32[2,5,32,128]{3,2,1,0:T(8,128)}, f32[2,5,32,128]{3,2,1,0:T(8,128)S(1)}, u32[]{:S(2)}, u32[]{:S(2)}) %collective-permute-start.15) | collective-permute-done | bytes 163872 | tf_op jit(solution)/shard_map/ppermute | solution.py:110
  128.7 5.0 %shard_map.50 = (f32[2,10,32,128]{3,2,1,0:T(8,128)}, f32[2,10,32,128]{3,2,1,0:T(8,128)}, f32[2,10,32,128]{3,2,1,0:T(8,128)}, f32[2,10,32,128]{3,2,1,0:T(8,128)},...) custom-call(f32[2]{0:T(128)} %diff_ref.11, ...), custom_call_target="tpu_custom_call" | custom-call | tf_op jit(solution)/shard_map/pallas_call | solution.py:284
  133.7 1.7 %collective-permute-start.19 = (f32[2,2,16,128]{3,2,1,0:T(8,128)}, f32[2,2,16,128]{3,2,1,0:T(8,128)S(1)}, u32[]{:S(2)}, u32[]{:S(2)}) collective-permute-start(f32[2,2,16,128]{3,2,1,0:T(8,128)} %get-tuple-element.75), channel_id=1, source_target_pairs={{0,1},{1,2},{2,3},{3,4},{4,5},{5,6},{6,7},{7,0},{8,9},{9,10},{10,1... | collective-permute-start | bytes 98312 | tf_op jit(solution)/shard_map/ppermute | solution.py:504
  135.3 3.1 %collective-permute-start.20 = (f32[2,2,16,128]{3,2,1,0:T(8,128)}, f32[2,2,16,128]{3,2,1,0:T(8,128)S(1)}, u32[]{:S(2)}, u32[]{:S(2)}) collective-permute-start(f32[2,2,16,128]{3,2,1,0:T(8,128)} %get-tuple-element.76), channel_id=1, source_target_pairs={{1,0},{2,1},{3,2},{4,3},{5,4},{6,5},{7,6},{0,7},{9,8},{10,9},{11,1... | collective-permute-start | bytes 98312 | tf_op jit(solution)/shard_map/ppermute | solution.py:505
  138.4 2.1 %collective-permute-done.19.cbefore_ref = f32[2,2,16,128]{3,2,1,0:T(8,128)S(1)} collective-permute-done((f32[2,2,16,128]{3,2,1,0:T(8,128)}, f32[2,2,16,128]{3,2,1,0:T(8,128)S(1)}, u32[]{:S(2)}, u32[]{:S(2)}) %collective-permute-start.19) | collective-permute-done | bytes 32800 | tf_op jit(solution)/shard_map/ppermute | solution.py:504
  141.1 2.9 %shard_map.51 = f32[2,8,32,128]{3,2,1,0:T(8,128)} custom-call(f32[2]{0:T(128)} %diff_ref.11, f32[4,2,4,16,128]{4,3,2,1,0:T(8,128)} %get-tuple-element.74.cown_ref, f32[2,2,16,128]{3,2,1,0:T(8,128)} %copy-done.19, f32[2,2,16,128]{3,2,1,0:T(8,128)} %copy-done.20, f32[2,8,16,128]{3,2,1,0:T(8,128)} %fusion.15.rate_ref, f32[2,8,16,128]{3,2,1,0:T(8,128)} %fusion.10.csrc_ref, ...), custom_call_target="tpu_custom_call" | custom-call | tf_op jit(solution)/shard_map/pallas_call | solution.py:411
  144.0 1.0 slice_bitcast_fusion.8
  145.1 0.8 copy.22
  (85 shorter events, 9.0 us)
Async XLA Ops:
  6.0 12.2 %copy-start.21 = (f32[2]{0:T(128)S(1)}, f32[2]{0:T(128)}, u32[]{:S(2)}) copy-start(f32[2]{0:T(128)} %diff_ref.11) | copy-start | bytes 28
  6.1 27.9 %collective-permute-start = (f32[3,2,5,32,128]{4,3,2,1,0:T(8,128)S(1)}, f32[3,2,5,32,128]{4,3,2,1,0:T(8,128)S(1)}, u32[]{:S(2)}, u32[]{:S(2)}) collective-permute-start(f32[3,2,5,32,128]{4,3,2,1,0:T(8,128)S(1)} %get-tuple-element.93), channel_id=1, source_target_pairs={{0,1},{1,2},{2,3},{3,4},{4,5},{5,6},{6,7},{7,0},{8,9},{9,10},{10,1... | collective-permute-start | bytes 1474568 | tf_op jit(solution)/shard_map/ppermute | solution.py:94
  7.7 28.5 %collective-permute-start.1 = (f32[3,2,5,32,128]{4,3,2,1,0:T(8,128)S(1)}, f32[3,2,5,32,128]{4,3,2,1,0:T(8,128)S(1)}, u32[]{:S(2)}, u32[]{:S(2)}) collective-permute-start(f32[3,2,5,32,128]{4,3,2,1,0:T(8,128)S(1)} %get-tuple-element.94), channel_id=1, source_target_pairs={{1,0},{2,1},{3,2},{4,3},{5,4},{6,5},{7,6},{0,7},{9,8},{10,9},{11,1... | collective-permute-start | bytes 1474568 | tf_op jit(solution)/shard_map/ppermute | solution.py:95
  11.7 31.7 %collective-permute-start.4 = (f32[2,5,32,128]{3,2,1,0:T(8,128)}, f32[2,5,32,128]{3,2,1,0:T(8,128)S(1)}, u32[]{:S(2)}, u32[]{:S(2)}) collective-permute-start(f32[2,5,32,128]{3,2,1,0:T(8,128)} %get-tuple-element.116), channel_id=1, source_target_pairs={{0,15},{1,8},{2,9},{3,10},{4,11},{5,12},{6,13},{7,14},{8,23},{9,16... | collective-permute-start | bytes 491528 | tf_op jit(solution)/shard_map/ppermute | solution.py:110
  14.3 29.1 %collective-permute-start.3 = (f32[2,5,32,128]{3,2,1,0:T(8,128)}, f32[2,5,32,128]{3,2,1,0:T(8,128)}, u32[]{:S(2)}, u32[]{:S(2)}) collective-permute-start(f32[2,5,32,128]{3,2,1,0:T(8,128)} %get-tuple-element.117), channel_id=1, source_target_pairs={{0,9},{1,10},{2,11},{3,12},{4,13},{5,14},{6,15},{7,8},{8,17},{9,18... | collective-permute-start | bytes 491528 | tf_op jit(solution)/shard_map/ppermute | solution.py:110
  16.3 27.2 %collective-permute-start.2 = (f32[2,8,32,128]{3,2,1,0:T(8,128)S(1)}, f32[2,8,32,128]{3,2,1,0:T(8,128)S(1)}, u32[]{:S(2)}, u32[]{:S(2)}) collective-permute-start(f32[2,8,32,128]{3,2,1,0:T(8,128)S(1)} %get-tuple-element.118), channel_id=1, source_target_pairs={{0,8},{1,9},{2,10},{3,11},{4,12},{5,13},{6,14},{7,15},{8,16},{9,17... | collective-permute-start | bytes 786440 | tf_op jit(solution)/shard_map/ppermute | solution.py:110
  36.6 2.8 %copy-start = (f32[2,18,32,128]{3,2,1,0:T(8,128)}, f32[2,18,32,128]{3,2,1,0:T(8,128)S(1)}, u32[]{:S(2)}) copy-start(f32[2,18,32,128]{3,2,1,0:T(8,128)S(1)} %get-tuple-element.90.start_ref) | copy-start | bytes 1769476
  36.6 2.8 %copy-start.1 = (f32[2,18,32,128]{3,2,1,0:T(8,128)}, f32[2,18,32,128]{3,2,1,0:T(8,128)S(1)}, u32[]{:S(2)}) copy-start(f32[2,18,32,128]{3,2,1,0:T(8,128)S(1)} %get-tuple-element.88.dec_ref) | copy-start | bytes 1769476
  36.6 5.7 %copy-start.2 = (f32[2,18,32,128]{3,2,1,0:T(8,128)}, f32[2,18,32,128]{3,2,1,0:T(8,128)S(1)}, u32[]{:S(2)}) copy-start(f32[2,18,32,128]{3,2,1,0:T(8,128)S(1)} %get-tuple-element.89.src_ref) | copy-start | bytes 1769476
  43.4 0.7 copy-start.10
  43.5 0.7 copy-start.7
  49.1 7.6 %collective-permute-start.5 = (f32[2,6,16,128]{3,2,1,0:T(8,128)}, f32[2,6,16,128]{3,2,1,0:T(8,128)S(1)}, u32[]{:S(2)}, u32[]{:S(2)}) collective-permute-start(f32[2,6,16,128]{3,2,1,0:T(8,128)} %get-tuple-element.45), channel_id=1, source_target_pairs={{0,1},{1,2},{2,3},{3,4},{4,5},{5,6},{6,7},{7,0},{8,9},{9,10},{10,1... | collective-permute-start | bytes 294920 | tf_op jit(solution)/shard_map/ppermute | solution.py:504
  49.4 7.4 %collective-permute-start.6 = (f32[2,6,16,128]{3,2,1,0:T(8,128)}, f32[2,6,16,128]{3,2,1,0:T(8,128)S(1)}, u32[]{:S(2)}, u32[]{:S(2)}) collective-permute-start(f32[2,6,16,128]{3,2,1,0:T(8,128)} %get-tuple-element.46), channel_id=1, source_target_pairs={{1,0},{2,1},{3,2},{4,3},{5,4},{6,5},{7,6},{0,7},{9,8},{10,9},{11,1... | collective-permute-start | bytes 294920 | tf_op jit(solution)/shard_map/ppermute | solution.py:505
  56.7 0.6 copy-start.15
  56.8 0.6 copy-start.17
  62.0 20.9 %collective-permute-start.10 = (f32[2,10,32,128]{3,2,1,0:T(8,128)}, f32[2,10,32,128]{3,2,1,0:T(8,128)S(1)}, u32[]{:S(2)}, u32[]{:S(2)}) collective-permute-start(f32[2,10,32,128]{3,2,1,0:T(8,128)} %get-tuple-element.57), channel_id=1, source_target_pairs={{0,1},{1,2},{2,3},{3,4},{4,5},{5,6},{6,7},{7,0},{8,9},{9,10},{10,1... | collective-permute-start | bytes 983048 | tf_op jit(solution)/shard_map/ppermute | solution.py:542
  62.8 22.3 %collective-permute-start.11 = (f32[2,10,32,128]{3,2,1,0:T(8,128)}, f32[2,10,32,128]{3,2,1,0:T(8,128)S(1)}, u32[]{:S(2)}, u32[]{:S(2)}) collective-permute-start(f32[2,10,32,128]{3,2,1,0:T(8,128)} %get-tuple-element.58), channel_id=1, source_target_pairs={{1,0},{2,1},{3,2},{4,3},{5,4},{6,5},{7,6},{0,7},{9,8},{10,9},{11,1... | collective-permute-start | bytes 983048 | tf_op jit(solution)/shard_map/ppermute | solution.py:543
  66.8 16.1 %collective-permute-start.7 = (f32[2,8,32,128]{3,2,1,0:T(8,128)}, f32[2,8,32,128]{3,2,1,0:T(8,128)S(1)}, u32[]{:S(2)}, u32[]{:S(2)}) collective-permute-start(f32[2,8,32,128]{3,2,1,0:T(8,128)} %get-tuple-element.53), channel_id=1, source_target_pairs={{0,8},{1,9},{2,10},{3,11},{4,12},{5,13},{6,14},{7,15},{8,16},{9,17... | collective-permute-start | bytes 786440 | tf_op jit(solution)/shard_map/ppermute | solution.py:110
  68.7 14.2 %collective-permute-start.8 = (f32[2,5,32,128]{3,2,1,0:T(8,128)}, f32[2,5,32,128]{3,2,1,0:T(8,128)S(1)}, u32[]{:S(2)}, u32[]{:S(2)}) collective-permute-start(f32[2,5,32,128]{3,2,1,0:T(8,128)} %get-tuple-element.54), channel_id=1, source_target_pairs={{0,9},{1,10},{2,11},{3,12},{4,13},{5,14},{6,15},{7,8},{8,17},{9,18... | collective-permute-start | bytes 491528 | tf_op jit(solution)/shard_map/ppermute | solution.py:110
  70.6 12.2 %collective-permute-start.9 = (f32[2,5,32,128]{3,2,1,0:T(8,128)}, f32[2,5,32,128]{3,2,1,0:T(8,128)S(1)}, u32[]{:S(2)}, u32[]{:S(2)}) collective-permute-start(f32[2,5,32,128]{3,2,1,0:T(8,128)} %get-tuple-element.55), channel_id=1, source_target_pairs={{0,15},{1,8},{2,9},{3,10},{4,11},{5,12},{6,13},{7,14},{8,23},{9,16... | collective-permute-start | bytes 491528 | tf_op jit(solution)/shard_map/ppermute | solution.py:110
  82.9 2.2 %copy-start.12 = (f32[2,5,32,128]{3,2,1,0:T(8,128)}, f32[2,5,32,128]{3,2,1,0:T(8,128)S(1)}, u32[]{:S(2)}) copy-start(f32[2,5,32,128]{3,2,1,0:T(8,128)S(1)} %collective-permute-done.8.bbefore_ref) | copy-start | bytes 491524
  82.9 2.2 %copy-start.14 = (f32[2,5,32,128]{3,2,1,0:T(8,128)}, f32[2,5,32,128]{3,2,1,0:T(8,128)S(1)}, u32[]{:S(2)}) copy-start(f32[2,5,32,128]{3,2,1,0:T(8,128)S(1)} %collective-permute-done.9.bafter_ref) | copy-start | bytes 491524
  82.9 2.2 %copy-start.9 = (f32[2,8,32,128]{3,2,1,0:T(8,128)}, f32[2,8,32,128]{3,2,1,0:T(8,128)S(1)}, u32[]{:S(2)}) copy-start(f32[2,8,32,128]{3,2,1,0:T(8,128)S(1)} %collective-permute-done.7.centre_ref) | copy-start | bytes 786436
  82.9 2.2 %copy-start.4 = (f32[2,10,32,128]{3,2,1,0:T(8,128)}, f32[2,10,32,128]{3,2,1,0:T(8,128)S(1)}, u32[]{:S(2)}) copy-start(f32[2,10,32,128]{3,2,1,0:T(8,128)S(1)} %collective-permute-done.10.before_ref) | copy-start | bytes 983044
  85.1 0.7 copy-start.6
  90.7 7.8 %collective-permute-start.12 = (f32[2,6,16,128]{3,2,1,0:T(8,128)}, f32[2,6,16,128]{3,2,1,0:T(8,128)S(1)}, u32[]{:S(2)}, u32[]{:S(2)}) collective-permute-start(f32[2,6,16,128]{3,2,1,0:T(8,128)} %get-tuple-element.60), channel_id=1, source_target_pairs={{0,1},{1,2},{2,3},{3,4},{4,5},{5,6},{6,7},{7,0},{8,9},{9,10},{10,1... | collective-permute-start | bytes 294920 | tf_op jit(solution)/shard_map/ppermute | solution.py:504
  92.4 7.9 %collective-permute-start.13 = (f32[2,6,16,128]{3,2,1,0:T(8,128)}, f32[2,6,16,128]{3,2,1,0:T(8,128)S(1)}, u32[]{:S(2)}, u32[]{:S(2)}) collective-permute-start(f32[2,6,16,128]{3,2,1,0:T(8,128)} %get-tuple-element.61), channel_id=1, source_target_pairs={{1,0},{2,1},{3,2},{4,3},{5,4},{6,5},{7,6},{0,7},{9,8},{10,9},{11,1... | collective-permute-start | bytes 294920 | tf_op jit(solution)/shard_map/ppermute | solution.py:505
  98.6 1.7 %copy-start.16 = (f32[2,6,16,128]{3,2,1,0:T(8,128)}, f32[2,6,16,128]{3,2,1,0:T(8,128)S(1)}, u32[]{:S(2)}) copy-start(f32[2,6,16,128]{3,2,1,0:T(8,128)S(1)} %collective-permute-done.12.cbefore_ref) | copy-start | bytes 294916
  100.3 0.6 copy-start.18
  105.5 22.0 %collective-permute-start.17 = (f32[2,10,32,128]{3,2,1,0:T(8,128)}, f32[2,10,32,128]{3,2,1,0:T(8,128)S(1)}, u32[]{:S(2)}, u32[]{:S(2)}) collective-permute-start(f32[2,10,32,128]{3,2,1,0:T(8,128)} %get-tuple-element.72), channel_id=1, source_target_pairs={{0,1},{1,2},{2,3},{3,4},{4,5},{5,6},{6,7},{7,0},{8,9},{9,10},{10,1... | collective-permute-start | bytes 983048 | tf_op jit(solution)/shard_map/ppermute | solution.py:542
  105.6 22.4 %collective-permute-start.18 = (f32[2,10,32,128]{3,2,1,0:T(8,128)}, f32[2,10,32,128]{3,2,1,0:T(8,128)S(1)}, u32[]{:S(2)}, u32[]{:S(2)}) collective-permute-start(f32[2,10,32,128]{3,2,1,0:T(8,128)} %get-tuple-element.73), channel_id=1, source_target_pairs={{1,0},{2,1},{3,2},{4,3},{5,4},{6,5},{7,6},{0,7},{9,8},{10,9},{11,1... | collective-permute-start | bytes 983048 | tf_op jit(solution)/shard_map/ppermute | solution.py:543
  110.3 17.2 %collective-permute-start.14 = (f32[2,8,32,128]{3,2,1,0:T(8,128)}, f32[2,8,32,128]{3,2,1,0:T(8,128)S(1)}, u32[]{:S(2)}, u32[]{:S(2)}) collective-permute-start(f32[2,8,32,128]{3,2,1,0:T(8,128)} %get-tuple-element.68), channel_id=1, source_target_pairs={{0,8},{1,9},{2,10},{3,11},{4,12},{5,13},{6,14},{7,15},{8,16},{9,17... | collective-permute-start | bytes 786440 | tf_op jit(solution)/shard_map/ppermute | solution.py:110
  112.2 15.3 %collective-permute-start.15 = (f32[2,5,32,128]{3,2,1,0:T(8,128)}, f32[2,5,32,128]{3,2,1,0:T(8,128)S(1)}, u32[]{:S(2)}, u32[]{:S(2)}) collective-permute-start(f32[2,5,32,128]{3,2,1,0:T(8,128)} %get-tuple-element.69), channel_id=1, source_target_pairs={{0,9},{1,10},{2,11},{3,12},{4,13},{5,14},{6,15},{7,8},{8,17},{9,18... | collective-permute-start | bytes 491528 | tf_op jit(solution)/shard_map/ppermute | solution.py:110
  114.1 13.3 %collective-permute-start.16 = (f32[2,5,32,128]{3,2,1,0:T(8,128)}, f32[2,5,32,128]{3,2,1,0:T(8,128)S(1)}, u32[]{:S(2)}, u32[]{:S(2)}) collective-permute-start(f32[2,5,32,128]{3,2,1,0:T(8,128)} %get-tuple-element.70), channel_id=1, source_target_pairs={{0,15},{1,8},{2,9},{3,10},{4,11},{5,12},{6,13},{7,14},{8,23},{9,16... | collective-permute-start | bytes 491528 | tf_op jit(solution)/shard_map/ppermute | solution.py:110
  127.5 0.7 copy-start.11
  127.5 0.7 copy-start.13
  127.5 0.8 copy-start.8
  127.5 0.9 copy-start.3
  128.0 0.7 copy-start.5
  133.7 6.8 %collective-permute-start.19 = (f32[2,2,16,128]{3,2,1,0:T(8,128)}, f32[2,2,16,128]{3,2,1,0:T(8,128)S(1)}, u32[]{:S(2)}, u32[]{:S(2)}) collective-permute-start(f32[2,2,16,128]{3,2,1,0:T(8,128)} %get-tuple-element.75), channel_id=1, source_target_pairs={{0,1},{1,2},{2,3},{3,4},{4,5},{5,6},{6,7},{7,0},{8,9},{9,10},{10,1... | collective-permute-start | bytes 98312 | tf_op jit(solution)/shard_map/ppermute | solution.py:504
  135.3 5.2 %collective-permute-start.20 = (f32[2,2,16,128]{3,2,1,0:T(8,128)}, f32[2,2,16,128]{3,2,1,0:T(8,128)S(1)}, u32[]{:S(2)}, u32[]{:S(2)}) collective-permute-start(f32[2,2,16,128]{3,2,1,0:T(8,128)} %get-tuple-element.76), channel_id=1, source_target_pairs={{1,0},{2,1},{3,2},{4,3},{5,4},{6,5},{7,6},{0,7},{9,8},{10,9},{11,1... | collective-permute-start | bytes 98312 | tf_op jit(solution)/shard_map/ppermute | solution.py:505
  140.5 0.6 copy-start.19
  140.5 0.6 copy-start.20

commit v5 on v4

--- a/solution.py
+++ b/solution.py
@@ -416,6 +416,56 @@
     )(*args)
 
 
+def start_kernel(diff_ref, init_ref, dec_ref, src_ref, own_ref, before_ref, after_ref,
+                 rate_ref, csrc_ref):
+    spread_table, grouped_table, interp_table, widths = node_tables()
+    rows = own_ref.shape[2]
+    hs = (init_ref.shape[1] - rows) // 2
+    d0 = diff_ref[0]
+    d1 = diff_ref[1]
+    state = init_ref[...]
+    inner = state[:, 1:-1]
+    dec = dec_ref[:, 1:-1]
+    s = src_ref[:, 1:-1]
+    laplace = kernel_laplace(state)
+    product = inner[0] * inner[1] * inner[1]
+    terms = jnp.stack([d0 * laplace[0] - product + s[0], d1 * laplace[1] + product + s[1]])
+    full = terms - dec * inner
+    edge = hs - 1
+    offset = 0
+    for m in range(4):
+        summed = spread_table[m][0] * full
+        for j in range(1, 5):
+            summed = summed + spread_table[m][j] * full
+        part = (widths[m] * dec * inner - widths[m] * terms) + summed
+        own_ref[m] = part[:, edge:edge + rows]
+        w = edge - m
+        before_ref[:, offset:offset + w] = part[:, m:edge]
+        after_ref[:, offset:offset + w] = part[:, edge + rows:edge + rows + w]
+        offset += w
+    rate_ref[...] = kernel_restrict(dec)
+    csrc_ref[...] = kernel_restrict(s)
+
+
+def start_terms(diffusivity, own_ext, decay, src):
+    shape = own_ext.shape
+    rows = shape[1] - 2 * START_HALO
+    sent = sum(START_HALO - 1 - m for m in range(4))
+    edge = jax.ShapeDtypeStruct((shape[0], sent) + shape[2:], jnp.float32)
+    cshape = (shape[0], (rows + 2 * (START_HALO - 1)) // 2, shape[2] // 2, shape[3])
+    coarse = jax.ShapeDtypeStruct(cshape, jnp.float32)
+    vmem = pl.BlockSpec(memory_space=pltpu.VMEM)
+    return pl.pallas_call(
+        start_kernel,
+        out_shape=(
+            jax.ShapeDtypeStruct((4, shape[0], rows) + shape[2:], jnp.float32),
+            edge, edge, coarse, coarse,
+        ),
+        in_specs=[pl.BlockSpec(memory_space=pltpu.SMEM)] + [vmem] * 3,
+        out_specs=(vmem,) * 5,
+    )(diffusivity, own_ext, decay, src)
+
+
 def packed_halo(fields):
     size = lax.axis_size("space")
     rows = fields[0][0].shape[-3]
@@ -455,14 +505,13 @@
     assert hs == 5 and initial.shape[-3] >= hs
 
     own_start = to_even_odd(initial[0])
-    fixed = space_halo(
-        jnp.stack([own_start, to_even_odd(decay_rate), to_even_odd(source)]), hs
-    )
-    own_ext = fixed[0]
-    decay = (fixed[1], hs)
-    src = (fixed[2], hs)
-    rate_c = restrict(decay)
-    source_c = restrict(src)
+    own_ext = space_halo(own_start, hs)
+    fixed = space_halo(jnp.stack([to_even_odd(decay_rate), to_even_odd(source)]), hs)
+    decay = (fixed[0], hs)
+    src = (fixed[1], hs)
+    own4, before4, after4, rate_own, csrc_own = start_terms(diffusivity, own_ext, decay[0], src[0])
+    rate_c = (rate_own, (hs - 1) // 2)
+    source_c = (csrc_own, (hs - 1) // 2)
 
     def fine_E(field):
         a, h = field
@@ -514,21 +563,7 @@
     down = [((i + 1) % size, i) for i in range(size)]
     rows = own_start.shape[-3]
     flag = jnp.where(first_slice, 1, 0).astype(jnp.int32).reshape(1)
-    state = (own_ext, hs)
-    state_terms = fine_E(state)
-    parts = step_terms([state] * 5, [state_terms] * 5)
-    wide = [crop(parts[m], hs - 1) for m in range(4)]
-    edge = hs - 1
-    pieces = (
-        jnp.stack([lax.slice_in_dim(p, edge, edge + rows, axis=1) for p in wide]),
-        jnp.concatenate(
-            [lax.slice_in_dim(p, m, edge, axis=1) for m, p in enumerate(wide)], axis=1
-        ),
-        jnp.concatenate(
-            [lax.slice_in_dim(p, edge + rows, edge + rows + edge - m, axis=1)
-             for m, p in enumerate(wide)], axis=1
-        ),
-    )
+    pieces = (own4, before4, after4)
     prior = from_previous_slice(
         (own_start, own_start[:, rows - hs:], own_start[:, :hs])
     )

time: 147 us -> 143 us (0.973)
  starting transfers between devices: 46.6 us -> 54.8 us
  waiting for transfers between devices: 50.8 us -> 43.6 us
  other arithmetic: 7.81 us -> 2.07 us
  Pallas kernels: 26.8 us -> 30.2 us
  local copies, waits for them, and re-layouts: 13.4 us -> 11.2 us
    ppermute x1 -> x2, starting transfers between devices: 3.2 us -> 7.91 us  [space_halo(): lax.ppermute(lax.slice_in_dim(a, 0, h, axis=a.ndim - 3), 'space', down)]
    pallas_call x0 -> x1, Pallas kernels: none -> 3.56 us  [start_terms(): pl.pallas_call(start_kernel, out_shape=(jax.ShapeDtypeStruct((4, shape[0]...]
    ppermute x9, starting transfers between devices: 18.2 us -> 21.5 us  [moved(): return lax.ppermute(piece, axes, pairs)]
    ppermute x1 -> x2, waiting for transfers between devices: 15.2 us -> 12.6 us  [space_halo(): lax.ppermute(lax.slice_in_dim(a, rows - h, rows, axis=a.ndim - 3), 'space...]
    add x4 -> x0, other arithmetic: 2.37 us -> none  [the longest x1 1.36 us: react_terms(): diffusivity[0] * laplace[0] - product + source[0]]
    ppermute x9, waiting for transfers between devices: 21.5 us -> 19.3 us  [moved(): return lax.ppermute(piece, axes, pairs)]
    ppermute x1 -> x2, waiting for transfers between devices: 2.2 us -> 0.01 us  [space_halo(): lax.ppermute(lax.slice_in_dim(a, 0, h, axis=a.ndim - 3), 'space', down)]
    slice x6, local copies, waits for them, and re-layouts: 5.84 us -> 4.06 us  [to_even_odd(): return jnp.concatenate([a[..., 0::2, :], a[..., 1::2, :]], axis=-2)]
  transfers between devices with their start and end apart: 21 -> 23, of which waited for: 11 -> 9; matrix products, arithmetic and copies ran while one was open for 6% -> 2% of each run, Pallas kernels for 0% -> 3%
where the time goes in v5:
time: 143 us; the launch traced here: 142 us
  starting transfers between devices  54.8 us (38%)
  waiting for transfers between devices  43.6 us (30%)
  Pallas kernels  30.2 us (21%)
  local copies, waits for them, and re-layouts  11.2 us (8%)
  other arithmetic  2.07 us (1%)
    ppermute x9, starting transfers between devices, moved(): return lax.ppermute(piece, axes, pairs)  21.5 us
    ppermute x9, waiting for transfers between devices, moved(): return lax.ppermute(piece, axes, pairs)  19.3 us
    pallas_call x3, Pallas kernels, fine_sweep(): pl.pallas_call(functools.partial(sweep_kernel, widths_sent), out_shape=(w...  14.6 us
    ppermute x2, waiting for transfers between devices, space_halo(): lax.ppermute(lax.slice_in_dim(a, rows - h, rows, axis=a.ndim - 3), 'space...  12.6 us
    pallas_call x3, Pallas kernels, finish_round(): pl.pallas_call(functools.partial(finish_kernel, widths_sent), out_shape=o...  12 us
    ppermute x3, starting transfers between devices, advance(): lax.ppermute(cfirsts, 'space', down)  10.9 us
    ppermute x2, starting transfers between devices, per_device(): lax.ppermute(firsts, 'space', down)  9.44 us
    ppermute x3, waiting for transfers between devices, advance(): lax.ppermute(clasts, 'space', up)  8.02 us
  transfers between devices with their start and end apart: 23, of which 9 were waited for; matrix products, arithmetic and copies ran while one was open for 2% of the time, Pallas kernels for 3%

profile of v5, /device:TPU:2, one launch (start us, length us, event | category | flops | bytes accessed | tf_op | source)
XLA Modules:
  0.0 142.1 jit_solution(18280798239917801809)
XLA Ops:
  0.0 1.0 slice.49
  1.0 1.0 slice.48
  1.9 1.0 slice.51
  2.9 1.0 slice.50
  4.0 1.6 %collective-permute-start.5 = (f32[2,2,5,32,128]{4,3,2,1,0:T(8,128)S(1)}, f32[2,2,5,32,128]{4,3,2,1,0:T(8,128)S(1)}, u32[]{:S(2)}, u32[]{:S(2)}) collective-permute-start(f32[2,2,5,32,128]{4,3,2,1,0:T(8,128)S(1)} %get-tuple-element.95), channel_id=1, source_target_pairs={{0,1},{1,2},{2,3},{3,4},{4,5},{5,6},{6,7},{7,0},{8,9},{9,10},{10,1... | collective-permute-start | bytes 983048 | tf_op jit(solution)/shard_map/ppermute | solution.py:94
  5.6 3.2 %collective-permute-start.6 = (f32[2,2,5,32,128]{4,3,2,1,0:T(8,128)S(1)}, f32[2,2,5,32,128]{4,3,2,1,0:T(8,128)S(1)}, u32[]{:S(2)}, u32[]{:S(2)}) collective-permute-start(f32[2,2,5,32,128]{4,3,2,1,0:T(8,128)S(1)} %get-tuple-element.96), channel_id=1, source_target_pairs={{1,0},{2,1},{3,2},{4,3},{5,4},{6,5},{7,6},{0,7},{9,8},{10,9},{11,1... | collective-permute-start | bytes 983048 | tf_op jit(solution)/shard_map/ppermute | solution.py:95
  9.1 4.7 %collective-permute-start.1 = (f32[2,5,32,128]{3,2,1,0:T(8,128)S(1)}, f32[2,5,32,128]{3,2,1,0:T(8,128)}, u32[]{:S(2)}, u32[]{:S(2)}) collective-permute-start(f32[2,5,32,128]{3,2,1,0:T(8,128)S(1)} %get-tuple-element.100), channel_id=1, source_target_pairs={{1,0},{2,1},{3,2},{4,3},{5,4},{6,5},{7,6},{0,7},{9,8},{10,9},{11,1... | collective-permute-start | bytes 491528 | tf_op jit(solution)/shard_map/ppermute | solution.py:95
  13.8 1.9 %collective-permute-start.3 = (f32[2,5,32,128]{3,2,1,0:T(8,128)S(1)}, f32[2,5,32,128]{3,2,1,0:T(8,128)S(1)}, u32[]{:S(2)}, u32[]{:S(2)}) collective-permute-start(f32[2,5,32,128]{3,2,1,0:T(8,128)S(1)} %get-tuple-element.99), channel_id=1, source_target_pairs={{0,9},{1,10},{2,11},{3,12},{4,13},{5,14},{6,15},{7,8},{8,17},{9,18... | collective-permute-start | bytes 491528 | tf_op jit(solution)/shard_map/ppermute | solution.py:110
  15.8 12.6 %collective-permute-done = f32[2,5,32,128]{3,2,1,0:T(8,128)S(1)} collective-permute-done((f32[2,5,32,128]{3,2,1,0:T(8,128)S(1)}, f32[2,5,32,128]{3,2,1,0:T(8,128)S(1)}, u32[]{:S(2)}, u32[]{:S(2)}) %collective-permute-start) | collective-permute-done | bytes 163872 | tf_op jit(solution)/shard_map/ppermute | solution.py:94
  28.4 6.0 %collective-permute-start.4 = (f32[2,5,32,128]{3,2,1,0:T(8,128)S(1)}, f32[2,5,32,128]{3,2,1,0:T(8,128)S(1)}, u32[]{:S(2)}, u32[]{:S(2)}) collective-permute-start(f32[2,5,32,128]{3,2,1,0:T(8,128)S(1)} %get-tuple-element.100), channel_id=1, source_target_pairs={{0,15},{1,8},{2,9},{3,10},{4,11},{5,12},{6,13},{7,14},{8,23},{9,16... | collective-permute-start | bytes 491528 | tf_op jit(solution)/shard_map/ppermute | solution.py:110
  34.4 1.9 %collective-permute-start.2 = (f32[2,8,32,128]{3,2,1,0:T(8,128)S(1)}, f32[2,8,32,128]{3,2,1,0:T(8,128)S(1)}, u32[]{:S(2)}, u32[]{:S(2)}) collective-permute-start(f32[2,8,32,128]{3,2,1,0:T(8,128)S(1)} %pad_maximum_fusion.2), channel_id=1, source_target_pairs={{0,8},{1,9},{2,10},{3,11},{4,12},{5,13},{6,14},{7,15},{8,16},{9,17... | collective-permute-start | bytes 786440 | tf_op jit(solution)/shard_map/ppermute | solution.py:110
  36.3 1.8 %pad_maximum_fusion.1.init_ref.start_ref = f32[2,18,32,128]{3,2,1,0:T(8,128)} fusion(f32[2,5,32,128]{3,2,1,0:T(8,128)} %collective-permute-done.1, f32[2,8,16,128]{3,2,1,0:T(8,128)S(1)} %slice.45, f32[2,8,16,128]{3,2,1,0:T(8,128)S(1)} %slice.44, f32[2,5,32,128]{3,2,1,0:T(8,128)S(1)} %collective-permute-done), kind=kLoop, calls=%fused_computation.3 | loop fusion | flops 442368 | bytes 1179648 | tf_op jit(solution)/shard_map/concatenate | solution.py:96
  38.2 1.1 slice_bitcast_fusion
  39.3 3.6 %shard_map.46 = (f32[4,2,8,32,128]{4,3,2,1,0:T(8,128)}, f32[2,10,32,128]{3,2,1,0:T(8,128)}, f32[2,10,32,128]{3,2,1,0:T(8,128)}, f32[2,8,16,128]{3,2,1,0:T(8,128)}, f32[2,8,16,128]{3,2,1,0:T(8,128)}) custom-call(f32[2]{0:T(128)} %diff_ref.13, f32[2,18,32,128]{3,2,1,0:T(8,128)} %pad_maximum_fusion.1.init_ref.start_ref, ...), custom_call_target="tpu_custom_call" | custom-call | tf_op jit(solution)/shard_map/pallas_call | solution.py:458
  43.0 0.6 copy-done.8
  43.7 4.8 %shard_map.47 = (f32[2,10,32,128]{3,2,1,0:T(8,128)}, f32[2,10,32,128]{3,2,1,0:T(8,128)}, f32[2,10,32,128]{3,2,1,0:T(8,128)}, f32[2,10,32,128]{3,2,1,0:T(8,128)},...) custom-call(f32[2]{0:T(128)} %diff_ref.13, ...), custom_call_target="tpu_custom_call" | custom-call | tf_op jit(solution)/shard_map/pallas_call | solution.py:284
  48.6 4.7 %collective-permute-start.8 = (f32[2,6,16,128]{3,2,1,0:T(8,128)}, f32[2,6,16,128]{3,2,1,0:T(8,128)S(1)}, u32[]{:S(2)}, u32[]{:S(2)}) collective-permute-start(f32[2,6,16,128]{3,2,1,0:T(8,128)} %get-tuple-element.55), channel_id=1, source_target_pairs={{1,0},{2,1},{3,2},{4,3},{5,4},{6,5},{7,6},{0,7},{9,8},{10,9},{11,1... | collective-permute-start | bytes 294920 | tf_op jit(solution)/shard_map/ppermute | solution.py:554
  53.3 2.8 %collective-permute-done.7.cbefore_ref = f32[2,6,16,128]{3,2,1,0:T(8,128)S(1)} collective-permute-done((f32[2,6,16,128]{3,2,1,0:T(8,128)}, f32[2,6,16,128]{3,2,1,0:T(8,128)S(1)}, u32[]{:S(2)}, u32[]{:S(2)}) %collective-permute-start.7) | collective-permute-done | bytes 98336 | tf_op jit(solution)/shard_map/ppermute | solution.py:553
  56.1 0.6 copy-done.14
  56.8 4.5 %shard_map.48 = (f32[4,2,8,32,128]{4,3,2,1,0:T(8,128)}, f32[2,10,32,128]{3,2,1,0:T(8,128)}, f32[2,10,32,128]{3,2,1,0:T(8,128)}, f32[2,8,32,128]{3,2,1,0:T(8,128)...) custom-call(f32[2]{0:T(128)} %diff_ref.13, f32[4,2,4,16,128]{4,3,2,1,0:T(8,128)} %get-tuple-element.53.cown_ref, ...), custom_call_target="tpu_custom_call" | custom-call | tf_op jit(solution)/shard_map/pallas_call | solution.py:411
  61.4 4.7 %collective-permute-start.13 = (f32[2,10,32,128]{3,2,1,0:T(8,128)}, f32[2,10,32,128]{3,2,1,0:T(8,128)S(1)}, u32[]{:S(2)}, u32[]{:S(2)}) collective-permute-start(f32[2,10,32,128]{3,2,1,0:T(8,128)} %get-tuple-element.68), channel_id=1, source_target_pairs={{1,0},{2,1},{3,2},{4,3},{5,4},{6,5},{7,6},{0,7},{9,8},{10,9},{11,1... | collective-permute-start | bytes 983048 | tf_op jit(solution)/shard_map/ppermute | solution.py:578
  66.1 1.9 %collective-permute-start.9 = (f32[2,8,32,128]{3,2,1,0:T(8,128)}, f32[2,8,32,128]{3,2,1,0:T(8,128)S(1)}, u32[]{:S(2)}, u32[]{:S(2)}) collective-permute-start(f32[2,8,32,128]{3,2,1,0:T(8,128)} %get-tuple-element.63), channel_id=1, source_target_pairs={{0,8},{1,9},{2,10},{3,11},{4,12},{5,13},{6,14},{7,15},{8,16},{9,17... | collective-permute-start | bytes 786440 | tf_op jit(solution)/shard_map/ppermute | solution.py:110
  68.0 1.9 %collective-permute-start.10 = (f32[2,5,32,128]{3,2,1,0:T(8,128)}, f32[2,5,32,128]{3,2,1,0:T(8,128)S(1)}, u32[]{:S(2)}, u32[]{:S(2)}) collective-permute-start(f32[2,5,32,128]{3,2,1,0:T(8,128)} %get-tuple-element.64), channel_id=1, source_target_pairs={{0,9},{1,10},{2,11},{3,12},{4,13},{5,14},{6,15},{7,8},{8,17},{9,18... | collective-permute-start | bytes 491528 | tf_op jit(solution)/shard_map/ppermute | solution.py:110
  69.9 1.9 %collective-permute-start.11 = (f32[2,5,32,128]{3,2,1,0:T(8,128)}, f32[2,5,32,128]{3,2,1,0:T(8,128)S(1)}, u32[]{:S(2)}, u32[]{:S(2)}) collective-permute-start(f32[2,5,32,128]{3,2,1,0:T(8,128)} %get-tuple-element.65), channel_id=1, source_target_pairs={{0,15},{1,8},{2,9},{3,10},{4,11},{5,12},{6,13},{7,14},{8,23},{9,16... | collective-permute-start | bytes 491528 | tf_op jit(solution)/shard_map/ppermute | solution.py:110
  71.9 8.1 %collective-permute-done.10.bbefore_ref = f32[2,5,32,128]{3,2,1,0:T(8,128)S(1)} collective-permute-done((f32[2,5,32,128]{3,2,1,0:T(8,128)}, f32[2,5,32,128]{3,2,1,0:T(8,128)S(1)}, u32[]{:S(2)}, u32[]{:S(2)}) %collective-permute-start.10) | collective-permute-done | bytes 163872 | tf_op jit(solution)/shard_map/ppermute | solution.py:110
  80.0 1.4 %collective-permute-done.13.after_ref = f32[2,10,32,128]{3,2,1,0:T(8,128)S(1)} collective-permute-done((f32[2,10,32,128]{3,2,1,0:T(8,128)}, f32[2,10,32,128]{3,2,1,0:T(8,128)S(1)}, u32[]{:S(2)}, u32[]{:S(2)}) %collective-permute-start.13) | collective-permute-done | bytes 327712 | tf_op jit(solution)/shard_map/ppermute | solution.py:578
  81.5 0.7 copy-done.3
  82.2 4.8 %shard_map.49 = (f32[2,10,32,128]{3,2,1,0:T(8,128)}, f32[2,10,32,128]{3,2,1,0:T(8,128)}, f32[2,10,32,128]{3,2,1,0:T(8,128)}, f32[2,10,32,128]{3,2,1,0:T(8,128)},...) custom-call(f32[2]{0:T(128)} %diff_ref.13, ...), custom_call_target="tpu_custom_call" | custom-call | tf_op jit(solution)/shard_map/pallas_call | solution.py:284
  87.0 1.7 %collective-permute-start.14 = (f32[2,6,16,128]{3,2,1,0:T(8,128)}, f32[2,6,16,128]{3,2,1,0:T(8,128)S(1)}, u32[]{:S(2)}, u32[]{:S(2)}) collective-permute-start(f32[2,6,16,128]{3,2,1,0:T(8,128)} %get-tuple-element.70), channel_id=1, source_target_pairs={{0,1},{1,2},{2,3},{3,4},{4,5},{5,6},{6,7},{7,0},{8,9},{9,10},{10,1... | collective-permute-start | bytes 294920 | tf_op jit(solution)/shard_map/ppermute | solution.py:553
  88.7 3.1 %collective-permute-start.15 = (f32[2,6,16,128]{3,2,1,0:T(8,128)}, f32[2,6,16,128]{3,2,1,0:T(8,128)S(1)}, u32[]{:S(2)}, u32[]{:S(2)}) collective-permute-start(f32[2,6,16,128]{3,2,1,0:T(8,128)} %get-tuple-element.71), channel_id=1, source_target_pairs={{1,0},{2,1},{3,2},{4,3},{5,4},{6,5},{7,6},{0,7},{9,8},{10,9},{11,1... | collective-permute-start | bytes 294920 | tf_op jit(solution)/shard_map/ppermute | solution.py:554
  91.7 3.1 %collective-permute-done.14.cbefore_ref = f32[2,6,16,128]{3,2,1,0:T(8,128)S(1)} collective-permute-done((f32[2,6,16,128]{3,2,1,0:T(8,128)}, f32[2,6,16,128]{3,2,1,0:T(8,128)S(1)}, u32[]{:S(2)}, u32[]{:S(2)}) %collective-permute-start.14) | collective-permute-done | bytes 98336 | tf_op jit(solution)/shard_map/ppermute | solution.py:553
  94.9 1.7 %collective-permute-done.15.cafter_ref = f32[2,6,16,128]{3,2,1,0:T(8,128)S(1)} collective-permute-done((f32[2,6,16,128]{3,2,1,0:T(8,128)}, f32[2,6,16,128]{3,2,1,0:T(8,128)S(1)}, u32[]{:S(2)}, u32[]{:S(2)}) %collective-permute-start.15) | collective-permute-done | bytes 98336 | tf_op jit(solution)/shard_map/ppermute | solution.py:554
  96.6 0.6 copy-done.17
  97.2 4.5 %shard_map.50 = (f32[4,2,8,32,128]{4,3,2,1,0:T(8,128)}, f32[2,10,32,128]{3,2,1,0:T(8,128)}, f32[2,10,32,128]{3,2,1,0:T(8,128)}, f32[2,8,32,128]{3,2,1,0:T(8,128)...) custom-call(f32[2]{0:T(128)} %diff_ref.13, f32[4,2,4,16,128]{4,3,2,1,0:T(8,128)} %get-tuple-element.69.cown_ref, ...), custom_call_target="tpu_custom_call" | custom-call | tf_op jit(solution)/shard_map/pallas_call | solution.py:411
  101.8 4.7 %collective-permute-start.20 = (f32[2,10,32,128]{3,2,1,0:T(8,128)}, f32[2,10,32,128]{3,2,1,0:T(8,128)S(1)}, u32[]{:S(2)}, u32[]{:S(2)}) collective-permute-start(f32[2,10,32,128]{3,2,1,0:T(8,128)} %get-tuple-element.83), channel_id=1, source_target_pairs={{1,0},{2,1},{3,2},{4,3},{5,4},{6,5},{7,6},{0,7},{9,8},{10,9},{11,1... | collective-permute-start | bytes 983048 | tf_op jit(solution)/shard_map/ppermute | solution.py:578
  106.5 1.9 %collective-permute-start.16 = (f32[2,8,32,128]{3,2,1,0:T(8,128)}, f32[2,8,32,128]{3,2,1,0:T(8,128)S(1)}, u32[]{:S(2)}, u32[]{:S(2)}) collective-permute-start(f32[2,8,32,128]{3,2,1,0:T(8,128)} %get-tuple-element.78), channel_id=1, source_target_pairs={{0,8},{1,9},{2,10},{3,11},{4,12},{5,13},{6,14},{7,15},{8,16},{9,17... | collective-permute-start | bytes 786440 | tf_op jit(solution)/shard_map/ppermute | solution.py:110
  108.4 1.9 %collective-permute-start.17 = (f32[2,5,32,128]{3,2,1,0:T(8,128)}, f32[2,5,32,128]{3,2,1,0:T(8,128)S(1)}, u32[]{:S(2)}, u32[]{:S(2)}) collective-permute-start(f32[2,5,32,128]{3,2,1,0:T(8,128)} %get-tuple-element.79), channel_id=1, source_target_pairs={{0,9},{1,10},{2,11},{3,12},{4,13},{5,14},{6,15},{7,8},{8,17},{9,18... | collective-permute-start | bytes 491528 | tf_op jit(solution)/shard_map/ppermute | solution.py:110
  110.3 2.1 %collective-permute-start.18 = (f32[2,5,32,128]{3,2,1,0:T(8,128)}, f32[2,5,32,128]{3,2,1,0:T(8,128)S(1)}, u32[]{:S(2)}, u32[]{:S(2)}) collective-permute-start(f32[2,5,32,128]{3,2,1,0:T(8,128)} %get-tuple-element.80), channel_id=1, source_target_pairs={{0,15},{1,8},{2,9},{3,10},{4,11},{5,12},{6,13},{7,14},{8,23},{9,16... | collective-permute-start | bytes 491528 | tf_op jit(solution)/shard_map/ppermute | solution.py:110
  112.5 11.2 %collective-permute-done.17.bbefore_ref = f32[2,5,32,128]{3,2,1,0:T(8,128)S(1)} collective-permute-done((f32[2,5,32,128]{3,2,1,0:T(8,128)}, f32[2,5,32,128]{3,2,1,0:T(8,128)S(1)}, u32[]{:S(2)}, u32[]{:S(2)}) %collective-permute-start.17) | collective-permute-done | bytes 163872 | tf_op jit(solution)/shard_map/ppermute | solution.py:110
  123.7 0.5 collective-permute-done.20.after_ref
  124.9 4.9 %shard_map.51 = (f32[2,10,32,128]{3,2,1,0:T(8,128)}, f32[2,10,32,128]{3,2,1,0:T(8,128)}, f32[2,10,32,128]{3,2,1,0:T(8,128)}, f32[2,10,32,128]{3,2,1,0:T(8,128)},...) custom-call(f32[2]{0:T(128)} %diff_ref.13, ...), custom_call_target="tpu_custom_call" | custom-call | tf_op jit(solution)/shard_map/pallas_call | solution.py:284
  129.8 1.7 %collective-permute-start.21 = (f32[2,2,16,128]{3,2,1,0:T(8,128)}, f32[2,2,16,128]{3,2,1,0:T(8,128)S(1)}, u32[]{:S(2)}, u32[]{:S(2)}) collective-permute-start(f32[2,2,16,128]{3,2,1,0:T(8,128)} %get-tuple-element.85), channel_id=1, source_target_pairs={{0,1},{1,2},{2,3},{3,4},{4,5},{5,6},{6,7},{7,0},{8,9},{9,10},{10,1... | collective-permute-start | bytes 98312 | tf_op jit(solution)/shard_map/ppermute | solution.py:553
  131.5 3.1 %collective-permute-start.22 = (f32[2,2,16,128]{3,2,1,0:T(8,128)}, f32[2,2,16,128]{3,2,1,0:T(8,128)S(1)}, u32[]{:S(2)}, u32[]{:S(2)}) collective-permute-start(f32[2,2,16,128]{3,2,1,0:T(8,128)} %get-tuple-element.86), channel_id=1, source_target_pairs={{1,0},{2,1},{3,2},{4,3},{5,4},{6,5},{7,6},{0,7},{9,8},{10,9},{11,1... | collective-permute-start | bytes 98312 | tf_op jit(solution)/shard_map/ppermute | solution.py:554
  134.6 2.1 %collective-permute-done.21.cbefore_ref = f32[2,2,16,128]{3,2,1,0:T(8,128)S(1)} collective-permute-done((f32[2,2,16,128]{3,2,1,0:T(8,128)}, f32[2,2,16,128]{3,2,1,0:T(8,128)S(1)}, u32[]{:S(2)}, u32[]{:S(2)}) %collective-permute-start.21) | collective-permute-done | bytes 32800 | tf_op jit(solution)/shard_map/ppermute | solution.py:553
  136.7 0.6 copy-done.18
  137.3 2.9 %shard_map.52 = f32[2,8,32,128]{3,2,1,0:T(8,128)} custom-call(f32[2]{0:T(128)} %diff_ref.13, f32[4,2,4,16,128]{4,3,2,1,0:T(8,128)} %get-tuple-element.84.cown_ref, f32[2,2,16,128]{3,2,1,0:T(8,128)} %copy-done.18, f32[2,2,16,128]{3,2,1,0:T(8,128)} %copy-done.19, f32[2,8,16,128]{3,2,1,0:T(8,128)} %get-tuple-element.52.rate_ref, ...), custom_call_target="tpu_custom_call" | custom-call | tf_op jit(solution)/shard_map/pallas_call | solution.py:411
  140.2 1.0 slice_bitcast_fusion.3
  141.3 0.8 copy.6
  (62 shorter events, 1.7 us)
Async XLA Ops:
  3.9 4.9 %copy-start.7 = (f32[1,2,8,32,128]{4,3,2,1,0:T(8,128)S(1)}, f32[1,2,8,32,128]{4,3,2,1,0:T(8,128)}, u32[]{:S(2)}) copy-start(f32[1,2,8,32,128]{4,3,2,1,0:T(8,128)} %param.4) | copy-start | bytes 786436
  4.0 34.1 %collective-permute-start.5 = (f32[2,2,5,32,128]{4,3,2,1,0:T(8,128)S(1)}, f32[2,2,5,32,128]{4,3,2,1,0:T(8,128)S(1)}, u32[]{:S(2)}, u32[]{:S(2)}) collective-permute-start(f32[2,2,5,32,128]{4,3,2,1,0:T(8,128)S(1)} %get-tuple-element.95), channel_id=1, source_target_pairs={{0,1},{1,2},{2,3},{3,4},{4,5},{5,6},{6,7},{7,0},{8,9},{9,10},{10,1... | collective-permute-start | bytes 983048 | tf_op jit(solution)/shard_map/ppermute | solution.py:94
  5.6 32.5 %collective-permute-start.6 = (f32[2,2,5,32,128]{4,3,2,1,0:T(8,128)S(1)}, f32[2,2,5,32,128]{4,3,2,1,0:T(8,128)S(1)}, u32[]{:S(2)}, u32[]{:S(2)}) collective-permute-start(f32[2,2,5,32,128]{4,3,2,1,0:T(8,128)S(1)} %get-tuple-element.96), channel_id=1, source_target_pairs={{1,0},{2,1},{3,2},{4,3},{5,4},{6,5},{7,6},{0,7},{9,8},{10,9},{11,1... | collective-permute-start | bytes 983048 | tf_op jit(solution)/shard_map/ppermute | solution.py:95
  9.0 19.3 %collective-permute-start = (f32[2,5,32,128]{3,2,1,0:T(8,128)S(1)}, f32[2,5,32,128]{3,2,1,0:T(8,128)S(1)}, u32[]{:S(2)}, u32[]{:S(2)}) collective-permute-start(f32[2,5,32,128]{3,2,1,0:T(8,128)S(1)} %get-tuple-element.99), channel_id=1, source_target_pairs={{0,1},{1,2},{2,3},{3,4},{4,5},{5,6},{6,7},{7,0},{8,9},{9,10},{10,1... | collective-permute-start | bytes 491528 | tf_op jit(solution)/shard_map/ppermute | solution.py:94
  9.1 25.3 %collective-permute-start.1 = (f32[2,5,32,128]{3,2,1,0:T(8,128)S(1)}, f32[2,5,32,128]{3,2,1,0:T(8,128)}, u32[]{:S(2)}, u32[]{:S(2)}) collective-permute-start(f32[2,5,32,128]{3,2,1,0:T(8,128)S(1)} %get-tuple-element.100), channel_id=1, source_target_pairs={{1,0},{2,1},{3,2},{4,3},{5,4},{6,5},{7,6},{0,7},{9,8},{10,9},{11,1... | collective-permute-start | bytes 491528 | tf_op jit(solution)/shard_map/ppermute | solution.py:95
  13.8 29.1 %collective-permute-start.3 = (f32[2,5,32,128]{3,2,1,0:T(8,128)S(1)}, f32[2,5,32,128]{3,2,1,0:T(8,128)S(1)}, u32[]{:S(2)}, u32[]{:S(2)}) collective-permute-start(f32[2,5,32,128]{3,2,1,0:T(8,128)S(1)} %get-tuple-element.99), channel_id=1, source_target_pairs={{0,9},{1,10},{2,11},{3,12},{4,13},{5,14},{6,15},{7,8},{8,17},{9,18... | collective-permute-start | bytes 491528 | tf_op jit(solution)/shard_map/ppermute | solution.py:110
  28.4 14.5 %collective-permute-start.4 = (f32[2,5,32,128]{3,2,1,0:T(8,128)S(1)}, f32[2,5,32,128]{3,2,1,0:T(8,128)S(1)}, u32[]{:S(2)}, u32[]{:S(2)}) collective-permute-start(f32[2,5,32,128]{3,2,1,0:T(8,128)S(1)} %get-tuple-element.100), channel_id=1, source_target_pairs={{0,15},{1,8},{2,9},{3,10},{4,11},{5,12},{6,13},{7,14},{8,23},{9,16... | collective-permute-start | bytes 491528 | tf_op jit(solution)/shard_map/ppermute | solution.py:110
  34.4 8.6 %collective-permute-start.2 = (f32[2,8,32,128]{3,2,1,0:T(8,128)S(1)}, f32[2,8,32,128]{3,2,1,0:T(8,128)S(1)}, u32[]{:S(2)}, u32[]{:S(2)}) collective-permute-start(f32[2,8,32,128]{3,2,1,0:T(8,128)S(1)} %pad_maximum_fusion.2), channel_id=1, source_target_pairs={{0,8},{1,9},{2,10},{3,11},{4,12},{5,13},{6,14},{7,15},{8,16},{9,17... | collective-permute-start | bytes 786440 | tf_op jit(solution)/shard_map/ppermute | solution.py:110
  42.9 0.7 copy-start.8
  42.9 0.7 copy-start.9
  42.9 0.8 copy-start.4
  48.6 7.5 %collective-permute-start.7 = (f32[2,6,16,128]{3,2,1,0:T(8,128)}, f32[2,6,16,128]{3,2,1,0:T(8,128)S(1)}, u32[]{:S(2)}, u32[]{:S(2)}) collective-permute-start(f32[2,6,16,128]{3,2,1,0:T(8,128)} %get-tuple-element.54), channel_id=1, source_target_pairs={{0,1},{1,2},{2,3},{3,4},{4,5},{5,6},{6,7},{7,0},{8,9},{9,10},{10,1... | collective-permute-start | bytes 294920 | tf_op jit(solution)/shard_map/ppermute | solution.py:553
  48.6 7.5 %collective-permute-start.8 = (f32[2,6,16,128]{3,2,1,0:T(8,128)}, f32[2,6,16,128]{3,2,1,0:T(8,128)S(1)}, u32[]{:S(2)}, u32[]{:S(2)}) collective-permute-start(f32[2,6,16,128]{3,2,1,0:T(8,128)} %get-tuple-element.55), channel_id=1, source_target_pairs={{1,0},{2,1},{3,2},{4,3},{5,4},{6,5},{7,6},{0,7},{9,8},{10,9},{11,1... | collective-permute-start | bytes 294920 | tf_op jit(solution)/shard_map/ppermute | solution.py:554
  56.1 0.6 copy-start.14
  56.1 0.7 copy-start.16
  61.3 18.7 %collective-permute-start.12 = (f32[2,10,32,128]{3,2,1,0:T(8,128)}, f32[2,10,32,128]{3,2,1,0:T(8,128)S(1)}, u32[]{:S(2)}, u32[]{:S(2)}) collective-permute-start(f32[2,10,32,128]{3,2,1,0:T(8,128)} %get-tuple-element.67), channel_id=1, source_target_pairs={{0,1},{1,2},{2,3},{3,4},{4,5},{5,6},{6,7},{7,0},{8,9},{9,10},{10,1... | collective-permute-start | bytes 983048 | tf_op jit(solution)/shard_map/ppermute | solution.py:577
  61.4 20.1 %collective-permute-start.13 = (f32[2,10,32,128]{3,2,1,0:T(8,128)}, f32[2,10,32,128]{3,2,1,0:T(8,128)S(1)}, u32[]{:S(2)}, u32[]{:S(2)}) collective-permute-start(f32[2,10,32,128]{3,2,1,0:T(8,128)} %get-tuple-element.68), channel_id=1, source_target_pairs={{1,0},{2,1},{3,2},{4,3},{5,4},{6,5},{7,6},{0,7},{9,8},{10,9},{11,1... | collective-permute-start | bytes 983048 | tf_op jit(solution)/shard_map/ppermute | solution.py:578
  66.1 13.9 %collective-permute-start.9 = (f32[2,8,32,128]{3,2,1,0:T(8,128)}, f32[2,8,32,128]{3,2,1,0:T(8,128)S(1)}, u32[]{:S(2)}, u32[]{:S(2)}) collective-permute-start(f32[2,8,32,128]{3,2,1,0:T(8,128)} %get-tuple-element.63), channel_id=1, source_target_pairs={{0,8},{1,9},{2,10},{3,11},{4,12},{5,13},{6,14},{7,15},{8,16},{9,17... | collective-permute-start | bytes 786440 | tf_op jit(solution)/shard_map/ppermute | solution.py:110
  68.0 11.9 %collective-permute-start.10 = (f32[2,5,32,128]{3,2,1,0:T(8,128)}, f32[2,5,32,128]{3,2,1,0:T(8,128)S(1)}, u32[]{:S(2)}, u32[]{:S(2)}) collective-permute-start(f32[2,5,32,128]{3,2,1,0:T(8,128)} %get-tuple-element.64), channel_id=1, source_target_pairs={{0,9},{1,10},{2,11},{3,12},{4,13},{5,14},{6,15},{7,8},{8,17},{9,18... | collective-permute-start | bytes 491528 | tf_op jit(solution)/shard_map/ppermute | solution.py:110
  69.9 10.0 %collective-permute-start.11 = (f32[2,5,32,128]{3,2,1,0:T(8,128)}, f32[2,5,32,128]{3,2,1,0:T(8,128)S(1)}, u32[]{:S(2)}, u32[]{:S(2)}) collective-permute-start(f32[2,5,32,128]{3,2,1,0:T(8,128)} %get-tuple-element.65), channel_id=1, source_target_pairs={{0,15},{1,8},{2,9},{3,10},{4,11},{5,12},{6,13},{7,14},{8,23},{9,16... | collective-permute-start | bytes 491528 | tf_op jit(solution)/shard_map/ppermute | solution.py:110
  79.9 1.5 %copy-start.11 = (f32[2,5,32,128]{3,2,1,0:T(8,128)}, f32[2,5,32,128]{3,2,1,0:T(8,128)S(1)}, u32[]{:S(2)}) copy-start(f32[2,5,32,128]{3,2,1,0:T(8,128)S(1)} %collective-permute-done.10.bbefore_ref) | copy-start | bytes 491524
  79.9 1.5 %copy-start.13 = (f32[2,5,32,128]{3,2,1,0:T(8,128)}, f32[2,5,32,128]{3,2,1,0:T(8,128)S(1)}, u32[]{:S(2)}) copy-start(f32[2,5,32,128]{3,2,1,0:T(8,128)S(1)} %collective-permute-done.11.bafter_ref) | copy-start | bytes 491524
  80.0 1.5 %copy-start.6 = (f32[2,8,32,128]{3,2,1,0:T(8,128)}, f32[2,8,32,128]{3,2,1,0:T(8,128)S(1)}, u32[]{:S(2)}) copy-start(f32[2,8,32,128]{3,2,1,0:T(8,128)S(1)} %collective-permute-done.9.centre_ref) | copy-start | bytes 786436
  80.0 1.5 %copy-start.1 = (f32[2,10,32,128]{3,2,1,0:T(8,128)}, f32[2,10,32,128]{3,2,1,0:T(8,128)S(1)}, u32[]{:S(2)}) copy-start(f32[2,10,32,128]{3,2,1,0:T(8,128)S(1)} %collective-permute-done.12.before_ref) | copy-start | bytes 983044
  81.4 0.7 copy-start.3
  87.0 7.8 %collective-permute-start.14 = (f32[2,6,16,128]{3,2,1,0:T(8,128)}, f32[2,6,16,128]{3,2,1,0:T(8,128)S(1)}, u32[]{:S(2)}, u32[]{:S(2)}) collective-permute-start(f32[2,6,16,128]{3,2,1,0:T(8,128)} %get-tuple-element.70), channel_id=1, source_target_pairs={{0,1},{1,2},{2,3},{3,4},{4,5},{5,6},{6,7},{7,0},{8,9},{9,10},{10,1... | collective-permute-start | bytes 294920 | tf_op jit(solution)/shard_map/ppermute | solution.py:553
  88.7 7.9 %collective-permute-start.15 = (f32[2,6,16,128]{3,2,1,0:T(8,128)}, f32[2,6,16,128]{3,2,1,0:T(8,128)S(1)}, u32[]{:S(2)}, u32[]{:S(2)}) collective-permute-start(f32[2,6,16,128]{3,2,1,0:T(8,128)} %get-tuple-element.71), channel_id=1, source_target_pairs={{1,0},{2,1},{3,2},{4,3},{5,4},{6,5},{7,6},{0,7},{9,8},{10,9},{11,1... | collective-permute-start | bytes 294920 | tf_op jit(solution)/shard_map/ppermute | solution.py:554
  94.9 1.7 %copy-start.15 = (f32[2,6,16,128]{3,2,1,0:T(8,128)}, f32[2,6,16,128]{3,2,1,0:T(8,128)S(1)}, u32[]{:S(2)}) copy-start(f32[2,6,16,128]{3,2,1,0:T(8,128)S(1)} %collective-permute-done.14.cbefore_ref) | copy-start | bytes 294916
  96.6 0.6 copy-start.17
  101.7 22.0 %collective-permute-start.19 = (f32[2,10,32,128]{3,2,1,0:T(8,128)}, f32[2,10,32,128]{3,2,1,0:T(8,128)S(1)}, u32[]{:S(2)}, u32[]{:S(2)}) collective-permute-start(f32[2,10,32,128]{3,2,1,0:T(8,128)} %get-tuple-element.82), channel_id=1, source_target_pairs={{0,1},{1,2},{2,3},{3,4},{4,5},{5,6},{6,7},{7,0},{8,9},{9,10},{10,1... | collective-permute-start | bytes 983048 | tf_op jit(solution)/shard_map/ppermute | solution.py:577
  101.8 22.4 %collective-permute-start.20 = (f32[2,10,32,128]{3,2,1,0:T(8,128)}, f32[2,10,32,128]{3,2,1,0:T(8,128)S(1)}, u32[]{:S(2)}, u32[]{:S(2)}) collective-permute-start(f32[2,10,32,128]{3,2,1,0:T(8,128)} %get-tuple-element.83), channel_id=1, source_target_pairs={{1,0},{2,1},{3,2},{4,3},{5,4},{6,5},{7,6},{0,7},{9,8},{10,9},{11,1... | collective-permute-start | bytes 983048 | tf_op jit(solution)/shard_map/ppermute | solution.py:578
  106.5 17.2 %collective-permute-start.16 = (f32[2,8,32,128]{3,2,1,0:T(8,128)}, f32[2,8,32,128]{3,2,1,0:T(8,128)S(1)}, u32[]{:S(2)}, u32[]{:S(2)}) collective-permute-start(f32[2,8,32,128]{3,2,1,0:T(8,128)} %get-tuple-element.78), channel_id=1, source_target_pairs={{0,8},{1,9},{2,10},{3,11},{4,12},{5,13},{6,14},{7,15},{8,16},{9,17... | collective-permute-start | bytes 786440 | tf_op jit(solution)/shard_map/ppermute | solution.py:110
  108.4 15.3 %collective-permute-start.17 = (f32[2,5,32,128]{3,2,1,0:T(8,128)}, f32[2,5,32,128]{3,2,1,0:T(8,128)S(1)}, u32[]{:S(2)}, u32[]{:S(2)}) collective-permute-start(f32[2,5,32,128]{3,2,1,0:T(8,128)} %get-tuple-element.79), channel_id=1, source_target_pairs={{0,9},{1,10},{2,11},{3,12},{4,13},{5,14},{6,15},{7,8},{8,17},{9,18... | collective-permute-start | bytes 491528 | tf_op jit(solution)/shard_map/ppermute | solution.py:110
  110.3 13.3 %collective-permute-start.18 = (f32[2,5,32,128]{3,2,1,0:T(8,128)}, f32[2,5,32,128]{3,2,1,0:T(8,128)S(1)}, u32[]{:S(2)}, u32[]{:S(2)}) collective-permute-start(f32[2,5,32,128]{3,2,1,0:T(8,128)} %get-tuple-element.80), channel_id=1, source_target_pairs={{0,15},{1,8},{2,9},{3,10},{4,11},{5,12},{6,13},{7,14},{8,23},{9,16... | collective-permute-start | bytes 491528 | tf_op jit(solution)/shard_map/ppermute | solution.py:110
  123.7 0.7 copy-start.10
  123.7 0.7 copy-start.12
  123.7 0.8 copy-start.5
  123.7 0.9 copy-start
  124.2 0.7 copy-start.2
  129.8 6.8 %collective-permute-start.21 = (f32[2,2,16,128]{3,2,1,0:T(8,128)}, f32[2,2,16,128]{3,2,1,0:T(8,128)S(1)}, u32[]{:S(2)}, u32[]{:S(2)}) collective-permute-start(f32[2,2,16,128]{3,2,1,0:T(8,128)} %get-tuple-element.85), channel_id=1, source_target_pairs={{0,1},{1,2},{2,3},{3,4},{4,5},{5,6},{6,7},{7,0},{8,9},{9,10},{10,1... | collective-permute-start | bytes 98312 | tf_op jit(solution)/shard_map/ppermute | solution.py:553
  131.5 5.2 %collective-permute-start.22 = (f32[2,2,16,128]{3,2,1,0:T(8,128)}, f32[2,2,16,128]{3,2,1,0:T(8,128)S(1)}, u32[]{:S(2)}, u32[]{:S(2)}) collective-permute-start(f32[2,2,16,128]{3,2,1,0:T(8,128)} %get-tuple-element.86), channel_id=1, source_target_pairs={{1,0},{2,1},{3,2},{4,3},{5,4},{6,5},{7,6},{0,7},{9,8},{10,9},{11,1... | collective-permute-start | bytes 98312 | tf_op jit(solution)/shard_map/ppermute | solution.py:554
  136.7 0.6 copy-start.18
  136.7 0.6 copy-start.19

commit v6 on v5

--- a/solution.py
+++ b/solution.py
@@ -168,6 +168,15 @@
     return jnp.concatenate([rows, rows], axis=-2)
 
 
+def even_odd_load(ref, index=()):
+    view = ref.at[index] if index else ref
+    lead = (slice(None),) * (len(view.shape) - 2)
+    half = view.shape[-2] // 2
+    even = view[lead + (pl.ds(0, half, stride=2), slice(None))]
+    odd = view[lead + (pl.ds(1, half, stride=2), slice(None))]
+    return jnp.concatenate([even, odd], axis=-2)
+
+
 def kernel_laplace(f):
     centre = f[:, 1:-1]
     pair_x = f[:, 2:] + f[:, :-2]
@@ -193,7 +202,7 @@
     return (upper + lower) * 0.25
 
 
-def sweep_kernel(widths_sent, diff_ref, flag_ref, start_ref, centre_ref, bbefore_ref, bafter_ref,
+def sweep_kernel(widths_sent, natural_prior, diff_ref, flag_ref, start_ref, centre_ref, bbefore_ref, bafter_ref,
                  own_ref, before_ref, after_ref, dec_ref, src_ref,
                  rate_ref, n1_ref, n2_ref, n3_ref, n4_ref, e0_ref, b0_ref, cown_ref, clasts_ref,
                  cfirsts_ref):
@@ -230,7 +239,11 @@
             )
         )
         offset += w
-    joined = jnp.concatenate([bbefore_ref[...], centre_ref[...], bafter_ref[...]], axis=1)
+    if natural_prior:
+        pieces = [even_odd_load(r) for r in (bbefore_ref, centre_ref, bafter_ref)]
+    else:
+        pieces = [r[...] for r in (bbefore_ref, centre_ref, bafter_ref)]
+    joined = jnp.concatenate(pieces, axis=1)
     swept = [jnp.where(flag_ref[0] == 1, start_ref[...], joined)]
     found = []
     for m in range(4):
@@ -272,7 +285,8 @@
     b0_ref[...] = cut(swept[0], hs, 0)
 
 
-def fine_sweep(diffusivity, flag, start, prior, parts, decay, src, rate_c, widths_sent):
+def fine_sweep(diffusivity, flag, start, prior, parts, decay, src, rate_c, widths_sent,
+               natural_prior):
     rows = start.shape[1] - 2 * START_HALO
     shape = start.shape
     wide = jax.ShapeDtypeStruct((shape[0], rows + 2) + shape[2:], jnp.float32)
@@ -282,7 +296,7 @@
     cedge = jax.ShapeDtypeStruct((shape[0], sum(widths_sent)) + cshape[2:], jnp.float32)
     vmem = pl.BlockSpec(memory_space=pltpu.VMEM)
     return pl.pallas_call(
-        functools.partial(sweep_kernel, widths_sent),
+        functools.partial(sweep_kernel, widths_sent, natural_prior),
         out_shape=(wide, wide, wide, wide, own, own, cown, cedge, cedge),
         in_specs=[pl.BlockSpec(memory_space=pltpu.SMEM)] * 2 + [vmem] * 10,
         out_specs=(vmem,) * 9,
@@ -368,7 +382,9 @@
         fine = prolonged(interp_table[m][1] * delta_one + interp_table[m][2] * delta_two)
         news[m] = cut(ref[...], 1, ho) + cut(fine, 2 * ho, ho)
     if last:
-        outs[0][...] = news[4]
+        half = news[4].shape[2] // 2
+        outs[0][:, :, pl.ds(0, half, stride=2), :] = news[4][:, :, :half]
+        outs[0][:, :, pl.ds(1, half, stride=2), :] = news[4][:, :, half:]
         return
     own_out, lasts_out, firsts_out, u4_out, u4_last_out, u4_first_out = outs
     src1 = at(src_ref, 0, rows, hd)
@@ -416,17 +432,22 @@
     )(*args)
 
 
-def start_kernel(diff_ref, init_ref, dec_ref, src_ref, own_ref, before_ref, after_ref,
-                 rate_ref, csrc_ref):
+def start_kernel(diff_ref, stacked_ref, own_ref, before_ref, after_ref, rate_ref, csrc_ref,
+                 ext_ref, dec_ref, src_ref):
     spread_table, grouped_table, interp_table, widths = node_tables()
     rows = own_ref.shape[2]
-    hs = (init_ref.shape[1] - rows) // 2
+    hs = (stacked_ref.shape[2] - rows) // 2
     d0 = diff_ref[0]
     d1 = diff_ref[1]
-    state = init_ref[...]
+    state = even_odd_load(stacked_ref, (0,))
+    decay = even_odd_load(stacked_ref, (1,))
+    source = even_odd_load(stacked_ref, (2,))
+    ext_ref[...] = state
+    dec_ref[...] = decay
+    src_ref[...] = source
     inner = state[:, 1:-1]
-    dec = dec_ref[:, 1:-1]
-    s = src_ref[:, 1:-1]
+    dec = decay[:, 1:-1]
+    s = source[:, 1:-1]
     laplace = kernel_laplace(state)
     product = inner[0] * inner[1] * inner[1]
     terms = jnp.stack([d0 * laplace[0] - product + s[0], d1 * laplace[1] + product + s[1]])
@@ -447,8 +468,8 @@
     csrc_ref[...] = kernel_restrict(s)
 
 
-def start_terms(diffusivity, own_ext, decay, src):
-    shape = own_ext.shape
+def start_terms(diffusivity, stacked):
+    shape = stacked.shape[1:]
     rows = shape[1] - 2 * START_HALO
     sent = sum(START_HALO - 1 - m for m in range(4))
     edge = jax.ShapeDtypeStruct((shape[0], sent) + shape[2:], jnp.float32)
@@ -460,10 +481,13 @@
         out_shape=(
             jax.ShapeDtypeStruct((4, shape[0], rows) + shape[2:], jnp.float32),
             edge, edge, coarse, coarse,
+            jax.ShapeDtypeStruct(shape, jnp.float32),
+            jax.ShapeDtypeStruct(shape, jnp.float32),
+            jax.ShapeDtypeStruct(shape, jnp.float32),
         ),
-        in_specs=[pl.BlockSpec(memory_space=pltpu.SMEM)] + [vmem] * 3,
-        out_specs=(vmem,) * 5,
-    )(diffusivity, own_ext, decay, src)
+        in_specs=[pl.BlockSpec(memory_space=pltpu.SMEM)] + [vmem],
+        out_specs=(vmem,) * 8,
+    )(diffusivity, stacked)
 
 
 def packed_halo(fields):
@@ -504,12 +528,13 @@
     hs = START_HALO
     assert hs == 5 and initial.shape[-3] >= hs
 
-    own_start = to_even_odd(initial[0])
-    own_ext = space_halo(own_start, hs)
-    fixed = space_halo(jnp.stack([to_even_odd(decay_rate), to_even_odd(source)]), hs)
-    decay = (fixed[0], hs)
-    src = (fixed[1], hs)
-    own4, before4, after4, rate_own, csrc_own = start_terms(diffusivity, own_ext, decay[0], src[0])
+    own_start = initial[0]
+    stacked = space_halo(jnp.stack([own_start, decay_rate, source]), hs)
+    own4, before4, after4, rate_own, csrc_own, own_ext, dec_ext, src_ext = start_terms(
+        diffusivity, stacked
+    )
+    decay = (dec_ext, hs)
+    src = (src_ext, hs)
     rate_c = (rate_own, (hs - 1) // 2)
     source_c = (csrc_own, (hs - 1) // 2)
 
@@ -543,10 +568,11 @@
             out.append((own, h))
         return out
 
-    def advance(prior, pieces, last):
+    def advance(prior, pieces, last, natural):
         widths_sent = (1, 1, 0, 0) if last else (2, 2, 1, 1)
         n1, n2, n3, n4, e0, b0, cown, clasts, cfirsts = fine_sweep(
-            diffusivity, flag, own_ext, prior, pieces, decay[0], src[0], rate_c[0], widths_sent
+            diffusivity, flag, own_ext, prior, pieces, decay[0], src[0], rate_c[0], widths_sent,
+            natural,
         )
         coarse = (
             cown,
@@ -569,7 +595,7 @@
     )
     for k in range(ROUNDS):
         last = k + 1 == ROUNDS
-        outs = advance(prior, pieces, last)
+        outs = advance(prior, pieces, last, k == 0)
         if not last:
             own4, lasts, firsts, u4, u4_last, u4_first = outs
             pieces = (
@@ -578,7 +604,7 @@
                 lax.ppermute(firsts, "space", down),
             )
             prior = from_previous_slice((u4, u4_last, u4_first))
-    return from_even_odd(outs[0])[None]
+    return outs[0][None]
 
 
 def solution(mesh):

time: 143 us -> 139 us (0.972)
  waiting for transfers between devices: 43.6 us -> 53 us
  starting transfers between devices: 54.8 us -> 45.8 us
  local copies, waits for them, and re-layouts: 11.2 us -> 4.95 us
    ppermute x2 -> x1, starting transfers between devices: 7.91 us -> 3.2 us  [space_halo(): lax.ppermute(lax.slice_in_dim(a, 0, h, axis=a.ndim - 3), 'space', down)]
    ppermute x9, starting transfers between devices: 21.5 us -> 17.3 us  [moved(): return lax.ppermute(piece, axes, pairs)]
    ppermute x2 -> x1, waiting for transfers between devices: 12.6 us -> 16.5 us  [space_halo(): lax.ppermute(lax.slice_in_dim(a, rows - h, rows, axis=a.ndim - 3), 'space...]
    slice x6 -> x2, local copies, waits for them, and re-layouts: 4.06 us -> 0.8 us  [the longest x1 0.7 us: per_device(): own_start[:, :hs]]
    ppermute x9, waiting for transfers between devices: 19.3 us -> 21.7 us  [moved(): return lax.ppermute(piece, axes, pairs)]
    ppermute x2 -> x1, waiting for transfers between devices: 0.01 us -> 2.2 us  [space_halo(): lax.ppermute(lax.slice_in_dim(a, 0, h, axis=a.ndim - 3), 'space', down)]
    another operation x3 -> x0, local copies, waits for them, and re-layouts: 1.83 us -> none  [the longest x2 1.07 us: from_even_odd(): woven = jnp.stack([a[..., :half, :], a[..., half:, :]], axis=-2)]
    unnamed x40 -> x44, local copies, waits for them, and re-layouts: 4.14 us -> 4.15 us
  transfers between devices with their start and end apart: 23 -> 21, of which waited for: 9 -> 11; matrix products, arithmetic and copies ran while one was open for 2% -> 2% of each run, Pallas kernels for 3% -> 3%
where the time goes in v6:
time: 139 us; the launch traced here: 138 us
  waiting for transfers between devices  53 us (38%)
  starting transfers between devices  45.8 us (33%)
  Pallas kernels  30.8 us (22%)
  local copies, waits for them, and re-layouts  4.95 us (4%)
  other arithmetic  2.73 us (2%)
    ppermute x9, waiting for transfers between devices, moved(): return lax.ppermute(piece, axes, pairs)  21.7 us
    ppermute x9, starting transfers between devices, moved(): return lax.ppermute(piece, axes, pairs)  17.3 us
    ppermute x1, waiting for transfers between devices, space_halo(): lax.ppermute(lax.slice_in_dim(a, rows - h, rows, axis=a.ndim - 3), 'space...  16.5 us
    pallas_call x3, Pallas kernels, fine_sweep(): pl.pallas_call(functools.partial(sweep_kernel, widths_sent, natural_prior...  14.6 us
    pallas_call x3, Pallas kernels, finish_round(): pl.pallas_call(functools.partial(finish_kernel, widths_sent), out_shape=o...  12 us
    ppermute x3, starting transfers between devices, advance(): lax.ppermute(cfirsts, 'space', down)  10.6 us
    ppermute x2, starting transfers between devices, per_device(): lax.ppermute(firsts, 'space', down)  8.72 us
    ppermute x3, waiting for transfers between devices, advance(): lax.ppermute(clasts, 'space', up)  8.13 us
  transfers between devices with their start and end apart: 21, of which 11 were waited for; matrix products, arithmetic and copies ran while one was open for 2% of the time, Pallas kernels for 3%

profile of v6, /device:TPU:2, one launch (start us, length us, event | category | flops | bytes accessed | tf_op | source)
XLA Modules:
  0.0 137.6 jit_solution(11427095443108974824)
XLA Ops:
  0.0 1.3 pad_maximum_fusion.1
  1.4 1.6 %collective-permute-start = (f32[3,2,5,32,128]{4,3,2,1,0:T(8,128)S(1)}, f32[3,2,5,32,128]{4,3,2,1,0:T(8,128)S(1)}, u32[]{:S(2)}, u32[]{:S(2)}) collective-permute-start(f32[3,2,5,32,128]{4,3,2,1,0:T(8,128)S(1)} %get-tuple-element.99), channel_id=1, source_target_pairs={{0,1},{1,2},{2,3},{3,4},{4,5},{5,6},{6,7},{7,0},{8,9},{9,10},{10,1... | collective-permute-start | bytes 1474568 | tf_op jit(solution)/shard_map/ppermute | solution.py:94
  3.0 3.2 %collective-permute-start.1 = (f32[3,2,5,32,128]{4,3,2,1,0:T(8,128)S(1)}, f32[3,2,5,32,128]{4,3,2,1,0:T(8,128)S(1)}, u32[]{:S(2)}, u32[]{:S(2)}) collective-permute-start(f32[3,2,5,32,128]{4,3,2,1,0:T(8,128)S(1)} %get-tuple-element.100), channel_id=1, source_target_pairs={{1,0},{2,1},{3,2},{4,3},{5,4},{6,5},{7,6},{0,7},{9,8},{10,9},{11,1... | collective-permute-start | bytes 1474568 | tf_op jit(solution)/shard_map/ppermute | solution.py:95
  6.2 1.9 %collective-permute-start.2 = (f32[2,8,32,128]{3,2,1,0:T(8,128)S(1)}, f32[2,8,32,128]{3,2,1,0:T(8,128)S(1)}, u32[]{:S(2)}, u32[]{:S(2)}) collective-permute-start(f32[2,8,32,128]{3,2,1,0:T(8,128)S(1)} %bitcast.5), channel_id=1, source_target_pairs={{0,8},{1,9},{2,10},{3,11},{4,12},{5,13},{6,14},{7,15},{8,16},{9,17... | collective-permute-start | bytes 786440 | tf_op jit(solution)/shard_map/ppermute | solution.py:110
  8.1 0.7 fusion.1
  8.8 2.0 %collective-permute-start.4 = (f32[2,5,32,128]{3,2,1,0:T(8,128)}, f32[2,5,32,128]{3,2,1,0:T(8,128)S(1)}, u32[]{:S(2)}, u32[]{:S(2)}) collective-permute-start(f32[2,5,32,128]{3,2,1,0:T(8,128)} %get-tuple-element.101), channel_id=1, source_target_pairs={{0,15},{1,8},{2,9},{3,10},{4,11},{5,12},{6,13},{7,14},{8,23},{9,16... | collective-permute-start | bytes 491528 | tf_op jit(solution)/shard_map/ppermute | solution.py:110
  10.8 1.9 %collective-permute-start.3 = (f32[2,5,32,128]{3,2,1,0:T(8,128)S(1)}, f32[2,5,32,128]{3,2,1,0:T(8,128)S(1)}, u32[]{:S(2)}, u32[]{:S(2)}) collective-permute-start(f32[2,5,32,128]{3,2,1,0:T(8,128)S(1)} %get-tuple-element.102), channel_id=1, source_target_pairs={{0,9},{1,10},{2,11},{3,12},{4,13},{5,14},{6,15},{7,8},{8,17},{9,18... | collective-permute-start | bytes 491528 | tf_op jit(solution)/shard_map/ppermute | solution.py:110
  12.7 16.5 %collective-permute-done = f32[3,2,5,32,128]{4,3,2,1,0:T(8,128)S(1)} collective-permute-done((f32[3,2,5,32,128]{4,3,2,1,0:T(8,128)S(1)}, f32[3,2,5,32,128]{4,3,2,1,0:T(8,128)S(1)}, u32[]{:S(2)}, u32[]{:S(2)}) %collective-permute-start) | collective-permute-done | bytes 491552 | tf_op jit(solution)/shard_map/ppermute | solution.py:94
  29.2 2.2 %collective-permute-done.1 = f32[3,2,5,32,128]{4,3,2,1,0:T(8,128)S(1)} collective-permute-done((f32[3,2,5,32,128]{4,3,2,1,0:T(8,128)S(1)}, f32[3,2,5,32,128]{4,3,2,1,0:T(8,128)S(1)}, u32[]{:S(2)}, u32[]{:S(2)}) %collective-permute-start.1) | collective-permute-done | bytes 491552 | tf_op jit(solution)/shard_map/ppermute | solution.py:95
  31.4 1.5 %pad_maximum_fusion.stacked_ref = f32[3,2,18,32,128]{4,3,2,1,0:T(8,128)} fusion(f32[3,2,5,32,128]{4,3,2,1,0:T(8,128)S(1)} %collective-permute-done.1, f32[1,2,8,32,128]{4,3,2,1,0:T(8,128)S(1)} %bitcast.8, f32[1,2,8,32,128]{4,3,2,1,0:T(8,128)S(1)} %bitcast.10, f32[1,2,8,32,128]{4,3,2,1,0:T(8,128)S(1)} %copy-done, f32[3,2,5,32,128]{4,3,2,1,0:T(8,128)S(1)} %collective-permute-done), kind=kLoop, calls=%fused_computation | loop fusion | flops 1769472 | bytes 3538944 | tf_op jit(solution)/shard_map/concatenate | solution.py:96
  32.9 4.2 %shard_map.46 = (f32[4,2,8,32,128]{4,3,2,1,0:T(8,128)}, f32[2,10,32,128]{3,2,1,0:T(8,128)}, f32[2,10,32,128]{3,2,1,0:T(8,128)}, f32[2,8,16,128]{3,2,1,0:T(8,128)...) custom-call(f32[2]{0:T(128)} %diff_ref.13, ...), custom_call_target="tpu_custom_call" | custom-call | tf_op jit(solution)/shard_map/pallas_call | solution.py:479
  37.1 0.6 copy-done.10
  37.9 4.8 %shard_map.47 = (f32[2,10,32,128]{3,2,1,0:T(8,128)}, f32[2,10,32,128]{3,2,1,0:T(8,128)}, f32[2,10,32,128]{3,2,1,0:T(8,128)}, f32[2,10,32,128]{3,2,1,0:T(8,128)},...) custom-call(f32[2]{0:T(128)} %diff_ref.13, ...), custom_call_target="tpu_custom_call" | custom-call | tf_op jit(solution)/shard_map/pallas_call | solution.py:298
  42.7 0.3 collective-permute-start.5
  43.0 4.4 %collective-permute-start.6 = (f32[2,6,16,128]{3,2,1,0:T(8,128)}, f32[2,6,16,128]{3,2,1,0:T(8,128)S(1)}, u32[]{:S(2)}, u32[]{:S(2)}) collective-permute-start(f32[2,6,16,128]{3,2,1,0:T(8,128)} %get-tuple-element.61), channel_id=1, source_target_pairs={{1,0},{2,1},{3,2},{4,3},{5,4},{6,5},{7,6},{0,7},{9,8},{10,9},{11,1... | collective-permute-start | bytes 294920 | tf_op jit(solution)/shard_map/ppermute | solution.py:580
  47.5 2.9 %collective-permute-done.5.cbefore_ref = f32[2,6,16,128]{3,2,1,0:T(8,128)S(1)} collective-permute-done((f32[2,6,16,128]{3,2,1,0:T(8,128)}, f32[2,6,16,128]{3,2,1,0:T(8,128)S(1)}, u32[]{:S(2)}, u32[]{:S(2)}) %collective-permute-start.5) | collective-permute-done | bytes 98336 | tf_op jit(solution)/shard_map/ppermute | solution.py:579
  50.5 0.6 copy-done.16
  51.1 4.6 %shard_map.48 = (f32[4,2,8,32,128]{4,3,2,1,0:T(8,128)}, f32[2,10,32,128]{3,2,1,0:T(8,128)}, f32[2,10,32,128]{3,2,1,0:T(8,128)}, f32[2,8,32,128]{3,2,1,0:T(8,128)...) custom-call(f32[2]{0:T(128)} %diff_ref.13, f32[4,2,4,16,128]{4,3,2,1,0:T(8,128)} %get-tuple-element.59.cown_ref, ...), custom_call_target="tpu_custom_call" | custom-call | tf_op jit(solution)/shard_map/pallas_call | solution.py:427
  55.7 0.8 collective-permute-start.10
  56.4 4.0 %collective-permute-start.11 = (f32[2,10,32,128]{3,2,1,0:T(8,128)}, f32[2,10,32,128]{3,2,1,0:T(8,128)S(1)}, u32[]{:S(2)}, u32[]{:S(2)}) collective-permute-start(f32[2,10,32,128]{3,2,1,0:T(8,128)} %get-tuple-element.74), channel_id=1, source_target_pairs={{1,0},{2,1},{3,2},{4,3},{5,4},{6,5},{7,6},{0,7},{9,8},{10,9},{11,1... | collective-permute-start | bytes 983048 | tf_op jit(solution)/shard_map/ppermute | solution.py:604
  60.4 1.9 %collective-permute-start.7 = (f32[2,8,32,128]{3,2,1,0:T(8,128)}, f32[2,8,32,128]{3,2,1,0:T(8,128)S(1)}, u32[]{:S(2)}, u32[]{:S(2)}) collective-permute-start(f32[2,8,32,128]{3,2,1,0:T(8,128)} %get-tuple-element.69), channel_id=1, source_target_pairs={{0,8},{1,9},{2,10},{3,11},{4,12},{5,13},{6,14},{7,15},{8,16},{9,17... | collective-permute-start | bytes 786440 | tf_op jit(solution)/shard_map/ppermute | solution.py:110
  62.4 1.9 %collective-permute-start.8 = (f32[2,5,32,128]{3,2,1,0:T(8,128)}, f32[2,5,32,128]{3,2,1,0:T(8,128)S(1)}, u32[]{:S(2)}, u32[]{:S(2)}) collective-permute-start(f32[2,5,32,128]{3,2,1,0:T(8,128)} %get-tuple-element.70), channel_id=1, source_target_pairs={{0,9},{1,10},{2,11},{3,12},{4,13},{5,14},{6,15},{7,8},{8,17},{9,18... | collective-permute-start | bytes 491528 | tf_op jit(solution)/shard_map/ppermute | solution.py:110
  64.3 1.9 %collective-permute-start.9 = (f32[2,5,32,128]{3,2,1,0:T(8,128)}, f32[2,5,32,128]{3,2,1,0:T(8,128)S(1)}, u32[]{:S(2)}, u32[]{:S(2)}) collective-permute-start(f32[2,5,32,128]{3,2,1,0:T(8,128)} %get-tuple-element.71), channel_id=1, source_target_pairs={{0,15},{1,8},{2,9},{3,10},{4,11},{5,12},{6,13},{7,14},{8,23},{9,16... | collective-permute-start | bytes 491528 | tf_op jit(solution)/shard_map/ppermute | solution.py:110
  66.2 10.3 %collective-permute-done.8.bbefore_ref = f32[2,5,32,128]{3,2,1,0:T(8,128)S(1)} collective-permute-done((f32[2,5,32,128]{3,2,1,0:T(8,128)}, f32[2,5,32,128]{3,2,1,0:T(8,128)S(1)}, u32[]{:S(2)}, u32[]{:S(2)}) %collective-permute-start.8) | collective-permute-done | bytes 163872 | tf_op jit(solution)/shard_map/ppermute | solution.py:110
  76.6 2.2 %collective-permute-done.11.after_ref = f32[2,10,32,128]{3,2,1,0:T(8,128)S(1)} collective-permute-done((f32[2,10,32,128]{3,2,1,0:T(8,128)}, f32[2,10,32,128]{3,2,1,0:T(8,128)S(1)}, u32[]{:S(2)}, u32[]{:S(2)}) %collective-permute-start.11) | collective-permute-done | bytes 327712 | tf_op jit(solution)/shard_map/ppermute | solution.py:604
  78.8 0.7 copy-done.6
  79.5 4.9 %shard_map.49 = (f32[2,10,32,128]{3,2,1,0:T(8,128)}, f32[2,10,32,128]{3,2,1,0:T(8,128)}, f32[2,10,32,128]{3,2,1,0:T(8,128)}, f32[2,10,32,128]{3,2,1,0:T(8,128)},...) custom-call(f32[2]{0:T(128)} %diff_ref.13, ...), custom_call_target="tpu_custom_call" | custom-call | tf_op jit(solution)/shard_map/pallas_call | solution.py:298
  84.3 1.7 %collective-permute-start.12 = (f32[2,6,16,128]{3,2,1,0:T(8,128)}, f32[2,6,16,128]{3,2,1,0:T(8,128)S(1)}, u32[]{:S(2)}, u32[]{:S(2)}) collective-permute-start(f32[2,6,16,128]{3,2,1,0:T(8,128)} %get-tuple-element.76), channel_id=1, source_target_pairs={{0,1},{1,2},{2,3},{3,4},{4,5},{5,6},{6,7},{7,0},{8,9},{9,10},{10,1... | collective-permute-start | bytes 294920 | tf_op jit(solution)/shard_map/ppermute | solution.py:579
  86.0 3.1 %collective-permute-start.13 = (f32[2,6,16,128]{3,2,1,0:T(8,128)}, f32[2,6,16,128]{3,2,1,0:T(8,128)S(1)}, u32[]{:S(2)}, u32[]{:S(2)}) collective-permute-start(f32[2,6,16,128]{3,2,1,0:T(8,128)} %get-tuple-element.77), channel_id=1, source_target_pairs={{1,0},{2,1},{3,2},{4,3},{5,4},{6,5},{7,6},{0,7},{9,8},{10,9},{11,1... | collective-permute-start | bytes 294920 | tf_op jit(solution)/shard_map/ppermute | solution.py:580
  89.1 3.1 %collective-permute-done.12.cbefore_ref = f32[2,6,16,128]{3,2,1,0:T(8,128)S(1)} collective-permute-done((f32[2,6,16,128]{3,2,1,0:T(8,128)}, f32[2,6,16,128]{3,2,1,0:T(8,128)S(1)}, u32[]{:S(2)}, u32[]{:S(2)}) %collective-permute-start.12) | collective-permute-done | bytes 98336 | tf_op jit(solution)/shard_map/ppermute | solution.py:579
  92.2 1.7 %collective-permute-done.13.cafter_ref = f32[2,6,16,128]{3,2,1,0:T(8,128)S(1)} collective-permute-done((f32[2,6,16,128]{3,2,1,0:T(8,128)}, f32[2,6,16,128]{3,2,1,0:T(8,128)S(1)}, u32[]{:S(2)}, u32[]{:S(2)}) %collective-permute-start.13) | collective-permute-done | bytes 98336 | tf_op jit(solution)/shard_map/ppermute | solution.py:580
  93.9 0.6 copy-done.19
  94.5 4.6 %shard_map.50 = (f32[4,2,8,32,128]{4,3,2,1,0:T(8,128)}, f32[2,10,32,128]{3,2,1,0:T(8,128)}, f32[2,10,32,128]{3,2,1,0:T(8,128)}, f32[2,8,32,128]{3,2,1,0:T(8,128)...) custom-call(f32[2]{0:T(128)} %diff_ref.13, f32[4,2,4,16,128]{4,3,2,1,0:T(8,128)} %get-tuple-element.75.cown_ref, ...), custom_call_target="tpu_custom_call" | custom-call | tf_op jit(solution)/shard_map/pallas_call | solution.py:427
  99.2 4.7 %collective-permute-start.18 = (f32[2,10,32,128]{3,2,1,0:T(8,128)}, f32[2,10,32,128]{3,2,1,0:T(8,128)S(1)}, u32[]{:S(2)}, u32[]{:S(2)}) collective-permute-start(f32[2,10,32,128]{3,2,1,0:T(8,128)} %get-tuple-element.89), channel_id=1, source_target_pairs={{1,0},{2,1},{3,2},{4,3},{5,4},{6,5},{7,6},{0,7},{9,8},{10,9},{11,1... | collective-permute-start | bytes 983048 | tf_op jit(solution)/shard_map/ppermute | solution.py:604
  103.9 1.9 %collective-permute-start.14 = (f32[2,8,32,128]{3,2,1,0:T(8,128)}, f32[2,8,32,128]{3,2,1,0:T(8,128)S(1)}, u32[]{:S(2)}, u32[]{:S(2)}) collective-permute-start(f32[2,8,32,128]{3,2,1,0:T(8,128)} %get-tuple-element.84), channel_id=1, source_target_pairs={{0,8},{1,9},{2,10},{3,11},{4,12},{5,13},{6,14},{7,15},{8,16},{9,17... | collective-permute-start | bytes 786440 | tf_op jit(solution)/shard_map/ppermute | solution.py:110
  105.8 1.9 %collective-permute-start.15 = (f32[2,5,32,128]{3,2,1,0:T(8,128)}, f32[2,5,32,128]{3,2,1,0:T(8,128)S(1)}, u32[]{:S(2)}, u32[]{:S(2)}) collective-permute-start(f32[2,5,32,128]{3,2,1,0:T(8,128)} %get-tuple-element.85), channel_id=1, source_target_pairs={{0,9},{1,10},{2,11},{3,12},{4,13},{5,14},{6,15},{7,8},{8,17},{9,18... | collective-permute-start | bytes 491528 | tf_op jit(solution)/shard_map/ppermute | solution.py:110
  107.7 1.9 %collective-permute-start.16 = (f32[2,5,32,128]{3,2,1,0:T(8,128)}, f32[2,5,32,128]{3,2,1,0:T(8,128)S(1)}, u32[]{:S(2)}, u32[]{:S(2)}) collective-permute-start(f32[2,5,32,128]{3,2,1,0:T(8,128)} %get-tuple-element.86), channel_id=1, source_target_pairs={{0,15},{1,8},{2,9},{3,10},{4,11},{5,12},{6,13},{7,14},{8,23},{9,16... | collective-permute-start | bytes 491528 | tf_op jit(solution)/shard_map/ppermute | solution.py:110
  109.6 11.4 %collective-permute-done.15.bbefore_ref = f32[2,5,32,128]{3,2,1,0:T(8,128)S(1)} collective-permute-done((f32[2,5,32,128]{3,2,1,0:T(8,128)}, f32[2,5,32,128]{3,2,1,0:T(8,128)S(1)}, u32[]{:S(2)}, u32[]{:S(2)}) %collective-permute-start.15) | collective-permute-done | bytes 163872 | tf_op jit(solution)/shard_map/ppermute | solution.py:110
  121.1 0.5 collective-permute-done.18.after_ref
  121.6 0.1 copy-done.12
  121.8 0.1 copy-done.3
  122.0 0.3 copy-done.5
  122.3 4.9 %shard_map.51 = (f32[2,10,32,128]{3,2,1,0:T(8,128)}, f32[2,10,32,128]{3,2,1,0:T(8,128)}, f32[2,10,32,128]{3,2,1,0:T(8,128)}, f32[2,10,32,128]{3,2,1,0:T(8,128)},...) custom-call(f32[2]{0:T(128)} %diff_ref.13, ...), custom_call_target="tpu_custom_call" | custom-call | tf_op jit(solution)/shard_map/pallas_call | solution.py:298
  127.2 1.7 %collective-permute-start.19 = (f32[2,2,16,128]{3,2,1,0:T(8,128)}, f32[2,2,16,128]{3,2,1,0:T(8,128)S(1)}, u32[]{:S(2)}, u32[]{:S(2)}) collective-permute-start(f32[2,2,16,128]{3,2,1,0:T(8,128)} %get-tuple-element.91), channel_id=1, source_target_pairs={{0,1},{1,2},{2,3},{3,4},{4,5},{5,6},{6,7},{7,0},{8,9},{9,10},{10,1... | collective-permute-start | bytes 98312 | tf_op jit(solution)/shard_map/ppermute | solution.py:579
  128.9 3.1 %collective-permute-start.20 = (f32[2,2,16,128]{3,2,1,0:T(8,128)}, f32[2,2,16,128]{3,2,1,0:T(8,128)S(1)}, u32[]{:S(2)}, u32[]{:S(2)}) collective-permute-start(f32[2,2,16,128]{3,2,1,0:T(8,128)} %get-tuple-element.92), channel_id=1, source_target_pairs={{1,0},{2,1},{3,2},{4,3},{5,4},{6,5},{7,6},{0,7},{9,8},{10,9},{11,1... | collective-permute-start | bytes 98312 | tf_op jit(solution)/shard_map/ppermute | solution.py:580
  131.9 2.1 %collective-permute-done.19.cbefore_ref = f32[2,2,16,128]{3,2,1,0:T(8,128)S(1)} collective-permute-done((f32[2,2,16,128]{3,2,1,0:T(8,128)}, f32[2,2,16,128]{3,2,1,0:T(8,128)S(1)}, u32[]{:S(2)}, u32[]{:S(2)}) %collective-permute-start.19) | collective-permute-done | bytes 32800 | tf_op jit(solution)/shard_map/ppermute | solution.py:579
  134.0 0.6 copy-done.20
  134.7 2.9 %shard_map.52 = f32[2,8,32,128]{3,2,1,0:T(8,128)} custom-call(f32[2]{0:T(128)} %diff_ref.13, f32[4,2,4,16,128]{4,3,2,1,0:T(8,128)} %get-tuple-element.90.cown_ref, f32[2,2,16,128]{3,2,1,0:T(8,128)} %copy-done.20, f32[2,2,16,128]{3,2,1,0:T(8,128)} %copy-done.21, f32[2,8,16,128]{3,2,1,0:T(8,128)} %get-tuple-element.58.rate_ref, ...), custom_call_target="tpu_custom_call" | custom-call | tf_op jit(solution)/shard_map/pallas_call | solution.py:427
  (49 shorter events, 0.7 us)
Async XLA Ops:
  0.0 6.2 %copy-start = (f32[1,2,8,32,128]{4,3,2,1,0:T(8,128)S(1)}, f32[1,2,8,32,128]{4,3,2,1,0:T(8,128)}, u32[]{:S(2)}) copy-start(f32[1,2,8,32,128]{4,3,2,1,0:T(8,128)} %param.4) | copy-start | bytes 786436
  0.0 31.4 %copy-start.1 = (f32[2,8,32,128]{3,2,1,0:T(8,128)S(1)}, f32[2,8,32,128]{3,2,1,0:T(8,128)}, u32[]{:S(2)}) copy-start(f32[2,8,32,128]{3,2,1,0:T(8,128)} %param.6) | copy-start | bytes 786436
  0.0 31.4 %copy-start.2 = (f32[2,8,32,128]{3,2,1,0:T(8,128)S(1)}, f32[2,8,32,128]{3,2,1,0:T(8,128)}, u32[]{:S(2)}) copy-start(f32[2,8,32,128]{3,2,1,0:T(8,128)} %param.5) | copy-start | bytes 786436
  1.4 27.9 %collective-permute-start = (f32[3,2,5,32,128]{4,3,2,1,0:T(8,128)S(1)}, f32[3,2,5,32,128]{4,3,2,1,0:T(8,128)S(1)}, u32[]{:S(2)}, u32[]{:S(2)}) collective-permute-start(f32[3,2,5,32,128]{4,3,2,1,0:T(8,128)S(1)} %get-tuple-element.99), channel_id=1, source_target_pairs={{0,1},{1,2},{2,3},{3,4},{4,5},{5,6},{6,7},{7,0},{8,9},{9,10},{10,1... | collective-permute-start | bytes 1474568 | tf_op jit(solution)/shard_map/ppermute | solution.py:94
  3.0 28.5 %collective-permute-start.1 = (f32[3,2,5,32,128]{4,3,2,1,0:T(8,128)S(1)}, f32[3,2,5,32,128]{4,3,2,1,0:T(8,128)S(1)}, u32[]{:S(2)}, u32[]{:S(2)}) collective-permute-start(f32[3,2,5,32,128]{4,3,2,1,0:T(8,128)S(1)} %get-tuple-element.100), channel_id=1, source_target_pairs={{1,0},{2,1},{3,2},{4,3},{5,4},{6,5},{7,6},{0,7},{9,8},{10,9},{11,1... | collective-permute-start | bytes 1474568 | tf_op jit(solution)/shard_map/ppermute | solution.py:95
  6.2 31.0 %collective-permute-start.2 = (f32[2,8,32,128]{3,2,1,0:T(8,128)S(1)}, f32[2,8,32,128]{3,2,1,0:T(8,128)S(1)}, u32[]{:S(2)}, u32[]{:S(2)}) collective-permute-start(f32[2,8,32,128]{3,2,1,0:T(8,128)S(1)} %bitcast.5), channel_id=1, source_target_pairs={{0,8},{1,9},{2,10},{3,11},{4,12},{5,13},{6,14},{7,15},{8,16},{9,17... | collective-permute-start | bytes 786440 | tf_op jit(solution)/shard_map/ppermute | solution.py:110
  8.8 28.3 %collective-permute-start.4 = (f32[2,5,32,128]{3,2,1,0:T(8,128)}, f32[2,5,32,128]{3,2,1,0:T(8,128)S(1)}, u32[]{:S(2)}, u32[]{:S(2)}) collective-permute-start(f32[2,5,32,128]{3,2,1,0:T(8,128)} %get-tuple-element.101), channel_id=1, source_target_pairs={{0,15},{1,8},{2,9},{3,10},{4,11},{5,12},{6,13},{7,14},{8,23},{9,16... | collective-permute-start | bytes 491528 | tf_op jit(solution)/shard_map/ppermute | solution.py:110
  10.8 26.3 %collective-permute-start.3 = (f32[2,5,32,128]{3,2,1,0:T(8,128)S(1)}, f32[2,5,32,128]{3,2,1,0:T(8,128)S(1)}, u32[]{:S(2)}, u32[]{:S(2)}) collective-permute-start(f32[2,5,32,128]{3,2,1,0:T(8,128)S(1)} %get-tuple-element.102), channel_id=1, source_target_pairs={{0,9},{1,10},{2,11},{3,12},{4,13},{5,14},{6,15},{7,8},{8,17},{9,18... | collective-permute-start | bytes 491528 | tf_op jit(solution)/shard_map/ppermute | solution.py:110
  37.1 0.7 copy-start.10
  37.1 0.7 copy-start.11
  37.1 0.8 copy-start.7
  42.7 7.6 %collective-permute-start.5 = (f32[2,6,16,128]{3,2,1,0:T(8,128)}, f32[2,6,16,128]{3,2,1,0:T(8,128)S(1)}, u32[]{:S(2)}, u32[]{:S(2)}) collective-permute-start(f32[2,6,16,128]{3,2,1,0:T(8,128)} %get-tuple-element.60), channel_id=1, source_target_pairs={{0,1},{1,2},{2,3},{3,4},{4,5},{5,6},{6,7},{7,0},{8,9},{9,10},{10,1... | collective-permute-start | bytes 294920 | tf_op jit(solution)/shard_map/ppermute | solution.py:579
  43.0 7.4 %collective-permute-start.6 = (f32[2,6,16,128]{3,2,1,0:T(8,128)}, f32[2,6,16,128]{3,2,1,0:T(8,128)S(1)}, u32[]{:S(2)}, u32[]{:S(2)}) collective-permute-start(f32[2,6,16,128]{3,2,1,0:T(8,128)} %get-tuple-element.61), channel_id=1, source_target_pairs={{1,0},{2,1},{3,2},{4,3},{5,4},{6,5},{7,6},{0,7},{9,8},{10,9},{11,1... | collective-permute-start | bytes 294920 | tf_op jit(solution)/shard_map/ppermute | solution.py:580
  50.4 0.6 copy-start.16
  50.5 0.6 copy-start.18
  55.7 20.9 %collective-permute-start.10 = (f32[2,10,32,128]{3,2,1,0:T(8,128)}, f32[2,10,32,128]{3,2,1,0:T(8,128)S(1)}, u32[]{:S(2)}, u32[]{:S(2)}) collective-permute-start(f32[2,10,32,128]{3,2,1,0:T(8,128)} %get-tuple-element.73), channel_id=1, source_target_pairs={{0,1},{1,2},{2,3},{3,4},{4,5},{5,6},{6,7},{7,0},{8,9},{9,10},{10,1... | collective-permute-start | bytes 983048 | tf_op jit(solution)/shard_map/ppermute | solution.py:603
  56.4 22.3 %collective-permute-start.11 = (f32[2,10,32,128]{3,2,1,0:T(8,128)}, f32[2,10,32,128]{3,2,1,0:T(8,128)S(1)}, u32[]{:S(2)}, u32[]{:S(2)}) collective-permute-start(f32[2,10,32,128]{3,2,1,0:T(8,128)} %get-tuple-element.74), channel_id=1, source_target_pairs={{1,0},{2,1},{3,2},{4,3},{5,4},{6,5},{7,6},{0,7},{9,8},{10,9},{11,1... | collective-permute-start | bytes 983048 | tf_op jit(solution)/shard_map/ppermute | solution.py:604
  60.4 16.1 %collective-permute-start.7 = (f32[2,8,32,128]{3,2,1,0:T(8,128)}, f32[2,8,32,128]{3,2,1,0:T(8,128)S(1)}, u32[]{:S(2)}, u32[]{:S(2)}) collective-permute-start(f32[2,8,32,128]{3,2,1,0:T(8,128)} %get-tuple-element.69), channel_id=1, source_target_pairs={{0,8},{1,9},{2,10},{3,11},{4,12},{5,13},{6,14},{7,15},{8,16},{9,17... | collective-permute-start | bytes 786440 | tf_op jit(solution)/shard_map/ppermute | solution.py:110
  62.4 14.2 %collective-permute-start.8 = (f32[2,5,32,128]{3,2,1,0:T(8,128)}, f32[2,5,32,128]{3,2,1,0:T(8,128)S(1)}, u32[]{:S(2)}, u32[]{:S(2)}) collective-permute-start(f32[2,5,32,128]{3,2,1,0:T(8,128)} %get-tuple-element.70), channel_id=1, source_target_pairs={{0,9},{1,10},{2,11},{3,12},{4,13},{5,14},{6,15},{7,8},{8,17},{9,18... | collective-permute-start | bytes 491528 | tf_op jit(solution)/shard_map/ppermute | solution.py:110
  64.3 12.2 %collective-permute-start.9 = (f32[2,5,32,128]{3,2,1,0:T(8,128)}, f32[2,5,32,128]{3,2,1,0:T(8,128)S(1)}, u32[]{:S(2)}, u32[]{:S(2)}) collective-permute-start(f32[2,5,32,128]{3,2,1,0:T(8,128)} %get-tuple-element.71), channel_id=1, source_target_pairs={{0,15},{1,8},{2,9},{3,10},{4,11},{5,12},{6,13},{7,14},{8,23},{9,16... | collective-permute-start | bytes 491528 | tf_op jit(solution)/shard_map/ppermute | solution.py:110
  76.5 2.2 %copy-start.13 = (f32[2,5,32,128]{3,2,1,0:T(8,128)}, f32[2,5,32,128]{3,2,1,0:T(8,128)S(1)}, u32[]{:S(2)}) copy-start(f32[2,5,32,128]{3,2,1,0:T(8,128)S(1)} %collective-permute-done.8.bbefore_ref) | copy-start | bytes 491524
  76.5 2.2 %copy-start.15 = (f32[2,5,32,128]{3,2,1,0:T(8,128)}, f32[2,5,32,128]{3,2,1,0:T(8,128)S(1)}, u32[]{:S(2)}) copy-start(f32[2,5,32,128]{3,2,1,0:T(8,128)S(1)} %collective-permute-done.9.bafter_ref) | copy-start | bytes 491524
  76.5 2.2 %copy-start.9 = (f32[2,8,32,128]{3,2,1,0:T(8,128)}, f32[2,8,32,128]{3,2,1,0:T(8,128)S(1)}, u32[]{:S(2)}) copy-start(f32[2,8,32,128]{3,2,1,0:T(8,128)S(1)} %collective-permute-done.7.centre_ref) | copy-start | bytes 786436
  76.5 2.2 %copy-start.4 = (f32[2,10,32,128]{3,2,1,0:T(8,128)}, f32[2,10,32,128]{3,2,1,0:T(8,128)S(1)}, u32[]{:S(2)}) copy-start(f32[2,10,32,128]{3,2,1,0:T(8,128)S(1)} %collective-permute-done.10.before_ref) | copy-start | bytes 983044
  78.7 0.7 copy-start.6
  84.3 7.8 %collective-permute-start.12 = (f32[2,6,16,128]{3,2,1,0:T(8,128)}, f32[2,6,16,128]{3,2,1,0:T(8,128)S(1)}, u32[]{:S(2)}, u32[]{:S(2)}) collective-permute-start(f32[2,6,16,128]{3,2,1,0:T(8,128)} %get-tuple-element.76), channel_id=1, source_target_pairs={{0,1},{1,2},{2,3},{3,4},{4,5},{5,6},{6,7},{7,0},{8,9},{9,10},{10,1... | collective-permute-start | bytes 294920 | tf_op jit(solution)/shard_map/ppermute | solution.py:579
  86.0 7.9 %collective-permute-start.13 = (f32[2,6,16,128]{3,2,1,0:T(8,128)}, f32[2,6,16,128]{3,2,1,0:T(8,128)S(1)}, u32[]{:S(2)}, u32[]{:S(2)}) collective-permute-start(f32[2,6,16,128]{3,2,1,0:T(8,128)} %get-tuple-element.77), channel_id=1, source_target_pairs={{1,0},{2,1},{3,2},{4,3},{5,4},{6,5},{7,6},{0,7},{9,8},{10,9},{11,1... | collective-permute-start | bytes 294920 | tf_op jit(solution)/shard_map/ppermute | solution.py:580
  92.2 1.7 %copy-start.17 = (f32[2,6,16,128]{3,2,1,0:T(8,128)}, f32[2,6,16,128]{3,2,1,0:T(8,128)S(1)}, u32[]{:S(2)}) copy-start(f32[2,6,16,128]{3,2,1,0:T(8,128)S(1)} %collective-permute-done.12.cbefore_ref) | copy-start | bytes 294916
  93.9 0.6 copy-start.19
  99.1 22.0 %collective-permute-start.17 = (f32[2,10,32,128]{3,2,1,0:T(8,128)}, f32[2,10,32,128]{3,2,1,0:T(8,128)S(1)}, u32[]{:S(2)}, u32[]{:S(2)}) collective-permute-start(f32[2,10,32,128]{3,2,1,0:T(8,128)} %get-tuple-element.88), channel_id=1, source_target_pairs={{0,1},{1,2},{2,3},{3,4},{4,5},{5,6},{6,7},{7,0},{8,9},{9,10},{10,1... | collective-permute-start | bytes 983048 | tf_op jit(solution)/shard_map/ppermute | solution.py:603
  99.2 22.4 %collective-permute-start.18 = (f32[2,10,32,128]{3,2,1,0:T(8,128)}, f32[2,10,32,128]{3,2,1,0:T(8,128)S(1)}, u32[]{:S(2)}, u32[]{:S(2)}) collective-permute-start(f32[2,10,32,128]{3,2,1,0:T(8,128)} %get-tuple-element.89), channel_id=1, source_target_pairs={{1,0},{2,1},{3,2},{4,3},{5,4},{6,5},{7,6},{0,7},{9,8},{10,9},{11,1... | collective-permute-start | bytes 983048 | tf_op jit(solution)/shard_map/ppermute | solution.py:604
  103.9 17.2 %collective-permute-start.14 = (f32[2,8,32,128]{3,2,1,0:T(8,128)}, f32[2,8,32,128]{3,2,1,0:T(8,128)S(1)}, u32[]{:S(2)}, u32[]{:S(2)}) collective-permute-start(f32[2,8,32,128]{3,2,1,0:T(8,128)} %get-tuple-element.84), channel_id=1, source_target_pairs={{0,8},{1,9},{2,10},{3,11},{4,12},{5,13},{6,14},{7,15},{8,16},{9,17... | collective-permute-start | bytes 786440 | tf_op jit(solution)/shard_map/ppermute | solution.py:110
  105.8 15.3 %collective-permute-start.15 = (f32[2,5,32,128]{3,2,1,0:T(8,128)}, f32[2,5,32,128]{3,2,1,0:T(8,128)S(1)}, u32[]{:S(2)}, u32[]{:S(2)}) collective-permute-start(f32[2,5,32,128]{3,2,1,0:T(8,128)} %get-tuple-element.85), channel_id=1, source_target_pairs={{0,9},{1,10},{2,11},{3,12},{4,13},{5,14},{6,15},{7,8},{8,17},{9,18... | collective-permute-start | bytes 491528 | tf_op jit(solution)/shard_map/ppermute | solution.py:110
  107.7 13.3 %collective-permute-start.16 = (f32[2,5,32,128]{3,2,1,0:T(8,128)}, f32[2,5,32,128]{3,2,1,0:T(8,128)S(1)}, u32[]{:S(2)}, u32[]{:S(2)}) collective-permute-start(f32[2,5,32,128]{3,2,1,0:T(8,128)} %get-tuple-element.86), channel_id=1, source_target_pairs={{0,15},{1,8},{2,9},{3,10},{4,11},{5,12},{6,13},{7,14},{8,23},{9,16... | collective-permute-start | bytes 491528 | tf_op jit(solution)/shard_map/ppermute | solution.py:110
  121.0 0.7 copy-start.12
  121.0 0.7 copy-start.14
  121.0 0.8 copy-start.8
  121.1 0.9 copy-start.3
  121.6 0.7 copy-start.5
  127.2 6.8 %collective-permute-start.19 = (f32[2,2,16,128]{3,2,1,0:T(8,128)}, f32[2,2,16,128]{3,2,1,0:T(8,128)S(1)}, u32[]{:S(2)}, u32[]{:S(2)}) collective-permute-start(f32[2,2,16,128]{3,2,1,0:T(8,128)} %get-tuple-element.91), channel_id=1, source_target_pairs={{0,1},{1,2},{2,3},{3,4},{4,5},{5,6},{6,7},{7,0},{8,9},{9,10},{10,1... | collective-permute-start | bytes 98312 | tf_op jit(solution)/shard_map/ppermute | solution.py:579
  128.9 5.2 %collective-permute-start.20 = (f32[2,2,16,128]{3,2,1,0:T(8,128)}, f32[2,2,16,128]{3,2,1,0:T(8,128)S(1)}, u32[]{:S(2)}, u32[]{:S(2)}) collective-permute-start(f32[2,2,16,128]{3,2,1,0:T(8,128)} %get-tuple-element.92), channel_id=1, source_target_pairs={{1,0},{2,1},{3,2},{4,3},{5,4},{6,5},{7,6},{0,7},{9,8},{10,9},{11,1... | collective-permute-start | bytes 98312 | tf_op jit(solution)/shard_map/ppermute | solution.py:580
  134.0 0.6 copy-start.20
  134.0 0.6 copy-start.21

commit v7 on v6

--- a/solution.py
+++ b/solution.py
@@ -204,7 +204,7 @@
 
 def sweep_kernel(widths_sent, natural_prior, diff_ref, flag_ref, start_ref, centre_ref, bbefore_ref, bafter_ref,
                  own_ref, before_ref, after_ref, dec_ref, src_ref,
-                 rate_ref, n1_ref, n2_ref, n3_ref, n4_ref, e0_ref, b0_ref, cown_ref, clasts_ref,
+                 rate_ref, recip_ref, n1_ref, n2_ref, n3_ref, n4_ref, e0_ref, b0_ref, cown_ref, clasts_ref,
                  cfirsts_ref):
     spread_table, grouped_table, interp_table, widths = node_tables()
     rows = e0_ref.shape[1]
@@ -252,7 +252,8 @@
         found.append(e)
         h = have - 1
         numerator = (cut(swept[m], have, h) + widths[m] * e) + parts[m]
-        swept.append(numerator / (1.0 + widths[m] * at(dec_ref, h)))
+        off = hd - 1 - h
+        swept.append(numerator * recip_ref[m, :, off:off + rows + 2 * h])
     found.append(terms(swept[4], hs - 4))
     dec0 = at(dec_ref, 0)
     fulls = [cut(found[j], hs - 1 - j, 0) - dec0 * cut(swept[j], hs - j, 0) for j in range(5)]
@@ -285,7 +286,7 @@
     b0_ref[...] = cut(swept[0], hs, 0)
 
 
-def fine_sweep(diffusivity, flag, start, prior, parts, decay, src, rate_c, widths_sent,
+def fine_sweep(diffusivity, flag, start, prior, parts, decay, src, rate_c, recip, widths_sent,
                natural_prior):
     rows = start.shape[1] - 2 * START_HALO
     shape = start.shape
@@ -298,9 +299,9 @@
     return pl.pallas_call(
         functools.partial(sweep_kernel, widths_sent, natural_prior),
         out_shape=(wide, wide, wide, wide, own, own, cown, cedge, cedge),
-        in_specs=[pl.BlockSpec(memory_space=pltpu.SMEM)] * 2 + [vmem] * 10,
+        in_specs=[pl.BlockSpec(memory_space=pltpu.SMEM)] * 2 + [vmem] * 11,
         out_specs=(vmem,) * 9,
-    )(diffusivity, flag, start, *prior, *parts, decay, src, rate_c)
+    )(diffusivity, flag, start, *prior, *parts, decay, src, rate_c, recip)
 
 
 def coarse_kernel_laplace(f):
@@ -433,7 +434,7 @@
 
 
 def start_kernel(diff_ref, stacked_ref, own_ref, before_ref, after_ref, rate_ref, csrc_ref,
-                 ext_ref, dec_ref, src_ref):
+                 ext_ref, dec_ref, src_ref, recip_ref):
     spread_table, grouped_table, interp_table, widths = node_tables()
     rows = own_ref.shape[2]
     hs = (stacked_ref.shape[2] - rows) // 2
@@ -466,6 +467,8 @@
         offset += w
     rate_ref[...] = kernel_restrict(dec)
     csrc_ref[...] = kernel_restrict(s)
+    for m in range(4):
+        recip_ref[m] = 1.0 / (1.0 + widths[m] * dec)
 
 
 def start_terms(diffusivity, stacked):
@@ -484,9 +487,10 @@
             jax.ShapeDtypeStruct(shape, jnp.float32),
             jax.ShapeDtypeStruct(shape, jnp.float32),
             jax.ShapeDtypeStruct(shape, jnp.float32),
+            jax.ShapeDtypeStruct((4, shape[0], shape[1] - 2) + shape[2:], jnp.float32),
         ),
         in_specs=[pl.BlockSpec(memory_space=pltpu.SMEM)] + [vmem],
-        out_specs=(vmem,) * 8,
+        out_specs=(vmem,) * 9,
     )(diffusivity, stacked)
 
 
@@ -530,7 +534,7 @@
 
     own_start = initial[0]
     stacked = space_halo(jnp.stack([own_start, decay_rate, source]), hs)
-    own4, before4, after4, rate_own, csrc_own, own_ext, dec_ext, src_ext = start_terms(
+    own4, before4, after4, rate_own, csrc_own, own_ext, dec_ext, src_ext, recip = start_terms(
         diffusivity, stacked
     )
     decay = (dec_ext, hs)
@@ -571,8 +575,8 @@
     def advance(prior, pieces, last, natural):
         widths_sent = (1, 1, 0, 0) if last else (2, 2, 1, 1)
         n1, n2, n3, n4, e0, b0, cown, clasts, cfirsts = fine_sweep(
-            diffusivity, flag, own_ext, prior, pieces, decay[0], src[0], rate_c[0], widths_sent,
-            natural,
+            diffusivity, flag, own_ext, prior, pieces, decay[0], src[0], rate_c[0], recip,
+            widths_sent, natural,
         )
         coarse = (
             cown,

time: 139 us -> 141 us (1.014)
  Pallas kernels: 30.8 us -> 33.3 us
    pallas_call x3, Pallas kernels: 14.6 us -> 16.4 us  [fine_sweep(): pl.pallas_call(functools.partial(sweep_kernel, widths_sent, natural_prior...]
    unnamed x44 -> x42, local copies, waits for them, and re-layouts: 4.15 us -> 4.16 us
  transfers between devices with their start and end apart: 21 -> 21, of which waited for: 11 -> 11; matrix products, arithmetic and copies ran while one was open for 2% -> 1% of each run, Pallas kernels for 3% -> 3%
where the time goes in v7:
time: 141 us; the launch traced here: 140 us
  waiting for transfers between devices  53.7 us (38%)
  starting transfers between devices  45.8 us (32%)
  Pallas kernels  33.3 us (24%)
  local copies, waits for them, and re-layouts  4.29 us (3%)
  other arithmetic  2.72 us (2%)
    ppermute x9, waiting for transfers between devices, moved(): return lax.ppermute(piece, axes, pairs)  21.7 us
    ppermute x9, starting transfers between devices, moved(): return lax.ppermute(piece, axes, pairs)  17.3 us
    ppermute x1, waiting for transfers between devices, space_halo(): lax.ppermute(lax.slice_in_dim(a, rows - h, rows, axis=a.ndim - 3), 'space...  17.2 us
    pallas_call x3, Pallas kernels, fine_sweep(): pl.pallas_call(functools.partial(sweep_kernel, widths_sent, natural_prior...  16.4 us
    pallas_call x3, Pallas kernels, finish_round(): pl.pallas_call(functools.partial(finish_kernel, widths_sent), out_shape=o...  12.1 us
    ppermute x3, starting transfers between devices, advance(): lax.ppermute(cfirsts, 'space', down)  10.6 us
    ppermute x2, starting transfers between devices, per_device(): lax.ppermute(firsts, 'space', down)  8.72 us
    ppermute x3, waiting for transfers between devices, advance(): lax.ppermute(clasts, 'space', up)  8.13 us
  transfers between devices with their start and end apart: 21, of which 11 were waited for; matrix products, arithmetic and copies ran while one was open for 1% of the time, Pallas kernels for 3%

profile of v7, /device:TPU:2, one launch (start us, length us, event | category | flops | bytes accessed | tf_op | source)
XLA Modules:
  0.0 140.1 jit_solution(10937528274542268759)
XLA Ops:
  0.0 1.3 pad_maximum_fusion.1
  1.3 0.1 fusion
  1.4 1.6 %collective-permute-start = (f32[3,2,5,32,128]{4,3,2,1,0:T(8,128)S(1)}, f32[3,2,5,32,128]{4,3,2,1,0:T(8,128)S(1)}, u32[]{:S(2)}, u32[]{:S(2)}) collective-permute-start(f32[3,2,5,32,128]{4,3,2,1,0:T(8,128)S(1)} %get-tuple-element.101), channel_id=1, source_target_pairs={{0,1},{1,2},{2,3},{3,4},{4,5},{5,6},{6,7},{7,0},{8,9},{9,10},{10,1... | collective-permute-start | bytes 1474568 | tf_op jit(solution)/shard_map/ppermute | solution.py:94
  3.0 3.2 %collective-permute-start.1 = (f32[3,2,5,32,128]{4,3,2,1,0:T(8,128)S(1)}, f32[3,2,5,32,128]{4,3,2,1,0:T(8,128)S(1)}, u32[]{:S(2)}, u32[]{:S(2)}) collective-permute-start(f32[3,2,5,32,128]{4,3,2,1,0:T(8,128)S(1)} %get-tuple-element.102), channel_id=1, source_target_pairs={{1,0},{2,1},{3,2},{4,3},{5,4},{6,5},{7,6},{0,7},{9,8},{10,9},{11,1... | collective-permute-start | bytes 1474568 | tf_op jit(solution)/shard_map/ppermute | solution.py:95
  6.2 1.9 %collective-permute-start.2 = (f32[2,8,32,128]{3,2,1,0:T(8,128)S(1)}, f32[2,8,32,128]{3,2,1,0:T(8,128)S(1)}, u32[]{:S(2)}, u32[]{:S(2)}) collective-permute-start(f32[2,8,32,128]{3,2,1,0:T(8,128)S(1)} %bitcast.5), channel_id=1, source_target_pairs={{0,8},{1,9},{2,10},{3,11},{4,12},{5,13},{6,14},{7,15},{8,16},{9,17... | collective-permute-start | bytes 786440 | tf_op jit(solution)/shard_map/ppermute | solution.py:110
  8.1 2.0 %collective-permute-start.4 = (f32[2,5,32,128]{3,2,1,0:T(8,128)S(1)}, f32[2,5,32,128]{3,2,1,0:T(8,128)S(1)}, u32[]{:S(2)}, u32[]{:S(2)}) collective-permute-start(f32[2,5,32,128]{3,2,1,0:T(8,128)S(1)} %get-tuple-element.103), channel_id=1, source_target_pairs={{0,15},{1,8},{2,9},{3,10},{4,11},{5,12},{6,13},{7,14},{8,23},{9,16... | collective-permute-start | bytes 491528 | tf_op jit(solution)/shard_map/ppermute | solution.py:110
  10.1 1.9 %collective-permute-start.3 = (f32[2,5,32,128]{3,2,1,0:T(8,128)S(1)}, f32[2,5,32,128]{3,2,1,0:T(8,128)}, u32[]{:S(2)}, u32[]{:S(2)}) collective-permute-start(f32[2,5,32,128]{3,2,1,0:T(8,128)S(1)} %get-tuple-element.104), channel_id=1, source_target_pairs={{0,9},{1,10},{2,11},{3,12},{4,13},{5,14},{6,15},{7,8},{8,17},{9,18... | collective-permute-start | bytes 491528 | tf_op jit(solution)/shard_map/ppermute | solution.py:110
  12.1 17.2 %collective-permute-done = f32[3,2,5,32,128]{4,3,2,1,0:T(8,128)S(1)} collective-permute-done((f32[3,2,5,32,128]{4,3,2,1,0:T(8,128)S(1)}, f32[3,2,5,32,128]{4,3,2,1,0:T(8,128)S(1)}, u32[]{:S(2)}, u32[]{:S(2)}) %collective-permute-start) | collective-permute-done | bytes 491552 | tf_op jit(solution)/shard_map/ppermute | solution.py:94
  29.2 2.2 %collective-permute-done.1 = f32[3,2,5,32,128]{4,3,2,1,0:T(8,128)S(1)} collective-permute-done((f32[3,2,5,32,128]{4,3,2,1,0:T(8,128)S(1)}, f32[3,2,5,32,128]{4,3,2,1,0:T(8,128)S(1)}, u32[]{:S(2)}, u32[]{:S(2)}) %collective-permute-start.1) | collective-permute-done | bytes 491552 | tf_op jit(solution)/shard_map/ppermute | solution.py:95
  31.4 1.5 %pad_maximum_fusion.stacked_ref = f32[3,2,18,32,128]{4,3,2,1,0:T(8,128)} fusion(f32[3,2,5,32,128]{4,3,2,1,0:T(8,128)S(1)} %collective-permute-done.1, f32[1,2,8,32,128]{4,3,2,1,0:T(8,128)S(1)} %bitcast.8, f32[1,2,8,32,128]{4,3,2,1,0:T(8,128)S(1)} %bitcast.10, f32[1,2,8,32,128]{4,3,2,1,0:T(8,128)S(1)} %copy-done, f32[3,2,5,32,128]{4,3,2,1,0:T(8,128)S(1)} %collective-permute-done), kind=kLoop, calls=%fused_computation | loop fusion | flops 1769472 | bytes 3538944 | tf_op jit(solution)/shard_map/concatenate | solution.py:96
  32.9 4.8 %shard_map.46 = (f32[4,2,8,32,128]{4,3,2,1,0:T(8,128)}, f32[2,10,32,128]{3,2,1,0:T(8,128)}, f32[2,10,32,128]{3,2,1,0:T(8,128)}, f32[2,8,16,128]{3,2,1,0:T(8,128)...) custom-call(f32[2]{0:T(128)} %diff_ref.13, ...), custom_call_target="tpu_custom_call" | custom-call | tf_op jit(solution)/shard_map/pallas_call | solution.py:482
  37.8 0.6 copy-done.10
  38.5 5.5 %shard_map.47 = (f32[2,10,32,128]{3,2,1,0:T(8,128)}, f32[2,10,32,128]{3,2,1,0:T(8,128)}, f32[2,10,32,128]{3,2,1,0:T(8,128)}, f32[2,10,32,128]{3,2,1,0:T(8,128)},...) custom-call(f32[2]{0:T(128)} %diff_ref.13, ...), custom_call_target="tpu_custom_call" | custom-call | tf_op jit(solution)/shard_map/pallas_call | solution.py:299
  44.0 0.3 collective-permute-start.5
  44.3 4.4 %collective-permute-start.6 = (f32[2,6,16,128]{3,2,1,0:T(8,128)}, f32[2,6,16,128]{3,2,1,0:T(8,128)S(1)}, u32[]{:S(2)}, u32[]{:S(2)}) collective-permute-start(f32[2,6,16,128]{3,2,1,0:T(8,128)} %get-tuple-element.63), channel_id=1, source_target_pairs={{1,0},{2,1},{3,2},{4,3},{5,4},{6,5},{7,6},{0,7},{9,8},{10,9},{11,1... | collective-permute-start | bytes 294920 | tf_op jit(solution)/shard_map/ppermute | solution.py:584
  48.7 2.9 %collective-permute-done.5.cbefore_ref = f32[2,6,16,128]{3,2,1,0:T(8,128)S(1)} collective-permute-done((f32[2,6,16,128]{3,2,1,0:T(8,128)}, f32[2,6,16,128]{3,2,1,0:T(8,128)S(1)}, u32[]{:S(2)}, u32[]{:S(2)}) %collective-permute-start.5) | collective-permute-done | bytes 98336 | tf_op jit(solution)/shard_map/ppermute | solution.py:583
  51.7 0.6 copy-done.15
  52.3 4.6 %shard_map.48 = (f32[4,2,8,32,128]{4,3,2,1,0:T(8,128)}, f32[2,10,32,128]{3,2,1,0:T(8,128)}, f32[2,10,32,128]{3,2,1,0:T(8,128)}, f32[2,8,32,128]{3,2,1,0:T(8,128)...) custom-call(f32[2]{0:T(128)} %diff_ref.13, f32[4,2,4,16,128]{4,3,2,1,0:T(8,128)} %get-tuple-element.61.cown_ref, ...), custom_call_target="tpu_custom_call" | custom-call | tf_op jit(solution)/shard_map/pallas_call | solution.py:428
  56.9 0.8 collective-permute-start.10
  57.7 4.0 %collective-permute-start.11 = (f32[2,10,32,128]{3,2,1,0:T(8,128)}, f32[2,10,32,128]{3,2,1,0:T(8,128)S(1)}, u32[]{:S(2)}, u32[]{:S(2)}) collective-permute-start(f32[2,10,32,128]{3,2,1,0:T(8,128)} %get-tuple-element.76), channel_id=1, source_target_pairs={{1,0},{2,1},{3,2},{4,3},{5,4},{6,5},{7,6},{0,7},{9,8},{10,9},{11,1... | collective-permute-start | bytes 983048 | tf_op jit(solution)/shard_map/ppermute | solution.py:608
  61.7 1.9 %collective-permute-start.7 = (f32[2,8,32,128]{3,2,1,0:T(8,128)}, f32[2,8,32,128]{3,2,1,0:T(8,128)S(1)}, u32[]{:S(2)}, u32[]{:S(2)}) collective-permute-start(f32[2,8,32,128]{3,2,1,0:T(8,128)} %get-tuple-element.71), channel_id=1, source_target_pairs={{0,8},{1,9},{2,10},{3,11},{4,12},{5,13},{6,14},{7,15},{8,16},{9,17... | collective-permute-start | bytes 786440 | tf_op jit(solution)/shard_map/ppermute | solution.py:110
  63.6 1.9 %collective-permute-start.8 = (f32[2,5,32,128]{3,2,1,0:T(8,128)}, f32[2,5,32,128]{3,2,1,0:T(8,128)S(1)}, u32[]{:S(2)}, u32[]{:S(2)}) collective-permute-start(f32[2,5,32,128]{3,2,1,0:T(8,128)} %get-tuple-element.72), channel_id=1, source_target_pairs={{0,9},{1,10},{2,11},{3,12},{4,13},{5,14},{6,15},{7,8},{8,17},{9,18... | collective-permute-start | bytes 491528 | tf_op jit(solution)/shard_map/ppermute | solution.py:110
  65.5 1.9 %collective-permute-start.9 = (f32[2,5,32,128]{3,2,1,0:T(8,128)}, f32[2,5,32,128]{3,2,1,0:T(8,128)S(1)}, u32[]{:S(2)}, u32[]{:S(2)}) collective-permute-start(f32[2,5,32,128]{3,2,1,0:T(8,128)} %get-tuple-element.73), channel_id=1, source_target_pairs={{0,15},{1,8},{2,9},{3,10},{4,11},{5,12},{6,13},{7,14},{8,23},{9,16... | collective-permute-start | bytes 491528 | tf_op jit(solution)/shard_map/ppermute | solution.py:110
  67.5 10.3 %collective-permute-done.8.bbefore_ref = f32[2,5,32,128]{3,2,1,0:T(8,128)S(1)} collective-permute-done((f32[2,5,32,128]{3,2,1,0:T(8,128)}, f32[2,5,32,128]{3,2,1,0:T(8,128)S(1)}, u32[]{:S(2)}, u32[]{:S(2)}) %collective-permute-start.8) | collective-permute-done | bytes 163872 | tf_op jit(solution)/shard_map/ppermute | solution.py:110
  77.8 2.2 %collective-permute-done.11.after_ref = f32[2,10,32,128]{3,2,1,0:T(8,128)S(1)} collective-permute-done((f32[2,10,32,128]{3,2,1,0:T(8,128)}, f32[2,10,32,128]{3,2,1,0:T(8,128)S(1)}, u32[]{:S(2)}, u32[]{:S(2)}) %collective-permute-start.11) | collective-permute-done | bytes 327712 | tf_op jit(solution)/shard_map/ppermute | solution.py:608
  80.0 0.7 copy-done.6
  80.8 5.5 %shard_map.49 = (f32[2,10,32,128]{3,2,1,0:T(8,128)}, f32[2,10,32,128]{3,2,1,0:T(8,128)}, f32[2,10,32,128]{3,2,1,0:T(8,128)}, f32[2,10,32,128]{3,2,1,0:T(8,128)},...) custom-call(f32[2]{0:T(128)} %diff_ref.13, ...), custom_call_target="tpu_custom_call" | custom-call | tf_op jit(solution)/shard_map/pallas_call | solution.py:299
  86.3 1.7 %collective-permute-start.12 = (f32[2,6,16,128]{3,2,1,0:T(8,128)}, f32[2,6,16,128]{3,2,1,0:T(8,128)S(1)}, u32[]{:S(2)}, u32[]{:S(2)}) collective-permute-start(f32[2,6,16,128]{3,2,1,0:T(8,128)} %get-tuple-element.78), channel_id=1, source_target_pairs={{0,1},{1,2},{2,3},{3,4},{4,5},{5,6},{6,7},{7,0},{8,9},{9,10},{10,1... | collective-permute-start | bytes 294920 | tf_op jit(solution)/shard_map/ppermute | solution.py:583
  87.9 3.1 %collective-permute-start.13 = (f32[2,6,16,128]{3,2,1,0:T(8,128)}, f32[2,6,16,128]{3,2,1,0:T(8,128)S(1)}, u32[]{:S(2)}, u32[]{:S(2)}) collective-permute-start(f32[2,6,16,128]{3,2,1,0:T(8,128)} %get-tuple-element.79), channel_id=1, source_target_pairs={{1,0},{2,1},{3,2},{4,3},{5,4},{6,5},{7,6},{0,7},{9,8},{10,9},{11,1... | collective-permute-start | bytes 294920 | tf_op jit(solution)/shard_map/ppermute | solution.py:584
  91.0 3.1 %collective-permute-done.12.cbefore_ref = f32[2,6,16,128]{3,2,1,0:T(8,128)S(1)} collective-permute-done((f32[2,6,16,128]{3,2,1,0:T(8,128)}, f32[2,6,16,128]{3,2,1,0:T(8,128)S(1)}, u32[]{:S(2)}, u32[]{:S(2)}) %collective-permute-start.12) | collective-permute-done | bytes 98336 | tf_op jit(solution)/shard_map/ppermute | solution.py:583
  94.1 1.7 %collective-permute-done.13.cafter_ref = f32[2,6,16,128]{3,2,1,0:T(8,128)S(1)} collective-permute-done((f32[2,6,16,128]{3,2,1,0:T(8,128)}, f32[2,6,16,128]{3,2,1,0:T(8,128)S(1)}, u32[]{:S(2)}, u32[]{:S(2)}) %collective-permute-start.13) | collective-permute-done | bytes 98336 | tf_op jit(solution)/shard_map/ppermute | solution.py:584
  95.8 0.6 copy-done.18
  96.4 4.6 %shard_map.50 = (f32[4,2,8,32,128]{4,3,2,1,0:T(8,128)}, f32[2,10,32,128]{3,2,1,0:T(8,128)}, f32[2,10,32,128]{3,2,1,0:T(8,128)}, f32[2,8,32,128]{3,2,1,0:T(8,128)...) custom-call(f32[2]{0:T(128)} %diff_ref.13, f32[4,2,4,16,128]{4,3,2,1,0:T(8,128)} %get-tuple-element.77.cown_ref, ...), custom_call_target="tpu_custom_call" | custom-call | tf_op jit(solution)/shard_map/pallas_call | solution.py:428
  101.1 4.7 %collective-permute-start.18 = (f32[2,10,32,128]{3,2,1,0:T(8,128)}, f32[2,10,32,128]{3,2,1,0:T(8,128)S(1)}, u32[]{:S(2)}, u32[]{:S(2)}) collective-permute-start(f32[2,10,32,128]{3,2,1,0:T(8,128)} %get-tuple-element.91), channel_id=1, source_target_pairs={{1,0},{2,1},{3,2},{4,3},{5,4},{6,5},{7,6},{0,7},{9,8},{10,9},{11,1... | collective-permute-start | bytes 983048 | tf_op jit(solution)/shard_map/ppermute | solution.py:608
  105.8 1.9 %collective-permute-start.14 = (f32[2,8,32,128]{3,2,1,0:T(8,128)}, f32[2,8,32,128]{3,2,1,0:T(8,128)S(1)}, u32[]{:S(2)}, u32[]{:S(2)}) collective-permute-start(f32[2,8,32,128]{3,2,1,0:T(8,128)} %get-tuple-element.86), channel_id=1, source_target_pairs={{0,8},{1,9},{2,10},{3,11},{4,12},{5,13},{6,14},{7,15},{8,16},{9,17... | collective-permute-start | bytes 786440 | tf_op jit(solution)/shard_map/ppermute | solution.py:110
  107.8 1.9 %collective-permute-start.15 = (f32[2,5,32,128]{3,2,1,0:T(8,128)}, f32[2,5,32,128]{3,2,1,0:T(8,128)S(1)}, u32[]{:S(2)}, u32[]{:S(2)}) collective-permute-start(f32[2,5,32,128]{3,2,1,0:T(8,128)} %get-tuple-element.87), channel_id=1, source_target_pairs={{0,9},{1,10},{2,11},{3,12},{4,13},{5,14},{6,15},{7,8},{8,17},{9,18... | collective-permute-start | bytes 491528 | tf_op jit(solution)/shard_map/ppermute | solution.py:110
  109.7 1.9 %collective-permute-start.16 = (f32[2,5,32,128]{3,2,1,0:T(8,128)}, f32[2,5,32,128]{3,2,1,0:T(8,128)S(1)}, u32[]{:S(2)}, u32[]{:S(2)}) collective-permute-start(f32[2,5,32,128]{3,2,1,0:T(8,128)} %get-tuple-element.88), channel_id=1, source_target_pairs={{0,15},{1,8},{2,9},{3,10},{4,11},{5,12},{6,13},{7,14},{8,23},{9,16... | collective-permute-start | bytes 491528 | tf_op jit(solution)/shard_map/ppermute | solution.py:110
  111.6 11.4 %collective-permute-done.15.bbefore_ref = f32[2,5,32,128]{3,2,1,0:T(8,128)S(1)} collective-permute-done((f32[2,5,32,128]{3,2,1,0:T(8,128)}, f32[2,5,32,128]{3,2,1,0:T(8,128)S(1)}, u32[]{:S(2)}, u32[]{:S(2)}) %collective-permute-start.15) | collective-permute-done | bytes 163872 | tf_op jit(solution)/shard_map/ppermute | solution.py:110
  123.1 0.5 collective-permute-done.18.after_ref
  123.5 0.1 copy-done.11
  123.8 0.1 copy-done.3
  124.0 0.3 copy-done.5
  124.3 5.4 %shard_map.51 = (f32[2,10,32,128]{3,2,1,0:T(8,128)}, f32[2,10,32,128]{3,2,1,0:T(8,128)}, f32[2,10,32,128]{3,2,1,0:T(8,128)}, f32[2,10,32,128]{3,2,1,0:T(8,128)},...) custom-call(f32[2]{0:T(128)} %diff_ref.13, ...), custom_call_target="tpu_custom_call" | custom-call | tf_op jit(solution)/shard_map/pallas_call | solution.py:299
  129.7 1.7 %collective-permute-start.19 = (f32[2,2,16,128]{3,2,1,0:T(8,128)}, f32[2,2,16,128]{3,2,1,0:T(8,128)S(1)}, u32[]{:S(2)}, u32[]{:S(2)}) collective-permute-start(f32[2,2,16,128]{3,2,1,0:T(8,128)} %get-tuple-element.93), channel_id=1, source_target_pairs={{0,1},{1,2},{2,3},{3,4},{4,5},{5,6},{6,7},{7,0},{8,9},{9,10},{10,1... | collective-permute-start | bytes 98312 | tf_op jit(solution)/shard_map/ppermute | solution.py:583
  131.4 3.1 %collective-permute-start.20 = (f32[2,2,16,128]{3,2,1,0:T(8,128)}, f32[2,2,16,128]{3,2,1,0:T(8,128)S(1)}, u32[]{:S(2)}, u32[]{:S(2)}) collective-permute-start(f32[2,2,16,128]{3,2,1,0:T(8,128)} %get-tuple-element.94), channel_id=1, source_target_pairs={{1,0},{2,1},{3,2},{4,3},{5,4},{6,5},{7,6},{0,7},{9,8},{10,9},{11,1... | collective-permute-start | bytes 98312 | tf_op jit(solution)/shard_map/ppermute | solution.py:584
  134.4 2.1 %collective-permute-done.19.cbefore_ref = f32[2,2,16,128]{3,2,1,0:T(8,128)S(1)} collective-permute-done((f32[2,2,16,128]{3,2,1,0:T(8,128)}, f32[2,2,16,128]{3,2,1,0:T(8,128)S(1)}, u32[]{:S(2)}, u32[]{:S(2)}) %collective-permute-start.19) | collective-permute-done | bytes 32800 | tf_op jit(solution)/shard_map/ppermute | solution.py:583
  136.5 0.6 copy-done.19
  137.2 2.9 %shard_map.52 = f32[2,8,32,128]{3,2,1,0:T(8,128)} custom-call(f32[2]{0:T(128)} %diff_ref.13, f32[4,2,4,16,128]{4,3,2,1,0:T(8,128)} %get-tuple-element.92.cown_ref, f32[2,2,16,128]{3,2,1,0:T(8,128)} %copy-done.19, f32[2,2,16,128]{3,2,1,0:T(8,128)} %copy-done.20, f32[2,8,16,128]{3,2,1,0:T(8,128)} %get-tuple-element.59.rate_ref, ...), custom_call_target="tpu_custom_call" | custom-call | tf_op jit(solution)/shard_map/pallas_call | solution.py:428
  (47 shorter events, 0.6 us)
Async XLA Ops:
  0.0 6.2 %copy-start = (f32[1,2,8,32,128]{4,3,2,1,0:T(8,128)S(1)}, f32[1,2,8,32,128]{4,3,2,1,0:T(8,128)}, u32[]{:S(2)}) copy-start(f32[1,2,8,32,128]{4,3,2,1,0:T(8,128)} %param.4) | copy-start | bytes 786436
  0.0 31.4 %copy-start.1 = (f32[2,8,32,128]{3,2,1,0:T(8,128)S(1)}, f32[2,8,32,128]{3,2,1,0:T(8,128)}, u32[]{:S(2)}) copy-start(f32[2,8,32,128]{3,2,1,0:T(8,128)} %param.6) | copy-start | bytes 786436
  0.0 31.4 %copy-start.2 = (f32[2,8,32,128]{3,2,1,0:T(8,128)S(1)}, f32[2,8,32,128]{3,2,1,0:T(8,128)}, u32[]{:S(2)}) copy-start(f32[2,8,32,128]{3,2,1,0:T(8,128)} %param.5) | copy-start | bytes 786436
  1.4 27.9 %collective-permute-start = (f32[3,2,5,32,128]{4,3,2,1,0:T(8,128)S(1)}, f32[3,2,5,32,128]{4,3,2,1,0:T(8,128)S(1)}, u32[]{:S(2)}, u32[]{:S(2)}) collective-permute-start(f32[3,2,5,32,128]{4,3,2,1,0:T(8,128)S(1)} %get-tuple-element.101), channel_id=1, source_target_pairs={{0,1},{1,2},{2,3},{3,4},{4,5},{5,6},{6,7},{7,0},{8,9},{9,10},{10,1... | collective-permute-start | bytes 1474568 | tf_op jit(solution)/shard_map/ppermute | solution.py:94
  3.0 28.5 %collective-permute-start.1 = (f32[3,2,5,32,128]{4,3,2,1,0:T(8,128)S(1)}, f32[3,2,5,32,128]{4,3,2,1,0:T(8,128)S(1)}, u32[]{:S(2)}, u32[]{:S(2)}) collective-permute-start(f32[3,2,5,32,128]{4,3,2,1,0:T(8,128)S(1)} %get-tuple-element.102), channel_id=1, source_target_pairs={{1,0},{2,1},{3,2},{4,3},{5,4},{6,5},{7,6},{0,7},{9,8},{10,9},{11,1... | collective-permute-start | bytes 1474568 | tf_op jit(solution)/shard_map/ppermute | solution.py:95
  6.2 31.6 %collective-permute-start.2 = (f32[2,8,32,128]{3,2,1,0:T(8,128)S(1)}, f32[2,8,32,128]{3,2,1,0:T(8,128)S(1)}, u32[]{:S(2)}, u32[]{:S(2)}) collective-permute-start(f32[2,8,32,128]{3,2,1,0:T(8,128)S(1)} %bitcast.5), channel_id=1, source_target_pairs={{0,8},{1,9},{2,10},{3,11},{4,12},{5,13},{6,14},{7,15},{8,16},{9,17... | collective-permute-start | bytes 786440 | tf_op jit(solution)/shard_map/ppermute | solution.py:110
  8.1 29.6 %collective-permute-start.4 = (f32[2,5,32,128]{3,2,1,0:T(8,128)S(1)}, f32[2,5,32,128]{3,2,1,0:T(8,128)S(1)}, u32[]{:S(2)}, u32[]{:S(2)}) collective-permute-start(f32[2,5,32,128]{3,2,1,0:T(8,128)S(1)} %get-tuple-element.103), channel_id=1, source_target_pairs={{0,15},{1,8},{2,9},{3,10},{4,11},{5,12},{6,13},{7,14},{8,23},{9,16... | collective-permute-start | bytes 491528 | tf_op jit(solution)/shard_map/ppermute | solution.py:110
  10.1 27.6 %collective-permute-start.3 = (f32[2,5,32,128]{3,2,1,0:T(8,128)S(1)}, f32[2,5,32,128]{3,2,1,0:T(8,128)}, u32[]{:S(2)}, u32[]{:S(2)}) collective-permute-start(f32[2,5,32,128]{3,2,1,0:T(8,128)S(1)} %get-tuple-element.104), channel_id=1, source_target_pairs={{0,9},{1,10},{2,11},{3,12},{4,13},{5,14},{6,15},{7,8},{8,17},{9,18... | collective-permute-start | bytes 491528 | tf_op jit(solution)/shard_map/ppermute | solution.py:110
  37.7 0.7 copy-start.10
  37.8 0.7 copy-start.7
  44.0 7.6 %collective-permute-start.5 = (f32[2,6,16,128]{3,2,1,0:T(8,128)}, f32[2,6,16,128]{3,2,1,0:T(8,128)S(1)}, u32[]{:S(2)}, u32[]{:S(2)}) collective-permute-start(f32[2,6,16,128]{3,2,1,0:T(8,128)} %get-tuple-element.62), channel_id=1, source_target_pairs={{0,1},{1,2},{2,3},{3,4},{4,5},{5,6},{6,7},{7,0},{8,9},{9,10},{10,1... | collective-permute-start | bytes 294920 | tf_op jit(solution)/shard_map/ppermute | solution.py:583
  44.3 7.4 %collective-permute-start.6 = (f32[2,6,16,128]{3,2,1,0:T(8,128)}, f32[2,6,16,128]{3,2,1,0:T(8,128)S(1)}, u32[]{:S(2)}, u32[]{:S(2)}) collective-permute-start(f32[2,6,16,128]{3,2,1,0:T(8,128)} %get-tuple-element.63), channel_id=1, source_target_pairs={{1,0},{2,1},{3,2},{4,3},{5,4},{6,5},{7,6},{0,7},{9,8},{10,9},{11,1... | collective-permute-start | bytes 294920 | tf_op jit(solution)/shard_map/ppermute | solution.py:584
  51.6 0.6 copy-start.15
  51.7 0.7 copy-start.17
  56.9 20.9 %collective-permute-start.10 = (f32[2,10,32,128]{3,2,1,0:T(8,128)}, f32[2,10,32,128]{3,2,1,0:T(8,128)S(1)}, u32[]{:S(2)}, u32[]{:S(2)}) collective-permute-start(f32[2,10,32,128]{3,2,1,0:T(8,128)} %get-tuple-element.75), channel_id=1, source_target_pairs={{0,1},{1,2},{2,3},{3,4},{4,5},{5,6},{6,7},{7,0},{8,9},{9,10},{10,1... | collective-permute-start | bytes 983048 | tf_op jit(solution)/shard_map/ppermute | solution.py:607
  57.7 22.3 %collective-permute-start.11 = (f32[2,10,32,128]{3,2,1,0:T(8,128)}, f32[2,10,32,128]{3,2,1,0:T(8,128)S(1)}, u32[]{:S(2)}, u32[]{:S(2)}) collective-permute-start(f32[2,10,32,128]{3,2,1,0:T(8,128)} %get-tuple-element.76), channel_id=1, source_target_pairs={{1,0},{2,1},{3,2},{4,3},{5,4},{6,5},{7,6},{0,7},{9,8},{10,9},{11,1... | collective-permute-start | bytes 983048 | tf_op jit(solution)/shard_map/ppermute | solution.py:608
  61.7 16.1 %collective-permute-start.7 = (f32[2,8,32,128]{3,2,1,0:T(8,128)}, f32[2,8,32,128]{3,2,1,0:T(8,128)S(1)}, u32[]{:S(2)}, u32[]{:S(2)}) collective-permute-start(f32[2,8,32,128]{3,2,1,0:T(8,128)} %get-tuple-element.71), channel_id=1, source_target_pairs={{0,8},{1,9},{2,10},{3,11},{4,12},{5,13},{6,14},{7,15},{8,16},{9,17... | collective-permute-start | bytes 786440 | tf_op jit(solution)/shard_map/ppermute | solution.py:110
  63.6 14.2 %collective-permute-start.8 = (f32[2,5,32,128]{3,2,1,0:T(8,128)}, f32[2,5,32,128]{3,2,1,0:T(8,128)S(1)}, u32[]{:S(2)}, u32[]{:S(2)}) collective-permute-start(f32[2,5,32,128]{3,2,1,0:T(8,128)} %get-tuple-element.72), channel_id=1, source_target_pairs={{0,9},{1,10},{2,11},{3,12},{4,13},{5,14},{6,15},{7,8},{8,17},{9,18... | collective-permute-start | bytes 491528 | tf_op jit(solution)/shard_map/ppermute | solution.py:110
  65.5 12.2 %collective-permute-start.9 = (f32[2,5,32,128]{3,2,1,0:T(8,128)}, f32[2,5,32,128]{3,2,1,0:T(8,128)S(1)}, u32[]{:S(2)}, u32[]{:S(2)}) collective-permute-start(f32[2,5,32,128]{3,2,1,0:T(8,128)} %get-tuple-element.73), channel_id=1, source_target_pairs={{0,15},{1,8},{2,9},{3,10},{4,11},{5,12},{6,13},{7,14},{8,23},{9,16... | collective-permute-start | bytes 491528 | tf_op jit(solution)/shard_map/ppermute | solution.py:110
  77.8 2.2 %copy-start.12 = (f32[2,5,32,128]{3,2,1,0:T(8,128)}, f32[2,5,32,128]{3,2,1,0:T(8,128)S(1)}, u32[]{:S(2)}) copy-start(f32[2,5,32,128]{3,2,1,0:T(8,128)S(1)} %collective-permute-done.8.bbefore_ref) | copy-start | bytes 491524
  77.8 2.2 %copy-start.14 = (f32[2,5,32,128]{3,2,1,0:T(8,128)}, f32[2,5,32,128]{3,2,1,0:T(8,128)S(1)}, u32[]{:S(2)}) copy-start(f32[2,5,32,128]{3,2,1,0:T(8,128)S(1)} %collective-permute-done.9.bafter_ref) | copy-start | bytes 491524
  77.8 2.2 %copy-start.9 = (f32[2,8,32,128]{3,2,1,0:T(8,128)}, f32[2,8,32,128]{3,2,1,0:T(8,128)S(1)}, u32[]{:S(2)}) copy-start(f32[2,8,32,128]{3,2,1,0:T(8,128)S(1)} %collective-permute-done.7.centre_ref) | copy-start | bytes 786436
  77.8 2.2 %copy-start.4 = (f32[2,10,32,128]{3,2,1,0:T(8,128)}, f32[2,10,32,128]{3,2,1,0:T(8,128)S(1)}, u32[]{:S(2)}) copy-start(f32[2,10,32,128]{3,2,1,0:T(8,128)S(1)} %collective-permute-done.10.before_ref) | copy-start | bytes 983044
  80.0 0.8 copy-start.6
  86.3 7.8 %collective-permute-start.12 = (f32[2,6,16,128]{3,2,1,0:T(8,128)}, f32[2,6,16,128]{3,2,1,0:T(8,128)S(1)}, u32[]{:S(2)}, u32[]{:S(2)}) collective-permute-start(f32[2,6,16,128]{3,2,1,0:T(8,128)} %get-tuple-element.78), channel_id=1, source_target_pairs={{0,1},{1,2},{2,3},{3,4},{4,5},{5,6},{6,7},{7,0},{8,9},{9,10},{10,1... | collective-permute-start | bytes 294920 | tf_op jit(solution)/shard_map/ppermute | solution.py:583
  87.9 7.9 %collective-permute-start.13 = (f32[2,6,16,128]{3,2,1,0:T(8,128)}, f32[2,6,16,128]{3,2,1,0:T(8,128)S(1)}, u32[]{:S(2)}, u32[]{:S(2)}) collective-permute-start(f32[2,6,16,128]{3,2,1,0:T(8,128)} %get-tuple-element.79), channel_id=1, source_target_pairs={{1,0},{2,1},{3,2},{4,3},{5,4},{6,5},{7,6},{0,7},{9,8},{10,9},{11,1... | collective-permute-start | bytes 294920 | tf_op jit(solution)/shard_map/ppermute | solution.py:584
  94.1 1.7 %copy-start.16 = (f32[2,6,16,128]{3,2,1,0:T(8,128)}, f32[2,6,16,128]{3,2,1,0:T(8,128)S(1)}, u32[]{:S(2)}) copy-start(f32[2,6,16,128]{3,2,1,0:T(8,128)S(1)} %collective-permute-done.12.cbefore_ref) | copy-start | bytes 294916
  95.8 0.6 copy-start.18
  101.1 22.0 %collective-permute-start.17 = (f32[2,10,32,128]{3,2,1,0:T(8,128)}, f32[2,10,32,128]{3,2,1,0:T(8,128)S(1)}, u32[]{:S(2)}, u32[]{:S(2)}) collective-permute-start(f32[2,10,32,128]{3,2,1,0:T(8,128)} %get-tuple-element.90), channel_id=1, source_target_pairs={{0,1},{1,2},{2,3},{3,4},{4,5},{5,6},{6,7},{7,0},{8,9},{9,10},{10,1... | collective-permute-start | bytes 983048 | tf_op jit(solution)/shard_map/ppermute | solution.py:607
  101.1 22.4 %collective-permute-start.18 = (f32[2,10,32,128]{3,2,1,0:T(8,128)}, f32[2,10,32,128]{3,2,1,0:T(8,128)S(1)}, u32[]{:S(2)}, u32[]{:S(2)}) collective-permute-start(f32[2,10,32,128]{3,2,1,0:T(8,128)} %get-tuple-element.91), channel_id=1, source_target_pairs={{1,0},{2,1},{3,2},{4,3},{5,4},{6,5},{7,6},{0,7},{9,8},{10,9},{11,1... | collective-permute-start | bytes 983048 | tf_op jit(solution)/shard_map/ppermute | solution.py:608
  105.8 17.2 %collective-permute-start.14 = (f32[2,8,32,128]{3,2,1,0:T(8,128)}, f32[2,8,32,128]{3,2,1,0:T(8,128)S(1)}, u32[]{:S(2)}, u32[]{:S(2)}) collective-permute-start(f32[2,8,32,128]{3,2,1,0:T(8,128)} %get-tuple-element.86), channel_id=1, source_target_pairs={{0,8},{1,9},{2,10},{3,11},{4,12},{5,13},{6,14},{7,15},{8,16},{9,17... | collective-permute-start | bytes 786440 | tf_op jit(solution)/shard_map/ppermute | solution.py:110
  107.8 15.3 %collective-permute-start.15 = (f32[2,5,32,128]{3,2,1,0:T(8,128)}, f32[2,5,32,128]{3,2,1,0:T(8,128)S(1)}, u32[]{:S(2)}, u32[]{:S(2)}) collective-permute-start(f32[2,5,32,128]{3,2,1,0:T(8,128)} %get-tuple-element.87), channel_id=1, source_target_pairs={{0,9},{1,10},{2,11},{3,12},{4,13},{5,14},{6,15},{7,8},{8,17},{9,18... | collective-permute-start | bytes 491528 | tf_op jit(solution)/shard_map/ppermute | solution.py:110
  109.7 13.3 %collective-permute-start.16 = (f32[2,5,32,128]{3,2,1,0:T(8,128)}, f32[2,5,32,128]{3,2,1,0:T(8,128)S(1)}, u32[]{:S(2)}, u32[]{:S(2)}) collective-permute-start(f32[2,5,32,128]{3,2,1,0:T(8,128)} %get-tuple-element.88), channel_id=1, source_target_pairs={{0,15},{1,8},{2,9},{3,10},{4,11},{5,12},{6,13},{7,14},{8,23},{9,16... | collective-permute-start | bytes 491528 | tf_op jit(solution)/shard_map/ppermute | solution.py:110
  123.0 0.7 copy-start.11
  123.0 0.7 copy-start.13
  123.0 0.8 copy-start.8
  123.0 0.9 copy-start.3
  123.5 0.8 copy-start.5
  129.7 6.8 %collective-permute-start.19 = (f32[2,2,16,128]{3,2,1,0:T(8,128)}, f32[2,2,16,128]{3,2,1,0:T(8,128)S(1)}, u32[]{:S(2)}, u32[]{:S(2)}) collective-permute-start(f32[2,2,16,128]{3,2,1,0:T(8,128)} %get-tuple-element.93), channel_id=1, source_target_pairs={{0,1},{1,2},{2,3},{3,4},{4,5},{5,6},{6,7},{7,0},{8,9},{9,10},{10,1... | collective-permute-start | bytes 98312 | tf_op jit(solution)/shard_map/ppermute | solution.py:583
  131.4 5.2 %collective-permute-start.20 = (f32[2,2,16,128]{3,2,1,0:T(8,128)}, f32[2,2,16,128]{3,2,1,0:T(8,128)S(1)}, u32[]{:S(2)}, u32[]{:S(2)}) collective-permute-start(f32[2,2,16,128]{3,2,1,0:T(8,128)} %get-tuple-element.94), channel_id=1, source_target_pairs={{1,0},{2,1},{3,2},{4,3},{5,4},{6,5},{7,6},{0,7},{9,8},{10,9},{11,1... | collective-permute-start | bytes 98312 | tf_op jit(solution)/shard_map/ppermute | solution.py:584
  136.5 0.6 copy-start.19
  136.5 0.6 copy-start.20

commit v8 on v6

--- a/solution.py
+++ b/solution.py
@@ -455,10 +455,8 @@
     edge = hs - 1
     offset = 0
     for m in range(4):
-        summed = spread_table[m][0] * full
-        for j in range(1, 5):
-            summed = summed + spread_table[m][j] * full
-        part = (widths[m] * dec * inner - widths[m] * terms) + summed
+        weight = sum(spread_table[m][j] for j in range(5))
+        part = (widths[m] * dec * inner - widths[m] * terms) + weight * full
         own_ref[m] = part[:, edge:edge + rows]
         w = edge - m
         before_ref[:, offset:offset + w] = part[:, m:edge]

time: 139 us -> 138 us (level)
  no operation moved by 1% of the time
where the time goes in v8:
time: 138 us; the launch traced here: 137 us
  waiting for transfers between devices  53 us (38%)
  starting transfers between devices  45.8 us (33%)
  Pallas kernels  30.5 us (22%)
  local copies, waits for them, and re-layouts  4.95 us (4%)
  other arithmetic  2.73 us (2%)
    ppermute x9, waiting for transfers between devices, moved(): return lax.ppermute(piece, axes, pairs)  21.7 us
    ppermute x9, starting transfers between devices, moved(): return lax.ppermute(piece, axes, pairs)  17.3 us
    ppermute x1, waiting for transfers between devices, space_halo(): lax.ppermute(lax.slice_in_dim(a, rows - h, rows, axis=a.ndim - 3), 'space...  16.5 us
    pallas_call x3, Pallas kernels, fine_sweep(): pl.pallas_call(functools.partial(sweep_kernel, widths_sent, natural_prior...  14.6 us
    pallas_call x3, Pallas kernels, finish_round(): pl.pallas_call(functools.partial(finish_kernel, widths_sent), out_shape=o...  12 us
    ppermute x3, starting transfers between devices, advance(): lax.ppermute(cfirsts, 'space', down)  10.6 us
    ppermute x2, starting transfers between devices, per_device(): lax.ppermute(firsts, 'space', down)  8.72 us
    ppermute x3, waiting for transfers between devices, advance(): lax.ppermute(clasts, 'space', up)  8.13 us
  transfers between devices with their start and end apart: 21, of which 11 were waited for; matrix products, arithmetic and copies ran while one was open for 2% of the time, Pallas kernels for 3%

profile of v8, /device:TPU:2, one launch (start us, length us, event | category | flops | bytes accessed | tf_op | source)
XLA Modules:
  0.0 137.2 jit_solution(1403854469299586853)
XLA Ops:
  0.0 1.3 pad_maximum_fusion.1
  1.4 1.6 %collective-permute-start = (f32[3,2,5,32,128]{4,3,2,1,0:T(8,128)S(1)}, f32[3,2,5,32,128]{4,3,2,1,0:T(8,128)S(1)}, u32[]{:S(2)}, u32[]{:S(2)}) collective-permute-start(f32[3,2,5,32,128]{4,3,2,1,0:T(8,128)S(1)} %get-tuple-element.99), channel_id=1, source_target_pairs={{0,1},{1,2},{2,3},{3,4},{4,5},{5,6},{6,7},{7,0},{8,9},{9,10},{10,1... | collective-permute-start | bytes 1474568 | tf_op jit(solution)/shard_map/ppermute | solution.py:94
  3.0 3.2 %collective-permute-start.1 = (f32[3,2,5,32,128]{4,3,2,1,0:T(8,128)S(1)}, f32[3,2,5,32,128]{4,3,2,1,0:T(8,128)S(1)}, u32[]{:S(2)}, u32[]{:S(2)}) collective-permute-start(f32[3,2,5,32,128]{4,3,2,1,0:T(8,128)S(1)} %get-tuple-element.100), channel_id=1, source_target_pairs={{1,0},{2,1},{3,2},{4,3},{5,4},{6,5},{7,6},{0,7},{9,8},{10,9},{11,1... | collective-permute-start | bytes 1474568 | tf_op jit(solution)/shard_map/ppermute | solution.py:95
  6.2 1.9 %collective-permute-start.2 = (f32[2,8,32,128]{3,2,1,0:T(8,128)S(1)}, f32[2,8,32,128]{3,2,1,0:T(8,128)S(1)}, u32[]{:S(2)}, u32[]{:S(2)}) collective-permute-start(f32[2,8,32,128]{3,2,1,0:T(8,128)S(1)} %bitcast.5), channel_id=1, source_target_pairs={{0,8},{1,9},{2,10},{3,11},{4,12},{5,13},{6,14},{7,15},{8,16},{9,17... | collective-permute-start | bytes 786440 | tf_op jit(solution)/shard_map/ppermute | solution.py:110
  8.1 0.7 fusion.1
  8.8 2.0 %collective-permute-start.4 = (f32[2,5,32,128]{3,2,1,0:T(8,128)}, f32[2,5,32,128]{3,2,1,0:T(8,128)S(1)}, u32[]{:S(2)}, u32[]{:S(2)}) collective-permute-start(f32[2,5,32,128]{3,2,1,0:T(8,128)} %get-tuple-element.101), channel_id=1, source_target_pairs={{0,15},{1,8},{2,9},{3,10},{4,11},{5,12},{6,13},{7,14},{8,23},{9,16... | collective-permute-start | bytes 491528 | tf_op jit(solution)/shard_map/ppermute | solution.py:110
  10.8 1.9 %collective-permute-start.3 = (f32[2,5,32,128]{3,2,1,0:T(8,128)S(1)}, f32[2,5,32,128]{3,2,1,0:T(8,128)S(1)}, u32[]{:S(2)}, u32[]{:S(2)}) collective-permute-start(f32[2,5,32,128]{3,2,1,0:T(8,128)S(1)} %get-tuple-element.102), channel_id=1, source_target_pairs={{0,9},{1,10},{2,11},{3,12},{4,13},{5,14},{6,15},{7,8},{8,17},{9,18... | collective-permute-start | bytes 491528 | tf_op jit(solution)/shard_map/ppermute | solution.py:110
  12.7 16.5 %collective-permute-done = f32[3,2,5,32,128]{4,3,2,1,0:T(8,128)S(1)} collective-permute-done((f32[3,2,5,32,128]{4,3,2,1,0:T(8,128)S(1)}, f32[3,2,5,32,128]{4,3,2,1,0:T(8,128)S(1)}, u32[]{:S(2)}, u32[]{:S(2)}) %collective-permute-start) | collective-permute-done | bytes 491552 | tf_op jit(solution)/shard_map/ppermute | solution.py:94
  29.2 2.2 %collective-permute-done.1 = f32[3,2,5,32,128]{4,3,2,1,0:T(8,128)S(1)} collective-permute-done((f32[3,2,5,32,128]{4,3,2,1,0:T(8,128)S(1)}, f32[3,2,5,32,128]{4,3,2,1,0:T(8,128)S(1)}, u32[]{:S(2)}, u32[]{:S(2)}) %collective-permute-start.1) | collective-permute-done | bytes 491552 | tf_op jit(solution)/shard_map/ppermute | solution.py:95
  31.4 1.5 %pad_maximum_fusion.stacked_ref = f32[3,2,18,32,128]{4,3,2,1,0:T(8,128)} fusion(f32[3,2,5,32,128]{4,3,2,1,0:T(8,128)S(1)} %collective-permute-done.1, f32[1,2,8,32,128]{4,3,2,1,0:T(8,128)S(1)} %bitcast.8, f32[1,2,8,32,128]{4,3,2,1,0:T(8,128)S(1)} %bitcast.10, f32[1,2,8,32,128]{4,3,2,1,0:T(8,128)S(1)} %copy-done, f32[3,2,5,32,128]{4,3,2,1,0:T(8,128)S(1)} %collective-permute-done), kind=kLoop, calls=%fused_computation | loop fusion | flops 1769472 | bytes 3538944 | tf_op jit(solution)/shard_map/concatenate | solution.py:96
  32.9 3.8 %shard_map.46 = (f32[4,2,8,32,128]{4,3,2,1,0:T(8,128)}, f32[2,10,32,128]{3,2,1,0:T(8,128)}, f32[2,10,32,128]{3,2,1,0:T(8,128)}, f32[2,8,16,128]{3,2,1,0:T(8,128)...) custom-call(f32[2]{0:T(128)} %diff_ref.13, ...), custom_call_target="tpu_custom_call" | custom-call | tf_op jit(solution)/shard_map/pallas_call | solution.py:477
  36.8 0.6 copy-done.10
  37.5 4.8 %shard_map.47 = (f32[2,10,32,128]{3,2,1,0:T(8,128)}, f32[2,10,32,128]{3,2,1,0:T(8,128)}, f32[2,10,32,128]{3,2,1,0:T(8,128)}, f32[2,10,32,128]{3,2,1,0:T(8,128)},...) custom-call(f32[2]{0:T(128)} %diff_ref.13, ...), custom_call_target="tpu_custom_call" | custom-call | tf_op jit(solution)/shard_map/pallas_call | solution.py:298
  42.4 0.3 collective-permute-start.5
  42.7 4.4 %collective-permute-start.6 = (f32[2,6,16,128]{3,2,1,0:T(8,128)}, f32[2,6,16,128]{3,2,1,0:T(8,128)S(1)}, u32[]{:S(2)}, u32[]{:S(2)}) collective-permute-start(f32[2,6,16,128]{3,2,1,0:T(8,128)} %get-tuple-element.61), channel_id=1, source_target_pairs={{1,0},{2,1},{3,2},{4,3},{5,4},{6,5},{7,6},{0,7},{9,8},{10,9},{11,1... | collective-permute-start | bytes 294920 | tf_op jit(solution)/shard_map/ppermute | solution.py:578
  47.1 2.9 %collective-permute-done.5.cbefore_ref = f32[2,6,16,128]{3,2,1,0:T(8,128)S(1)} collective-permute-done((f32[2,6,16,128]{3,2,1,0:T(8,128)}, f32[2,6,16,128]{3,2,1,0:T(8,128)S(1)}, u32[]{:S(2)}, u32[]{:S(2)}) %collective-permute-start.5) | collective-permute-done | bytes 98336 | tf_op jit(solution)/shard_map/ppermute | solution.py:577
  50.1 0.6 copy-done.16
  50.7 4.6 %shard_map.48 = (f32[4,2,8,32,128]{4,3,2,1,0:T(8,128)}, f32[2,10,32,128]{3,2,1,0:T(8,128)}, f32[2,10,32,128]{3,2,1,0:T(8,128)}, f32[2,8,32,128]{3,2,1,0:T(8,128)...) custom-call(f32[2]{0:T(128)} %diff_ref.13, f32[4,2,4,16,128]{4,3,2,1,0:T(8,128)} %get-tuple-element.59.cown_ref, ...), custom_call_target="tpu_custom_call" | custom-call | tf_op jit(solution)/shard_map/pallas_call | solution.py:427
  55.3 0.8 collective-permute-start.10
  56.1 4.0 %collective-permute-start.11 = (f32[2,10,32,128]{3,2,1,0:T(8,128)}, f32[2,10,32,128]{3,2,1,0:T(8,128)S(1)}, u32[]{:S(2)}, u32[]{:S(2)}) collective-permute-start(f32[2,10,32,128]{3,2,1,0:T(8,128)} %get-tuple-element.74), channel_id=1, source_target_pairs={{1,0},{2,1},{3,2},{4,3},{5,4},{6,5},{7,6},{0,7},{9,8},{10,9},{11,1... | collective-permute-start | bytes 983048 | tf_op jit(solution)/shard_map/ppermute | solution.py:602
  60.1 1.9 %collective-permute-start.7 = (f32[2,8,32,128]{3,2,1,0:T(8,128)}, f32[2,8,32,128]{3,2,1,0:T(8,128)S(1)}, u32[]{:S(2)}, u32[]{:S(2)}) collective-permute-start(f32[2,8,32,128]{3,2,1,0:T(8,128)} %get-tuple-element.69), channel_id=1, source_target_pairs={{0,8},{1,9},{2,10},{3,11},{4,12},{5,13},{6,14},{7,15},{8,16},{9,17... | collective-permute-start | bytes 786440 | tf_op jit(solution)/shard_map/ppermute | solution.py:110
  62.0 1.9 %collective-permute-start.8 = (f32[2,5,32,128]{3,2,1,0:T(8,128)}, f32[2,5,32,128]{3,2,1,0:T(8,128)S(1)}, u32[]{:S(2)}, u32[]{:S(2)}) collective-permute-start(f32[2,5,32,128]{3,2,1,0:T(8,128)} %get-tuple-element.70), channel_id=1, source_target_pairs={{0,9},{1,10},{2,11},{3,12},{4,13},{5,14},{6,15},{7,8},{8,17},{9,18... | collective-permute-start | bytes 491528 | tf_op jit(solution)/shard_map/ppermute | solution.py:110
  63.9 1.9 %collective-permute-start.9 = (f32[2,5,32,128]{3,2,1,0:T(8,128)}, f32[2,5,32,128]{3,2,1,0:T(8,128)S(1)}, u32[]{:S(2)}, u32[]{:S(2)}) collective-permute-start(f32[2,5,32,128]{3,2,1,0:T(8,128)} %get-tuple-element.71), channel_id=1, source_target_pairs={{0,15},{1,8},{2,9},{3,10},{4,11},{5,12},{6,13},{7,14},{8,23},{9,16... | collective-permute-start | bytes 491528 | tf_op jit(solution)/shard_map/ppermute | solution.py:110
  65.8 10.3 %collective-permute-done.8.bbefore_ref = f32[2,5,32,128]{3,2,1,0:T(8,128)S(1)} collective-permute-done((f32[2,5,32,128]{3,2,1,0:T(8,128)}, f32[2,5,32,128]{3,2,1,0:T(8,128)S(1)}, u32[]{:S(2)}, u32[]{:S(2)}) %collective-permute-start.8) | collective-permute-done | bytes 163872 | tf_op jit(solution)/shard_map/ppermute | solution.py:110
  76.2 2.2 %collective-permute-done.11.after_ref = f32[2,10,32,128]{3,2,1,0:T(8,128)S(1)} collective-permute-done((f32[2,10,32,128]{3,2,1,0:T(8,128)}, f32[2,10,32,128]{3,2,1,0:T(8,128)S(1)}, u32[]{:S(2)}, u32[]{:S(2)}) %collective-permute-start.11) | collective-permute-done | bytes 327712 | tf_op jit(solution)/shard_map/ppermute | solution.py:602
  78.4 0.7 copy-done.6
  79.1 4.9 %shard_map.49 = (f32[2,10,32,128]{3,2,1,0:T(8,128)}, f32[2,10,32,128]{3,2,1,0:T(8,128)}, f32[2,10,32,128]{3,2,1,0:T(8,128)}, f32[2,10,32,128]{3,2,1,0:T(8,128)},...) custom-call(f32[2]{0:T(128)} %diff_ref.13, ...), custom_call_target="tpu_custom_call" | custom-call | tf_op jit(solution)/shard_map/pallas_call | solution.py:298
  84.0 1.7 %collective-permute-start.12 = (f32[2,6,16,128]{3,2,1,0:T(8,128)}, f32[2,6,16,128]{3,2,1,0:T(8,128)S(1)}, u32[]{:S(2)}, u32[]{:S(2)}) collective-permute-start(f32[2,6,16,128]{3,2,1,0:T(8,128)} %get-tuple-element.76), channel_id=1, source_target_pairs={{0,1},{1,2},{2,3},{3,4},{4,5},{5,6},{6,7},{7,0},{8,9},{9,10},{10,1... | collective-permute-start | bytes 294920 | tf_op jit(solution)/shard_map/ppermute | solution.py:577
  85.6 3.1 %collective-permute-start.13 = (f32[2,6,16,128]{3,2,1,0:T(8,128)}, f32[2,6,16,128]{3,2,1,0:T(8,128)S(1)}, u32[]{:S(2)}, u32[]{:S(2)}) collective-permute-start(f32[2,6,16,128]{3,2,1,0:T(8,128)} %get-tuple-element.77), channel_id=1, source_target_pairs={{1,0},{2,1},{3,2},{4,3},{5,4},{6,5},{7,6},{0,7},{9,8},{10,9},{11,1... | collective-permute-start | bytes 294920 | tf_op jit(solution)/shard_map/ppermute | solution.py:578
  88.7 3.1 %collective-permute-done.12.cbefore_ref = f32[2,6,16,128]{3,2,1,0:T(8,128)S(1)} collective-permute-done((f32[2,6,16,128]{3,2,1,0:T(8,128)}, f32[2,6,16,128]{3,2,1,0:T(8,128)S(1)}, u32[]{:S(2)}, u32[]{:S(2)}) %collective-permute-start.12) | collective-permute-done | bytes 98336 | tf_op jit(solution)/shard_map/ppermute | solution.py:577
  91.8 1.7 %collective-permute-done.13.cafter_ref = f32[2,6,16,128]{3,2,1,0:T(8,128)S(1)} collective-permute-done((f32[2,6,16,128]{3,2,1,0:T(8,128)}, f32[2,6,16,128]{3,2,1,0:T(8,128)S(1)}, u32[]{:S(2)}, u32[]{:S(2)}) %collective-permute-start.13) | collective-permute-done | bytes 98336 | tf_op jit(solution)/shard_map/ppermute | solution.py:578
  93.5 0.6 copy-done.19
  94.1 4.6 %shard_map.50 = (f32[4,2,8,32,128]{4,3,2,1,0:T(8,128)}, f32[2,10,32,128]{3,2,1,0:T(8,128)}, f32[2,10,32,128]{3,2,1,0:T(8,128)}, f32[2,8,32,128]{3,2,1,0:T(8,128)...) custom-call(f32[2]{0:T(128)} %diff_ref.13, f32[4,2,4,16,128]{4,3,2,1,0:T(8,128)} %get-tuple-element.75.cown_ref, ...), custom_call_target="tpu_custom_call" | custom-call | tf_op jit(solution)/shard_map/pallas_call | solution.py:427
  98.8 4.7 %collective-permute-start.18 = (f32[2,10,32,128]{3,2,1,0:T(8,128)}, f32[2,10,32,128]{3,2,1,0:T(8,128)S(1)}, u32[]{:S(2)}, u32[]{:S(2)}) collective-permute-start(f32[2,10,32,128]{3,2,1,0:T(8,128)} %get-tuple-element.89), channel_id=1, source_target_pairs={{1,0},{2,1},{3,2},{4,3},{5,4},{6,5},{7,6},{0,7},{9,8},{10,9},{11,1... | collective-permute-start | bytes 983048 | tf_op jit(solution)/shard_map/ppermute | solution.py:602
  103.5 1.9 %collective-permute-start.14 = (f32[2,8,32,128]{3,2,1,0:T(8,128)}, f32[2,8,32,128]{3,2,1,0:T(8,128)S(1)}, u32[]{:S(2)}, u32[]{:S(2)}) collective-permute-start(f32[2,8,32,128]{3,2,1,0:T(8,128)} %get-tuple-element.84), channel_id=1, source_target_pairs={{0,8},{1,9},{2,10},{3,11},{4,12},{5,13},{6,14},{7,15},{8,16},{9,17... | collective-permute-start | bytes 786440 | tf_op jit(solution)/shard_map/ppermute | solution.py:110
  105.4 1.9 %collective-permute-start.15 = (f32[2,5,32,128]{3,2,1,0:T(8,128)}, f32[2,5,32,128]{3,2,1,0:T(8,128)S(1)}, u32[]{:S(2)}, u32[]{:S(2)}) collective-permute-start(f32[2,5,32,128]{3,2,1,0:T(8,128)} %get-tuple-element.85), channel_id=1, source_target_pairs={{0,9},{1,10},{2,11},{3,12},{4,13},{5,14},{6,15},{7,8},{8,17},{9,18... | collective-permute-start | bytes 491528 | tf_op jit(solution)/shard_map/ppermute | solution.py:110
  107.3 1.9 %collective-permute-start.16 = (f32[2,5,32,128]{3,2,1,0:T(8,128)}, f32[2,5,32,128]{3,2,1,0:T(8,128)S(1)}, u32[]{:S(2)}, u32[]{:S(2)}) collective-permute-start(f32[2,5,32,128]{3,2,1,0:T(8,128)} %get-tuple-element.86), channel_id=1, source_target_pairs={{0,15},{1,8},{2,9},{3,10},{4,11},{5,12},{6,13},{7,14},{8,23},{9,16... | collective-permute-start | bytes 491528 | tf_op jit(solution)/shard_map/ppermute | solution.py:110
  109.3 11.4 %collective-permute-done.15.bbefore_ref = f32[2,5,32,128]{3,2,1,0:T(8,128)S(1)} collective-permute-done((f32[2,5,32,128]{3,2,1,0:T(8,128)}, f32[2,5,32,128]{3,2,1,0:T(8,128)S(1)}, u32[]{:S(2)}, u32[]{:S(2)}) %collective-permute-start.15) | collective-permute-done | bytes 163872 | tf_op jit(solution)/shard_map/ppermute | solution.py:110
  120.7 0.5 collective-permute-done.18.after_ref
  121.2 0.1 copy-done.12
  121.5 0.1 copy-done.3
  121.6 0.3 copy-done.5
  121.9 4.9 %shard_map.51 = (f32[2,10,32,128]{3,2,1,0:T(8,128)}, f32[2,10,32,128]{3,2,1,0:T(8,128)}, f32[2,10,32,128]{3,2,1,0:T(8,128)}, f32[2,10,32,128]{3,2,1,0:T(8,128)},...) custom-call(f32[2]{0:T(128)} %diff_ref.13, ...), custom_call_target="tpu_custom_call" | custom-call | tf_op jit(solution)/shard_map/pallas_call | solution.py:298
  126.8 1.7 %collective-permute-start.19 = (f32[2,2,16,128]{3,2,1,0:T(8,128)}, f32[2,2,16,128]{3,2,1,0:T(8,128)S(1)}, u32[]{:S(2)}, u32[]{:S(2)}) collective-permute-start(f32[2,2,16,128]{3,2,1,0:T(8,128)} %get-tuple-element.91), channel_id=1, source_target_pairs={{0,1},{1,2},{2,3},{3,4},{4,5},{5,6},{6,7},{7,0},{8,9},{9,10},{10,1... | collective-permute-start | bytes 98312 | tf_op jit(solution)/shard_map/ppermute | solution.py:577
  128.5 3.1 %collective-permute-start.20 = (f32[2,2,16,128]{3,2,1,0:T(8,128)}, f32[2,2,16,128]{3,2,1,0:T(8,128)S(1)}, u32[]{:S(2)}, u32[]{:S(2)}) collective-permute-start(f32[2,2,16,128]{3,2,1,0:T(8,128)} %get-tuple-element.92), channel_id=1, source_target_pairs={{1,0},{2,1},{3,2},{4,3},{5,4},{6,5},{7,6},{0,7},{9,8},{10,9},{11,1... | collective-permute-start | bytes 98312 | tf_op jit(solution)/shard_map/ppermute | solution.py:578
  131.6 2.1 %collective-permute-done.19.cbefore_ref = f32[2,2,16,128]{3,2,1,0:T(8,128)S(1)} collective-permute-done((f32[2,2,16,128]{3,2,1,0:T(8,128)}, f32[2,2,16,128]{3,2,1,0:T(8,128)S(1)}, u32[]{:S(2)}, u32[]{:S(2)}) %collective-permute-start.19) | collective-permute-done | bytes 32800 | tf_op jit(solution)/shard_map/ppermute | solution.py:577
  133.7 0.6 copy-done.20
  134.3 2.9 %shard_map.52 = f32[2,8,32,128]{3,2,1,0:T(8,128)} custom-call(f32[2]{0:T(128)} %diff_ref.13, f32[4,2,4,16,128]{4,3,2,1,0:T(8,128)} %get-tuple-element.90.cown_ref, f32[2,2,16,128]{3,2,1,0:T(8,128)} %copy-done.20, f32[2,2,16,128]{3,2,1,0:T(8,128)} %copy-done.21, f32[2,8,16,128]{3,2,1,0:T(8,128)} %get-tuple-element.58.rate_ref, ...), custom_call_target="tpu_custom_call" | custom-call | tf_op jit(solution)/shard_map/pallas_call | solution.py:427
  (49 shorter events, 0.7 us)
Async XLA Ops:
  0.0 6.2 %copy-start = (f32[1,2,8,32,128]{4,3,2,1,0:T(8,128)S(1)}, f32[1,2,8,32,128]{4,3,2,1,0:T(8,128)}, u32[]{:S(2)}) copy-start(f32[1,2,8,32,128]{4,3,2,1,0:T(8,128)} %param.4) | copy-start | bytes 786436
  0.0 31.4 %copy-start.1 = (f32[2,8,32,128]{3,2,1,0:T(8,128)S(1)}, f32[2,8,32,128]{3,2,1,0:T(8,128)}, u32[]{:S(2)}) copy-start(f32[2,8,32,128]{3,2,1,0:T(8,128)} %param.6) | copy-start | bytes 786436
  0.0 31.4 %copy-start.2 = (f32[2,8,32,128]{3,2,1,0:T(8,128)S(1)}, f32[2,8,32,128]{3,2,1,0:T(8,128)}, u32[]{:S(2)}) copy-start(f32[2,8,32,128]{3,2,1,0:T(8,128)} %param.5) | copy-start | bytes 786436
  1.4 27.9 %collective-permute-start = (f32[3,2,5,32,128]{4,3,2,1,0:T(8,128)S(1)}, f32[3,2,5,32,128]{4,3,2,1,0:T(8,128)S(1)}, u32[]{:S(2)}, u32[]{:S(2)}) collective-permute-start(f32[3,2,5,32,128]{4,3,2,1,0:T(8,128)S(1)} %get-tuple-element.99), channel_id=1, source_target_pairs={{0,1},{1,2},{2,3},{3,4},{4,5},{5,6},{6,7},{7,0},{8,9},{9,10},{10,1... | collective-permute-start | bytes 1474568 | tf_op jit(solution)/shard_map/ppermute | solution.py:94
  3.0 28.5 %collective-permute-start.1 = (f32[3,2,5,32,128]{4,3,2,1,0:T(8,128)S(1)}, f32[3,2,5,32,128]{4,3,2,1,0:T(8,128)S(1)}, u32[]{:S(2)}, u32[]{:S(2)}) collective-permute-start(f32[3,2,5,32,128]{4,3,2,1,0:T(8,128)S(1)} %get-tuple-element.100), channel_id=1, source_target_pairs={{1,0},{2,1},{3,2},{4,3},{5,4},{6,5},{7,6},{0,7},{9,8},{10,9},{11,1... | collective-permute-start | bytes 1474568 | tf_op jit(solution)/shard_map/ppermute | solution.py:95
  6.2 30.6 %collective-permute-start.2 = (f32[2,8,32,128]{3,2,1,0:T(8,128)S(1)}, f32[2,8,32,128]{3,2,1,0:T(8,128)S(1)}, u32[]{:S(2)}, u32[]{:S(2)}) collective-permute-start(f32[2,8,32,128]{3,2,1,0:T(8,128)S(1)} %bitcast.5), channel_id=1, source_target_pairs={{0,8},{1,9},{2,10},{3,11},{4,12},{5,13},{6,14},{7,15},{8,16},{9,17... | collective-permute-start | bytes 786440 | tf_op jit(solution)/shard_map/ppermute | solution.py:110
  8.8 27.9 %collective-permute-start.4 = (f32[2,5,32,128]{3,2,1,0:T(8,128)}, f32[2,5,32,128]{3,2,1,0:T(8,128)S(1)}, u32[]{:S(2)}, u32[]{:S(2)}) collective-permute-start(f32[2,5,32,128]{3,2,1,0:T(8,128)} %get-tuple-element.101), channel_id=1, source_target_pairs={{0,15},{1,8},{2,9},{3,10},{4,11},{5,12},{6,13},{7,14},{8,23},{9,16... | collective-permute-start | bytes 491528 | tf_op jit(solution)/shard_map/ppermute | solution.py:110
  10.8 25.9 %collective-permute-start.3 = (f32[2,5,32,128]{3,2,1,0:T(8,128)S(1)}, f32[2,5,32,128]{3,2,1,0:T(8,128)S(1)}, u32[]{:S(2)}, u32[]{:S(2)}) collective-permute-start(f32[2,5,32,128]{3,2,1,0:T(8,128)S(1)} %get-tuple-element.102), channel_id=1, source_target_pairs={{0,9},{1,10},{2,11},{3,12},{4,13},{5,14},{6,15},{7,8},{8,17},{9,18... | collective-permute-start | bytes 491528 | tf_op jit(solution)/shard_map/ppermute | solution.py:110
  36.7 0.7 copy-start.10
  36.7 0.7 copy-start.11
  36.8 0.8 copy-start.7
  42.4 7.6 %collective-permute-start.5 = (f32[2,6,16,128]{3,2,1,0:T(8,128)}, f32[2,6,16,128]{3,2,1,0:T(8,128)S(1)}, u32[]{:S(2)}, u32[]{:S(2)}) collective-permute-start(f32[2,6,16,128]{3,2,1,0:T(8,128)} %get-tuple-element.60), channel_id=1, source_target_pairs={{0,1},{1,2},{2,3},{3,4},{4,5},{5,6},{6,7},{7,0},{8,9},{9,10},{10,1... | collective-permute-start | bytes 294920 | tf_op jit(solution)/shard_map/ppermute | solution.py:577
  42.7 7.4 %collective-permute-start.6 = (f32[2,6,16,128]{3,2,1,0:T(8,128)}, f32[2,6,16,128]{3,2,1,0:T(8,128)S(1)}, u32[]{:S(2)}, u32[]{:S(2)}) collective-permute-start(f32[2,6,16,128]{3,2,1,0:T(8,128)} %get-tuple-element.61), channel_id=1, source_target_pairs={{1,0},{2,1},{3,2},{4,3},{5,4},{6,5},{7,6},{0,7},{9,8},{10,9},{11,1... | collective-permute-start | bytes 294920 | tf_op jit(solution)/shard_map/ppermute | solution.py:578
  50.0 0.6 copy-start.16
  50.1 0.6 copy-start.18
  55.3 20.9 %collective-permute-start.10 = (f32[2,10,32,128]{3,2,1,0:T(8,128)}, f32[2,10,32,128]{3,2,1,0:T(8,128)S(1)}, u32[]{:S(2)}, u32[]{:S(2)}) collective-permute-start(f32[2,10,32,128]{3,2,1,0:T(8,128)} %get-tuple-element.73), channel_id=1, source_target_pairs={{0,1},{1,2},{2,3},{3,4},{4,5},{5,6},{6,7},{7,0},{8,9},{9,10},{10,1... | collective-permute-start | bytes 983048 | tf_op jit(solution)/shard_map/ppermute | solution.py:601
  56.1 22.3 %collective-permute-start.11 = (f32[2,10,32,128]{3,2,1,0:T(8,128)}, f32[2,10,32,128]{3,2,1,0:T(8,128)S(1)}, u32[]{:S(2)}, u32[]{:S(2)}) collective-permute-start(f32[2,10,32,128]{3,2,1,0:T(8,128)} %get-tuple-element.74), channel_id=1, source_target_pairs={{1,0},{2,1},{3,2},{4,3},{5,4},{6,5},{7,6},{0,7},{9,8},{10,9},{11,1... | collective-permute-start | bytes 983048 | tf_op jit(solution)/shard_map/ppermute | solution.py:602
  60.1 16.1 %collective-permute-start.7 = (f32[2,8,32,128]{3,2,1,0:T(8,128)}, f32[2,8,32,128]{3,2,1,0:T(8,128)S(1)}, u32[]{:S(2)}, u32[]{:S(2)}) collective-permute-start(f32[2,8,32,128]{3,2,1,0:T(8,128)} %get-tuple-element.69), channel_id=1, source_target_pairs={{0,8},{1,9},{2,10},{3,11},{4,12},{5,13},{6,14},{7,15},{8,16},{9,17... | collective-permute-start | bytes 786440 | tf_op jit(solution)/shard_map/ppermute | solution.py:110
  62.0 14.2 %collective-permute-start.8 = (f32[2,5,32,128]{3,2,1,0:T(8,128)}, f32[2,5,32,128]{3,2,1,0:T(8,128)S(1)}, u32[]{:S(2)}, u32[]{:S(2)}) collective-permute-start(f32[2,5,32,128]{3,2,1,0:T(8,128)} %get-tuple-element.70), channel_id=1, source_target_pairs={{0,9},{1,10},{2,11},{3,12},{4,13},{5,14},{6,15},{7,8},{8,17},{9,18... | collective-permute-start | bytes 491528 | tf_op jit(solution)/shard_map/ppermute | solution.py:110
  63.9 12.2 %collective-permute-start.9 = (f32[2,5,32,128]{3,2,1,0:T(8,128)}, f32[2,5,32,128]{3,2,1,0:T(8,128)S(1)}, u32[]{:S(2)}, u32[]{:S(2)}) collective-permute-start(f32[2,5,32,128]{3,2,1,0:T(8,128)} %get-tuple-element.71), channel_id=1, source_target_pairs={{0,15},{1,8},{2,9},{3,10},{4,11},{5,12},{6,13},{7,14},{8,23},{9,16... | collective-permute-start | bytes 491528 | tf_op jit(solution)/shard_map/ppermute | solution.py:110
  76.1 2.2 %copy-start.13 = (f32[2,5,32,128]{3,2,1,0:T(8,128)}, f32[2,5,32,128]{3,2,1,0:T(8,128)S(1)}, u32[]{:S(2)}) copy-start(f32[2,5,32,128]{3,2,1,0:T(8,128)S(1)} %collective-permute-done.8.bbefore_ref) | copy-start | bytes 491524
  76.1 2.2 %copy-start.15 = (f32[2,5,32,128]{3,2,1,0:T(8,128)}, f32[2,5,32,128]{3,2,1,0:T(8,128)S(1)}, u32[]{:S(2)}) copy-start(f32[2,5,32,128]{3,2,1,0:T(8,128)S(1)} %collective-permute-done.9.bafter_ref) | copy-start | bytes 491524
  76.1 2.2 %copy-start.9 = (f32[2,8,32,128]{3,2,1,0:T(8,128)}, f32[2,8,32,128]{3,2,1,0:T(8,128)S(1)}, u32[]{:S(2)}) copy-start(f32[2,8,32,128]{3,2,1,0:T(8,128)S(1)} %collective-permute-done.7.centre_ref) | copy-start | bytes 786436
  76.2 2.2 %copy-start.4 = (f32[2,10,32,128]{3,2,1,0:T(8,128)}, f32[2,10,32,128]{3,2,1,0:T(8,128)S(1)}, u32[]{:S(2)}) copy-start(f32[2,10,32,128]{3,2,1,0:T(8,128)S(1)} %collective-permute-done.10.before_ref) | copy-start | bytes 983044
  78.4 0.7 copy-start.6
  84.0 7.8 %collective-permute-start.12 = (f32[2,6,16,128]{3,2,1,0:T(8,128)}, f32[2,6,16,128]{3,2,1,0:T(8,128)S(1)}, u32[]{:S(2)}, u32[]{:S(2)}) collective-permute-start(f32[2,6,16,128]{3,2,1,0:T(8,128)} %get-tuple-element.76), channel_id=1, source_target_pairs={{0,1},{1,2},{2,3},{3,4},{4,5},{5,6},{6,7},{7,0},{8,9},{9,10},{10,1... | collective-permute-start | bytes 294920 | tf_op jit(solution)/shard_map/ppermute | solution.py:577
  85.6 7.9 %collective-permute-start.13 = (f32[2,6,16,128]{3,2,1,0:T(8,128)}, f32[2,6,16,128]{3,2,1,0:T(8,128)S(1)}, u32[]{:S(2)}, u32[]{:S(2)}) collective-permute-start(f32[2,6,16,128]{3,2,1,0:T(8,128)} %get-tuple-element.77), channel_id=1, source_target_pairs={{1,0},{2,1},{3,2},{4,3},{5,4},{6,5},{7,6},{0,7},{9,8},{10,9},{11,1... | collective-permute-start | bytes 294920 | tf_op jit(solution)/shard_map/ppermute | solution.py:578
  91.8 1.7 %copy-start.17 = (f32[2,6,16,128]{3,2,1,0:T(8,128)}, f32[2,6,16,128]{3,2,1,0:T(8,128)S(1)}, u32[]{:S(2)}) copy-start(f32[2,6,16,128]{3,2,1,0:T(8,128)S(1)} %collective-permute-done.12.cbefore_ref) | copy-start | bytes 294916
  93.5 0.6 copy-start.19
  98.7 22.0 %collective-permute-start.17 = (f32[2,10,32,128]{3,2,1,0:T(8,128)}, f32[2,10,32,128]{3,2,1,0:T(8,128)S(1)}, u32[]{:S(2)}, u32[]{:S(2)}) collective-permute-start(f32[2,10,32,128]{3,2,1,0:T(8,128)} %get-tuple-element.88), channel_id=1, source_target_pairs={{0,1},{1,2},{2,3},{3,4},{4,5},{5,6},{6,7},{7,0},{8,9},{9,10},{10,1... | collective-permute-start | bytes 983048 | tf_op jit(solution)/shard_map/ppermute | solution.py:601
  98.8 22.4 %collective-permute-start.18 = (f32[2,10,32,128]{3,2,1,0:T(8,128)}, f32[2,10,32,128]{3,2,1,0:T(8,128)S(1)}, u32[]{:S(2)}, u32[]{:S(2)}) collective-permute-start(f32[2,10,32,128]{3,2,1,0:T(8,128)} %get-tuple-element.89), channel_id=1, source_target_pairs={{1,0},{2,1},{3,2},{4,3},{5,4},{6,5},{7,6},{0,7},{9,8},{10,9},{11,1... | collective-permute-start | bytes 983048 | tf_op jit(solution)/shard_map/ppermute | solution.py:602
  103.5 17.2 %collective-permute-start.14 = (f32[2,8,32,128]{3,2,1,0:T(8,128)}, f32[2,8,32,128]{3,2,1,0:T(8,128)S(1)}, u32[]{:S(2)}, u32[]{:S(2)}) collective-permute-start(f32[2,8,32,128]{3,2,1,0:T(8,128)} %get-tuple-element.84), channel_id=1, source_target_pairs={{0,8},{1,9},{2,10},{3,11},{4,12},{5,13},{6,14},{7,15},{8,16},{9,17... | collective-permute-start | bytes 786440 | tf_op jit(solution)/shard_map/ppermute | solution.py:110
  105.4 15.3 %collective-permute-start.15 = (f32[2,5,32,128]{3,2,1,0:T(8,128)}, f32[2,5,32,128]{3,2,1,0:T(8,128)S(1)}, u32[]{:S(2)}, u32[]{:S(2)}) collective-permute-start(f32[2,5,32,128]{3,2,1,0:T(8,128)} %get-tuple-element.85), channel_id=1, source_target_pairs={{0,9},{1,10},{2,11},{3,12},{4,13},{5,14},{6,15},{7,8},{8,17},{9,18... | collective-permute-start | bytes 491528 | tf_op jit(solution)/shard_map/ppermute | solution.py:110
  107.3 13.3 %collective-permute-start.16 = (f32[2,5,32,128]{3,2,1,0:T(8,128)}, f32[2,5,32,128]{3,2,1,0:T(8,128)S(1)}, u32[]{:S(2)}, u32[]{:S(2)}) collective-permute-start(f32[2,5,32,128]{3,2,1,0:T(8,128)} %get-tuple-element.86), channel_id=1, source_target_pairs={{0,15},{1,8},{2,9},{3,10},{4,11},{5,12},{6,13},{7,14},{8,23},{9,16... | collective-permute-start | bytes 491528 | tf_op jit(solution)/shard_map/ppermute | solution.py:110
  120.7 0.7 copy-start.12
  120.7 0.7 copy-start.14
  120.7 0.8 copy-start.8
  120.7 0.9 copy-start.3
  121.2 0.7 copy-start.5
  126.8 6.8 %collective-permute-start.19 = (f32[2,2,16,128]{3,2,1,0:T(8,128)}, f32[2,2,16,128]{3,2,1,0:T(8,128)S(1)}, u32[]{:S(2)}, u32[]{:S(2)}) collective-permute-start(f32[2,2,16,128]{3,2,1,0:T(8,128)} %get-tuple-element.91), channel_id=1, source_target_pairs={{0,1},{1,2},{2,3},{3,4},{4,5},{5,6},{6,7},{7,0},{8,9},{9,10},{10,1... | collective-permute-start | bytes 98312 | tf_op jit(solution)/shard_map/ppermute | solution.py:577
  128.5 5.2 %collective-permute-start.20 = (f32[2,2,16,128]{3,2,1,0:T(8,128)}, f32[2,2,16,128]{3,2,1,0:T(8,128)S(1)}, u32[]{:S(2)}, u32[]{:S(2)}) collective-permute-start(f32[2,2,16,128]{3,2,1,0:T(8,128)} %get-tuple-element.92), channel_id=1, source_target_pairs={{1,0},{2,1},{3,2},{4,3},{5,4},{6,5},{7,6},{0,7},{9,8},{10,9},{11,1... | collective-permute-start | bytes 98312 | tf_op jit(solution)/shard_map/ppermute | solution.py:578
  133.7 0.6 copy-start.20
  133.7 0.6 copy-start.21

commit v9 on v8

--- a/solution.py
+++ b/solution.py
@@ -169,7 +169,7 @@
 
 
 def even_odd_load(ref, index=()):
-    view = ref.at[index] if index else ref
+    view = ref.at[index] if index != () else ref
     lead = (slice(None),) * (len(view.shape) - 2)
     half = view.shape[-2] // 2
     even = view[lead + (pl.ds(0, half, stride=2), slice(None))]
@@ -432,22 +432,32 @@
     )(*args)
 
 
-def start_kernel(diff_ref, stacked_ref, own_ref, before_ref, after_ref, rate_ref, csrc_ref,
-                 ext_ref, dec_ref, src_ref):
+def start_kernel(diff_ref, init_ref, decay_ref, source_ref, got_before_ref, got_after_ref,
+                 own_ref, before_ref, after_ref, rate_ref, csrc_ref, ext_ref, dec_ref, src_ref):
     spread_table, grouped_table, interp_table, widths = node_tables()
     rows = own_ref.shape[2]
-    hs = (stacked_ref.shape[2] - rows) // 2
+    hs = (ext_ref.shape[1] - rows) // 2
+    hd = hs - 1
     d0 = diff_ref[0]
     d1 = diff_ref[1]
-    state = even_odd_load(stacked_ref, (0,))
-    decay = even_odd_load(stacked_ref, (1,))
-    source = even_odd_load(stacked_ref, (2,))
+
+    def joined(ref, offset, w):
+        return jnp.concatenate(
+            [
+                even_odd_load(got_before_ref, (slice(None), pl.ds(offset, w))),
+                even_odd_load(ref),
+                even_odd_load(got_after_ref, (slice(None), pl.ds(offset, w))),
+            ],
+            axis=1,
+        )
+
+    state = joined(init_ref, 0, hs)
+    dec = joined(decay_ref, hs, hd)
+    s = joined(source_ref, hs + hd, hd)
     ext_ref[...] = state
-    dec_ref[...] = decay
-    src_ref[...] = source
+    dec_ref[...] = dec
+    src_ref[...] = s
     inner = state[:, 1:-1]
-    dec = decay[:, 1:-1]
-    s = source[:, 1:-1]
     laplace = kernel_laplace(state)
     product = inner[0] * inner[1] * inner[1]
     terms = jnp.stack([d0 * laplace[0] - product + s[0], d1 * laplace[1] + product + s[1]])
@@ -466,9 +476,13 @@
     csrc_ref[...] = kernel_restrict(s)
 
 
-def start_terms(diffusivity, stacked):
-    shape = stacked.shape[1:]
-    rows = shape[1] - 2 * START_HALO
+def start_terms(diffusivity, own_arrays, got_before, got_after):
+    own_shape = own_arrays[0].shape
+    rows = own_shape[1]
+    shape = (own_shape[0], rows + 2 * START_HALO) + own_shape[2:]
+    fixed = jax.ShapeDtypeStruct(
+        (own_shape[0], rows + 2 * (START_HALO - 1)) + own_shape[2:], jnp.float32
+    )
     sent = sum(START_HALO - 1 - m for m in range(4))
     edge = jax.ShapeDtypeStruct((shape[0], sent) + shape[2:], jnp.float32)
     cshape = (shape[0], (rows + 2 * (START_HALO - 1)) // 2, shape[2] // 2, shape[3])
@@ -480,12 +494,12 @@
             jax.ShapeDtypeStruct((4, shape[0], rows) + shape[2:], jnp.float32),
             edge, edge, coarse, coarse,
             jax.ShapeDtypeStruct(shape, jnp.float32),
-            jax.ShapeDtypeStruct(shape, jnp.float32),
-            jax.ShapeDtypeStruct(shape, jnp.float32),
+            fixed,
+            fixed,
         ),
-        in_specs=[pl.BlockSpec(memory_space=pltpu.SMEM)] + [vmem],
+        in_specs=[pl.BlockSpec(memory_space=pltpu.SMEM)] + [vmem] * 5,
         out_specs=(vmem,) * 8,
-    )(diffusivity, stacked)
+    )(diffusivity, *own_arrays, got_before, got_after)
 
 
 def packed_halo(fields):
@@ -527,12 +541,25 @@
     assert hs == 5 and initial.shape[-3] >= hs
 
     own_start = initial[0]
-    stacked = space_halo(jnp.stack([own_start, decay_rate, source]), hs)
+    size = lax.axis_size("space")
+    up = [(i, (i + 1) % size) for i in range(size)]
+    down = [((i + 1) % size, i) for i in range(size)]
+    rows = own_start.shape[-3]
+    widths_in = (hs, hs - 1, hs - 1)
+    own_arrays = (own_start, decay_rate, source)
+    got_before = lax.ppermute(
+        jnp.concatenate([a[:, rows - w:] for a, w in zip(own_arrays, widths_in)], axis=1),
+        "space", up,
+    )
+    got_after = lax.ppermute(
+        jnp.concatenate([a[:, :w] for a, w in zip(own_arrays, widths_in)], axis=1),
+        "space", down,
+    )
     own4, before4, after4, rate_own, csrc_own, own_ext, dec_ext, src_ext = start_terms(
-        diffusivity, stacked
-    )
-    decay = (dec_ext, hs)
-    src = (src_ext, hs)
+        diffusivity, own_arrays, got_before, got_after
+    )
+    decay = (dec_ext, hs - 1)
+    src = (src_ext, hs - 1)
     rate_c = (rate_own, (hs - 1) // 2)
     source_c = (csrc_own, (hs - 1) // 2)
 

time: 138 us -> 135 us (0.978)
  other arithmetic: 2.73 us -> 0.06 us
  waiting for transfers between devices: 53 us -> 50.7 us
    ppermute x2, waiting for transfers between devices: 18.7 us -> 16.6 us  [the longest x1 14.3 us: per_device(): lax.ppermute(jnp.concatenate([a[:, rows - w:] for a, w in zip(own_arrays,...]
    concatenate x1 -> x2, other arithmetic: 1.47 us -> 0.06 us  [the longest x1 0.03 us: per_device(): jnp.concatenate([a[:, rows - w:] for a, w in zip(own_arrays, widths_in)],...]
    unnamed x44 -> x48, local copies, waits for them, and re-layouts: 4.15 us -> 5.07 us
  transfers between devices with their start and end apart: 21 -> 21, of which waited for: 11 -> 10; matrix products, arithmetic and copies ran while one was open for 2% -> 0% of each run, Pallas kernels for 3% -> 3%
where the time goes in v9:
time: 135 us; the launch traced here: 133 us
  waiting for transfers between devices  50.7 us (38%)
  starting transfers between devices  45.9 us (34%)
  Pallas kernels  30.1 us (22%)
  local copies, waits for them, and re-layouts  6.18 us (5%)
    ppermute x9, waiting for transfers between devices, moved(): return lax.ppermute(piece, axes, pairs)  21.7 us
    ppermute x9, starting transfers between devices, moved(): return lax.ppermute(piece, axes, pairs)  17.3 us
    pallas_call x3, Pallas kernels, fine_sweep(): pl.pallas_call(functools.partial(sweep_kernel, widths_sent, natural_prior...  14.5 us
    ppermute x1, waiting for transfers between devices, per_device(): lax.ppermute(jnp.concatenate([a[:, rows - w:] for a, w in zip(own_arrays,...  14.3 us
    pallas_call x3, Pallas kernels, finish_round(): pl.pallas_call(functools.partial(finish_kernel, widths_sent), out_shape=o...  11.9 us
    ppermute x3, starting transfers between devices, advance(): lax.ppermute(cfirsts, 'space', down)  9.92 us
    ppermute x2, starting transfers between devices, per_device(): lax.ppermute(firsts, 'space', down)  8.75 us
    ppermute x3, waiting for transfers between devices, advance(): lax.ppermute(clasts, 'space', up)  8.12 us
  transfers between devices with their start and end apart: 21, of which 10 were waited for; matrix products, arithmetic and copies ran while one was open for 0% of the time, Pallas kernels for 3%

profile of v9, /device:TPU:2, one launch (start us, length us, event | category | flops | bytes accessed | tf_op | source)
XLA Modules:
  0.0 133.3 jit_solution(8729927266939691842)
XLA Ops:
  0.0 1.1 fusion
  1.3 1.6 %collective-permute-start = (f32[2,13,32,128]{3,2,1,0:T(8,128)S(1)}, f32[2,13,32,128]{3,2,1,0:T(8,128)S(1)}, u32[]{:S(2)}, u32[]{:S(2)}) collective-permute-start(f32[2,13,32,128]{3,2,1,0:T(8,128)S(1)} %pad_maximum_fusion), channel_id=1, source_target_pairs={{0,1},{1,2},{2,3},{3,4},{4,5},{5,6},{6,7},{7,0},{8,9},{9,10},{10,1... | collective-permute-start | bytes 1277960 | tf_op jit(solution)/shard_map/ppermute | solution.py:550
  2.9 3.3 %collective-permute-start.1 = (f32[2,13,32,128]{3,2,1,0:T(8,128)S(1)}, f32[2,13,32,128]{3,2,1,0:T(8,128)S(1)}, u32[]{:S(2)}, u32[]{:S(2)}) collective-permute-start(f32[2,13,32,128]{3,2,1,0:T(8,128)S(1)} %pad_maximum_fusion.1), channel_id=1, source_target_pairs={{1,0},{2,1},{3,2},{4,3},{5,4},{6,5},{7,6},{0,7},{9,8},{10,9},{11,1... | collective-permute-start | bytes 1277960 | tf_op jit(solution)/shard_map/ppermute | solution.py:554
  6.1 1.9 %collective-permute-start.2 = (f32[2,8,32,128]{3,2,1,0:T(8,128)S(1)}, f32[2,8,32,128]{3,2,1,0:T(8,128)S(1)}, u32[]{:S(2)}, u32[]{:S(2)}) collective-permute-start(f32[2,8,32,128]{3,2,1,0:T(8,128)S(1)} %bitcast.5), channel_id=1, source_target_pairs={{0,8},{1,9},{2,10},{3,11},{4,12},{5,13},{6,14},{7,15},{8,16},{9,17... | collective-permute-start | bytes 786440 | tf_op jit(solution)/shard_map/ppermute | solution.py:110
  8.0 2.0 %collective-permute-start.4 = (f32[2,5,32,128]{3,2,1,0:T(8,128)S(1)}, f32[2,5,32,128]{3,2,1,0:T(8,128)S(1)}, u32[]{:S(2)}, u32[]{:S(2)}) collective-permute-start(f32[2,5,32,128]{3,2,1,0:T(8,128)S(1)} %get-tuple-element.99), channel_id=1, source_target_pairs={{0,15},{1,8},{2,9},{3,10},{4,11},{5,12},{6,13},{7,14},{8,23},{9,16... | collective-permute-start | bytes 491528 | tf_op jit(solution)/shard_map/ppermute | solution.py:110
  10.1 1.9 %collective-permute-start.3 = (f32[2,5,32,128]{3,2,1,0:T(8,128)S(1)}, f32[2,5,32,128]{3,2,1,0:T(8,128)S(1)}, u32[]{:S(2)}, u32[]{:S(2)}) collective-permute-start(f32[2,5,32,128]{3,2,1,0:T(8,128)S(1)} %get-tuple-element.100), channel_id=1, source_target_pairs={{0,9},{1,10},{2,11},{3,12},{4,13},{5,14},{6,15},{7,8},{8,17},{9,18... | collective-permute-start | bytes 491528 | tf_op jit(solution)/shard_map/ppermute | solution.py:110
  12.0 14.3 %collective-permute-done.got_before_ref = f32[2,13,32,128]{3,2,1,0:T(8,128)S(1)} collective-permute-done((f32[2,13,32,128]{3,2,1,0:T(8,128)S(1)}, f32[2,13,32,128]{3,2,1,0:T(8,128)S(1)}, u32[]{:S(2)}, u32[]{:S(2)}) %collective-permute-start) | collective-permute-done | bytes 426016 | tf_op jit(solution)/shard_map/ppermute | solution.py:550
  26.3 2.3 %collective-permute-done.1.got_after_ref = f32[2,13,32,128]{3,2,1,0:T(8,128)S(1)} collective-permute-done((f32[2,13,32,128]{3,2,1,0:T(8,128)S(1)}, f32[2,13,32,128]{3,2,1,0:T(8,128)S(1)}, u32[]{:S(2)}, u32[]{:S(2)}) %collective-permute-start.1) | collective-permute-done | bytes 426016 | tf_op jit(solution)/shard_map/ppermute | solution.py:554
  28.6 0.8 copy-done.4
  29.4 3.7 %shard_map.46 = (f32[4,2,8,32,128]{4,3,2,1,0:T(8,128)}, f32[2,10,32,128]{3,2,1,0:T(8,128)}, f32[2,10,32,128]{3,2,1,0:T(8,128)}, f32[2,8,16,128]{3,2,1,0:T(8,128)...) custom-call(f32[2]{0:T(128)} %diff_ref.13, ...), custom_call_target="tpu_custom_call" | custom-call | tf_op jit(solution)/shard_map/pallas_call | solution.py:491
  33.1 0.6 copy-done.12
  33.8 0.1 copy-done.9
  33.8 4.8 %shard_map.47 = (f32[2,10,32,128]{3,2,1,0:T(8,128)}, f32[2,10,32,128]{3,2,1,0:T(8,128)}, f32[2,10,32,128]{3,2,1,0:T(8,128)}, f32[2,10,32,128]{3,2,1,0:T(8,128)},...) custom-call(f32[2]{0:T(128)} %diff_ref.13, ...), custom_call_target="tpu_custom_call" | custom-call | tf_op jit(solution)/shard_map/pallas_call | solution.py:298
  38.7 0.9 collective-permute-start.5
  39.6 3.8 %collective-permute-start.6 = (f32[2,6,16,128]{3,2,1,0:T(8,128)}, f32[2,6,16,128]{3,2,1,0:T(8,128)S(1)}, u32[]{:S(2)}, u32[]{:S(2)}) collective-permute-start(f32[2,6,16,128]{3,2,1,0:T(8,128)} %get-tuple-element.61), channel_id=1, source_target_pairs={{1,0},{2,1},{3,2},{4,3},{5,4},{6,5},{7,6},{0,7},{9,8},{10,9},{11,1... | collective-permute-start | bytes 294920 | tf_op jit(solution)/shard_map/ppermute | solution.py:605
  43.4 2.9 %collective-permute-done.5.cbefore_ref = f32[2,6,16,128]{3,2,1,0:T(8,128)S(1)} collective-permute-done((f32[2,6,16,128]{3,2,1,0:T(8,128)}, f32[2,6,16,128]{3,2,1,0:T(8,128)S(1)}, u32[]{:S(2)}, u32[]{:S(2)}) %collective-permute-start.5) | collective-permute-done | bytes 98336 | tf_op jit(solution)/shard_map/ppermute | solution.py:604
  46.3 0.6 copy-done.18
  47.0 4.5 %shard_map.48 = (f32[4,2,8,32,128]{4,3,2,1,0:T(8,128)}, f32[2,10,32,128]{3,2,1,0:T(8,128)}, f32[2,10,32,128]{3,2,1,0:T(8,128)}, f32[2,8,32,128]{3,2,1,0:T(8,128)...) custom-call(f32[2]{0:T(128)} %diff_ref.13, f32[4,2,4,16,128]{4,3,2,1,0:T(8,128)} %get-tuple-element.59.cown_ref, ...), custom_call_target="tpu_custom_call" | custom-call | tf_op jit(solution)/shard_map/pallas_call | solution.py:427
  51.5 0.7 collective-permute-start.10
  52.2 4.0 %collective-permute-start.11 = (f32[2,10,32,128]{3,2,1,0:T(8,128)}, f32[2,10,32,128]{3,2,1,0:T(8,128)S(1)}, u32[]{:S(2)}, u32[]{:S(2)}) collective-permute-start(f32[2,10,32,128]{3,2,1,0:T(8,128)} %get-tuple-element.74), channel_id=1, source_target_pairs={{1,0},{2,1},{3,2},{4,3},{5,4},{6,5},{7,6},{0,7},{9,8},{10,9},{11,1... | collective-permute-start | bytes 983048 | tf_op jit(solution)/shard_map/ppermute | solution.py:629
  56.3 1.9 %collective-permute-start.7 = (f32[2,8,32,128]{3,2,1,0:T(8,128)}, f32[2,8,32,128]{3,2,1,0:T(8,128)S(1)}, u32[]{:S(2)}, u32[]{:S(2)}) collective-permute-start(f32[2,8,32,128]{3,2,1,0:T(8,128)} %get-tuple-element.69), channel_id=1, source_target_pairs={{0,8},{1,9},{2,10},{3,11},{4,12},{5,13},{6,14},{7,15},{8,16},{9,17... | collective-permute-start | bytes 786440 | tf_op jit(solution)/shard_map/ppermute | solution.py:110
  58.2 1.9 %collective-permute-start.8 = (f32[2,5,32,128]{3,2,1,0:T(8,128)}, f32[2,5,32,128]{3,2,1,0:T(8,128)S(1)}, u32[]{:S(2)}, u32[]{:S(2)}) collective-permute-start(f32[2,5,32,128]{3,2,1,0:T(8,128)} %get-tuple-element.70), channel_id=1, source_target_pairs={{0,9},{1,10},{2,11},{3,12},{4,13},{5,14},{6,15},{7,8},{8,17},{9,18... | collective-permute-start | bytes 491528 | tf_op jit(solution)/shard_map/ppermute | solution.py:110
  60.1 1.9 %collective-permute-start.9 = (f32[2,5,32,128]{3,2,1,0:T(8,128)}, f32[2,5,32,128]{3,2,1,0:T(8,128)S(1)}, u32[]{:S(2)}, u32[]{:S(2)}) collective-permute-start(f32[2,5,32,128]{3,2,1,0:T(8,128)} %get-tuple-element.71), channel_id=1, source_target_pairs={{0,15},{1,8},{2,9},{3,10},{4,11},{5,12},{6,13},{7,14},{8,23},{9,16... | collective-permute-start | bytes 491528 | tf_op jit(solution)/shard_map/ppermute | solution.py:110
  62.1 10.3 %collective-permute-done.8.bbefore_ref = f32[2,5,32,128]{3,2,1,0:T(8,128)S(1)} collective-permute-done((f32[2,5,32,128]{3,2,1,0:T(8,128)}, f32[2,5,32,128]{3,2,1,0:T(8,128)S(1)}, u32[]{:S(2)}, u32[]{:S(2)}) %collective-permute-start.8) | collective-permute-done | bytes 163872 | tf_op jit(solution)/shard_map/ppermute | solution.py:110
  72.4 2.2 %collective-permute-done.11.after_ref = f32[2,10,32,128]{3,2,1,0:T(8,128)S(1)} collective-permute-done((f32[2,10,32,128]{3,2,1,0:T(8,128)}, f32[2,10,32,128]{3,2,1,0:T(8,128)S(1)}, u32[]{:S(2)}, u32[]{:S(2)}) %collective-permute-start.11) | collective-permute-done | bytes 327712 | tf_op jit(solution)/shard_map/ppermute | solution.py:629
  74.6 0.7 copy-done.8
  75.3 4.8 %shard_map.49 = (f32[2,10,32,128]{3,2,1,0:T(8,128)}, f32[2,10,32,128]{3,2,1,0:T(8,128)}, f32[2,10,32,128]{3,2,1,0:T(8,128)}, f32[2,10,32,128]{3,2,1,0:T(8,128)},...) custom-call(f32[2]{0:T(128)} %diff_ref.13, ...), custom_call_target="tpu_custom_call" | custom-call | tf_op jit(solution)/shard_map/pallas_call | solution.py:298
  80.1 1.7 %collective-permute-start.12 = (f32[2,6,16,128]{3,2,1,0:T(8,128)}, f32[2,6,16,128]{3,2,1,0:T(8,128)S(1)}, u32[]{:S(2)}, u32[]{:S(2)}) collective-permute-start(f32[2,6,16,128]{3,2,1,0:T(8,128)} %get-tuple-element.76), channel_id=1, source_target_pairs={{0,1},{1,2},{2,3},{3,4},{4,5},{5,6},{6,7},{7,0},{8,9},{9,10},{10,1... | collective-permute-start | bytes 294920 | tf_op jit(solution)/shard_map/ppermute | solution.py:604
  81.8 3.1 %collective-permute-start.13 = (f32[2,6,16,128]{3,2,1,0:T(8,128)}, f32[2,6,16,128]{3,2,1,0:T(8,128)S(1)}, u32[]{:S(2)}, u32[]{:S(2)}) collective-permute-start(f32[2,6,16,128]{3,2,1,0:T(8,128)} %get-tuple-element.77), channel_id=1, source_target_pairs={{1,0},{2,1},{3,2},{4,3},{5,4},{6,5},{7,6},{0,7},{9,8},{10,9},{11,1... | collective-permute-start | bytes 294920 | tf_op jit(solution)/shard_map/ppermute | solution.py:605
  84.8 3.1 %collective-permute-done.12.cbefore_ref = f32[2,6,16,128]{3,2,1,0:T(8,128)S(1)} collective-permute-done((f32[2,6,16,128]{3,2,1,0:T(8,128)}, f32[2,6,16,128]{3,2,1,0:T(8,128)S(1)}, u32[]{:S(2)}, u32[]{:S(2)}) %collective-permute-start.12) | collective-permute-done | bytes 98336 | tf_op jit(solution)/shard_map/ppermute | solution.py:604
  87.9 1.7 %collective-permute-done.13.cafter_ref = f32[2,6,16,128]{3,2,1,0:T(8,128)S(1)} collective-permute-done((f32[2,6,16,128]{3,2,1,0:T(8,128)}, f32[2,6,16,128]{3,2,1,0:T(8,128)S(1)}, u32[]{:S(2)}, u32[]{:S(2)}) %collective-permute-start.13) | collective-permute-done | bytes 98336 | tf_op jit(solution)/shard_map/ppermute | solution.py:605
  89.6 0.6 copy-done.21
  90.2 4.5 %shard_map.50 = (f32[4,2,8,32,128]{4,3,2,1,0:T(8,128)}, f32[2,10,32,128]{3,2,1,0:T(8,128)}, f32[2,10,32,128]{3,2,1,0:T(8,128)}, f32[2,8,32,128]{3,2,1,0:T(8,128)...) custom-call(f32[2]{0:T(128)} %diff_ref.13, f32[4,2,4,16,128]{4,3,2,1,0:T(8,128)} %get-tuple-element.75.cown_ref, ...), custom_call_target="tpu_custom_call" | custom-call | tf_op jit(solution)/shard_map/pallas_call | solution.py:427
  94.8 4.7 %collective-permute-start.18 = (f32[2,10,32,128]{3,2,1,0:T(8,128)}, f32[2,10,32,128]{3,2,1,0:T(8,128)S(1)}, u32[]{:S(2)}, u32[]{:S(2)}) collective-permute-start(f32[2,10,32,128]{3,2,1,0:T(8,128)} %get-tuple-element.89), channel_id=1, source_target_pairs={{1,0},{2,1},{3,2},{4,3},{5,4},{6,5},{7,6},{0,7},{9,8},{10,9},{11,1... | collective-permute-start | bytes 983048 | tf_op jit(solution)/shard_map/ppermute | solution.py:629
  99.5 1.9 %collective-permute-start.14 = (f32[2,8,32,128]{3,2,1,0:T(8,128)}, f32[2,8,32,128]{3,2,1,0:T(8,128)S(1)}, u32[]{:S(2)}, u32[]{:S(2)}) collective-permute-start(f32[2,8,32,128]{3,2,1,0:T(8,128)} %get-tuple-element.84), channel_id=1, source_target_pairs={{0,8},{1,9},{2,10},{3,11},{4,12},{5,13},{6,14},{7,15},{8,16},{9,17... | collective-permute-start | bytes 786440 | tf_op jit(solution)/shard_map/ppermute | solution.py:110
  101.5 1.9 %collective-permute-start.15 = (f32[2,5,32,128]{3,2,1,0:T(8,128)}, f32[2,5,32,128]{3,2,1,0:T(8,128)S(1)}, u32[]{:S(2)}, u32[]{:S(2)}) collective-permute-start(f32[2,5,32,128]{3,2,1,0:T(8,128)} %get-tuple-element.85), channel_id=1, source_target_pairs={{0,9},{1,10},{2,11},{3,12},{4,13},{5,14},{6,15},{7,8},{8,17},{9,18... | collective-permute-start | bytes 491528 | tf_op jit(solution)/shard_map/ppermute | solution.py:110
  103.4 1.9 %collective-permute-start.16 = (f32[2,5,32,128]{3,2,1,0:T(8,128)}, f32[2,5,32,128]{3,2,1,0:T(8,128)S(1)}, u32[]{:S(2)}, u32[]{:S(2)}) collective-permute-start(f32[2,5,32,128]{3,2,1,0:T(8,128)} %get-tuple-element.86), channel_id=1, source_target_pairs={{0,15},{1,8},{2,9},{3,10},{4,11},{5,12},{6,13},{7,14},{8,23},{9,16... | collective-permute-start | bytes 491528 | tf_op jit(solution)/shard_map/ppermute | solution.py:110
  105.3 11.4 %collective-permute-done.15.bbefore_ref = f32[2,5,32,128]{3,2,1,0:T(8,128)S(1)} collective-permute-done((f32[2,5,32,128]{3,2,1,0:T(8,128)}, f32[2,5,32,128]{3,2,1,0:T(8,128)S(1)}, u32[]{:S(2)}, u32[]{:S(2)}) %collective-permute-start.15) | collective-permute-done | bytes 163872 | tf_op jit(solution)/shard_map/ppermute | solution.py:110
  116.8 0.5 collective-permute-done.18.after_ref
  117.4 0.1 copy-done.10
  117.5 0.1 copy-done.5
  117.6 0.4 copy-done.7
  118.1 4.9 %shard_map.51 = (f32[2,10,32,128]{3,2,1,0:T(8,128)}, f32[2,10,32,128]{3,2,1,0:T(8,128)}, f32[2,10,32,128]{3,2,1,0:T(8,128)}, f32[2,10,32,128]{3,2,1,0:T(8,128)},...) custom-call(f32[2]{0:T(128)} %diff_ref.13, ...), custom_call_target="tpu_custom_call" | custom-call | tf_op jit(solution)/shard_map/pallas_call | solution.py:298
  123.0 1.7 %collective-permute-start.19 = (f32[2,2,16,128]{3,2,1,0:T(8,128)}, f32[2,2,16,128]{3,2,1,0:T(8,128)S(1)}, u32[]{:S(2)}, u32[]{:S(2)}) collective-permute-start(f32[2,2,16,128]{3,2,1,0:T(8,128)} %get-tuple-element.91), channel_id=1, source_target_pairs={{0,1},{1,2},{2,3},{3,4},{4,5},{5,6},{6,7},{7,0},{8,9},{9,10},{10,1... | collective-permute-start | bytes 98312 | tf_op jit(solution)/shard_map/ppermute | solution.py:604
  124.6 3.1 %collective-permute-start.20 = (f32[2,2,16,128]{3,2,1,0:T(8,128)}, f32[2,2,16,128]{3,2,1,0:T(8,128)S(1)}, u32[]{:S(2)}, u32[]{:S(2)}) collective-permute-start(f32[2,2,16,128]{3,2,1,0:T(8,128)} %get-tuple-element.92), channel_id=1, source_target_pairs={{1,0},{2,1},{3,2},{4,3},{5,4},{6,5},{7,6},{0,7},{9,8},{10,9},{11,1... | collective-permute-start | bytes 98312 | tf_op jit(solution)/shard_map/ppermute | solution.py:605
  127.7 2.1 %collective-permute-done.19.cbefore_ref = f32[2,2,16,128]{3,2,1,0:T(8,128)S(1)} collective-permute-done((f32[2,2,16,128]{3,2,1,0:T(8,128)}, f32[2,2,16,128]{3,2,1,0:T(8,128)S(1)}, u32[]{:S(2)}, u32[]{:S(2)}) %collective-permute-start.19) | collective-permute-done | bytes 32800 | tf_op jit(solution)/shard_map/ppermute | solution.py:604
  129.8 0.6 copy-done.22
  130.4 2.9 %shard_map.52 = f32[2,8,32,128]{3,2,1,0:T(8,128)} custom-call(f32[2]{0:T(128)} %diff_ref.13, f32[4,2,4,16,128]{4,3,2,1,0:T(8,128)} %get-tuple-element.90.cown_ref, f32[2,2,16,128]{3,2,1,0:T(8,128)} %copy-done.22, f32[2,2,16,128]{3,2,1,0:T(8,128)} %copy-done.23, f32[2,8,16,128]{3,2,1,0:T(8,128)} %get-tuple-element.58.rate_ref, ...), custom_call_target="tpu_custom_call" | custom-call | tf_op jit(solution)/shard_map/pallas_call | solution.py:427
  (53 shorter events, 0.6 us)
Async XLA Ops:
  0.0 1.1 copy-start.1
  0.0 1.2 copy-start.2
  1.3 25.0 %collective-permute-start = (f32[2,13,32,128]{3,2,1,0:T(8,128)S(1)}, f32[2,13,32,128]{3,2,1,0:T(8,128)S(1)}, u32[]{:S(2)}, u32[]{:S(2)}) collective-permute-start(f32[2,13,32,128]{3,2,1,0:T(8,128)S(1)} %pad_maximum_fusion), channel_id=1, source_target_pairs={{0,1},{1,2},{2,3},{3,4},{4,5},{5,6},{6,7},{7,0},{8,9},{9,10},{10,1... | collective-permute-start | bytes 1277960 | tf_op jit(solution)/shard_map/ppermute | solution.py:550
  2.8 3.3 %copy-start = (f32[1,2,8,32,128]{4,3,2,1,0:T(8,128)S(1)}, f32[1,2,8,32,128]{4,3,2,1,0:T(8,128)}, u32[]{:S(2)}) copy-start(f32[1,2,8,32,128]{4,3,2,1,0:T(8,128)} %param.4) | copy-start | bytes 786436
  2.9 25.7 %collective-permute-start.1 = (f32[2,13,32,128]{3,2,1,0:T(8,128)S(1)}, f32[2,13,32,128]{3,2,1,0:T(8,128)S(1)}, u32[]{:S(2)}, u32[]{:S(2)}) collective-permute-start(f32[2,13,32,128]{3,2,1,0:T(8,128)S(1)} %pad_maximum_fusion.1), channel_id=1, source_target_pairs={{1,0},{2,1},{3,2},{4,3},{5,4},{6,5},{7,6},{0,7},{9,8},{10,9},{11,1... | collective-permute-start | bytes 1277960 | tf_op jit(solution)/shard_map/ppermute | solution.py:554
  6.1 26.9 %collective-permute-start.2 = (f32[2,8,32,128]{3,2,1,0:T(8,128)S(1)}, f32[2,8,32,128]{3,2,1,0:T(8,128)S(1)}, u32[]{:S(2)}, u32[]{:S(2)}) collective-permute-start(f32[2,8,32,128]{3,2,1,0:T(8,128)S(1)} %bitcast.5), channel_id=1, source_target_pairs={{0,8},{1,9},{2,10},{3,11},{4,12},{5,13},{6,14},{7,15},{8,16},{9,17... | collective-permute-start | bytes 786440 | tf_op jit(solution)/shard_map/ppermute | solution.py:110
  8.0 25.0 %collective-permute-start.4 = (f32[2,5,32,128]{3,2,1,0:T(8,128)S(1)}, f32[2,5,32,128]{3,2,1,0:T(8,128)S(1)}, u32[]{:S(2)}, u32[]{:S(2)}) collective-permute-start(f32[2,5,32,128]{3,2,1,0:T(8,128)S(1)} %get-tuple-element.99), channel_id=1, source_target_pairs={{0,15},{1,8},{2,9},{3,10},{4,11},{5,12},{6,13},{7,14},{8,23},{9,16... | collective-permute-start | bytes 491528 | tf_op jit(solution)/shard_map/ppermute | solution.py:110
  10.1 23.0 %collective-permute-start.3 = (f32[2,5,32,128]{3,2,1,0:T(8,128)S(1)}, f32[2,5,32,128]{3,2,1,0:T(8,128)S(1)}, u32[]{:S(2)}, u32[]{:S(2)}) collective-permute-start(f32[2,5,32,128]{3,2,1,0:T(8,128)S(1)} %get-tuple-element.100), channel_id=1, source_target_pairs={{0,9},{1,10},{2,11},{3,12},{4,13},{5,14},{6,15},{7,8},{8,17},{9,18... | collective-permute-start | bytes 491528 | tf_op jit(solution)/shard_map/ppermute | solution.py:110
  26.3 2.3 %copy-start.3 = (f32[2,13,32,128]{3,2,1,0:T(8,128)}, f32[2,13,32,128]{3,2,1,0:T(8,128)S(1)}, u32[]{:S(2)}) copy-start(f32[2,13,32,128]{3,2,1,0:T(8,128)S(1)} %collective-permute-done.got_before_ref) | copy-start | bytes 1277956
  28.6 0.8 copy-start.4
  33.0 0.7 copy-start.12
  33.1 0.7 copy-start.13
  33.1 0.8 copy-start.9
  38.7 7.6 %collective-permute-start.5 = (f32[2,6,16,128]{3,2,1,0:T(8,128)}, f32[2,6,16,128]{3,2,1,0:T(8,128)S(1)}, u32[]{:S(2)}, u32[]{:S(2)}) collective-permute-start(f32[2,6,16,128]{3,2,1,0:T(8,128)} %get-tuple-element.60), channel_id=1, source_target_pairs={{0,1},{1,2},{2,3},{3,4},{4,5},{5,6},{6,7},{7,0},{8,9},{9,10},{10,1... | collective-permute-start | bytes 294920 | tf_op jit(solution)/shard_map/ppermute | solution.py:604
  39.6 6.7 %collective-permute-start.6 = (f32[2,6,16,128]{3,2,1,0:T(8,128)}, f32[2,6,16,128]{3,2,1,0:T(8,128)S(1)}, u32[]{:S(2)}, u32[]{:S(2)}) collective-permute-start(f32[2,6,16,128]{3,2,1,0:T(8,128)} %get-tuple-element.61), channel_id=1, source_target_pairs={{1,0},{2,1},{3,2},{4,3},{5,4},{6,5},{7,6},{0,7},{9,8},{10,9},{11,1... | collective-permute-start | bytes 294920 | tf_op jit(solution)/shard_map/ppermute | solution.py:605
  46.3 0.6 copy-start.18
  46.3 0.7 copy-start.20
  51.5 20.8 %collective-permute-start.10 = (f32[2,10,32,128]{3,2,1,0:T(8,128)}, f32[2,10,32,128]{3,2,1,0:T(8,128)S(1)}, u32[]{:S(2)}, u32[]{:S(2)}) collective-permute-start(f32[2,10,32,128]{3,2,1,0:T(8,128)} %get-tuple-element.73), channel_id=1, source_target_pairs={{0,1},{1,2},{2,3},{3,4},{4,5},{5,6},{6,7},{7,0},{8,9},{9,10},{10,1... | collective-permute-start | bytes 983048 | tf_op jit(solution)/shard_map/ppermute | solution.py:628
  52.2 22.3 %collective-permute-start.11 = (f32[2,10,32,128]{3,2,1,0:T(8,128)}, f32[2,10,32,128]{3,2,1,0:T(8,128)S(1)}, u32[]{:S(2)}, u32[]{:S(2)}) collective-permute-start(f32[2,10,32,128]{3,2,1,0:T(8,128)} %get-tuple-element.74), channel_id=1, source_target_pairs={{1,0},{2,1},{3,2},{4,3},{5,4},{6,5},{7,6},{0,7},{9,8},{10,9},{11,1... | collective-permute-start | bytes 983048 | tf_op jit(solution)/shard_map/ppermute | solution.py:629
  56.3 16.0 %collective-permute-start.7 = (f32[2,8,32,128]{3,2,1,0:T(8,128)}, f32[2,8,32,128]{3,2,1,0:T(8,128)S(1)}, u32[]{:S(2)}, u32[]{:S(2)}) collective-permute-start(f32[2,8,32,128]{3,2,1,0:T(8,128)} %get-tuple-element.69), channel_id=1, source_target_pairs={{0,8},{1,9},{2,10},{3,11},{4,12},{5,13},{6,14},{7,15},{8,16},{9,17... | collective-permute-start | bytes 786440 | tf_op jit(solution)/shard_map/ppermute | solution.py:110
  58.2 14.1 %collective-permute-start.8 = (f32[2,5,32,128]{3,2,1,0:T(8,128)}, f32[2,5,32,128]{3,2,1,0:T(8,128)S(1)}, u32[]{:S(2)}, u32[]{:S(2)}) collective-permute-start(f32[2,5,32,128]{3,2,1,0:T(8,128)} %get-tuple-element.70), channel_id=1, source_target_pairs={{0,9},{1,10},{2,11},{3,12},{4,13},{5,14},{6,15},{7,8},{8,17},{9,18... | collective-permute-start | bytes 491528 | tf_op jit(solution)/shard_map/ppermute | solution.py:110
  60.1 12.2 %collective-permute-start.9 = (f32[2,5,32,128]{3,2,1,0:T(8,128)}, f32[2,5,32,128]{3,2,1,0:T(8,128)S(1)}, u32[]{:S(2)}, u32[]{:S(2)}) collective-permute-start(f32[2,5,32,128]{3,2,1,0:T(8,128)} %get-tuple-element.71), channel_id=1, source_target_pairs={{0,15},{1,8},{2,9},{3,10},{4,11},{5,12},{6,13},{7,14},{8,23},{9,16... | collective-permute-start | bytes 491528 | tf_op jit(solution)/shard_map/ppermute | solution.py:110
  72.3 2.2 %copy-start.15 = (f32[2,5,32,128]{3,2,1,0:T(8,128)}, f32[2,5,32,128]{3,2,1,0:T(8,128)S(1)}, u32[]{:S(2)}) copy-start(f32[2,5,32,128]{3,2,1,0:T(8,128)S(1)} %collective-permute-done.8.bbefore_ref) | copy-start | bytes 491524
  72.3 2.2 %copy-start.17 = (f32[2,5,32,128]{3,2,1,0:T(8,128)}, f32[2,5,32,128]{3,2,1,0:T(8,128)S(1)}, u32[]{:S(2)}) copy-start(f32[2,5,32,128]{3,2,1,0:T(8,128)S(1)} %collective-permute-done.9.bafter_ref) | copy-start | bytes 491524
  72.3 2.2 %copy-start.11 = (f32[2,8,32,128]{3,2,1,0:T(8,128)}, f32[2,8,32,128]{3,2,1,0:T(8,128)S(1)}, u32[]{:S(2)}) copy-start(f32[2,8,32,128]{3,2,1,0:T(8,128)S(1)} %collective-permute-done.7.centre_ref) | copy-start | bytes 786436
  72.4 2.2 %copy-start.6 = (f32[2,10,32,128]{3,2,1,0:T(8,128)}, f32[2,10,32,128]{3,2,1,0:T(8,128)S(1)}, u32[]{:S(2)}) copy-start(f32[2,10,32,128]{3,2,1,0:T(8,128)S(1)} %collective-permute-done.10.before_ref) | copy-start | bytes 983044
  74.5 0.7 copy-start.8
  80.1 7.8 %collective-permute-start.12 = (f32[2,6,16,128]{3,2,1,0:T(8,128)}, f32[2,6,16,128]{3,2,1,0:T(8,128)S(1)}, u32[]{:S(2)}, u32[]{:S(2)}) collective-permute-start(f32[2,6,16,128]{3,2,1,0:T(8,128)} %get-tuple-element.76), channel_id=1, source_target_pairs={{0,1},{1,2},{2,3},{3,4},{4,5},{5,6},{6,7},{7,0},{8,9},{9,10},{10,1... | collective-permute-start | bytes 294920 | tf_op jit(solution)/shard_map/ppermute | solution.py:604
  81.8 7.8 %collective-permute-start.13 = (f32[2,6,16,128]{3,2,1,0:T(8,128)}, f32[2,6,16,128]{3,2,1,0:T(8,128)S(1)}, u32[]{:S(2)}, u32[]{:S(2)}) collective-permute-start(f32[2,6,16,128]{3,2,1,0:T(8,128)} %get-tuple-element.77), channel_id=1, source_target_pairs={{1,0},{2,1},{3,2},{4,3},{5,4},{6,5},{7,6},{0,7},{9,8},{10,9},{11,1... | collective-permute-start | bytes 294920 | tf_op jit(solution)/shard_map/ppermute | solution.py:605
  87.9 1.7 %copy-start.19 = (f32[2,6,16,128]{3,2,1,0:T(8,128)}, f32[2,6,16,128]{3,2,1,0:T(8,128)S(1)}, u32[]{:S(2)}) copy-start(f32[2,6,16,128]{3,2,1,0:T(8,128)S(1)} %collective-permute-done.12.cbefore_ref) | copy-start | bytes 294916
  89.6 0.6 copy-start.21
  94.8 22.0 %collective-permute-start.17 = (f32[2,10,32,128]{3,2,1,0:T(8,128)}, f32[2,10,32,128]{3,2,1,0:T(8,128)S(1)}, u32[]{:S(2)}, u32[]{:S(2)}) collective-permute-start(f32[2,10,32,128]{3,2,1,0:T(8,128)} %get-tuple-element.88), channel_id=1, source_target_pairs={{0,1},{1,2},{2,3},{3,4},{4,5},{5,6},{6,7},{7,0},{8,9},{9,10},{10,1... | collective-permute-start | bytes 983048 | tf_op jit(solution)/shard_map/ppermute | solution.py:628
  94.8 22.5 %collective-permute-start.18 = (f32[2,10,32,128]{3,2,1,0:T(8,128)}, f32[2,10,32,128]{3,2,1,0:T(8,128)S(1)}, u32[]{:S(2)}, u32[]{:S(2)}) collective-permute-start(f32[2,10,32,128]{3,2,1,0:T(8,128)} %get-tuple-element.89), channel_id=1, source_target_pairs={{1,0},{2,1},{3,2},{4,3},{5,4},{6,5},{7,6},{0,7},{9,8},{10,9},{11,1... | collective-permute-start | bytes 983048 | tf_op jit(solution)/shard_map/ppermute | solution.py:629
  99.5 17.2 %collective-permute-start.14 = (f32[2,8,32,128]{3,2,1,0:T(8,128)}, f32[2,8,32,128]{3,2,1,0:T(8,128)S(1)}, u32[]{:S(2)}, u32[]{:S(2)}) collective-permute-start(f32[2,8,32,128]{3,2,1,0:T(8,128)} %get-tuple-element.84), channel_id=1, source_target_pairs={{0,8},{1,9},{2,10},{3,11},{4,12},{5,13},{6,14},{7,15},{8,16},{9,17... | collective-permute-start | bytes 786440 | tf_op jit(solution)/shard_map/ppermute | solution.py:110
  101.5 15.3 %collective-permute-start.15 = (f32[2,5,32,128]{3,2,1,0:T(8,128)}, f32[2,5,32,128]{3,2,1,0:T(8,128)S(1)}, u32[]{:S(2)}, u32[]{:S(2)}) collective-permute-start(f32[2,5,32,128]{3,2,1,0:T(8,128)} %get-tuple-element.85), channel_id=1, source_target_pairs={{0,9},{1,10},{2,11},{3,12},{4,13},{5,14},{6,15},{7,8},{8,17},{9,18... | collective-permute-start | bytes 491528 | tf_op jit(solution)/shard_map/ppermute | solution.py:110
  103.4 13.3 %collective-permute-start.16 = (f32[2,5,32,128]{3,2,1,0:T(8,128)}, f32[2,5,32,128]{3,2,1,0:T(8,128)S(1)}, u32[]{:S(2)}, u32[]{:S(2)}) collective-permute-start(f32[2,5,32,128]{3,2,1,0:T(8,128)} %get-tuple-element.86), channel_id=1, source_target_pairs={{0,15},{1,8},{2,9},{3,10},{4,11},{5,12},{6,13},{7,14},{8,23},{9,16... | collective-permute-start | bytes 491528 | tf_op jit(solution)/shard_map/ppermute | solution.py:110
  116.7 0.7 copy-start.14
  116.7 0.7 copy-start.16
  116.7 0.8 copy-start.10
  116.7 0.9 copy-start.5
  117.3 0.8 copy-start.7
  123.0 6.8 %collective-permute-start.19 = (f32[2,2,16,128]{3,2,1,0:T(8,128)}, f32[2,2,16,128]{3,2,1,0:T(8,128)S(1)}, u32[]{:S(2)}, u32[]{:S(2)}) collective-permute-start(f32[2,2,16,128]{3,2,1,0:T(8,128)} %get-tuple-element.91), channel_id=1, source_target_pairs={{0,1},{1,2},{2,3},{3,4},{4,5},{5,6},{6,7},{7,0},{8,9},{9,10},{10,1... | collective-permute-start | bytes 98312 | tf_op jit(solution)/shard_map/ppermute | solution.py:604
  124.6 5.2 %collective-permute-start.20 = (f32[2,2,16,128]{3,2,1,0:T(8,128)}, f32[2,2,16,128]{3,2,1,0:T(8,128)S(1)}, u32[]{:S(2)}, u32[]{:S(2)}) collective-permute-start(f32[2,2,16,128]{3,2,1,0:T(8,128)} %get-tuple-element.92), channel_id=1, source_target_pairs={{1,0},{2,1},{3,2},{4,3},{5,4},{6,5},{7,6},{0,7},{9,8},{10,9},{11,1... | collective-permute-start | bytes 98312 | tf_op jit(solution)/shard_map/ppermute | solution.py:605
  129.8 0.6 copy-start.22
  129.8 0.6 copy-start.23

commit v10 on v9

--- a/solution.py
+++ b/solution.py
@@ -191,6 +191,13 @@
     return pair_x + pair_y + pair_z - 6.0 * centre
 
 
+def kernel_prolong(c):
+    shape = c.shape
+    doubled = jnp.broadcast_to(c[:, :, None], (shape[0], shape[1], 2) + shape[2:])
+    doubled = doubled.reshape((shape[0], 2 * shape[1]) + shape[2:])
+    return jnp.concatenate([doubled, doubled], axis=2)
+
+
 def kernel_restrict(v):
     shape = v.shape
     pairs = v.reshape((shape[0], shape[1] // 2, 2) + shape[2:])
@@ -202,10 +209,11 @@
     return (upper + lower) * 0.25
 
 
-def sweep_kernel(widths_sent, natural_prior, diff_ref, flag_ref, start_ref, centre_ref, bbefore_ref, bafter_ref,
-                 own_ref, before_ref, after_ref, dec_ref, src_ref,
-                 rate_ref, n1_ref, n2_ref, n3_ref, n4_ref, e0_ref, b0_ref, cown_ref, clasts_ref,
-                 cfirsts_ref):
+def sweep_kernel(widths_sent, n_prior, diff_ref, flag_ref, start_ref, *refs):
+    prior = refs[:n_prior]
+    own_ref, before_ref, after_ref, dec_ref, src_ref, rate_ref = refs[n_prior:n_prior + 6]
+    (n1_ref, n2_ref, n3_ref, n4_ref, e0_ref, b0_ref, cown_ref, clasts_ref, cfirsts_ref,
+     n4own_ref, n4last_ref, n4first_ref) = refs[n_prior + 6:]
     spread_table, grouped_table, interp_table, widths = node_tables()
     rows = e0_ref.shape[1]
     hs = (start_ref.shape[1] - rows) // 2
@@ -239,11 +247,16 @@
             )
         )
         offset += w
-    if natural_prior:
+    if n_prior == 3:
+        centre_ref, bbefore_ref, bafter_ref = prior
         pieces = [even_odd_load(r) for r in (bbefore_ref, centre_ref, bafter_ref)]
+        joined = jnp.concatenate(pieces, axis=1)
     else:
-        pieces = [r[...] for r in (bbefore_ref, centre_ref, bafter_ref)]
-    joined = jnp.concatenate(pieces, axis=1)
+        fc, fb, fa, cc, cb, ca = prior
+        fine = jnp.concatenate([fb[...], fc[...], fa[...]], axis=1)
+        coarse = jnp.concatenate([cb[...], cc[...], ca[...]], axis=1)
+        spare = (2 * coarse.shape[1] - fine.shape[1]) // 2
+        joined = fine + cut(kernel_prolong(coarse), hs + spare, hs)
     swept = [jnp.where(flag_ref[0] == 1, start_ref[...], joined)]
     found = []
     for m in range(4):
@@ -283,10 +296,13 @@
         out[...] = cut(swept[m], hs - m, 1)
     e0_ref[...] = cut(found[0], hs - 1, 0)
     b0_ref[...] = cut(swept[0], hs, 0)
-
-
-def fine_sweep(diffusivity, flag, start, prior, parts, decay, src, rate_c, widths_sent,
-               natural_prior):
+    last_node = cut(swept[4], hs - 4, 0)
+    n4own_ref[...] = last_node
+    n4last_ref[...] = last_node[:, rows - hs:]
+    n4first_ref[...] = last_node[:, :hs]
+
+
+def fine_sweep(diffusivity, flag, start, prior, parts, decay, src, rate_c, widths_sent):
     rows = start.shape[1] - 2 * START_HALO
     shape = start.shape
     wide = jax.ShapeDtypeStruct((shape[0], rows + 2) + shape[2:], jnp.float32)
@@ -294,12 +310,13 @@
     cshape = (shape[0], rows // 2, shape[2] // 2, shape[3])
     cown = jax.ShapeDtypeStruct((4,) + cshape, jnp.float32)
     cedge = jax.ShapeDtypeStruct((shape[0], sum(widths_sent)) + cshape[2:], jnp.float32)
+    rim = jax.ShapeDtypeStruct((shape[0], START_HALO) + shape[2:], jnp.float32)
     vmem = pl.BlockSpec(memory_space=pltpu.VMEM)
     return pl.pallas_call(
-        functools.partial(sweep_kernel, widths_sent, natural_prior),
-        out_shape=(wide, wide, wide, wide, own, own, cown, cedge, cedge),
-        in_specs=[pl.BlockSpec(memory_space=pltpu.SMEM)] * 2 + [vmem] * 10,
-        out_specs=(vmem,) * 9,
+        functools.partial(sweep_kernel, widths_sent, len(prior)),
+        out_shape=(wide, wide, wide, wide, own, own, cown, cedge, cedge, own, rim, rim),
+        in_specs=[pl.BlockSpec(memory_space=pltpu.SMEM)] * 2 + [vmem] * (7 + len(prior)),
+        out_specs=(vmem,) * 12,
     )(diffusivity, flag, start, *prior, *parts, decay, src, rate_c)
 
 
@@ -386,7 +403,7 @@
         outs[0][:, :, pl.ds(0, half, stride=2), :] = news[4][:, :, :half]
         outs[0][:, :, pl.ds(1, half, stride=2), :] = news[4][:, :, half:]
         return
-    own_out, lasts_out, firsts_out, u4_out, u4_last_out, u4_first_out = outs
+    own_out, lasts_out, firsts_out, c4_out, c4_last_out, c4_first_out = outs
     src1 = at(src_ref, 0, rows, hd)
     dec0 = at(dec_ref, 0, rows, hd)
     states = [b_ref[...]] + [cut(news[m], 1, 0) for m in range(1, 5)]
@@ -405,9 +422,11 @@
         lasts_out[:, offset:offset + w] = part[:, rows - w:]
         firsts_out[:, offset:offset + w] = part[:, :w]
         offset += w
-    u4_out[...] = states[4]
-    u4_last_out[...] = states[4][:, rows - hs:]
-    u4_first_out[...] = states[4][:, :hs]
+    c4 = cut(interp_table[4][1] * delta_one + interp_table[4][2] * delta_two, ho, 0)
+    ch = (hs + 1) // 2
+    c4_out[...] = c4
+    c4_last_out[...] = c4[:, crows - ch:]
+    c4_first_out[...] = c4[:, :ch]
 
 
 def finish_round(diffusivity, coarse, rate_c, source_c, swept, e0, decay, src, last, widths_sent):
@@ -420,8 +439,12 @@
     else:
         sent = sum(START_HALO - 1 - m for m in range(4))
         edge = jax.ShapeDtypeStruct((shape[0], sent) + shape[2:], jnp.float32)
-        rim = jax.ShapeDtypeStruct((shape[0], START_HALO) + shape[2:], jnp.float32)
-        out_shape = (jax.ShapeDtypeStruct((4,) + field.shape, jnp.float32), edge, edge, field, rim, rim)
+        cshape = (shape[0], rows // 2, shape[2] // 2, shape[3])
+        crim = jax.ShapeDtypeStruct((shape[0], (START_HALO + 1) // 2) + cshape[2:], jnp.float32)
+        out_shape = (
+            jax.ShapeDtypeStruct((4,) + field.shape, jnp.float32), edge, edge,
+            jax.ShapeDtypeStruct(cshape, jnp.float32), crim, crim,
+        )
     vmem = pl.BlockSpec(memory_space=pltpu.VMEM)
     args = (diffusivity, *coarse, rate_c, source_c, *swept[1:], begin, e0, decay, src)
     return pl.pallas_call(
@@ -593,12 +616,13 @@
             out.append((own, h))
         return out
 
-    def advance(prior, pieces, last, natural):
+    def advance(prior, pieces, last):
         widths_sent = (1, 1, 0, 0) if last else (2, 2, 1, 1)
-        n1, n2, n3, n4, e0, b0, cown, clasts, cfirsts = fine_sweep(
+        (n1, n2, n3, n4, e0, b0, cown, clasts, cfirsts,
+         n4own, n4last, n4first) = fine_sweep(
             diffusivity, flag, own_ext, prior, pieces, decay[0], src[0], rate_c[0], widths_sent,
-            natural,
         )
+        sent_node = None if last else from_previous_slice((n4own, n4last, n4first))
         coarse = (
             cown,
             lax.ppermute(clasts, "space", up),
@@ -607,7 +631,7 @@
         return finish_round(
             diffusivity, coarse, rate_c[0], source_c[0],
             (b0, n1, n2, n3, n4), e0, decay[0], src[0], last, widths_sent,
-        )
+        ), sent_node
 
     size = lax.axis_size("space")
     up = [(i, (i + 1) % size) for i in range(size)]
@@ -620,15 +644,15 @@
     )
     for k in range(ROUNDS):
         last = k + 1 == ROUNDS
-        outs = advance(prior, pieces, last, k == 0)
+        outs, sent_node = advance(prior, pieces, last)
         if not last:
-            own4, lasts, firsts, u4, u4_last, u4_first = outs
+            own4, lasts, firsts, c4, c4_last, c4_first = outs
             pieces = (
                 own4,
                 lax.ppermute(lasts, "space", up),
                 lax.ppermute(firsts, "space", down),
             )
-            prior = from_previous_slice((u4, u4_last, u4_first))
+            prior = sent_node + from_previous_slice((c4, c4_last, c4_first))
     return outs[0][None]
 
 

time: 135 us -> 161 us (1.19)
  starting transfers between devices: 45.9 us -> 76 us
  waiting for transfers between devices: 50.7 us -> 46.6 us
    ppermute x9 -> x15, starting transfers between devices: 17.3 us -> 47.3 us  [moved(): return lax.ppermute(piece, axes, pairs)]
    ppermute x3, starting transfers between devices: 9.92 us -> 13.2 us  [advance(): lax.ppermute(cfirsts, 'space', down)]
    ppermute x3, starting transfers between devices: 4.25 us -> 1.11 us  [advance(): lax.ppermute(clasts, 'space', up)]
    ppermute x2, waiting for transfers between devices: 2.7 us -> 0.01 us  [per_device(): lax.ppermute(firsts, 'space', down)]
    ppermute x3, waiting for transfers between devices: 1.66 us -> 0.01 us  [advance(): lax.ppermute(cfirsts, 'space', down)]
    ppermute x9 -> x15, waiting for transfers between devices: 21.7 us -> 22.1 us  [moved(): return lax.ppermute(piece, axes, pairs)]
    unnamed x48 -> x72, local copies, waits for them, and re-layouts: 5.07 us -> 5.42 us
  transfers between devices with their start and end apart: 21 -> 27, of which waited for: 10 -> 13; matrix products, arithmetic and copies ran while one was open for 0% -> 0% of each run, Pallas kernels for 3% -> 2%
where the time goes in v10:
time: 161 us; the launch traced here: 160 us
  starting transfers between devices  76 us (47%)
  waiting for transfers between devices  46.6 us (29%)
  Pallas kernels  30.5 us (19%)
  local copies, waits for them, and re-layouts  6.53 us (4%)
    ppermute x15, starting transfers between devices, moved(): return lax.ppermute(piece, axes, pairs)  47.3 us
    ppermute x15, waiting for transfers between devices, moved(): return lax.ppermute(piece, axes, pairs)  22.1 us
    pallas_call x3, Pallas kernels, fine_sweep(): pl.pallas_call(functools.partial(sweep_kernel, widths_sent, len(prior)),...  14.8 us
    ppermute x1, waiting for transfers between devices, per_device(): lax.ppermute(jnp.concatenate([a[:, rows - w:] for a, w in zip(own_arrays,...  14.3 us
    ppermute x3, starting transfers between devices, advance(): lax.ppermute(cfirsts, 'space', down)  13.2 us
    pallas_call x3, Pallas kernels, finish_round(): pl.pallas_call(functools.partial(finish_kernel, widths_sent), out_shape=o...  12 us
    ppermute x2, starting transfers between devices, per_device(): lax.ppermute(firsts, 'space', down)  7.98 us
    ppermute x3, waiting for transfers between devices, advance(): lax.ppermute(clasts, 'space', up)  7.83 us
  transfers between devices with their start and end apart: 27, of which 13 were waited for; matrix products, arithmetic and copies ran while one was open for 0% of the time, Pallas kernels for 2%

profile of v10, /device:TPU:2, one launch (start us, length us, event | category | flops | bytes accessed | tf_op | source)
XLA Modules:
  0.0 160.0 jit_solution(11848330740587861606)
XLA Ops:
  0.0 1.1 fusion
  1.3 1.6 collective-permute-start
  2.9 3.3 %collective-permute-start.1 = (f32[2,13,32,128]{3,2,1,0:T(8,128)S(1)}, f32[2,13,32,128]{3,2,1,0:T(8,128)S(1)}, u32[]{:S(2)}, u32[]{:S(2)}) collective-permute-start(f32[2,13,32,128]{3,2,1,0:T(8,128)S(1)} %pad_maximum_fusion.1), channel_id=1, source_target_pairs={{1,0},{2,1},{3,2},{4,3},{5,4},{6,5},{7,6},{0,7},{9,8},{10,9},{11,1... | collective-permute-start | bytes 1277960 | tf_op jit(solution)/shard_map/ppermute | solution.py:577
  6.1 1.9 %collective-permute-start.2 = (f32[2,8,32,128]{3,2,1,0:T(8,128)S(1)}, f32[2,8,32,128]{3,2,1,0:T(8,128)S(1)}, u32[]{:S(2)}, u32[]{:S(2)}) collective-permute-start(f32[2,8,32,128]{3,2,1,0:T(8,128)S(1)} %bitcast.5), channel_id=1, source_target_pairs={{0,8},{1,9},{2,10},{3,11},{4,12},{5,13},{6,14},{7,15},{8,16},{9,17... | collective-permute-start | bytes 786440 | tf_op jit(solution)/shard_map/ppermute | solution.py:110
  8.0 2.0 %collective-permute-start.4 = (f32[2,5,32,128]{3,2,1,0:T(8,128)S(1)}, f32[2,5,32,128]{3,2,1,0:T(8,128)S(1)}, u32[]{:S(2)}, u32[]{:S(2)}) collective-permute-start(f32[2,5,32,128]{3,2,1,0:T(8,128)S(1)} %get-tuple-element.111), channel_id=1, source_target_pairs={{0,15},{1,8},{2,9},{3,10},{4,11},{5,12},{6,13},{7,14},{8,23},{9,16... | collective-permute-start | bytes 491528 | tf_op jit(solution)/shard_map/ppermute | solution.py:110
  10.1 1.9 %collective-permute-start.3 = (f32[2,5,32,128]{3,2,1,0:T(8,128)S(1)}, f32[2,5,32,128]{3,2,1,0:T(8,128)S(1)}, u32[]{:S(2)}, u32[]{:S(2)}) collective-permute-start(f32[2,5,32,128]{3,2,1,0:T(8,128)S(1)} %get-tuple-element.112), channel_id=1, source_target_pairs={{0,9},{1,10},{2,11},{3,12},{4,13},{5,14},{6,15},{7,8},{8,17},{9,18... | collective-permute-start | bytes 491528 | tf_op jit(solution)/shard_map/ppermute | solution.py:110
  12.0 14.3 %collective-permute-done.got_before_ref = f32[2,13,32,128]{3,2,1,0:T(8,128)S(1)} collective-permute-done((f32[2,13,32,128]{3,2,1,0:T(8,128)S(1)}, f32[2,13,32,128]{3,2,1,0:T(8,128)S(1)}, u32[]{:S(2)}, u32[]{:S(2)}) %collective-permute-start) | collective-permute-done | bytes 426016 | tf_op jit(solution)/shard_map/ppermute | solution.py:573
  26.3 2.3 %collective-permute-done.1.got_after_ref = f32[2,13,32,128]{3,2,1,0:T(8,128)S(1)} collective-permute-done((f32[2,13,32,128]{3,2,1,0:T(8,128)S(1)}, f32[2,13,32,128]{3,2,1,0:T(8,128)S(1)}, u32[]{:S(2)}, u32[]{:S(2)}) %collective-permute-start.1) | collective-permute-done | bytes 426016 | tf_op jit(solution)/shard_map/ppermute | solution.py:577
  28.6 0.8 copy-done.4
  29.4 3.7 %shard_map.46 = (f32[4,2,8,32,128]{4,3,2,1,0:T(8,128)}, f32[2,10,32,128]{3,2,1,0:T(8,128)}, f32[2,10,32,128]{3,2,1,0:T(8,128)}, f32[2,8,16,128]{3,2,1,0:T(8,128)...) custom-call(f32[2]{0:T(128)} %diff_ref.13, ...), custom_call_target="tpu_custom_call" | custom-call | tf_op jit(solution)/shard_map/pallas_call | solution.py:514
  33.9 4.9 %shard_map.47 = (f32[2,10,32,128]{3,2,1,0:T(8,128)}, f32[2,10,32,128]{3,2,1,0:T(8,128)}, f32[2,10,32,128]{3,2,1,0:T(8,128)}, f32[2,10,32,128]{3,2,1,0:T(8,128)},...) custom-call(f32[2]{0:T(128)} %diff_ref.13, ...), custom_call_target="tpu_custom_call" | custom-call | tf_op jit(solution)/shard_map/pallas_call | solution.py:315
  38.7 1.0 collective-permute-start.8
  39.7 3.8 %collective-permute-start.9 = (f32[2,6,16,128]{3,2,1,0:T(8,128)}, f32[2,6,16,128]{3,2,1,0:T(8,128)S(1)}, u32[]{:S(2)}, u32[]{:S(2)}) collective-permute-start(f32[2,6,16,128]{3,2,1,0:T(8,128)} %get-tuple-element.70), channel_id=1, source_target_pairs={{1,0},{2,1},{3,2},{4,3},{5,4},{6,5},{7,6},{0,7},{9,8},{10,9},{11,1... | collective-permute-start | bytes 294920 | tf_op jit(solution)/shard_map/ppermute | solution.py:629
  43.5 2.9 %collective-permute-done.8.cbefore_ref = f32[2,6,16,128]{3,2,1,0:T(8,128)S(1)} collective-permute-done((f32[2,6,16,128]{3,2,1,0:T(8,128)}, f32[2,6,16,128]{3,2,1,0:T(8,128)S(1)}, u32[]{:S(2)}, u32[]{:S(2)}) %collective-permute-start.8) | collective-permute-done | bytes 98336 | tf_op jit(solution)/shard_map/ppermute | solution.py:628
  46.4 0.6 copy-done.18
  47.1 4.6 %shard_map.48 = (f32[4,2,8,32,128]{4,3,2,1,0:T(8,128)}, f32[2,10,32,128]{3,2,1,0:T(8,128)}, f32[2,10,32,128]{3,2,1,0:T(8,128)}, f32[2,4,16,128]{3,2,1,0:T(8,128)...) custom-call(f32[2]{0:T(128)} %diff_ref.13, f32[4,2,4,16,128]{4,3,2,1,0:T(8,128)} %get-tuple-element.68.cown_ref, ...), custom_call_target="tpu_custom_call" | custom-call | tf_op jit(solution)/shard_map/pallas_call | solution.py:450
  51.6 0.7 collective-permute-start.13
  52.4 4.0 %collective-permute-start.14 = (f32[2,10,32,128]{3,2,1,0:T(8,128)}, f32[2,10,32,128]{3,2,1,0:T(8,128)S(1)}, u32[]{:S(2)}, u32[]{:S(2)}) collective-permute-start(f32[2,10,32,128]{3,2,1,0:T(8,128)} %get-tuple-element.83), channel_id=1, source_target_pairs={{1,0},{2,1},{3,2},{4,3},{5,4},{6,5},{7,6},{0,7},{9,8},{10,9},{11,1... | collective-permute-start | bytes 983048 | tf_op jit(solution)/shard_map/ppermute | solution.py:653
  56.4 1.9 %collective-permute-start.11 = (f32[2,3,16,128]{3,2,1,0:T(8,128)}, f32[2,3,16,128]{3,2,1,0:T(8,128)S(1)}, u32[]{:S(2)}, u32[]{:S(2)}) collective-permute-start(f32[2,3,16,128]{3,2,1,0:T(8,128)} %get-tuple-element.79), channel_id=1, source_target_pairs={{0,9},{1,10},{2,11},{3,12},{4,13},{5,14},{6,15},{7,8},{8,17},{9,18... | collective-permute-start | bytes 147464 | tf_op jit(solution)/shard_map/ppermute | solution.py:110
  58.3 1.9 %collective-permute-start.5 = (f32[2,8,32,128]{3,2,1,0:T(8,128)S(1)}, f32[2,8,32,128]{3,2,1,0:T(8,128)S(1)}, u32[]{:S(2)}, u32[]{:S(2)}) collective-permute-start(f32[2,8,32,128]{3,2,1,0:T(8,128)S(1)} %copy-done.31), channel_id=1, source_target_pairs={{0,8},{1,9},{2,10},{3,11},{4,12},{5,13},{6,14},{7,15},{8,16},{9,17... | collective-permute-start | bytes 786440 | tf_op jit(solution)/shard_map/ppermute | solution.py:110
  60.3 1.9 %collective-permute-start.10 = (f32[2,4,16,128]{3,2,1,0:T(8,128)}, f32[2,4,16,128]{3,2,1,0:T(8,128)S(1)}, u32[]{:S(2)}, u32[]{:S(2)}) collective-permute-start(f32[2,4,16,128]{3,2,1,0:T(8,128)} %get-tuple-element.78), channel_id=1, source_target_pairs={{0,8},{1,9},{2,10},{3,11},{4,12},{5,13},{6,14},{7,15},{8,16},{9,17... | collective-permute-start | bytes 196616 | tf_op jit(solution)/shard_map/ppermute | solution.py:110
  62.2 4.3 %collective-permute-done.11.refs_4_ = f32[2,3,16,128]{3,2,1,0:T(8,128)S(1)} collective-permute-done((f32[2,3,16,128]{3,2,1,0:T(8,128)}, f32[2,3,16,128]{3,2,1,0:T(8,128)S(1)}, u32[]{:S(2)}, u32[]{:S(2)}) %collective-permute-start.11) | collective-permute-done | bytes 49184 | tf_op jit(solution)/shard_map/ppermute | solution.py:110
  66.5 6.3 %collective-permute-start.12 = (f32[2,3,16,128]{3,2,1,0:T(8,128)}, f32[2,3,16,128]{3,2,1,0:T(8,128)S(1)}, u32[]{:S(2)}, u32[]{:S(2)}) collective-permute-start(f32[2,3,16,128]{3,2,1,0:T(8,128)} %get-tuple-element.80), channel_id=1, source_target_pairs={{0,15},{1,8},{2,9},{3,10},{4,11},{5,12},{6,13},{7,14},{8,23},{9,16... | collective-permute-start | bytes 147464 | tf_op jit(solution)/shard_map/ppermute | solution.py:110
  72.8 2.0 %collective-permute-done.12.refs_5_ = f32[2,3,16,128]{3,2,1,0:T(8,128)S(1)} collective-permute-done((f32[2,3,16,128]{3,2,1,0:T(8,128)}, f32[2,3,16,128]{3,2,1,0:T(8,128)S(1)}, u32[]{:S(2)}, u32[]{:S(2)}) %collective-permute-start.12) | collective-permute-done | bytes 49184 | tf_op jit(solution)/shard_map/ppermute | solution.py:110
  74.9 1.9 %collective-permute-start.6 = (f32[2,5,32,128]{3,2,1,0:T(8,128)S(1)}, f32[2,5,32,128]{3,2,1,0:T(8,128)S(1)}, u32[]{:S(2)}, u32[]{:S(2)}) collective-permute-start(f32[2,5,32,128]{3,2,1,0:T(8,128)S(1)} %copy-done.34), channel_id=1, source_target_pairs={{0,9},{1,10},{2,11},{3,12},{4,13},{5,14},{6,15},{7,8},{8,17},{9,18... | collective-permute-start | bytes 491528 | tf_op jit(solution)/shard_map/ppermute | solution.py:110
  76.8 5.6 %collective-permute-start.7 = (f32[2,5,32,128]{3,2,1,0:T(8,128)S(1)}, f32[2,5,32,128]{3,2,1,0:T(8,128)S(1)}, u32[]{:S(2)}, u32[]{:S(2)}) collective-permute-start(f32[2,5,32,128]{3,2,1,0:T(8,128)S(1)} %copy-done.32), channel_id=1, source_target_pairs={{0,15},{1,8},{2,9},{3,10},{4,11},{5,12},{6,13},{7,14},{8,23},{9,16... | collective-permute-start | bytes 491528 | tf_op jit(solution)/shard_map/ppermute | solution.py:110
  82.5 2.7 %collective-permute-done.6.refs_1_ = f32[2,5,32,128]{3,2,1,0:T(8,128)S(1)} collective-permute-done((f32[2,5,32,128]{3,2,1,0:T(8,128)S(1)}, f32[2,5,32,128]{3,2,1,0:T(8,128)S(1)}, u32[]{:S(2)}, u32[]{:S(2)}) %collective-permute-start.6) | collective-permute-done | bytes 163872 | tf_op jit(solution)/shard_map/ppermute | solution.py:110
  85.2 0.9 collective-permute-done.7.refs_2_
  87.1 5.0 %shard_map.49 = (f32[2,10,32,128]{3,2,1,0:T(8,128)}, f32[2,10,32,128]{3,2,1,0:T(8,128)}, f32[2,10,32,128]{3,2,1,0:T(8,128)}, f32[2,10,32,128]{3,2,1,0:T(8,128)},...) custom-call(f32[2]{0:T(128)} %diff_ref.13, ...), custom_call_target="tpu_custom_call" | custom-call | tf_op jit(solution)/shard_map/pallas_call | solution.py:315
  92.1 4.7 %collective-permute-start.19 = (f32[2,6,16,128]{3,2,1,0:T(8,128)}, f32[2,6,16,128]{3,2,1,0:T(8,128)S(1)}, u32[]{:S(2)}, u32[]{:S(2)}) collective-permute-start(f32[2,6,16,128]{3,2,1,0:T(8,128)} %get-tuple-element.89), channel_id=1, source_target_pairs={{1,0},{2,1},{3,2},{4,3},{5,4},{6,5},{7,6},{0,7},{9,8},{10,9},{11,1... | collective-permute-start | bytes 294920 | tf_op jit(solution)/shard_map/ppermute | solution.py:629
  96.9 2.8 %collective-permute-done.18.cbefore_ref = f32[2,6,16,128]{3,2,1,0:T(8,128)S(1)} collective-permute-done((f32[2,6,16,128]{3,2,1,0:T(8,128)}, f32[2,6,16,128]{3,2,1,0:T(8,128)S(1)}, u32[]{:S(2)}, u32[]{:S(2)}) %collective-permute-start.18) | collective-permute-done | bytes 98336 | tf_op jit(solution)/shard_map/ppermute | solution.py:628
  100.4 4.6 %shard_map.50 = (f32[4,2,8,32,128]{4,3,2,1,0:T(8,128)}, f32[2,10,32,128]{3,2,1,0:T(8,128)}, f32[2,10,32,128]{3,2,1,0:T(8,128)}, f32[2,4,16,128]{3,2,1,0:T(8,128)...) custom-call(f32[2]{0:T(128)} %diff_ref.13, f32[4,2,4,16,128]{4,3,2,1,0:T(8,128)} %get-tuple-element.87.cown_ref, ...), custom_call_target="tpu_custom_call" | custom-call | tf_op jit(solution)/shard_map/pallas_call | solution.py:450
  104.9 0.8 collective-permute-start.23
  105.8 3.9 %collective-permute-start.24 = (f32[2,10,32,128]{3,2,1,0:T(8,128)}, f32[2,10,32,128]{3,2,1,0:T(8,128)S(1)}, u32[]{:S(2)}, u32[]{:S(2)}) collective-permute-start(f32[2,10,32,128]{3,2,1,0:T(8,128)} %get-tuple-element.101), channel_id=1, source_target_pairs={{1,0},{2,1},{3,2},{4,3},{5,4},{6,5},{7,6},{0,7},{9,8},{10,9},{11,1... | collective-permute-start | bytes 983048 | tf_op jit(solution)/shard_map/ppermute | solution.py:653
  109.7 1.9 %collective-permute-start.21 = (f32[2,3,16,128]{3,2,1,0:T(8,128)}, f32[2,3,16,128]{3,2,1,0:T(8,128)S(1)}, u32[]{:S(2)}, u32[]{:S(2)}) collective-permute-start(f32[2,3,16,128]{3,2,1,0:T(8,128)} %get-tuple-element.97), channel_id=1, source_target_pairs={{0,9},{1,10},{2,11},{3,12},{4,13},{5,14},{6,15},{7,8},{8,17},{9,18... | collective-permute-start | bytes 147464 | tf_op jit(solution)/shard_map/ppermute | solution.py:110
  111.6 1.9 %collective-permute-start.15 = (f32[2,8,32,128]{3,2,1,0:T(8,128)S(1)}, f32[2,8,32,128]{3,2,1,0:T(8,128)S(1)}, u32[]{:S(2)}, u32[]{:S(2)}) collective-permute-start(f32[2,8,32,128]{3,2,1,0:T(8,128)S(1)} %copy-done.30), channel_id=1, source_target_pairs={{0,8},{1,9},{2,10},{3,11},{4,12},{5,13},{6,14},{7,15},{8,16},{9,17... | collective-permute-start | bytes 786440 | tf_op jit(solution)/shard_map/ppermute | solution.py:110
  113.6 1.9 %collective-permute-start.16 = (f32[2,5,32,128]{3,2,1,0:T(8,128)S(1)}, f32[2,5,32,128]{3,2,1,0:T(8,128)S(1)}, u32[]{:S(2)}, u32[]{:S(2)}) collective-permute-start(f32[2,5,32,128]{3,2,1,0:T(8,128)S(1)} %copy-done.35), channel_id=1, source_target_pairs={{0,9},{1,10},{2,11},{3,12},{4,13},{5,14},{6,15},{7,8},{8,17},{9,18... | collective-permute-start | bytes 491528 | tf_op jit(solution)/shard_map/ppermute | solution.py:110
  115.5 6.2 %collective-permute-done.21.refs_4_ = f32[2,3,16,128]{3,2,1,0:T(8,128)S(1)} collective-permute-done((f32[2,3,16,128]{3,2,1,0:T(8,128)}, f32[2,3,16,128]{3,2,1,0:T(8,128)S(1)}, u32[]{:S(2)}, u32[]{:S(2)}) %collective-permute-start.21) | collective-permute-done | bytes 49184 | tf_op jit(solution)/shard_map/ppermute | solution.py:110
  121.7 7.9 %collective-permute-start.22 = (f32[2,3,16,128]{3,2,1,0:T(8,128)}, f32[2,3,16,128]{3,2,1,0:T(8,128)S(1)}, u32[]{:S(2)}, u32[]{:S(2)}) collective-permute-start(f32[2,3,16,128]{3,2,1,0:T(8,128)} %get-tuple-element.98), channel_id=1, source_target_pairs={{0,15},{1,8},{2,9},{3,10},{4,11},{5,12},{6,13},{7,14},{8,23},{9,16... | collective-permute-start | bytes 147464 | tf_op jit(solution)/shard_map/ppermute | solution.py:110
  129.6 2.0 %collective-permute-done.22.refs_5_ = f32[2,3,16,128]{3,2,1,0:T(8,128)S(1)} collective-permute-done((f32[2,3,16,128]{3,2,1,0:T(8,128)}, f32[2,3,16,128]{3,2,1,0:T(8,128)S(1)}, u32[]{:S(2)}, u32[]{:S(2)}) %collective-permute-start.22) | collective-permute-done | bytes 49184 | tf_op jit(solution)/shard_map/ppermute | solution.py:110
  131.7 6.3 %collective-permute-start.17 = (f32[2,5,32,128]{3,2,1,0:T(8,128)S(1)}, f32[2,5,32,128]{3,2,1,0:T(8,128)S(1)}, u32[]{:S(2)}, u32[]{:S(2)}) collective-permute-start(f32[2,5,32,128]{3,2,1,0:T(8,128)S(1)} %copy-done.33), channel_id=1, source_target_pairs={{0,15},{1,8},{2,9},{3,10},{4,11},{5,12},{6,13},{7,14},{8,23},{9,16... | collective-permute-start | bytes 491528 | tf_op jit(solution)/shard_map/ppermute | solution.py:110
  137.9 1.9 %collective-permute-start.20 = (f32[2,4,16,128]{3,2,1,0:T(8,128)}, f32[2,4,16,128]{3,2,1,0:T(8,128)S(1)}, u32[]{:S(2)}, u32[]{:S(2)}) collective-permute-start(f32[2,4,16,128]{3,2,1,0:T(8,128)} %get-tuple-element.96), channel_id=1, source_target_pairs={{0,8},{1,9},{2,10},{3,11},{4,12},{5,13},{6,14},{7,15},{8,16},{9,17... | collective-permute-start | bytes 196616 | tf_op jit(solution)/shard_map/ppermute | solution.py:110
  139.9 0.9 collective-permute-done.17.refs_2_
  140.7 3.0 %collective-permute-done.20.refs_3_ = f32[2,4,16,128]{3,2,1,0:T(8,128)S(1)} collective-permute-done((f32[2,4,16,128]{3,2,1,0:T(8,128)}, f32[2,4,16,128]{3,2,1,0:T(8,128)S(1)}, u32[]{:S(2)}, u32[]{:S(2)}) %collective-permute-start.20) | collective-permute-done | bytes 65568 | tf_op jit(solution)/shard_map/ppermute | solution.py:110
  144.7 5.0 %shard_map.51 = (f32[2,10,32,128]{3,2,1,0:T(8,128)}, f32[2,10,32,128]{3,2,1,0:T(8,128)}, f32[2,10,32,128]{3,2,1,0:T(8,128)}, f32[2,10,32,128]{3,2,1,0:T(8,128)},...) custom-call(f32[2]{0:T(128)} %diff_ref.13, ...), custom_call_target="tpu_custom_call" | custom-call | tf_op jit(solution)/shard_map/pallas_call | solution.py:315
  149.7 4.7 %collective-permute-start.26 = (f32[2,2,16,128]{3,2,1,0:T(8,128)}, f32[2,2,16,128]{3,2,1,0:T(8,128)S(1)}, u32[]{:S(2)}, u32[]{:S(2)}) collective-permute-start(f32[2,2,16,128]{3,2,1,0:T(8,128)} %get-tuple-element.104), channel_id=1, source_target_pairs={{1,0},{2,1},{3,2},{4,3},{5,4},{6,5},{7,6},{0,7},{9,8},{10,9},{11,1... | collective-permute-start | bytes 98312 | tf_op jit(solution)/shard_map/ppermute | solution.py:629
  154.4 2.1 %collective-permute-done.25.cbefore_ref = f32[2,2,16,128]{3,2,1,0:T(8,128)S(1)} collective-permute-done((f32[2,2,16,128]{3,2,1,0:T(8,128)}, f32[2,2,16,128]{3,2,1,0:T(8,128)S(1)}, u32[]{:S(2)}, u32[]{:S(2)}) %collective-permute-start.25) | collective-permute-done | bytes 32800 | tf_op jit(solution)/shard_map/ppermute | solution.py:628
  157.2 2.9 %shard_map.52 = f32[2,8,32,128]{3,2,1,0:T(8,128)} custom-call(f32[2]{0:T(128)} %diff_ref.13, f32[4,2,4,16,128]{4,3,2,1,0:T(8,128)} %get-tuple-element.102.cown_ref, f32[2,2,16,128]{3,2,1,0:T(8,128)} %copy-done.28, f32[2,2,16,128]{3,2,1,0:T(8,128)} %copy-done.29, f32[2,8,16,128]{3,2,1,0:T(8,128)} %get-tuple-element.64.refs_8_.rate_ref.refs_11_, ...), custom_call_target="tpu_custom_call" | custom-call | tf_op jit(solution)/shard_map/pallas_call | solution.py:450
  (89 shorter events, 4.3 us)
Async XLA Ops:
  0.0 1.1 copy-start.1
  0.0 1.2 copy-start.2
  1.3 25.0 %collective-permute-start = (f32[2,13,32,128]{3,2,1,0:T(8,128)S(1)}, f32[2,13,32,128]{3,2,1,0:T(8,128)S(1)}, u32[]{:S(2)}, u32[]{:S(2)}) collective-permute-start(f32[2,13,32,128]{3,2,1,0:T(8,128)S(1)} %pad_maximum_fusion), channel_id=1, source_target_pairs={{0,1},{1,2},{2,3},{3,4},{4,5},{5,6},{6,7},{7,0},{8,9},{9,10},{10,1... | collective-permute-start | bytes 1277960 | tf_op jit(solution)/shard_map/ppermute | solution.py:573
  2.8 3.3 %copy-start = (f32[1,2,8,32,128]{4,3,2,1,0:T(8,128)S(1)}, f32[1,2,8,32,128]{4,3,2,1,0:T(8,128)}, u32[]{:S(2)}) copy-start(f32[1,2,8,32,128]{4,3,2,1,0:T(8,128)} %param.4) | copy-start | bytes 786436
  2.9 25.7 %collective-permute-start.1 = (f32[2,13,32,128]{3,2,1,0:T(8,128)S(1)}, f32[2,13,32,128]{3,2,1,0:T(8,128)S(1)}, u32[]{:S(2)}, u32[]{:S(2)}) collective-permute-start(f32[2,13,32,128]{3,2,1,0:T(8,128)S(1)} %pad_maximum_fusion.1), channel_id=1, source_target_pairs={{1,0},{2,1},{3,2},{4,3},{5,4},{6,5},{7,6},{0,7},{9,8},{10,9},{11,1... | collective-permute-start | bytes 1277960 | tf_op jit(solution)/shard_map/ppermute | solution.py:577
  6.1 27.0 %collective-permute-start.2 = (f32[2,8,32,128]{3,2,1,0:T(8,128)S(1)}, f32[2,8,32,128]{3,2,1,0:T(8,128)S(1)}, u32[]{:S(2)}, u32[]{:S(2)}) collective-permute-start(f32[2,8,32,128]{3,2,1,0:T(8,128)S(1)} %bitcast.5), channel_id=1, source_target_pairs={{0,8},{1,9},{2,10},{3,11},{4,12},{5,13},{6,14},{7,15},{8,16},{9,17... | collective-permute-start | bytes 786440 | tf_op jit(solution)/shard_map/ppermute | solution.py:110
  8.0 25.0 %collective-permute-start.4 = (f32[2,5,32,128]{3,2,1,0:T(8,128)S(1)}, f32[2,5,32,128]{3,2,1,0:T(8,128)S(1)}, u32[]{:S(2)}, u32[]{:S(2)}) collective-permute-start(f32[2,5,32,128]{3,2,1,0:T(8,128)S(1)} %get-tuple-element.111), channel_id=1, source_target_pairs={{0,15},{1,8},{2,9},{3,10},{4,11},{5,12},{6,13},{7,14},{8,23},{9,16... | collective-permute-start | bytes 491528 | tf_op jit(solution)/shard_map/ppermute | solution.py:110
  10.1 23.0 %collective-permute-start.3 = (f32[2,5,32,128]{3,2,1,0:T(8,128)S(1)}, f32[2,5,32,128]{3,2,1,0:T(8,128)S(1)}, u32[]{:S(2)}, u32[]{:S(2)}) collective-permute-start(f32[2,5,32,128]{3,2,1,0:T(8,128)S(1)} %get-tuple-element.112), channel_id=1, source_target_pairs={{0,9},{1,10},{2,11},{3,12},{4,13},{5,14},{6,15},{7,8},{8,17},{9,18... | collective-permute-start | bytes 491528 | tf_op jit(solution)/shard_map/ppermute | solution.py:110
  26.3 2.3 %copy-start.3 = (f32[2,13,32,128]{3,2,1,0:T(8,128)}, f32[2,13,32,128]{3,2,1,0:T(8,128)S(1)}, u32[]{:S(2)}) copy-start(f32[2,13,32,128]{3,2,1,0:T(8,128)S(1)} %collective-permute-done.got_before_ref) | copy-start | bytes 1277956
  38.7 7.7 %collective-permute-start.8 = (f32[2,6,16,128]{3,2,1,0:T(8,128)}, f32[2,6,16,128]{3,2,1,0:T(8,128)S(1)}, u32[]{:S(2)}, u32[]{:S(2)}) collective-permute-start(f32[2,6,16,128]{3,2,1,0:T(8,128)} %get-tuple-element.69), channel_id=1, source_target_pairs={{0,1},{1,2},{2,3},{3,4},{4,5},{5,6},{6,7},{7,0},{8,9},{9,10},{10,1... | collective-permute-start | bytes 294920 | tf_op jit(solution)/shard_map/ppermute | solution.py:628
  39.7 6.7 %collective-permute-start.9 = (f32[2,6,16,128]{3,2,1,0:T(8,128)}, f32[2,6,16,128]{3,2,1,0:T(8,128)S(1)}, u32[]{:S(2)}, u32[]{:S(2)}) collective-permute-start(f32[2,6,16,128]{3,2,1,0:T(8,128)} %get-tuple-element.70), channel_id=1, source_target_pairs={{1,0},{2,1},{3,2},{4,3},{5,4},{6,5},{7,6},{0,7},{9,8},{10,9},{11,1... | collective-permute-start | bytes 294920 | tf_op jit(solution)/shard_map/ppermute | solution.py:629
  47.1 11.3 %copy-start.31 = (f32[2,8,32,128]{3,2,1,0:T(8,128)S(1)}, f32[2,8,32,128]{3,2,1,0:T(8,128)}, u32[]{:S(2)}) copy-start(f32[2,8,32,128]{3,2,1,0:T(8,128)} %get-tuple-element.65) | copy-start | bytes 786436
  47.1 27.8 %copy-start.34 = (f32[2,5,32,128]{3,2,1,0:T(8,128)S(1)}, f32[2,5,32,128]{3,2,1,0:T(8,128)}, u32[]{:S(2)}) copy-start(f32[2,5,32,128]{3,2,1,0:T(8,128)} %get-tuple-element.66) | copy-start | bytes 491524
  47.1 29.8 %copy-start.32 = (f32[2,5,32,128]{3,2,1,0:T(8,128)S(1)}, f32[2,5,32,128]{3,2,1,0:T(8,128)}, u32[]{:S(2)}) copy-start(f32[2,5,32,128]{3,2,1,0:T(8,128)} %get-tuple-element.67) | copy-start | bytes 491524
  51.6 34.5 %collective-permute-start.13 = (f32[2,10,32,128]{3,2,1,0:T(8,128)}, f32[2,10,32,128]{3,2,1,0:T(8,128)S(1)}, u32[]{:S(2)}, u32[]{:S(2)}) collective-permute-start(f32[2,10,32,128]{3,2,1,0:T(8,128)} %get-tuple-element.82), channel_id=1, source_target_pairs={{0,1},{1,2},{2,3},{3,4},{4,5},{5,6},{6,7},{7,0},{8,9},{9,10},{10,1... | collective-permute-start | bytes 983048 | tf_op jit(solution)/shard_map/ppermute | solution.py:652
  52.4 33.8 %collective-permute-start.14 = (f32[2,10,32,128]{3,2,1,0:T(8,128)}, f32[2,10,32,128]{3,2,1,0:T(8,128)S(1)}, u32[]{:S(2)}, u32[]{:S(2)}) collective-permute-start(f32[2,10,32,128]{3,2,1,0:T(8,128)} %get-tuple-element.83), channel_id=1, source_target_pairs={{1,0},{2,1},{3,2},{4,3},{5,4},{6,5},{7,6},{0,7},{9,8},{10,9},{11,1... | collective-permute-start | bytes 983048 | tf_op jit(solution)/shard_map/ppermute | solution.py:653
  56.4 10.1 %collective-permute-start.11 = (f32[2,3,16,128]{3,2,1,0:T(8,128)}, f32[2,3,16,128]{3,2,1,0:T(8,128)S(1)}, u32[]{:S(2)}, u32[]{:S(2)}) collective-permute-start(f32[2,3,16,128]{3,2,1,0:T(8,128)} %get-tuple-element.79), channel_id=1, source_target_pairs={{0,9},{1,10},{2,11},{3,12},{4,13},{5,14},{6,15},{7,8},{8,17},{9,18... | collective-permute-start | bytes 147464 | tf_op jit(solution)/shard_map/ppermute | solution.py:110
  58.3 27.8 %collective-permute-start.5 = (f32[2,8,32,128]{3,2,1,0:T(8,128)S(1)}, f32[2,8,32,128]{3,2,1,0:T(8,128)S(1)}, u32[]{:S(2)}, u32[]{:S(2)}) collective-permute-start(f32[2,8,32,128]{3,2,1,0:T(8,128)S(1)} %copy-done.31), channel_id=1, source_target_pairs={{0,8},{1,9},{2,10},{3,11},{4,12},{5,13},{6,14},{7,15},{8,16},{9,17... | collective-permute-start | bytes 786440 | tf_op jit(solution)/shard_map/ppermute | solution.py:110
  60.3 16.5 %collective-permute-start.10 = (f32[2,4,16,128]{3,2,1,0:T(8,128)}, f32[2,4,16,128]{3,2,1,0:T(8,128)S(1)}, u32[]{:S(2)}, u32[]{:S(2)}) collective-permute-start(f32[2,4,16,128]{3,2,1,0:T(8,128)} %get-tuple-element.78), channel_id=1, source_target_pairs={{0,8},{1,9},{2,10},{3,11},{4,12},{5,13},{6,14},{7,15},{8,16},{9,17... | collective-permute-start | bytes 196616 | tf_op jit(solution)/shard_map/ppermute | solution.py:110
  66.5 19.7 %copy-start.25 = (f32[2,3,16,128]{3,2,1,0:T(8,128)}, f32[2,3,16,128]{3,2,1,0:T(8,128)S(1)}, u32[]{:S(2)}) copy-start(f32[2,3,16,128]{3,2,1,0:T(8,128)S(1)} %collective-permute-done.11.refs_4_) | copy-start | bytes 147460
  66.5 8.4 %collective-permute-start.12 = (f32[2,3,16,128]{3,2,1,0:T(8,128)}, f32[2,3,16,128]{3,2,1,0:T(8,128)S(1)}, u32[]{:S(2)}, u32[]{:S(2)}) collective-permute-start(f32[2,3,16,128]{3,2,1,0:T(8,128)} %get-tuple-element.80), channel_id=1, source_target_pairs={{0,15},{1,8},{2,9},{3,10},{4,11},{5,12},{6,13},{7,14},{8,23},{9,16... | collective-permute-start | bytes 147464 | tf_op jit(solution)/shard_map/ppermute | solution.py:110
  74.9 11.3 %copy-start.27 = (f32[2,3,16,128]{3,2,1,0:T(8,128)}, f32[2,3,16,128]{3,2,1,0:T(8,128)S(1)}, u32[]{:S(2)}) copy-start(f32[2,3,16,128]{3,2,1,0:T(8,128)S(1)} %collective-permute-done.12.refs_5_) | copy-start | bytes 147460
  74.9 10.3 %collective-permute-start.6 = (f32[2,5,32,128]{3,2,1,0:T(8,128)S(1)}, f32[2,5,32,128]{3,2,1,0:T(8,128)S(1)}, u32[]{:S(2)}, u32[]{:S(2)}) collective-permute-start(f32[2,5,32,128]{3,2,1,0:T(8,128)S(1)} %copy-done.34), channel_id=1, source_target_pairs={{0,9},{1,10},{2,11},{3,12},{4,13},{5,14},{6,15},{7,8},{8,17},{9,18... | collective-permute-start | bytes 491528 | tf_op jit(solution)/shard_map/ppermute | solution.py:110
  76.8 9.4 %copy-start.22 = (f32[2,4,16,128]{3,2,1,0:T(8,128)}, f32[2,4,16,128]{3,2,1,0:T(8,128)S(1)}, u32[]{:S(2)}) copy-start(f32[2,4,16,128]{3,2,1,0:T(8,128)S(1)} %collective-permute-done.10.refs_3_) | copy-start | bytes 196612
  76.8 9.3 %collective-permute-start.7 = (f32[2,5,32,128]{3,2,1,0:T(8,128)S(1)}, f32[2,5,32,128]{3,2,1,0:T(8,128)S(1)}, u32[]{:S(2)}, u32[]{:S(2)}) collective-permute-start(f32[2,5,32,128]{3,2,1,0:T(8,128)S(1)} %copy-done.32), channel_id=1, source_target_pairs={{0,15},{1,8},{2,9},{3,10},{4,11},{5,12},{6,13},{7,14},{8,23},{9,16... | collective-permute-start | bytes 491528 | tf_op jit(solution)/shard_map/ppermute | solution.py:110
  85.2 1.0 copy-start.16
  86.1 0.8 copy-start.6
  86.2 0.9 copy-start.8
  92.1 7.6 %collective-permute-start.18 = (f32[2,6,16,128]{3,2,1,0:T(8,128)}, f32[2,6,16,128]{3,2,1,0:T(8,128)S(1)}, u32[]{:S(2)}, u32[]{:S(2)}) collective-permute-start(f32[2,6,16,128]{3,2,1,0:T(8,128)} %get-tuple-element.88), channel_id=1, source_target_pairs={{0,1},{1,2},{2,3},{3,4},{4,5},{5,6},{6,7},{7,0},{8,9},{9,10},{10,1... | collective-permute-start | bytes 294920 | tf_op jit(solution)/shard_map/ppermute | solution.py:628
  92.1 7.6 %collective-permute-start.19 = (f32[2,6,16,128]{3,2,1,0:T(8,128)}, f32[2,6,16,128]{3,2,1,0:T(8,128)S(1)}, u32[]{:S(2)}, u32[]{:S(2)}) collective-permute-start(f32[2,6,16,128]{3,2,1,0:T(8,128)} %get-tuple-element.89), channel_id=1, source_target_pairs={{1,0},{2,1},{3,2},{4,3},{5,4},{6,5},{7,6},{0,7},{9,8},{10,9},{11,1... | collective-permute-start | bytes 294920 | tf_op jit(solution)/shard_map/ppermute | solution.py:629
  100.4 11.3 %copy-start.30 = (f32[2,8,32,128]{3,2,1,0:T(8,128)S(1)}, f32[2,8,32,128]{3,2,1,0:T(8,128)}, u32[]{:S(2)}) copy-start(f32[2,8,32,128]{3,2,1,0:T(8,128)} %get-tuple-element.84) | copy-start | bytes 786436
  100.4 13.2 %copy-start.35 = (f32[2,5,32,128]{3,2,1,0:T(8,128)S(1)}, f32[2,5,32,128]{3,2,1,0:T(8,128)}, u32[]{:S(2)}) copy-start(f32[2,5,32,128]{3,2,1,0:T(8,128)} %get-tuple-element.85) | copy-start | bytes 491524
  100.4 31.3 %copy-start.33 = (f32[2,5,32,128]{3,2,1,0:T(8,128)S(1)}, f32[2,5,32,128]{3,2,1,0:T(8,128)}, u32[]{:S(2)}) copy-start(f32[2,5,32,128]{3,2,1,0:T(8,128)} %get-tuple-element.86) | copy-start | bytes 491524
  104.9 38.8 %collective-permute-start.23 = (f32[2,10,32,128]{3,2,1,0:T(8,128)}, f32[2,10,32,128]{3,2,1,0:T(8,128)S(1)}, u32[]{:S(2)}, u32[]{:S(2)}) collective-permute-start(f32[2,10,32,128]{3,2,1,0:T(8,128)} %get-tuple-element.100), channel_id=1, source_target_pairs={{0,1},{1,2},{2,3},{3,4},{4,5},{5,6},{6,7},{7,0},{8,9},{9,10},{10,1... | collective-permute-start | bytes 983048 | tf_op jit(solution)/shard_map/ppermute | solution.py:652
  105.8 38.0 %collective-permute-start.24 = (f32[2,10,32,128]{3,2,1,0:T(8,128)}, f32[2,10,32,128]{3,2,1,0:T(8,128)S(1)}, u32[]{:S(2)}, u32[]{:S(2)}) collective-permute-start(f32[2,10,32,128]{3,2,1,0:T(8,128)} %get-tuple-element.101), channel_id=1, source_target_pairs={{1,0},{2,1},{3,2},{4,3},{5,4},{6,5},{7,6},{0,7},{9,8},{10,9},{11,1... | collective-permute-start | bytes 983048 | tf_op jit(solution)/shard_map/ppermute | solution.py:653
  109.7 12.0 %collective-permute-start.21 = (f32[2,3,16,128]{3,2,1,0:T(8,128)}, f32[2,3,16,128]{3,2,1,0:T(8,128)S(1)}, u32[]{:S(2)}, u32[]{:S(2)}) collective-permute-start(f32[2,3,16,128]{3,2,1,0:T(8,128)} %get-tuple-element.97), channel_id=1, source_target_pairs={{0,9},{1,10},{2,11},{3,12},{4,13},{5,14},{6,15},{7,8},{8,17},{9,18... | collective-permute-start | bytes 147464 | tf_op jit(solution)/shard_map/ppermute | solution.py:110
  111.6 32.1 %collective-permute-start.15 = (f32[2,8,32,128]{3,2,1,0:T(8,128)S(1)}, f32[2,8,32,128]{3,2,1,0:T(8,128)S(1)}, u32[]{:S(2)}, u32[]{:S(2)}) collective-permute-start(f32[2,8,32,128]{3,2,1,0:T(8,128)S(1)} %copy-done.30), channel_id=1, source_target_pairs={{0,8},{1,9},{2,10},{3,11},{4,12},{5,13},{6,14},{7,15},{8,16},{9,17... | collective-permute-start | bytes 786440 | tf_op jit(solution)/shard_map/ppermute | solution.py:110
  113.6 24.3 %collective-permute-start.16 = (f32[2,5,32,128]{3,2,1,0:T(8,128)S(1)}, f32[2,5,32,128]{3,2,1,0:T(8,128)S(1)}, u32[]{:S(2)}, u32[]{:S(2)}) collective-permute-start(f32[2,5,32,128]{3,2,1,0:T(8,128)S(1)} %copy-done.35), channel_id=1, source_target_pairs={{0,9},{1,10},{2,11},{3,12},{4,13},{5,14},{6,15},{7,8},{8,17},{9,18... | collective-permute-start | bytes 491528 | tf_op jit(solution)/shard_map/ppermute | solution.py:110
  121.7 22.1 %copy-start.24 = (f32[2,3,16,128]{3,2,1,0:T(8,128)}, f32[2,3,16,128]{3,2,1,0:T(8,128)S(1)}, u32[]{:S(2)}) copy-start(f32[2,3,16,128]{3,2,1,0:T(8,128)S(1)} %collective-permute-done.21.refs_4_) | copy-start | bytes 147460
  121.7 9.9 %collective-permute-start.22 = (f32[2,3,16,128]{3,2,1,0:T(8,128)}, f32[2,3,16,128]{3,2,1,0:T(8,128)S(1)}, u32[]{:S(2)}, u32[]{:S(2)}) collective-permute-start(f32[2,3,16,128]{3,2,1,0:T(8,128)} %get-tuple-element.98), channel_id=1, source_target_pairs={{0,15},{1,8},{2,9},{3,10},{4,11},{5,12},{6,13},{7,14},{8,23},{9,16... | collective-permute-start | bytes 147464 | tf_op jit(solution)/shard_map/ppermute | solution.py:110
  131.7 12.1 %copy-start.26 = (f32[2,3,16,128]{3,2,1,0:T(8,128)}, f32[2,3,16,128]{3,2,1,0:T(8,128)S(1)}, u32[]{:S(2)}) copy-start(f32[2,3,16,128]{3,2,1,0:T(8,128)S(1)} %collective-permute-done.22.refs_5_) | copy-start | bytes 147460
  131.7 9.1 %collective-permute-start.17 = (f32[2,5,32,128]{3,2,1,0:T(8,128)S(1)}, f32[2,5,32,128]{3,2,1,0:T(8,128)S(1)}, u32[]{:S(2)}, u32[]{:S(2)}) collective-permute-start(f32[2,5,32,128]{3,2,1,0:T(8,128)S(1)} %copy-done.33), channel_id=1, source_target_pairs={{0,15},{1,8},{2,9},{3,10},{4,11},{5,12},{6,13},{7,14},{8,23},{9,16... | collective-permute-start | bytes 491528 | tf_op jit(solution)/shard_map/ppermute | solution.py:110
  137.9 5.9 %copy-start.12 = (f32[2,5,32,128]{3,2,1,0:T(8,128)}, f32[2,5,32,128]{3,2,1,0:T(8,128)S(1)}, u32[]{:S(2)}) copy-start(f32[2,5,32,128]{3,2,1,0:T(8,128)S(1)} %collective-permute-done.16.refs_1_) | copy-start | bytes 491524
  137.9 5.8 %collective-permute-start.20 = (f32[2,4,16,128]{3,2,1,0:T(8,128)}, f32[2,4,16,128]{3,2,1,0:T(8,128)S(1)}, u32[]{:S(2)}, u32[]{:S(2)}) collective-permute-start(f32[2,4,16,128]{3,2,1,0:T(8,128)} %get-tuple-element.96), channel_id=1, source_target_pairs={{0,8},{1,9},{2,10},{3,11},{4,12},{5,13},{6,14},{7,15},{8,16},{9,17... | collective-permute-start | bytes 196616 | tf_op jit(solution)/shard_map/ppermute | solution.py:110
  140.7 3.1 %copy-start.15 = (f32[2,5,32,128]{3,2,1,0:T(8,128)}, f32[2,5,32,128]{3,2,1,0:T(8,128)S(1)}, u32[]{:S(2)}) copy-start(f32[2,5,32,128]{3,2,1,0:T(8,128)S(1)} %collective-permute-done.17.refs_2_) | copy-start | bytes 491524
  143.8 0.9 copy-start.7
  149.7 6.9 %collective-permute-start.25 = (f32[2,2,16,128]{3,2,1,0:T(8,128)}, f32[2,2,16,128]{3,2,1,0:T(8,128)S(1)}, u32[]{:S(2)}, u32[]{:S(2)}) collective-permute-start(f32[2,2,16,128]{3,2,1,0:T(8,128)} %get-tuple-element.103), channel_id=1, source_target_pairs={{0,1},{1,2},{2,3},{3,4},{4,5},{5,6},{6,7},{7,0},{8,9},{9,10},{10,1... | collective-permute-start | bytes 98312 | tf_op jit(solution)/shard_map/ppermute | solution.py:628
  149.7 6.8 %collective-permute-start.26 = (f32[2,2,16,128]{3,2,1,0:T(8,128)}, f32[2,2,16,128]{3,2,1,0:T(8,128)S(1)}, u32[]{:S(2)}, u32[]{:S(2)}) collective-permute-start(f32[2,2,16,128]{3,2,1,0:T(8,128)} %get-tuple-element.104), channel_id=1, source_target_pairs={{1,0},{2,1},{3,2},{4,3},{5,4},{6,5},{7,6},{0,7},{9,8},{10,9},{11,1... | collective-permute-start | bytes 98312 | tf_op jit(solution)/shard_map/ppermute | solution.py:629
  (15 other events, 10.3 us)

commit v11 on v10

--- a/solution.py
+++ b/solution.py
@@ -628,6 +628,8 @@
             lax.ppermute(clasts, "space", up),
             lax.ppermute(cfirsts, "space", down),
         )
+        if sent_node is not None:
+            coarse, sent_node = lax.optimization_barrier((coarse, sent_node))
         return finish_round(
             diffusivity, coarse, rate_c[0], source_c[0],
             (b0, n1, n2, n3, n4), e0, decay[0], src[0], last, widths_sent,

time: 161 us -> 147 us (0.913)
  the two profiles are of different devices: /device:TPU:2 before, /device:TPU:0 now
where the time goes in v11:
time: 147 us; the launch traced here: 146 us
  starting transfers between devices  86.7 us (59%)
  Pallas kernels  30.3 us (21%)
  waiting for transfers between devices  22.6 us (15%)
  local copies, waits for them, and re-layouts  6.22 us (4%)
    ppermute x15, starting transfers between devices, moved(): return lax.ppermute(piece, axes, pairs)  56.7 us
    pallas_call x3, Pallas kernels, fine_sweep(): pl.pallas_call(functools.partial(sweep_kernel, widths_sent, len(prior)),...  14.8 us
    ppermute x3, starting transfers between devices, advance(): lax.ppermute(cfirsts, 'space', down)  14.1 us
    pallas_call x3, Pallas kernels, finish_round(): pl.pallas_call(functools.partial(finish_kernel, widths_sent), out_shape=o...  11.9 us
    ppermute x1, waiting for transfers between devices, per_device(): lax.ppermute(jnp.concatenate([a[:, rows - w:] for a, w in zip(own_arrays,...  8.23 us
    ppermute x3, waiting for transfers between devices, advance(): lax.ppermute(clasts, 'space', up)  7.76 us
    ppermute x2, starting transfers between devices, per_device(): lax.ppermute(firsts, 'space', down)  7.56 us
    unnamed x60, local copies, waits for them, and re-layouts  5.11 us
  transfers between devices with their start and end apart: 27, of which 10 were waited for; matrix products, arithmetic and copies ran while one was open for 0% of the time, Pallas kernels for 2%

profile of v11, /device:TPU:0, one launch (start us, length us, event | category | flops | bytes accessed | tf_op | source)
XLA Modules:
  0.0 146.4 jit_solution(4209682567217900178)
XLA Ops:
  0.0 1.1 fusion
  1.3 3.0 %collective-permute-start = (f32[2,13,32,128]{3,2,1,0:T(8,128)S(1)}, f32[2,13,32,128]{3,2,1,0:T(8,128)S(1)}, u32[]{:S(2)}, u32[]{:S(2)}) collective-permute-start(f32[2,13,32,128]{3,2,1,0:T(8,128)S(1)} %pad_maximum_fusion), channel_id=1, source_target_pairs={{0,1},{1,2},{2,3},{3,4},{4,5},{5,6},{6,7},{7,0},{8,9},{9,10},{10,1... | collective-permute-start | bytes 1277960 | tf_op jit(solution)/shard_map/ppermute | solution.py:573
  4.3 3.1 %collective-permute-start.1 = (f32[2,13,32,128]{3,2,1,0:T(8,128)S(1)}, f32[2,13,32,128]{3,2,1,0:T(8,128)S(1)}, u32[]{:S(2)}, u32[]{:S(2)}) collective-permute-start(f32[2,13,32,128]{3,2,1,0:T(8,128)S(1)} %pad_maximum_fusion.1), channel_id=1, source_target_pairs={{1,0},{2,1},{3,2},{4,3},{5,4},{6,5},{7,6},{0,7},{9,8},{10,9},{11,1... | collective-permute-start | bytes 1277960 | tf_op jit(solution)/shard_map/ppermute | solution.py:577
  7.4 1.5 collective-permute-start.2
  8.9 5.6 %collective-permute-start.4 = (f32[2,5,32,128]{3,2,1,0:T(8,128)S(1)}, f32[2,5,32,128]{3,2,1,0:T(8,128)S(1)}, u32[]{:S(2)}, u32[]{:S(2)}) collective-permute-start(f32[2,5,32,128]{3,2,1,0:T(8,128)S(1)} %get-tuple-element.135), channel_id=1, source_target_pairs={{0,15},{1,8},{2,9},{3,10},{4,11},{5,12},{6,13},{7,14},{8,23},{9,16... | collective-permute-start | bytes 491528 | tf_op jit(solution)/shard_map/ppermute | solution.py:110
  14.5 1.5 %collective-permute-start.3 = (f32[2,5,32,128]{3,2,1,0:T(8,128)S(1)}, f32[2,5,32,128]{3,2,1,0:T(8,128)S(1)}, u32[]{:S(2)}, u32[]{:S(2)}) collective-permute-start(f32[2,5,32,128]{3,2,1,0:T(8,128)S(1)} %get-tuple-element.136), channel_id=1, source_target_pairs={{0,9},{1,10},{2,11},{3,12},{4,13},{5,14},{6,15},{7,8},{8,17},{9,18... | collective-permute-start | bytes 491528 | tf_op jit(solution)/shard_map/ppermute | solution.py:110
  16.0 8.2 %collective-permute-done.got_before_ref = f32[2,13,32,128]{3,2,1,0:T(8,128)S(1)} collective-permute-done((f32[2,13,32,128]{3,2,1,0:T(8,128)S(1)}, f32[2,13,32,128]{3,2,1,0:T(8,128)S(1)}, u32[]{:S(2)}, u32[]{:S(2)}) %collective-permute-start) | collective-permute-done | bytes 426016 | tf_op jit(solution)/shard_map/ppermute | solution.py:573
  24.2 2.3 %collective-permute-done.1.got_after_ref = f32[2,13,32,128]{3,2,1,0:T(8,128)S(1)} collective-permute-done((f32[2,13,32,128]{3,2,1,0:T(8,128)S(1)}, f32[2,13,32,128]{3,2,1,0:T(8,128)S(1)}, u32[]{:S(2)}, u32[]{:S(2)}) %collective-permute-start.1) | collective-permute-done | bytes 426016 | tf_op jit(solution)/shard_map/ppermute | solution.py:577
  26.5 0.8 copy-done.4
  27.3 3.7 %shard_map.46 = (f32[4,2,8,32,128]{4,3,2,1,0:T(8,128)}, f32[2,10,32,128]{3,2,1,0:T(8,128)}, f32[2,10,32,128]{3,2,1,0:T(8,128)}, f32[2,8,16,128]{3,2,1,0:T(8,128)...) custom-call(f32[2]{0:T(128)} %diff_ref.13, ...), custom_call_target="tpu_custom_call" | custom-call | tf_op jit(solution)/shard_map/pallas_call | solution.py:514
  31.0 0.6 copy-done.16
  31.8 4.9 %shard_map.47 = (f32[2,10,32,128]{3,2,1,0:T(8,128)}, f32[2,10,32,128]{3,2,1,0:T(8,128)}, f32[2,10,32,128]{3,2,1,0:T(8,128)}, f32[2,10,32,128]{3,2,1,0:T(8,128)},...) custom-call(f32[2]{0:T(128)} %diff_ref.13, ...), custom_call_target="tpu_custom_call" | custom-call | tf_op jit(solution)/shard_map/pallas_call | solution.py:315
  36.6 1.3 collective-permute-start.7
  37.9 8.2 %collective-permute-start.8 = (f32[2,5,32,128]{3,2,1,0:T(8,128)}, f32[2,5,32,128]{3,2,1,0:T(8,128)S(1)}, u32[]{:S(2)}, u32[]{:S(2)}) collective-permute-start(f32[2,5,32,128]{3,2,1,0:T(8,128)} %get-tuple-element.81), channel_id=1, source_target_pairs={{0,9},{1,10},{2,11},{3,12},{4,13},{5,14},{6,15},{7,8},{8,17},{9,18... | collective-permute-start | bytes 491528 | tf_op jit(solution)/shard_map/ppermute | solution.py:110
  46.1 5.1 %collective-permute-start.9 = (f32[2,5,32,128]{3,2,1,0:T(8,128)}, f32[2,5,32,128]{3,2,1,0:T(8,128)S(1)}, u32[]{:S(2)}, u32[]{:S(2)}) collective-permute-start(f32[2,5,32,128]{3,2,1,0:T(8,128)} %get-tuple-element.82), channel_id=1, source_target_pairs={{0,15},{1,8},{2,9},{3,10},{4,11},{5,12},{6,13},{7,14},{8,23},{9,16... | collective-permute-start | bytes 491528 | tf_op jit(solution)/shard_map/ppermute | solution.py:110
  51.3 4.7 %collective-permute-start.6 = (f32[2,6,16,128]{3,2,1,0:T(8,128)}, f32[2,6,16,128]{3,2,1,0:T(8,128)S(1)}, u32[]{:S(2)}, u32[]{:S(2)}) collective-permute-start(f32[2,6,16,128]{3,2,1,0:T(8,128)} %get-tuple-element.79), channel_id=1, source_target_pairs={{1,0},{2,1},{3,2},{4,3},{5,4},{6,5},{7,6},{0,7},{9,8},{10,9},{11,1... | collective-permute-start | bytes 294920 | tf_op jit(solution)/shard_map/ppermute | solution.py:629
  56.0 2.9 %collective-permute-done.5.cbefore_ref = f32[2,6,16,128]{3,2,1,0:T(8,128)S(1)} collective-permute-done((f32[2,6,16,128]{3,2,1,0:T(8,128)}, f32[2,6,16,128]{3,2,1,0:T(8,128)S(1)}, u32[]{:S(2)}, u32[]{:S(2)}) %collective-permute-start.5) | collective-permute-done | bytes 98336 | tf_op jit(solution)/shard_map/ppermute | solution.py:628
  59.0 0.5 copy-done.18
  59.6 4.5 %shard_map.48 = (f32[4,2,8,32,128]{4,3,2,1,0:T(8,128)}, f32[2,10,32,128]{3,2,1,0:T(8,128)}, f32[2,10,32,128]{3,2,1,0:T(8,128)}, f32[2,4,16,128]{3,2,1,0:T(8,128)...) custom-call(f32[2]{0:T(128)} %diff_ref.13, f32[4,2,4,16,128]{4,3,2,1,0:T(8,128)} %get-tuple-element.86.cown_ref, ...), custom_call_target="tpu_custom_call" | custom-call | tf_op jit(solution)/shard_map/pallas_call | solution.py:450
  64.2 1.1 collective-permute-start.13
  65.2 3.7 %collective-permute-start.14 = (f32[2,10,32,128]{3,2,1,0:T(8,128)}, f32[2,10,32,128]{3,2,1,0:T(8,128)S(1)}, u32[]{:S(2)}, u32[]{:S(2)}) collective-permute-start(f32[2,10,32,128]{3,2,1,0:T(8,128)} %get-tuple-element.101), channel_id=1, source_target_pairs={{1,0},{2,1},{3,2},{4,3},{5,4},{6,5},{7,6},{0,7},{9,8},{10,9},{11,1... | collective-permute-start | bytes 983048 | tf_op jit(solution)/shard_map/ppermute | solution.py:655
  69.0 1.3 collective-permute-start.10
  70.3 1.5 %collective-permute-start.11 = (f32[2,3,16,128]{3,2,1,0:T(8,128)}, f32[2,3,16,128]{3,2,1,0:T(8,128)S(1)}, u32[]{:S(2)}, u32[]{:S(2)}) collective-permute-start(f32[2,3,16,128]{3,2,1,0:T(8,128)} %get-tuple-element.97), channel_id=1, source_target_pairs={{0,9},{1,10},{2,11},{3,12},{4,13},{5,14},{6,15},{7,8},{8,17},{9,18... | collective-permute-start | bytes 147464 | tf_op jit(solution)/shard_map/ppermute | solution.py:110
  71.8 8.1 %collective-permute-start.12 = (f32[2,3,16,128]{3,2,1,0:T(8,128)}, f32[2,3,16,128]{3,2,1,0:T(8,128)S(1)}, u32[]{:S(2)}, u32[]{:S(2)}) collective-permute-start(f32[2,3,16,128]{3,2,1,0:T(8,128)} %get-tuple-element.98), channel_id=1, source_target_pairs={{0,15},{1,8},{2,9},{3,10},{4,11},{5,12},{6,13},{7,14},{8,23},{9,16... | collective-permute-start | bytes 147464 | tf_op jit(solution)/shard_map/ppermute | solution.py:110
  79.8 0.7 collective-permute-done.11.refs_4_
  80.5 1.4 collective-permute-done.12.refs_5_
  81.9 0.2 collective-permute-done.14.refs_8_
  82.1 0.4 copy-done.27
  82.8 4.9 %shard_map.49 = (f32[2,10,32,128]{3,2,1,0:T(8,128)}, f32[2,10,32,128]{3,2,1,0:T(8,128)}, f32[2,10,32,128]{3,2,1,0:T(8,128)}, f32[2,10,32,128]{3,2,1,0:T(8,128)},...) custom-call(f32[2]{0:T(128)} %diff_ref.13, ...), custom_call_target="tpu_custom_call" | custom-call | tf_op jit(solution)/shard_map/pallas_call | solution.py:315
  87.8 2.4 %collective-permute-start.17 = (f32[2,8,32,128]{3,2,1,0:T(8,128)}, f32[2,8,32,128]{3,2,1,0:T(8,128)S(1)}, u32[]{:S(2)}, u32[]{:S(2)}) collective-permute-start(f32[2,8,32,128]{3,2,1,0:T(8,128)} %get-tuple-element.105), channel_id=1, source_target_pairs={{0,8},{1,9},{2,10},{3,11},{4,12},{5,13},{6,14},{7,15},{8,16},{9,17... | collective-permute-start | bytes 786440 | tf_op jit(solution)/shard_map/ppermute | solution.py:110
  90.2 2.3 %collective-permute-start.18 = (f32[2,5,32,128]{3,2,1,0:T(8,128)}, f32[2,5,32,128]{3,2,1,0:T(8,128)S(1)}, u32[]{:S(2)}, u32[]{:S(2)}) collective-permute-start(f32[2,5,32,128]{3,2,1,0:T(8,128)} %get-tuple-element.106), channel_id=1, source_target_pairs={{0,9},{1,10},{2,11},{3,12},{4,13},{5,14},{6,15},{7,8},{8,17},{9,18... | collective-permute-start | bytes 491528 | tf_op jit(solution)/shard_map/ppermute | solution.py:110
  92.5 6.2 %collective-permute-start.19 = (f32[2,5,32,128]{3,2,1,0:T(8,128)}, f32[2,5,32,128]{3,2,1,0:T(8,128)S(1)}, u32[]{:S(2)}, u32[]{:S(2)}) collective-permute-start(f32[2,5,32,128]{3,2,1,0:T(8,128)} %get-tuple-element.107), channel_id=1, source_target_pairs={{0,15},{1,8},{2,9},{3,10},{4,11},{5,12},{6,13},{7,14},{8,23},{9,16... | collective-permute-start | bytes 491528 | tf_op jit(solution)/shard_map/ppermute | solution.py:110
  98.8 4.7 %collective-permute-start.16 = (f32[2,6,16,128]{3,2,1,0:T(8,128)}, f32[2,6,16,128]{3,2,1,0:T(8,128)S(1)}, u32[]{:S(2)}, u32[]{:S(2)}) collective-permute-start(f32[2,6,16,128]{3,2,1,0:T(8,128)} %get-tuple-element.104), channel_id=1, source_target_pairs={{1,0},{2,1},{3,2},{4,3},{5,4},{6,5},{7,6},{0,7},{9,8},{10,9},{11,1... | collective-permute-start | bytes 294920 | tf_op jit(solution)/shard_map/ppermute | solution.py:629
  103.5 2.8 %collective-permute-done.15.cbefore_ref = f32[2,6,16,128]{3,2,1,0:T(8,128)S(1)} collective-permute-done((f32[2,6,16,128]{3,2,1,0:T(8,128)}, f32[2,6,16,128]{3,2,1,0:T(8,128)S(1)}, u32[]{:S(2)}, u32[]{:S(2)}) %collective-permute-start.15) | collective-permute-done | bytes 98336 | tf_op jit(solution)/shard_map/ppermute | solution.py:628
  106.4 0.6 copy-done.19
  107.0 4.5 %shard_map.50 = (f32[4,2,8,32,128]{4,3,2,1,0:T(8,128)}, f32[2,10,32,128]{3,2,1,0:T(8,128)}, f32[2,10,32,128]{3,2,1,0:T(8,128)}, f32[2,4,16,128]{3,2,1,0:T(8,128)...) custom-call(f32[2]{0:T(128)} %diff_ref.13, f32[4,2,4,16,128]{4,3,2,1,0:T(8,128)} %get-tuple-element.111.cown_ref, ...), custom_call_target="tpu_custom_call" | custom-call | tf_op jit(solution)/shard_map/pallas_call | solution.py:450
  111.5 1.0 collective-permute-start.23
  112.5 3.8 %collective-permute-start.24 = (f32[2,10,32,128]{3,2,1,0:T(8,128)}, f32[2,10,32,128]{3,2,1,0:T(8,128)S(1)}, u32[]{:S(2)}, u32[]{:S(2)}) collective-permute-start(f32[2,10,32,128]{3,2,1,0:T(8,128)} %get-tuple-element.125), channel_id=1, source_target_pairs={{1,0},{2,1},{3,2},{4,3},{5,4},{6,5},{7,6},{0,7},{9,8},{10,9},{11,1... | collective-permute-start | bytes 983048 | tf_op jit(solution)/shard_map/ppermute | solution.py:655
  116.3 1.3 collective-permute-start.20
  117.6 1.8 %collective-permute-start.21 = (f32[2,3,16,128]{3,2,1,0:T(8,128)}, f32[2,3,16,128]{3,2,1,0:T(8,128)S(1)}, u32[]{:S(2)}, u32[]{:S(2)}) collective-permute-start(f32[2,3,16,128]{3,2,1,0:T(8,128)} %get-tuple-element.121), channel_id=1, source_target_pairs={{0,9},{1,10},{2,11},{3,12},{4,13},{5,14},{6,15},{7,8},{8,17},{9,18... | collective-permute-start | bytes 147464 | tf_op jit(solution)/shard_map/ppermute | solution.py:110
  119.4 8.7 %collective-permute-start.22 = (f32[2,3,16,128]{3,2,1,0:T(8,128)}, f32[2,3,16,128]{3,2,1,0:T(8,128)S(1)}, u32[]{:S(2)}, u32[]{:S(2)}) collective-permute-start(f32[2,3,16,128]{3,2,1,0:T(8,128)} %get-tuple-element.122), channel_id=1, source_target_pairs={{0,15},{1,8},{2,9},{3,10},{4,11},{5,12},{6,13},{7,14},{8,23},{9,16... | collective-permute-start | bytes 147464 | tf_op jit(solution)/shard_map/ppermute | solution.py:110
  128.2 2.0 %collective-permute-done.22.refs_5_ = f32[2,3,16,128]{3,2,1,0:T(8,128)S(1)} collective-permute-done((f32[2,3,16,128]{3,2,1,0:T(8,128)}, f32[2,3,16,128]{3,2,1,0:T(8,128)S(1)}, u32[]{:S(2)}, u32[]{:S(2)}) %collective-permute-start.22) | collective-permute-done | bytes 49184 | tf_op jit(solution)/shard_map/ppermute | solution.py:110
  130.2 0.6 copy-done.26
  131.1 5.0 %shard_map.51 = (f32[2,10,32,128]{3,2,1,0:T(8,128)}, f32[2,10,32,128]{3,2,1,0:T(8,128)}, f32[2,10,32,128]{3,2,1,0:T(8,128)}, f32[2,10,32,128]{3,2,1,0:T(8,128)},...) custom-call(f32[2]{0:T(128)} %diff_ref.13, ...), custom_call_target="tpu_custom_call" | custom-call | tf_op jit(solution)/shard_map/pallas_call | solution.py:315
  136.1 4.7 %collective-permute-start.26 = (f32[2,2,16,128]{3,2,1,0:T(8,128)}, f32[2,2,16,128]{3,2,1,0:T(8,128)S(1)}, u32[]{:S(2)}, u32[]{:S(2)}) collective-permute-start(f32[2,2,16,128]{3,2,1,0:T(8,128)} %get-tuple-element.128), channel_id=1, source_target_pairs={{1,0},{2,1},{3,2},{4,3},{5,4},{6,5},{7,6},{0,7},{9,8},{10,9},{11,1... | collective-permute-start | bytes 98312 | tf_op jit(solution)/shard_map/ppermute | solution.py:629
  140.8 2.1 %collective-permute-done.25.cbefore_ref = f32[2,2,16,128]{3,2,1,0:T(8,128)S(1)} collective-permute-done((f32[2,2,16,128]{3,2,1,0:T(8,128)}, f32[2,2,16,128]{3,2,1,0:T(8,128)S(1)}, u32[]{:S(2)}, u32[]{:S(2)}) %collective-permute-start.25) | collective-permute-done | bytes 32800 | tf_op jit(solution)/shard_map/ppermute | solution.py:628
  142.9 0.6 copy-done.28
  143.6 2.9 %shard_map.52 = f32[2,8,32,128]{3,2,1,0:T(8,128)} custom-call(f32[2]{0:T(128)} %diff_ref.13, f32[4,2,4,16,128]{4,3,2,1,0:T(8,128)} %get-tuple-element.126.cown_ref, f32[2,2,16,128]{3,2,1,0:T(8,128)} %copy-done.28, f32[2,2,16,128]{3,2,1,0:T(8,128)} %copy-done.29, f32[2,8,16,128]{3,2,1,0:T(8,128)} %get-tuple-element.76.refs_8_.rate_ref.refs_11_, ...), custom_call_target="tpu_custom_call" | custom-call | tf_op jit(solution)/shard_map/pallas_call | solution.py:450
  (77 shorter events, 1.5 us)
Async XLA Ops:
  0.0 1.1 copy-start.1
  0.0 1.2 copy-start.2
  1.3 23.0 %collective-permute-start = (f32[2,13,32,128]{3,2,1,0:T(8,128)S(1)}, f32[2,13,32,128]{3,2,1,0:T(8,128)S(1)}, u32[]{:S(2)}, u32[]{:S(2)}) collective-permute-start(f32[2,13,32,128]{3,2,1,0:T(8,128)S(1)} %pad_maximum_fusion), channel_id=1, source_target_pairs={{0,1},{1,2},{2,3},{3,4},{4,5},{5,6},{6,7},{7,0},{8,9},{9,10},{10,1... | collective-permute-start | bytes 1277960 | tf_op jit(solution)/shard_map/ppermute | solution.py:573
  4.3 3.2 %copy-start = (f32[1,2,8,32,128]{4,3,2,1,0:T(8,128)S(1)}, f32[1,2,8,32,128]{4,3,2,1,0:T(8,128)}, u32[]{:S(2)}) copy-start(f32[1,2,8,32,128]{4,3,2,1,0:T(8,128)} %param.4) | copy-start | bytes 786436
  4.3 22.2 %collective-permute-start.1 = (f32[2,13,32,128]{3,2,1,0:T(8,128)S(1)}, f32[2,13,32,128]{3,2,1,0:T(8,128)S(1)}, u32[]{:S(2)}, u32[]{:S(2)}) collective-permute-start(f32[2,13,32,128]{3,2,1,0:T(8,128)S(1)} %pad_maximum_fusion.1), channel_id=1, source_target_pairs={{1,0},{2,1},{3,2},{4,3},{5,4},{6,5},{7,6},{0,7},{9,8},{10,9},{11,1... | collective-permute-start | bytes 1277960 | tf_op jit(solution)/shard_map/ppermute | solution.py:577
  7.4 23.5 %collective-permute-start.2 = (f32[2,8,32,128]{3,2,1,0:T(8,128)S(1)}, f32[2,8,32,128]{3,2,1,0:T(8,128)S(1)}, u32[]{:S(2)}, u32[]{:S(2)}) collective-permute-start(f32[2,8,32,128]{3,2,1,0:T(8,128)S(1)} %bitcast.5), channel_id=1, source_target_pairs={{0,8},{1,9},{2,10},{3,11},{4,12},{5,13},{6,14},{7,15},{8,16},{9,17... | collective-permute-start | bytes 786440 | tf_op jit(solution)/shard_map/ppermute | solution.py:110
  8.9 22.0 %collective-permute-start.4 = (f32[2,5,32,128]{3,2,1,0:T(8,128)S(1)}, f32[2,5,32,128]{3,2,1,0:T(8,128)S(1)}, u32[]{:S(2)}, u32[]{:S(2)}) collective-permute-start(f32[2,5,32,128]{3,2,1,0:T(8,128)S(1)} %get-tuple-element.135), channel_id=1, source_target_pairs={{0,15},{1,8},{2,9},{3,10},{4,11},{5,12},{6,13},{7,14},{8,23},{9,16... | collective-permute-start | bytes 491528 | tf_op jit(solution)/shard_map/ppermute | solution.py:110
  14.5 16.5 %collective-permute-start.3 = (f32[2,5,32,128]{3,2,1,0:T(8,128)S(1)}, f32[2,5,32,128]{3,2,1,0:T(8,128)S(1)}, u32[]{:S(2)}, u32[]{:S(2)}) collective-permute-start(f32[2,5,32,128]{3,2,1,0:T(8,128)S(1)} %get-tuple-element.136), channel_id=1, source_target_pairs={{0,9},{1,10},{2,11},{3,12},{4,13},{5,14},{6,15},{7,8},{8,17},{9,18... | collective-permute-start | bytes 491528 | tf_op jit(solution)/shard_map/ppermute | solution.py:110
  24.2 2.3 %copy-start.3 = (f32[2,13,32,128]{3,2,1,0:T(8,128)}, f32[2,13,32,128]{3,2,1,0:T(8,128)S(1)}, u32[]{:S(2)}) copy-start(f32[2,13,32,128]{3,2,1,0:T(8,128)S(1)} %collective-permute-done.got_before_ref) | copy-start | bytes 1277956
  26.5 0.8 copy-start.4
  31.0 0.7 copy-start.16
  31.0 0.7 copy-start.17
  31.0 0.8 copy-start.11
  36.6 22.4 %collective-permute-start.7 = (f32[2,8,32,128]{3,2,1,0:T(8,128)}, f32[2,8,32,128]{3,2,1,0:T(8,128)S(1)}, u32[]{:S(2)}, u32[]{:S(2)}) collective-permute-start(f32[2,8,32,128]{3,2,1,0:T(8,128)} %get-tuple-element.80), channel_id=1, source_target_pairs={{0,8},{1,9},{2,10},{3,11},{4,12},{5,13},{6,14},{7,15},{8,16},{9,17... | collective-permute-start | bytes 786440 | tf_op jit(solution)/shard_map/ppermute | solution.py:110
  37.9 21.1 %collective-permute-start.8 = (f32[2,5,32,128]{3,2,1,0:T(8,128)}, f32[2,5,32,128]{3,2,1,0:T(8,128)S(1)}, u32[]{:S(2)}, u32[]{:S(2)}) collective-permute-start(f32[2,5,32,128]{3,2,1,0:T(8,128)} %get-tuple-element.81), channel_id=1, source_target_pairs={{0,9},{1,10},{2,11},{3,12},{4,13},{5,14},{6,15},{7,8},{8,17},{9,18... | collective-permute-start | bytes 491528 | tf_op jit(solution)/shard_map/ppermute | solution.py:110
  46.1 12.8 %collective-permute-start.9 = (f32[2,5,32,128]{3,2,1,0:T(8,128)}, f32[2,5,32,128]{3,2,1,0:T(8,128)S(1)}, u32[]{:S(2)}, u32[]{:S(2)}) collective-permute-start(f32[2,5,32,128]{3,2,1,0:T(8,128)} %get-tuple-element.82), channel_id=1, source_target_pairs={{0,15},{1,8},{2,9},{3,10},{4,11},{5,12},{6,13},{7,14},{8,23},{9,16... | collective-permute-start | bytes 491528 | tf_op jit(solution)/shard_map/ppermute | solution.py:110
  51.3 7.6 %collective-permute-start.5 = (f32[2,6,16,128]{3,2,1,0:T(8,128)}, f32[2,6,16,128]{3,2,1,0:T(8,128)S(1)}, u32[]{:S(2)}, u32[]{:S(2)}) collective-permute-start(f32[2,6,16,128]{3,2,1,0:T(8,128)} %get-tuple-element.78), channel_id=1, source_target_pairs={{0,1},{1,2},{2,3},{3,4},{4,5},{5,6},{6,7},{7,0},{8,9},{9,10},{10,1... | collective-permute-start | bytes 294920 | tf_op jit(solution)/shard_map/ppermute | solution.py:628
  51.3 7.7 %collective-permute-start.6 = (f32[2,6,16,128]{3,2,1,0:T(8,128)}, f32[2,6,16,128]{3,2,1,0:T(8,128)S(1)}, u32[]{:S(2)}, u32[]{:S(2)}) collective-permute-start(f32[2,6,16,128]{3,2,1,0:T(8,128)} %get-tuple-element.79), channel_id=1, source_target_pairs={{1,0},{2,1},{3,2},{4,3},{5,4},{6,5},{7,6},{0,7},{9,8},{10,9},{11,1... | collective-permute-start | bytes 294920 | tf_op jit(solution)/shard_map/ppermute | solution.py:629
  59.0 5.2 %copy-start.13 = (f32[2,5,32,128]{3,2,1,0:T(8,128)}, f32[2,5,32,128]{3,2,1,0:T(8,128)S(1)}, u32[]{:S(2)}) copy-start(f32[2,5,32,128]{3,2,1,0:T(8,128)S(1)} %collective-permute-done.8.refs_1_) | copy-start | bytes 491524
  59.0 5.2 %copy-start.15 = (f32[2,5,32,128]{3,2,1,0:T(8,128)}, f32[2,5,32,128]{3,2,1,0:T(8,128)S(1)}, u32[]{:S(2)}) copy-start(f32[2,5,32,128]{3,2,1,0:T(8,128)S(1)} %collective-permute-done.9.refs_2_) | copy-start | bytes 491524
  59.0 5.2 %copy-start.10 = (f32[2,8,32,128]{3,2,1,0:T(8,128)}, f32[2,8,32,128]{3,2,1,0:T(8,128)S(1)}, u32[]{:S(2)}) copy-start(f32[2,8,32,128]{3,2,1,0:T(8,128)S(1)} %collective-permute-done.7.refs_0_) | copy-start | bytes 786436
  64.2 17.7 %collective-permute-start.13 = (f32[2,10,32,128]{3,2,1,0:T(8,128)}, f32[2,10,32,128]{3,2,1,0:T(8,128)S(1)}, u32[]{:S(2)}, u32[]{:S(2)}) collective-permute-start(f32[2,10,32,128]{3,2,1,0:T(8,128)} %get-tuple-element.100), channel_id=1, source_target_pairs={{0,1},{1,2},{2,3},{3,4},{4,5},{5,6},{6,7},{7,0},{8,9},{9,10},{10,1... | collective-permute-start | bytes 983048 | tf_op jit(solution)/shard_map/ppermute | solution.py:654
  65.2 16.8 %collective-permute-start.14 = (f32[2,10,32,128]{3,2,1,0:T(8,128)}, f32[2,10,32,128]{3,2,1,0:T(8,128)S(1)}, u32[]{:S(2)}, u32[]{:S(2)}) collective-permute-start(f32[2,10,32,128]{3,2,1,0:T(8,128)} %get-tuple-element.101), channel_id=1, source_target_pairs={{1,0},{2,1},{3,2},{4,3},{5,4},{6,5},{7,6},{0,7},{9,8},{10,9},{11,1... | collective-permute-start | bytes 983048 | tf_op jit(solution)/shard_map/ppermute | solution.py:655
  69.0 12.9 %collective-permute-start.10 = (f32[2,4,16,128]{3,2,1,0:T(8,128)}, f32[2,4,16,128]{3,2,1,0:T(8,128)S(1)}, u32[]{:S(2)}, u32[]{:S(2)}) collective-permute-start(f32[2,4,16,128]{3,2,1,0:T(8,128)} %get-tuple-element.96), channel_id=1, source_target_pairs={{0,8},{1,9},{2,10},{3,11},{4,12},{5,13},{6,14},{7,15},{8,16},{9,17... | collective-permute-start | bytes 196616 | tf_op jit(solution)/shard_map/ppermute | solution.py:110
  70.3 10.2 %collective-permute-start.11 = (f32[2,3,16,128]{3,2,1,0:T(8,128)}, f32[2,3,16,128]{3,2,1,0:T(8,128)S(1)}, u32[]{:S(2)}, u32[]{:S(2)}) collective-permute-start(f32[2,3,16,128]{3,2,1,0:T(8,128)} %get-tuple-element.97), channel_id=1, source_target_pairs={{0,9},{1,10},{2,11},{3,12},{4,13},{5,14},{6,15},{7,8},{8,17},{9,18... | collective-permute-start | bytes 147464 | tf_op jit(solution)/shard_map/ppermute | solution.py:110
  71.8 10.1 %collective-permute-start.12 = (f32[2,3,16,128]{3,2,1,0:T(8,128)}, f32[2,3,16,128]{3,2,1,0:T(8,128)S(1)}, u32[]{:S(2)}, u32[]{:S(2)}) collective-permute-start(f32[2,3,16,128]{3,2,1,0:T(8,128)} %get-tuple-element.98), channel_id=1, source_target_pairs={{0,15},{1,8},{2,9},{3,10},{4,11},{5,12},{6,13},{7,14},{8,23},{9,16... | collective-permute-start | bytes 147464 | tf_op jit(solution)/shard_map/ppermute | solution.py:110
  80.5 1.6 %copy-start.25 = (f32[2,3,16,128]{3,2,1,0:T(8,128)}, f32[2,3,16,128]{3,2,1,0:T(8,128)S(1)}, u32[]{:S(2)}) copy-start(f32[2,3,16,128]{3,2,1,0:T(8,128)S(1)} %collective-permute-done.11.refs_4_) | copy-start | bytes 147460
  81.9 0.8 copy-start.6
  82.1 0.7 copy-start.8
  87.8 18.6 %collective-permute-start.17 = (f32[2,8,32,128]{3,2,1,0:T(8,128)}, f32[2,8,32,128]{3,2,1,0:T(8,128)S(1)}, u32[]{:S(2)}, u32[]{:S(2)}) collective-permute-start(f32[2,8,32,128]{3,2,1,0:T(8,128)} %get-tuple-element.105), channel_id=1, source_target_pairs={{0,8},{1,9},{2,10},{3,11},{4,12},{5,13},{6,14},{7,15},{8,16},{9,17... | collective-permute-start | bytes 786440 | tf_op jit(solution)/shard_map/ppermute | solution.py:110
  90.2 16.1 %collective-permute-start.18 = (f32[2,5,32,128]{3,2,1,0:T(8,128)}, f32[2,5,32,128]{3,2,1,0:T(8,128)S(1)}, u32[]{:S(2)}, u32[]{:S(2)}) collective-permute-start(f32[2,5,32,128]{3,2,1,0:T(8,128)} %get-tuple-element.106), channel_id=1, source_target_pairs={{0,9},{1,10},{2,11},{3,12},{4,13},{5,14},{6,15},{7,8},{8,17},{9,18... | collective-permute-start | bytes 491528 | tf_op jit(solution)/shard_map/ppermute | solution.py:110
  92.5 13.8 %collective-permute-start.19 = (f32[2,5,32,128]{3,2,1,0:T(8,128)}, f32[2,5,32,128]{3,2,1,0:T(8,128)S(1)}, u32[]{:S(2)}, u32[]{:S(2)}) collective-permute-start(f32[2,5,32,128]{3,2,1,0:T(8,128)} %get-tuple-element.107), channel_id=1, source_target_pairs={{0,15},{1,8},{2,9},{3,10},{4,11},{5,12},{6,13},{7,14},{8,23},{9,16... | collective-permute-start | bytes 491528 | tf_op jit(solution)/shard_map/ppermute | solution.py:110
  98.7 7.6 %collective-permute-start.15 = (f32[2,6,16,128]{3,2,1,0:T(8,128)}, f32[2,6,16,128]{3,2,1,0:T(8,128)S(1)}, u32[]{:S(2)}, u32[]{:S(2)}) collective-permute-start(f32[2,6,16,128]{3,2,1,0:T(8,128)} %get-tuple-element.103), channel_id=1, source_target_pairs={{0,1},{1,2},{2,3},{3,4},{4,5},{5,6},{6,7},{7,0},{8,9},{9,10},{10,1... | collective-permute-start | bytes 294920 | tf_op jit(solution)/shard_map/ppermute | solution.py:628
  98.8 7.5 %collective-permute-start.16 = (f32[2,6,16,128]{3,2,1,0:T(8,128)}, f32[2,6,16,128]{3,2,1,0:T(8,128)S(1)}, u32[]{:S(2)}, u32[]{:S(2)}) collective-permute-start(f32[2,6,16,128]{3,2,1,0:T(8,128)} %get-tuple-element.104), channel_id=1, source_target_pairs={{1,0},{2,1},{3,2},{4,3},{5,4},{6,5},{7,6},{0,7},{9,8},{10,9},{11,1... | collective-permute-start | bytes 294920 | tf_op jit(solution)/shard_map/ppermute | solution.py:629
  106.3 0.7 copy-start.21
  106.3 5.2 %copy-start.12 = (f32[2,5,32,128]{3,2,1,0:T(8,128)}, f32[2,5,32,128]{3,2,1,0:T(8,128)S(1)}, u32[]{:S(2)}) copy-start(f32[2,5,32,128]{3,2,1,0:T(8,128)S(1)} %collective-permute-done.18.refs_1_) | copy-start | bytes 491524
  106.3 5.2 %copy-start.14 = (f32[2,5,32,128]{3,2,1,0:T(8,128)}, f32[2,5,32,128]{3,2,1,0:T(8,128)S(1)}, u32[]{:S(2)}) copy-start(f32[2,5,32,128]{3,2,1,0:T(8,128)S(1)} %collective-permute-done.19.refs_2_) | copy-start | bytes 491524
  106.4 5.2 %copy-start.9 = (f32[2,8,32,128]{3,2,1,0:T(8,128)}, f32[2,8,32,128]{3,2,1,0:T(8,128)S(1)}, u32[]{:S(2)}) copy-start(f32[2,8,32,128]{3,2,1,0:T(8,128)S(1)} %collective-permute-done.17.refs_0_) | copy-start | bytes 786436
  111.5 18.7 %collective-permute-start.23 = (f32[2,10,32,128]{3,2,1,0:T(8,128)}, f32[2,10,32,128]{3,2,1,0:T(8,128)S(1)}, u32[]{:S(2)}, u32[]{:S(2)}) collective-permute-start(f32[2,10,32,128]{3,2,1,0:T(8,128)} %get-tuple-element.124), channel_id=1, source_target_pairs={{0,1},{1,2},{2,3},{3,4},{4,5},{5,6},{6,7},{7,0},{8,9},{9,10},{10,1... | collective-permute-start | bytes 983048 | tf_op jit(solution)/shard_map/ppermute | solution.py:654
  112.5 17.7 %collective-permute-start.24 = (f32[2,10,32,128]{3,2,1,0:T(8,128)}, f32[2,10,32,128]{3,2,1,0:T(8,128)S(1)}, u32[]{:S(2)}, u32[]{:S(2)}) collective-permute-start(f32[2,10,32,128]{3,2,1,0:T(8,128)} %get-tuple-element.125), channel_id=1, source_target_pairs={{1,0},{2,1},{3,2},{4,3},{5,4},{6,5},{7,6},{0,7},{9,8},{10,9},{11,1... | collective-permute-start | bytes 983048 | tf_op jit(solution)/shard_map/ppermute | solution.py:655
  116.3 13.9 %collective-permute-start.20 = (f32[2,4,16,128]{3,2,1,0:T(8,128)}, f32[2,4,16,128]{3,2,1,0:T(8,128)S(1)}, u32[]{:S(2)}, u32[]{:S(2)}) collective-permute-start(f32[2,4,16,128]{3,2,1,0:T(8,128)} %get-tuple-element.120), channel_id=1, source_target_pairs={{0,8},{1,9},{2,10},{3,11},{4,12},{5,13},{6,14},{7,15},{8,16},{9,17... | collective-permute-start | bytes 196616 | tf_op jit(solution)/shard_map/ppermute | solution.py:110
  117.6 10.5 %collective-permute-start.21 = (f32[2,3,16,128]{3,2,1,0:T(8,128)}, f32[2,3,16,128]{3,2,1,0:T(8,128)S(1)}, u32[]{:S(2)}, u32[]{:S(2)}) collective-permute-start(f32[2,3,16,128]{3,2,1,0:T(8,128)} %get-tuple-element.121), channel_id=1, source_target_pairs={{0,9},{1,10},{2,11},{3,12},{4,13},{5,14},{6,15},{7,8},{8,17},{9,18... | collective-permute-start | bytes 147464 | tf_op jit(solution)/shard_map/ppermute | solution.py:110
  119.4 10.8 %collective-permute-start.22 = (f32[2,3,16,128]{3,2,1,0:T(8,128)}, f32[2,3,16,128]{3,2,1,0:T(8,128)S(1)}, u32[]{:S(2)}, u32[]{:S(2)}) collective-permute-start(f32[2,3,16,128]{3,2,1,0:T(8,128)} %get-tuple-element.122), channel_id=1, source_target_pairs={{0,15},{1,8},{2,9},{3,10},{4,11},{5,12},{6,13},{7,14},{8,23},{9,16... | collective-permute-start | bytes 147464 | tf_op jit(solution)/shard_map/ppermute | solution.py:110
  128.1 2.1 %copy-start.24 = (f32[2,3,16,128]{3,2,1,0:T(8,128)}, f32[2,3,16,128]{3,2,1,0:T(8,128)S(1)}, u32[]{:S(2)}) copy-start(f32[2,3,16,128]{3,2,1,0:T(8,128)S(1)} %collective-permute-done.21.refs_4_) | copy-start | bytes 147460
  130.2 0.8 copy-start.5
  130.2 0.9 copy-start.7
  136.0 6.9 %collective-permute-start.25 = (f32[2,2,16,128]{3,2,1,0:T(8,128)}, f32[2,2,16,128]{3,2,1,0:T(8,128)S(1)}, u32[]{:S(2)}, u32[]{:S(2)}) collective-permute-start(f32[2,2,16,128]{3,2,1,0:T(8,128)} %get-tuple-element.127), channel_id=1, source_target_pairs={{0,1},{1,2},{2,3},{3,4},{4,5},{5,6},{6,7},{7,0},{8,9},{9,10},{10,1... | collective-permute-start | bytes 98312 | tf_op jit(solution)/shard_map/ppermute | solution.py:628
  136.1 6.8 %collective-permute-start.26 = (f32[2,2,16,128]{3,2,1,0:T(8,128)}, f32[2,2,16,128]{3,2,1,0:T(8,128)S(1)}, u32[]{:S(2)}, u32[]{:S(2)}) collective-permute-start(f32[2,2,16,128]{3,2,1,0:T(8,128)} %get-tuple-element.128), channel_id=1, source_target_pairs={{1,0},{2,1},{3,2},{4,3},{5,4},{6,5},{7,6},{0,7},{9,8},{10,9},{11,1... | collective-permute-start | bytes 98312 | tf_op jit(solution)/shard_map/ppermute | solution.py:629
  (9 other events, 5.7 us)

commit v12 on v9

--- a/solution.py
+++ b/solution.py
@@ -205,7 +205,7 @@
 def sweep_kernel(widths_sent, natural_prior, diff_ref, flag_ref, start_ref, centre_ref, bbefore_ref, bafter_ref,
                  own_ref, before_ref, after_ref, dec_ref, src_ref,
                  rate_ref, n1_ref, n2_ref, n3_ref, n4_ref, e0_ref, b0_ref, cown_ref, clasts_ref,
-                 cfirsts_ref):
+                 cfirsts_ref, v1w_ref):
     spread_table, grouped_table, interp_table, widths = node_tables()
     rows = e0_ref.shape[1]
     hs = (start_ref.shape[1] - rows) // 2
@@ -266,6 +266,7 @@
     hcr = (rate_ref.shape[1] - crows) // 2
     rc = rate_ref[:, hcr:hcr + crows]
     coarse_vals = [kernel_restrict(cut(swept[j], hs - j, 0)) for j in (0, 2, 4)]
+    v1w_ref[...] = kernel_restrict(cut(swept[2], hs - 2, 2))
     half_step = 0.5 * step_length
     coarse_one = (
         coarse_vals[0] + half_step * rc * coarse_vals[1] + integrated[0]
@@ -275,10 +276,11 @@
     for i, piece in enumerate(sent):
         cown_ref[i] = piece
         w = widths_sent[i]
-        if w:
-            clasts_ref[:, offset:offset + w] = piece[:, crows - w:]
-            cfirsts_ref[:, offset:offset + w] = piece[:, :w]
-        offset += w
+        skip = 1 if i == 1 else 0
+        if w - skip:
+            clasts_ref[:, offset:offset + w - skip] = piece[:, crows - w:crows - skip]
+            cfirsts_ref[:, offset:offset + w - skip] = piece[:, skip:w]
+        offset += w - skip
     for m, out in ((1, n1_ref), (2, n2_ref), (3, n3_ref), (4, n4_ref)):
         out[...] = cut(swept[m], hs - m, 1)
     e0_ref[...] = cut(found[0], hs - 1, 0)
@@ -293,13 +295,14 @@
     own = jax.ShapeDtypeStruct((shape[0], rows) + shape[2:], jnp.float32)
     cshape = (shape[0], rows // 2, shape[2] // 2, shape[3])
     cown = jax.ShapeDtypeStruct((4,) + cshape, jnp.float32)
-    cedge = jax.ShapeDtypeStruct((shape[0], sum(widths_sent)) + cshape[2:], jnp.float32)
+    cedge = jax.ShapeDtypeStruct((shape[0], sum(widths_sent) - 1) + cshape[2:], jnp.float32)
+    cwide = jax.ShapeDtypeStruct((shape[0], rows // 2 + 2) + cshape[2:], jnp.float32)
     vmem = pl.BlockSpec(memory_space=pltpu.VMEM)
     return pl.pallas_call(
         functools.partial(sweep_kernel, widths_sent, natural_prior),
-        out_shape=(wide, wide, wide, wide, own, own, cown, cedge, cedge),
+        out_shape=(wide, wide, wide, wide, own, own, cown, cedge, cedge, cwide),
         in_specs=[pl.BlockSpec(memory_space=pltpu.SMEM)] * 2 + [vmem] * 10,
-        out_specs=(vmem,) * 9,
+        out_specs=(vmem,) * 10,
     )(diffusivity, flag, start, *prior, *parts, decay, src, rate_c)
 
 
@@ -315,7 +318,7 @@
     )
 
 
-def finish_kernel(widths_sent, diff_ref, cown_ref, cbefore_ref, cafter_ref, rate_ref, csrc_ref,
+def finish_kernel(widths_sent, diff_ref, cown_ref, cbefore_ref, cafter_ref, v1w_ref, rate_ref, csrc_ref,
                   n1_ref, n2_ref, n3_ref, n4_ref, b_ref, e0_ref, dec_ref, src_ref, *outs):
     spread_table, grouped_table, interp_table, widths = node_tables()
     last = len(outs) == 1
@@ -326,16 +329,19 @@
     offset = 0
     for i in range(4):
         w = widths_sent[i]
-        if w:
+        skip = 1 if i == 1 else 0
+        centre = v1w_ref[...] if skip else cown_ref[i]
+        sw = w - skip
+        if sw:
             joined.append(
                 jnp.concatenate(
-                    [cbefore_ref[:, offset:offset + w], cown_ref[i], cafter_ref[:, offset:offset + w]],
+                    [cbefore_ref[:, offset:offset + sw], centre, cafter_ref[:, offset:offset + sw]],
                     axis=1,
                 )
             )
         else:
-            joined.append(cown_ref[i])
-        offset += w
+            joined.append(centre)
+        offset += sw
     one, mid, low, late = joined
     hcr = (rate_ref.shape[1] - crows) // 2
     hd = (dec_ref.shape[1] - rows) // 2
@@ -595,7 +601,7 @@
 
     def advance(prior, pieces, last, natural):
         widths_sent = (1, 1, 0, 0) if last else (2, 2, 1, 1)
-        n1, n2, n3, n4, e0, b0, cown, clasts, cfirsts = fine_sweep(
+        n1, n2, n3, n4, e0, b0, cown, clasts, cfirsts, v1w = fine_sweep(
             diffusivity, flag, own_ext, prior, pieces, decay[0], src[0], rate_c[0], widths_sent,
             natural,
         )
@@ -603,6 +609,7 @@
             cown,
             lax.ppermute(clasts, "space", up),
             lax.ppermute(cfirsts, "space", down),
+            v1w,
         )
         return finish_round(
             diffusivity, coarse, rate_c[0], source_c[0],

time: 135 us -> 133 us (0.985)
  waiting for transfers between devices: 50.7 us -> 49.1 us
where the time goes in v12:
time: 133 us; the launch traced here: 132 us
  waiting for transfers between devices  49.1 us (37%)
  starting transfers between devices  46.1 us (35%)
  Pallas kernels  30 us (23%)
  local copies, waits for them, and re-layouts  6.15 us (5%)
    ppermute x9, waiting for transfers between devices, moved(): return lax.ppermute(piece, axes, pairs)  21.9 us
    ppermute x9, starting transfers between devices, moved(): return lax.ppermute(piece, axes, pairs)  17.3 us
    pallas_call x3, Pallas kernels, fine_sweep(): pl.pallas_call(functools.partial(sweep_kernel, widths_sent, natural_prior...  14.3 us
    ppermute x1, waiting for transfers between devices, per_device(): lax.ppermute(jnp.concatenate([a[:, rows - w:] for a, w in zip(own_arrays,...  14.3 us
    pallas_call x3, Pallas kernels, finish_round(): pl.pallas_call(functools.partial(finish_kernel, widths_sent), out_shape=o...  12 us
    ppermute x3, starting transfers between devices, advance(): lax.ppermute(cfirsts, 'space', down)  9.92 us
    ppermute x2, starting transfers between devices, per_device(): lax.ppermute(firsts, 'space', down)  8.44 us
    ppermute x3, waiting for transfers between devices, advance(): lax.ppermute(clasts, 'space', up)  7.32 us
  transfers between devices with their start and end apart: 21, of which 10 were waited for; matrix products, arithmetic and copies ran while one was open for 0% of the time, Pallas kernels for 3%

profile of v12, /device:TPU:2, one launch (start us, length us, event | category | flops | bytes accessed | tf_op | source)
XLA Modules:
  0.0 131.7 jit_solution(4328617971960786721)
XLA Ops:
  0.0 1.1 fusion
  1.3 1.6 %collective-permute-start = (f32[2,13,32,128]{3,2,1,0:T(8,128)S(1)}, f32[2,13,32,128]{3,2,1,0:T(8,128)S(1)}, u32[]{:S(2)}, u32[]{:S(2)}) collective-permute-start(f32[2,13,32,128]{3,2,1,0:T(8,128)S(1)} %pad_maximum_fusion), channel_id=1, source_target_pairs={{0,1},{1,2},{2,3},{3,4},{4,5},{5,6},{6,7},{7,0},{8,9},{9,10},{10,1... | collective-permute-start | bytes 1277960 | tf_op jit(solution)/shard_map/ppermute | solution.py:556
  2.9 3.3 %collective-permute-start.1 = (f32[2,13,32,128]{3,2,1,0:T(8,128)S(1)}, f32[2,13,32,128]{3,2,1,0:T(8,128)S(1)}, u32[]{:S(2)}, u32[]{:S(2)}) collective-permute-start(f32[2,13,32,128]{3,2,1,0:T(8,128)S(1)} %pad_maximum_fusion.1), channel_id=1, source_target_pairs={{1,0},{2,1},{3,2},{4,3},{5,4},{6,5},{7,6},{0,7},{9,8},{10,9},{11,1... | collective-permute-start | bytes 1277960 | tf_op jit(solution)/shard_map/ppermute | solution.py:560
  6.1 1.9 %collective-permute-start.2 = (f32[2,8,32,128]{3,2,1,0:T(8,128)S(1)}, f32[2,8,32,128]{3,2,1,0:T(8,128)S(1)}, u32[]{:S(2)}, u32[]{:S(2)}) collective-permute-start(f32[2,8,32,128]{3,2,1,0:T(8,128)S(1)} %bitcast.5), channel_id=1, source_target_pairs={{0,8},{1,9},{2,10},{3,11},{4,12},{5,13},{6,14},{7,15},{8,16},{9,17... | collective-permute-start | bytes 786440 | tf_op jit(solution)/shard_map/ppermute | solution.py:110
  8.0 2.0 %collective-permute-start.4 = (f32[2,5,32,128]{3,2,1,0:T(8,128)S(1)}, f32[2,5,32,128]{3,2,1,0:T(8,128)S(1)}, u32[]{:S(2)}, u32[]{:S(2)}) collective-permute-start(f32[2,5,32,128]{3,2,1,0:T(8,128)S(1)} %get-tuple-element.105), channel_id=1, source_target_pairs={{0,15},{1,8},{2,9},{3,10},{4,11},{5,12},{6,13},{7,14},{8,23},{9,16... | collective-permute-start | bytes 491528 | tf_op jit(solution)/shard_map/ppermute | solution.py:110
  10.1 1.9 %collective-permute-start.3 = (f32[2,5,32,128]{3,2,1,0:T(8,128)S(1)}, f32[2,5,32,128]{3,2,1,0:T(8,128)S(1)}, u32[]{:S(2)}, u32[]{:S(2)}) collective-permute-start(f32[2,5,32,128]{3,2,1,0:T(8,128)S(1)} %get-tuple-element.106), channel_id=1, source_target_pairs={{0,9},{1,10},{2,11},{3,12},{4,13},{5,14},{6,15},{7,8},{8,17},{9,18... | collective-permute-start | bytes 491528 | tf_op jit(solution)/shard_map/ppermute | solution.py:110
  12.0 14.3 %collective-permute-done.got_before_ref = f32[2,13,32,128]{3,2,1,0:T(8,128)S(1)} collective-permute-done((f32[2,13,32,128]{3,2,1,0:T(8,128)S(1)}, f32[2,13,32,128]{3,2,1,0:T(8,128)S(1)}, u32[]{:S(2)}, u32[]{:S(2)}) %collective-permute-start) | collective-permute-done | bytes 426016 | tf_op jit(solution)/shard_map/ppermute | solution.py:556
  26.3 2.3 %collective-permute-done.1.got_after_ref = f32[2,13,32,128]{3,2,1,0:T(8,128)S(1)} collective-permute-done((f32[2,13,32,128]{3,2,1,0:T(8,128)S(1)}, f32[2,13,32,128]{3,2,1,0:T(8,128)S(1)}, u32[]{:S(2)}, u32[]{:S(2)}) %collective-permute-start.1) | collective-permute-done | bytes 426016 | tf_op jit(solution)/shard_map/ppermute | solution.py:560
  28.6 0.8 copy-done.4
  29.4 3.7 %shard_map.46 = (f32[4,2,8,32,128]{4,3,2,1,0:T(8,128)}, f32[2,10,32,128]{3,2,1,0:T(8,128)}, f32[2,10,32,128]{3,2,1,0:T(8,128)}, f32[2,8,16,128]{3,2,1,0:T(8,128)...) custom-call(f32[2]{0:T(128)} %diff_ref.13, ...), custom_call_target="tpu_custom_call" | custom-call | tf_op jit(solution)/shard_map/pallas_call | solution.py:497
  33.1 0.6 copy-done.12
  33.8 0.1 copy-done.9
  33.8 4.8 %shard_map.47 = (f32[2,10,32,128]{3,2,1,0:T(8,128)}, f32[2,10,32,128]{3,2,1,0:T(8,128)}, f32[2,10,32,128]{3,2,1,0:T(8,128)}, f32[2,10,32,128]{3,2,1,0:T(8,128)},...) custom-call(f32[2]{0:T(128)} %diff_ref.13, ...), custom_call_target="tpu_custom_call" | custom-call | tf_op jit(solution)/shard_map/pallas_call | solution.py:301
  38.6 1.0 collective-permute-start.5
  39.6 3.8 %collective-permute-start.6 = (f32[2,5,16,128]{3,2,1,0:T(8,128)}, f32[2,5,16,128]{3,2,1,0:T(8,128)S(1)}, u32[]{:S(2)}, u32[]{:S(2)}) collective-permute-start(f32[2,5,16,128]{3,2,1,0:T(8,128)} %get-tuple-element.64), channel_id=1, source_target_pairs={{1,0},{2,1},{3,2},{4,3},{5,4},{6,5},{7,6},{0,7},{9,8},{10,9},{11,1... | collective-permute-start | bytes 245768 | tf_op jit(solution)/shard_map/ppermute | solution.py:611
  43.4 2.6 %collective-permute-done.5.cbefore_ref = f32[2,5,16,128]{3,2,1,0:T(8,128)S(1)} collective-permute-done((f32[2,5,16,128]{3,2,1,0:T(8,128)}, f32[2,5,16,128]{3,2,1,0:T(8,128)S(1)}, u32[]{:S(2)}, u32[]{:S(2)}) %collective-permute-start.5) | collective-permute-done | bytes 81952 | tf_op jit(solution)/shard_map/ppermute | solution.py:610
  46.0 0.6 copy-done.18
  46.7 4.6 %shard_map.48 = (f32[4,2,8,32,128]{4,3,2,1,0:T(8,128)}, f32[2,10,32,128]{3,2,1,0:T(8,128)}, f32[2,10,32,128]{3,2,1,0:T(8,128)}, f32[2,8,32,128]{3,2,1,0:T(8,128)...) custom-call(f32[2]{0:T(128)} %diff_ref.13, f32[4,2,4,16,128]{4,3,2,1,0:T(8,128)} %get-tuple-element.62.cown_ref, ...), custom_call_target="tpu_custom_call" | custom-call | tf_op jit(solution)/shard_map/pallas_call | solution.py:433
  51.3 0.8 collective-permute-start.10
  52.1 4.0 %collective-permute-start.11 = (f32[2,10,32,128]{3,2,1,0:T(8,128)}, f32[2,10,32,128]{3,2,1,0:T(8,128)S(1)}, u32[]{:S(2)}, u32[]{:S(2)}) collective-permute-start(f32[2,10,32,128]{3,2,1,0:T(8,128)} %get-tuple-element.78), channel_id=1, source_target_pairs={{1,0},{2,1},{3,2},{4,3},{5,4},{6,5},{7,6},{0,7},{9,8},{10,9},{11,1... | collective-permute-start | bytes 983048 | tf_op jit(solution)/shard_map/ppermute | solution.py:636
  56.1 1.9 %collective-permute-start.7 = (f32[2,8,32,128]{3,2,1,0:T(8,128)}, f32[2,8,32,128]{3,2,1,0:T(8,128)S(1)}, u32[]{:S(2)}, u32[]{:S(2)}) collective-permute-start(f32[2,8,32,128]{3,2,1,0:T(8,128)} %get-tuple-element.73), channel_id=1, source_target_pairs={{0,8},{1,9},{2,10},{3,11},{4,12},{5,13},{6,14},{7,15},{8,16},{9,17... | collective-permute-start | bytes 786440 | tf_op jit(solution)/shard_map/ppermute | solution.py:110
  58.0 1.9 %collective-permute-start.8 = (f32[2,5,32,128]{3,2,1,0:T(8,128)}, f32[2,5,32,128]{3,2,1,0:T(8,128)S(1)}, u32[]{:S(2)}, u32[]{:S(2)}) collective-permute-start(f32[2,5,32,128]{3,2,1,0:T(8,128)} %get-tuple-element.74), channel_id=1, source_target_pairs={{0,9},{1,10},{2,11},{3,12},{4,13},{5,14},{6,15},{7,8},{8,17},{9,18... | collective-permute-start | bytes 491528 | tf_op jit(solution)/shard_map/ppermute | solution.py:110
  59.9 1.9 %collective-permute-start.9 = (f32[2,5,32,128]{3,2,1,0:T(8,128)}, f32[2,5,32,128]{3,2,1,0:T(8,128)S(1)}, u32[]{:S(2)}, u32[]{:S(2)}) collective-permute-start(f32[2,5,32,128]{3,2,1,0:T(8,128)} %get-tuple-element.75), channel_id=1, source_target_pairs={{0,15},{1,8},{2,9},{3,10},{4,11},{5,12},{6,13},{7,14},{8,23},{9,16... | collective-permute-start | bytes 491528 | tf_op jit(solution)/shard_map/ppermute | solution.py:110
  61.9 10.3 %collective-permute-done.8.bbefore_ref = f32[2,5,32,128]{3,2,1,0:T(8,128)S(1)} collective-permute-done((f32[2,5,32,128]{3,2,1,0:T(8,128)}, f32[2,5,32,128]{3,2,1,0:T(8,128)S(1)}, u32[]{:S(2)}, u32[]{:S(2)}) %collective-permute-start.8) | collective-permute-done | bytes 163872 | tf_op jit(solution)/shard_map/ppermute | solution.py:110
  72.2 1.5 %collective-permute-done.11.after_ref = f32[2,10,32,128]{3,2,1,0:T(8,128)S(1)} collective-permute-done((f32[2,10,32,128]{3,2,1,0:T(8,128)}, f32[2,10,32,128]{3,2,1,0:T(8,128)S(1)}, u32[]{:S(2)}, u32[]{:S(2)}) %collective-permute-start.11) | collective-permute-done | bytes 327712 | tf_op jit(solution)/shard_map/ppermute | solution.py:636
  73.8 0.7 copy-done.8
  74.5 4.8 %shard_map.49 = (f32[2,10,32,128]{3,2,1,0:T(8,128)}, f32[2,10,32,128]{3,2,1,0:T(8,128)}, f32[2,10,32,128]{3,2,1,0:T(8,128)}, f32[2,10,32,128]{3,2,1,0:T(8,128)},...) custom-call(f32[2]{0:T(128)} %diff_ref.13, ...), custom_call_target="tpu_custom_call" | custom-call | tf_op jit(solution)/shard_map/pallas_call | solution.py:301
  79.3 1.7 %collective-permute-start.12 = (f32[2,5,16,128]{3,2,1,0:T(8,128)}, f32[2,5,16,128]{3,2,1,0:T(8,128)S(1)}, u32[]{:S(2)}, u32[]{:S(2)}) collective-permute-start(f32[2,5,16,128]{3,2,1,0:T(8,128)} %get-tuple-element.80), channel_id=1, source_target_pairs={{0,1},{1,2},{2,3},{3,4},{4,5},{5,6},{6,7},{7,0},{8,9},{9,10},{10,1... | collective-permute-start | bytes 245768 | tf_op jit(solution)/shard_map/ppermute | solution.py:610
  81.0 3.1 %collective-permute-start.13 = (f32[2,5,16,128]{3,2,1,0:T(8,128)}, f32[2,5,16,128]{3,2,1,0:T(8,128)S(1)}, u32[]{:S(2)}, u32[]{:S(2)}) collective-permute-start(f32[2,5,16,128]{3,2,1,0:T(8,128)} %get-tuple-element.81), channel_id=1, source_target_pairs={{1,0},{2,1},{3,2},{4,3},{5,4},{6,5},{7,6},{0,7},{9,8},{10,9},{11,1... | collective-permute-start | bytes 245768 | tf_op jit(solution)/shard_map/ppermute | solution.py:611
  84.1 2.8 %collective-permute-done.12.cbefore_ref = f32[2,5,16,128]{3,2,1,0:T(8,128)S(1)} collective-permute-done((f32[2,5,16,128]{3,2,1,0:T(8,128)}, f32[2,5,16,128]{3,2,1,0:T(8,128)S(1)}, u32[]{:S(2)}, u32[]{:S(2)}) %collective-permute-start.12) | collective-permute-done | bytes 81952 | tf_op jit(solution)/shard_map/ppermute | solution.py:610
  86.8 1.2 collective-permute-done.13.cafter_ref
  88.1 0.6 copy-done.21
  88.7 4.5 %shard_map.50 = (f32[4,2,8,32,128]{4,3,2,1,0:T(8,128)}, f32[2,10,32,128]{3,2,1,0:T(8,128)}, f32[2,10,32,128]{3,2,1,0:T(8,128)}, f32[2,8,32,128]{3,2,1,0:T(8,128)...) custom-call(f32[2]{0:T(128)} %diff_ref.13, f32[4,2,4,16,128]{4,3,2,1,0:T(8,128)} %get-tuple-element.79.cown_ref, ...), custom_call_target="tpu_custom_call" | custom-call | tf_op jit(solution)/shard_map/pallas_call | solution.py:433
  93.2 0.3 collective-permute-start.17
  93.5 4.5 %collective-permute-start.18 = (f32[2,10,32,128]{3,2,1,0:T(8,128)}, f32[2,10,32,128]{3,2,1,0:T(8,128)S(1)}, u32[]{:S(2)}, u32[]{:S(2)}) collective-permute-start(f32[2,10,32,128]{3,2,1,0:T(8,128)} %get-tuple-element.94), channel_id=1, source_target_pairs={{1,0},{2,1},{3,2},{4,3},{5,4},{6,5},{7,6},{0,7},{9,8},{10,9},{11,1... | collective-permute-start | bytes 983048 | tf_op jit(solution)/shard_map/ppermute | solution.py:636
  98.0 1.9 %collective-permute-start.14 = (f32[2,8,32,128]{3,2,1,0:T(8,128)}, f32[2,8,32,128]{3,2,1,0:T(8,128)S(1)}, u32[]{:S(2)}, u32[]{:S(2)}) collective-permute-start(f32[2,8,32,128]{3,2,1,0:T(8,128)} %get-tuple-element.89), channel_id=1, source_target_pairs={{0,8},{1,9},{2,10},{3,11},{4,12},{5,13},{6,14},{7,15},{8,16},{9,17... | collective-permute-start | bytes 786440 | tf_op jit(solution)/shard_map/ppermute | solution.py:110
  99.9 1.9 %collective-permute-start.15 = (f32[2,5,32,128]{3,2,1,0:T(8,128)}, f32[2,5,32,128]{3,2,1,0:T(8,128)S(1)}, u32[]{:S(2)}, u32[]{:S(2)}) collective-permute-start(f32[2,5,32,128]{3,2,1,0:T(8,128)} %get-tuple-element.90), channel_id=1, source_target_pairs={{0,9},{1,10},{2,11},{3,12},{4,13},{5,14},{6,15},{7,8},{8,17},{9,18... | collective-permute-start | bytes 491528 | tf_op jit(solution)/shard_map/ppermute | solution.py:110
  101.9 1.9 %collective-permute-start.16 = (f32[2,5,32,128]{3,2,1,0:T(8,128)}, f32[2,5,32,128]{3,2,1,0:T(8,128)S(1)}, u32[]{:S(2)}, u32[]{:S(2)}) collective-permute-start(f32[2,5,32,128]{3,2,1,0:T(8,128)} %get-tuple-element.91), channel_id=1, source_target_pairs={{0,15},{1,8},{2,9},{3,10},{4,11},{5,12},{6,13},{7,14},{8,23},{9,16... | collective-permute-start | bytes 491528 | tf_op jit(solution)/shard_map/ppermute | solution.py:110
  103.8 11.6 %collective-permute-done.15.bbefore_ref = f32[2,5,32,128]{3,2,1,0:T(8,128)S(1)} collective-permute-done((f32[2,5,32,128]{3,2,1,0:T(8,128)}, f32[2,5,32,128]{3,2,1,0:T(8,128)S(1)}, u32[]{:S(2)}, u32[]{:S(2)}) %collective-permute-start.15) | collective-permute-done | bytes 163872 | tf_op jit(solution)/shard_map/ppermute | solution.py:110
  115.4 0.5 collective-permute-done.18.after_ref
  116.2 0.1 copy-done.5
  116.3 0.4 copy-done.7
  116.7 4.8 %shard_map.51 = (f32[2,10,32,128]{3,2,1,0:T(8,128)}, f32[2,10,32,128]{3,2,1,0:T(8,128)}, f32[2,10,32,128]{3,2,1,0:T(8,128)}, f32[2,10,32,128]{3,2,1,0:T(8,128)},...) custom-call(f32[2]{0:T(128)} %diff_ref.13, ...), custom_call_target="tpu_custom_call" | custom-call | tf_op jit(solution)/shard_map/pallas_call | solution.py:301
  121.5 1.7 %collective-permute-start.19 = (f32[2,1,16,128]{3,2,1,0:T(8,128)}, f32[2,1,16,128]{3,2,1,0:T(8,128)S(1)}, u32[]{:S(2)}, u32[]{:S(2)}) collective-permute-start(f32[2,1,16,128]{3,2,1,0:T(8,128)} %get-tuple-element.96), channel_id=1, source_target_pairs={{0,1},{1,2},{2,3},{3,4},{4,5},{5,6},{6,7},{7,0},{8,9},{9,10},{10,1... | collective-permute-start | bytes 49160 | tf_op jit(solution)/shard_map/ppermute | solution.py:610
  123.2 3.1 %collective-permute-start.20 = (f32[2,1,16,128]{3,2,1,0:T(8,128)}, f32[2,1,16,128]{3,2,1,0:T(8,128)S(1)}, u32[]{:S(2)}, u32[]{:S(2)}) collective-permute-start(f32[2,1,16,128]{3,2,1,0:T(8,128)} %get-tuple-element.97), channel_id=1, source_target_pairs={{1,0},{2,1},{3,2},{4,3},{5,4},{6,5},{7,6},{0,7},{9,8},{10,9},{11,1... | collective-permute-start | bytes 49160 | tf_op jit(solution)/shard_map/ppermute | solution.py:611
  126.2 1.9 %collective-permute-done.19.cbefore_ref = f32[2,1,16,128]{3,2,1,0:T(8,128)S(1)} collective-permute-done((f32[2,1,16,128]{3,2,1,0:T(8,128)}, f32[2,1,16,128]{3,2,1,0:T(8,128)S(1)}, u32[]{:S(2)}, u32[]{:S(2)}) %collective-permute-start.19) | collective-permute-done | bytes 16416 | tf_op jit(solution)/shard_map/ppermute | solution.py:610
  128.2 0.6 copy-done.22
  128.8 2.9 %shard_map.52 = f32[2,8,32,128]{3,2,1,0:T(8,128)} custom-call(f32[2]{0:T(128)} %diff_ref.13, f32[4,2,4,16,128]{4,3,2,1,0:T(8,128)} %get-tuple-element.95.cown_ref, f32[2,1,16,128]{3,2,1,0:T(8,128)} %copy-done.22, f32[2,1,16,128]{3,2,1,0:T(8,128)} %copy-done.23, f32[2,6,16,128]{3,2,1,0:T(8,128)} %get-tuple-element.98.v1w_ref, ...), custom_call_target="tpu_custom_call" | custom-call | tf_op jit(solution)/shard_map/pallas_call | solution.py:433
  (53 shorter events, 0.6 us)
Async XLA Ops:
  0.0 1.1 copy-start.1
  0.0 1.2 copy-start.2
  1.3 25.0 %collective-permute-start = (f32[2,13,32,128]{3,2,1,0:T(8,128)S(1)}, f32[2,13,32,128]{3,2,1,0:T(8,128)S(1)}, u32[]{:S(2)}, u32[]{:S(2)}) collective-permute-start(f32[2,13,32,128]{3,2,1,0:T(8,128)S(1)} %pad_maximum_fusion), channel_id=1, source_target_pairs={{0,1},{1,2},{2,3},{3,4},{4,5},{5,6},{6,7},{7,0},{8,9},{9,10},{10,1... | collective-permute-start | bytes 1277960 | tf_op jit(solution)/shard_map/ppermute | solution.py:556
  2.8 3.3 %copy-start = (f32[1,2,8,32,128]{4,3,2,1,0:T(8,128)S(1)}, f32[1,2,8,32,128]{4,3,2,1,0:T(8,128)}, u32[]{:S(2)}) copy-start(f32[1,2,8,32,128]{4,3,2,1,0:T(8,128)} %param.4) | copy-start | bytes 786436
  2.9 25.7 %collective-permute-start.1 = (f32[2,13,32,128]{3,2,1,0:T(8,128)S(1)}, f32[2,13,32,128]{3,2,1,0:T(8,128)S(1)}, u32[]{:S(2)}, u32[]{:S(2)}) collective-permute-start(f32[2,13,32,128]{3,2,1,0:T(8,128)S(1)} %pad_maximum_fusion.1), channel_id=1, source_target_pairs={{1,0},{2,1},{3,2},{4,3},{5,4},{6,5},{7,6},{0,7},{9,8},{10,9},{11,1... | collective-permute-start | bytes 1277960 | tf_op jit(solution)/shard_map/ppermute | solution.py:560
  6.1 26.9 %collective-permute-start.2 = (f32[2,8,32,128]{3,2,1,0:T(8,128)S(1)}, f32[2,8,32,128]{3,2,1,0:T(8,128)S(1)}, u32[]{:S(2)}, u32[]{:S(2)}) collective-permute-start(f32[2,8,32,128]{3,2,1,0:T(8,128)S(1)} %bitcast.5), channel_id=1, source_target_pairs={{0,8},{1,9},{2,10},{3,11},{4,12},{5,13},{6,14},{7,15},{8,16},{9,17... | collective-permute-start | bytes 786440 | tf_op jit(solution)/shard_map/ppermute | solution.py:110
  8.0 25.0 %collective-permute-start.4 = (f32[2,5,32,128]{3,2,1,0:T(8,128)S(1)}, f32[2,5,32,128]{3,2,1,0:T(8,128)S(1)}, u32[]{:S(2)}, u32[]{:S(2)}) collective-permute-start(f32[2,5,32,128]{3,2,1,0:T(8,128)S(1)} %get-tuple-element.105), channel_id=1, source_target_pairs={{0,15},{1,8},{2,9},{3,10},{4,11},{5,12},{6,13},{7,14},{8,23},{9,16... | collective-permute-start | bytes 491528 | tf_op jit(solution)/shard_map/ppermute | solution.py:110
  10.1 23.0 %collective-permute-start.3 = (f32[2,5,32,128]{3,2,1,0:T(8,128)S(1)}, f32[2,5,32,128]{3,2,1,0:T(8,128)S(1)}, u32[]{:S(2)}, u32[]{:S(2)}) collective-permute-start(f32[2,5,32,128]{3,2,1,0:T(8,128)S(1)} %get-tuple-element.106), channel_id=1, source_target_pairs={{0,9},{1,10},{2,11},{3,12},{4,13},{5,14},{6,15},{7,8},{8,17},{9,18... | collective-permute-start | bytes 491528 | tf_op jit(solution)/shard_map/ppermute | solution.py:110
  26.3 2.3 %copy-start.3 = (f32[2,13,32,128]{3,2,1,0:T(8,128)}, f32[2,13,32,128]{3,2,1,0:T(8,128)S(1)}, u32[]{:S(2)}) copy-start(f32[2,13,32,128]{3,2,1,0:T(8,128)S(1)} %collective-permute-done.got_before_ref) | copy-start | bytes 1277956
  28.6 0.8 copy-start.4
  33.0 0.7 copy-start.12
  33.1 0.7 copy-start.13
  33.1 0.8 copy-start.9
  38.6 7.4 %collective-permute-start.5 = (f32[2,5,16,128]{3,2,1,0:T(8,128)}, f32[2,5,16,128]{3,2,1,0:T(8,128)S(1)}, u32[]{:S(2)}, u32[]{:S(2)}) collective-permute-start(f32[2,5,16,128]{3,2,1,0:T(8,128)} %get-tuple-element.63), channel_id=1, source_target_pairs={{0,1},{1,2},{2,3},{3,4},{4,5},{5,6},{6,7},{7,0},{8,9},{9,10},{10,1... | collective-permute-start | bytes 245768 | tf_op jit(solution)/shard_map/ppermute | solution.py:610
  39.6 6.4 %collective-permute-start.6 = (f32[2,5,16,128]{3,2,1,0:T(8,128)}, f32[2,5,16,128]{3,2,1,0:T(8,128)S(1)}, u32[]{:S(2)}, u32[]{:S(2)}) collective-permute-start(f32[2,5,16,128]{3,2,1,0:T(8,128)} %get-tuple-element.64), channel_id=1, source_target_pairs={{1,0},{2,1},{3,2},{4,3},{5,4},{6,5},{7,6},{0,7},{9,8},{10,9},{11,1... | collective-permute-start | bytes 245768 | tf_op jit(solution)/shard_map/ppermute | solution.py:611
  46.0 0.6 copy-start.18
  46.0 0.7 copy-start.20
  51.3 20.9 %collective-permute-start.10 = (f32[2,10,32,128]{3,2,1,0:T(8,128)}, f32[2,10,32,128]{3,2,1,0:T(8,128)S(1)}, u32[]{:S(2)}, u32[]{:S(2)}) collective-permute-start(f32[2,10,32,128]{3,2,1,0:T(8,128)} %get-tuple-element.77), channel_id=1, source_target_pairs={{0,1},{1,2},{2,3},{3,4},{4,5},{5,6},{6,7},{7,0},{8,9},{9,10},{10,1... | collective-permute-start | bytes 983048 | tf_op jit(solution)/shard_map/ppermute | solution.py:635
  52.1 21.6 %collective-permute-start.11 = (f32[2,10,32,128]{3,2,1,0:T(8,128)}, f32[2,10,32,128]{3,2,1,0:T(8,128)S(1)}, u32[]{:S(2)}, u32[]{:S(2)}) collective-permute-start(f32[2,10,32,128]{3,2,1,0:T(8,128)} %get-tuple-element.78), channel_id=1, source_target_pairs={{1,0},{2,1},{3,2},{4,3},{5,4},{6,5},{7,6},{0,7},{9,8},{10,9},{11,1... | collective-permute-start | bytes 983048 | tf_op jit(solution)/shard_map/ppermute | solution.py:636
  56.1 16.1 %collective-permute-start.7 = (f32[2,8,32,128]{3,2,1,0:T(8,128)}, f32[2,8,32,128]{3,2,1,0:T(8,128)S(1)}, u32[]{:S(2)}, u32[]{:S(2)}) collective-permute-start(f32[2,8,32,128]{3,2,1,0:T(8,128)} %get-tuple-element.73), channel_id=1, source_target_pairs={{0,8},{1,9},{2,10},{3,11},{4,12},{5,13},{6,14},{7,15},{8,16},{9,17... | collective-permute-start | bytes 786440 | tf_op jit(solution)/shard_map/ppermute | solution.py:110
  58.0 14.2 %collective-permute-start.8 = (f32[2,5,32,128]{3,2,1,0:T(8,128)}, f32[2,5,32,128]{3,2,1,0:T(8,128)S(1)}, u32[]{:S(2)}, u32[]{:S(2)}) collective-permute-start(f32[2,5,32,128]{3,2,1,0:T(8,128)} %get-tuple-element.74), channel_id=1, source_target_pairs={{0,9},{1,10},{2,11},{3,12},{4,13},{5,14},{6,15},{7,8},{8,17},{9,18... | collective-permute-start | bytes 491528 | tf_op jit(solution)/shard_map/ppermute | solution.py:110
  59.9 12.3 %collective-permute-start.9 = (f32[2,5,32,128]{3,2,1,0:T(8,128)}, f32[2,5,32,128]{3,2,1,0:T(8,128)S(1)}, u32[]{:S(2)}, u32[]{:S(2)}) collective-permute-start(f32[2,5,32,128]{3,2,1,0:T(8,128)} %get-tuple-element.75), channel_id=1, source_target_pairs={{0,15},{1,8},{2,9},{3,10},{4,11},{5,12},{6,13},{7,14},{8,23},{9,16... | collective-permute-start | bytes 491528 | tf_op jit(solution)/shard_map/ppermute | solution.py:110
  72.2 1.6 %copy-start.15 = (f32[2,5,32,128]{3,2,1,0:T(8,128)}, f32[2,5,32,128]{3,2,1,0:T(8,128)S(1)}, u32[]{:S(2)}) copy-start(f32[2,5,32,128]{3,2,1,0:T(8,128)S(1)} %collective-permute-done.8.bbefore_ref) | copy-start | bytes 491524
  72.2 1.6 %copy-start.17 = (f32[2,5,32,128]{3,2,1,0:T(8,128)}, f32[2,5,32,128]{3,2,1,0:T(8,128)S(1)}, u32[]{:S(2)}) copy-start(f32[2,5,32,128]{3,2,1,0:T(8,128)S(1)} %collective-permute-done.9.bafter_ref) | copy-start | bytes 491524
  72.2 1.5 %copy-start.11 = (f32[2,8,32,128]{3,2,1,0:T(8,128)}, f32[2,8,32,128]{3,2,1,0:T(8,128)S(1)}, u32[]{:S(2)}) copy-start(f32[2,8,32,128]{3,2,1,0:T(8,128)S(1)} %collective-permute-done.7.centre_ref) | copy-start | bytes 786436
  72.2 1.5 %copy-start.6 = (f32[2,10,32,128]{3,2,1,0:T(8,128)}, f32[2,10,32,128]{3,2,1,0:T(8,128)S(1)}, u32[]{:S(2)}) copy-start(f32[2,10,32,128]{3,2,1,0:T(8,128)S(1)} %collective-permute-done.10.before_ref) | copy-start | bytes 983044
  73.7 0.7 copy-start.8
  79.3 7.5 %collective-permute-start.12 = (f32[2,5,16,128]{3,2,1,0:T(8,128)}, f32[2,5,16,128]{3,2,1,0:T(8,128)S(1)}, u32[]{:S(2)}, u32[]{:S(2)}) collective-permute-start(f32[2,5,16,128]{3,2,1,0:T(8,128)} %get-tuple-element.80), channel_id=1, source_target_pairs={{0,1},{1,2},{2,3},{3,4},{4,5},{5,6},{6,7},{7,0},{8,9},{9,10},{10,1... | collective-permute-start | bytes 245768 | tf_op jit(solution)/shard_map/ppermute | solution.py:610
  81.0 7.1 %collective-permute-start.13 = (f32[2,5,16,128]{3,2,1,0:T(8,128)}, f32[2,5,16,128]{3,2,1,0:T(8,128)S(1)}, u32[]{:S(2)}, u32[]{:S(2)}) collective-permute-start(f32[2,5,16,128]{3,2,1,0:T(8,128)} %get-tuple-element.81), channel_id=1, source_target_pairs={{1,0},{2,1},{3,2},{4,3},{5,4},{6,5},{7,6},{0,7},{9,8},{10,9},{11,1... | collective-permute-start | bytes 245768 | tf_op jit(solution)/shard_map/ppermute | solution.py:611
  86.8 1.2 copy-start.19
  88.1 0.6 copy-start.21
  93.2 22.2 %collective-permute-start.17 = (f32[2,10,32,128]{3,2,1,0:T(8,128)}, f32[2,10,32,128]{3,2,1,0:T(8,128)S(1)}, u32[]{:S(2)}, u32[]{:S(2)}) collective-permute-start(f32[2,10,32,128]{3,2,1,0:T(8,128)} %get-tuple-element.93), channel_id=1, source_target_pairs={{0,1},{1,2},{2,3},{3,4},{4,5},{5,6},{6,7},{7,0},{8,9},{9,10},{10,1... | collective-permute-start | bytes 983048 | tf_op jit(solution)/shard_map/ppermute | solution.py:635
  93.5 22.4 %collective-permute-start.18 = (f32[2,10,32,128]{3,2,1,0:T(8,128)}, f32[2,10,32,128]{3,2,1,0:T(8,128)S(1)}, u32[]{:S(2)}, u32[]{:S(2)}) collective-permute-start(f32[2,10,32,128]{3,2,1,0:T(8,128)} %get-tuple-element.94), channel_id=1, source_target_pairs={{1,0},{2,1},{3,2},{4,3},{5,4},{6,5},{7,6},{0,7},{9,8},{10,9},{11,1... | collective-permute-start | bytes 983048 | tf_op jit(solution)/shard_map/ppermute | solution.py:636
  98.0 17.4 %collective-permute-start.14 = (f32[2,8,32,128]{3,2,1,0:T(8,128)}, f32[2,8,32,128]{3,2,1,0:T(8,128)S(1)}, u32[]{:S(2)}, u32[]{:S(2)}) collective-permute-start(f32[2,8,32,128]{3,2,1,0:T(8,128)} %get-tuple-element.89), channel_id=1, source_target_pairs={{0,8},{1,9},{2,10},{3,11},{4,12},{5,13},{6,14},{7,15},{8,16},{9,17... | collective-permute-start | bytes 786440 | tf_op jit(solution)/shard_map/ppermute | solution.py:110
  99.9 15.4 %collective-permute-start.15 = (f32[2,5,32,128]{3,2,1,0:T(8,128)}, f32[2,5,32,128]{3,2,1,0:T(8,128)S(1)}, u32[]{:S(2)}, u32[]{:S(2)}) collective-permute-start(f32[2,5,32,128]{3,2,1,0:T(8,128)} %get-tuple-element.90), channel_id=1, source_target_pairs={{0,9},{1,10},{2,11},{3,12},{4,13},{5,14},{6,15},{7,8},{8,17},{9,18... | collective-permute-start | bytes 491528 | tf_op jit(solution)/shard_map/ppermute | solution.py:110
  101.9 13.5 %collective-permute-start.16 = (f32[2,5,32,128]{3,2,1,0:T(8,128)}, f32[2,5,32,128]{3,2,1,0:T(8,128)S(1)}, u32[]{:S(2)}, u32[]{:S(2)}) collective-permute-start(f32[2,5,32,128]{3,2,1,0:T(8,128)} %get-tuple-element.91), channel_id=1, source_target_pairs={{0,15},{1,8},{2,9},{3,10},{4,11},{5,12},{6,13},{7,14},{8,23},{9,16... | collective-permute-start | bytes 491528 | tf_op jit(solution)/shard_map/ppermute | solution.py:110
  115.4 0.7 copy-start.14
  115.4 0.7 copy-start.16
  115.4 0.8 copy-start.10
  115.4 0.9 copy-start.5
  116.0 0.8 copy-start.7
  121.5 6.7 %collective-permute-start.19 = (f32[2,1,16,128]{3,2,1,0:T(8,128)}, f32[2,1,16,128]{3,2,1,0:T(8,128)S(1)}, u32[]{:S(2)}, u32[]{:S(2)}) collective-permute-start(f32[2,1,16,128]{3,2,1,0:T(8,128)} %get-tuple-element.96), channel_id=1, source_target_pairs={{0,1},{1,2},{2,3},{3,4},{4,5},{5,6},{6,7},{7,0},{8,9},{9,10},{10,1... | collective-permute-start | bytes 49160 | tf_op jit(solution)/shard_map/ppermute | solution.py:610
  123.2 5.0 %collective-permute-start.20 = (f32[2,1,16,128]{3,2,1,0:T(8,128)}, f32[2,1,16,128]{3,2,1,0:T(8,128)S(1)}, u32[]{:S(2)}, u32[]{:S(2)}) collective-permute-start(f32[2,1,16,128]{3,2,1,0:T(8,128)} %get-tuple-element.97), channel_id=1, source_target_pairs={{1,0},{2,1},{3,2},{4,3},{5,4},{6,5},{7,6},{0,7},{9,8},{10,9},{11,1... | collective-permute-start | bytes 49160 | tf_op jit(solution)/shard_map/ppermute | solution.py:611
  128.2 0.6 copy-start.22
  128.2 0.6 copy-start.23

commit v13 on v12

--- a/solution.py
+++ b/solution.py
@@ -411,9 +411,9 @@
         lasts_out[:, offset:offset + w] = part[:, rows - w:]
         firsts_out[:, offset:offset + w] = part[:, :w]
         offset += w
-    u4_out[...] = states[4]
-    u4_last_out[...] = states[4][:, rows - hs:]
-    u4_first_out[...] = states[4][:, :hs]
+    u4_out[...] = news[4]
+    u4_last_out[...] = states[4][:, rows - hs:rows - 1]
+    u4_first_out[...] = states[4][:, 1:hs]
 
 
 def finish_round(diffusivity, coarse, rate_c, source_c, swept, e0, decay, src, last, widths_sent):
@@ -426,8 +426,9 @@
     else:
         sent = sum(START_HALO - 1 - m for m in range(4))
         edge = jax.ShapeDtypeStruct((shape[0], sent) + shape[2:], jnp.float32)
-        rim = jax.ShapeDtypeStruct((shape[0], START_HALO) + shape[2:], jnp.float32)
-        out_shape = (jax.ShapeDtypeStruct((4,) + field.shape, jnp.float32), edge, edge, field, rim, rim)
+        rim = jax.ShapeDtypeStruct((shape[0], START_HALO - 1) + shape[2:], jnp.float32)
+        centre = jax.ShapeDtypeStruct((shape[0], rows + 2) + shape[2:], jnp.float32)
+        out_shape = (jax.ShapeDtypeStruct((4,) + field.shape, jnp.float32), edge, edge, centre, rim, rim)
     vmem = pl.BlockSpec(memory_space=pltpu.VMEM)
     args = (diffusivity, *coarse, rate_c, source_c, *swept[1:], begin, e0, decay, src)
     return pl.pallas_call(

time: 133 us -> 133 us (level)
  no operation moved by 1% of the time
where the time goes in v13:
time: 133 us; the launch traced here: 132 us
  waiting for transfers between devices  49.3 us (37%)
  starting transfers between devices  46.2 us (35%)
  Pallas kernels  30.3 us (23%)
  local copies, waits for them, and re-layouts  6.14 us (5%)
    ppermute x9, waiting for transfers between devices, moved(): return lax.ppermute(piece, axes, pairs)  21.9 us
    ppermute x9, starting transfers between devices, moved(): return lax.ppermute(piece, axes, pairs)  17.4 us
    pallas_call x3, Pallas kernels, fine_sweep(): pl.pallas_call(functools.partial(sweep_kernel, widths_sent, natural_prior...  14.3 us
    ppermute x1, waiting for transfers between devices, per_device(): lax.ppermute(jnp.concatenate([a[:, rows - w:] for a, w in zip(own_arrays,...  14.3 us
    pallas_call x3, Pallas kernels, finish_round(): pl.pallas_call(functools.partial(finish_kernel, widths_sent), out_shape=o...  12.3 us
    ppermute x3, starting transfers between devices, advance(): lax.ppermute(cfirsts, 'space', down)  10.5 us
    ppermute x2, starting transfers between devices, per_device(): lax.ppermute(firsts, 'space', down)  7.93 us
    ppermute x3, waiting for transfers between devices, advance(): lax.ppermute(clasts, 'space', up)  7.65 us
  transfers between devices with their start and end apart: 21, of which 10 were waited for; matrix products, arithmetic and copies ran while one was open for 0% of the time, Pallas kernels for 3%

profile of v13, /device:TPU:2, one launch (start us, length us, event | category | flops | bytes accessed | tf_op | source)
XLA Modules:
  0.0 132.2 jit_solution(3227799251674225990)
XLA Ops:
  0.0 1.1 fusion
  1.3 1.6 %collective-permute-start = (f32[2,13,32,128]{3,2,1,0:T(8,128)S(1)}, f32[2,13,32,128]{3,2,1,0:T(8,128)S(1)}, u32[]{:S(2)}, u32[]{:S(2)}) collective-permute-start(f32[2,13,32,128]{3,2,1,0:T(8,128)S(1)} %pad_maximum_fusion), channel_id=1, source_target_pairs={{0,1},{1,2},{2,3},{3,4},{4,5},{5,6},{6,7},{7,0},{8,9},{9,10},{10,1... | collective-permute-start | bytes 1277960 | tf_op jit(solution)/shard_map/ppermute | solution.py:557
  2.9 3.3 %collective-permute-start.1 = (f32[2,13,32,128]{3,2,1,0:T(8,128)S(1)}, f32[2,13,32,128]{3,2,1,0:T(8,128)S(1)}, u32[]{:S(2)}, u32[]{:S(2)}) collective-permute-start(f32[2,13,32,128]{3,2,1,0:T(8,128)S(1)} %pad_maximum_fusion.1), channel_id=1, source_target_pairs={{1,0},{2,1},{3,2},{4,3},{5,4},{6,5},{7,6},{0,7},{9,8},{10,9},{11,1... | collective-permute-start | bytes 1277960 | tf_op jit(solution)/shard_map/ppermute | solution.py:561
  6.1 1.9 %collective-permute-start.2 = (f32[2,8,32,128]{3,2,1,0:T(8,128)S(1)}, f32[2,8,32,128]{3,2,1,0:T(8,128)S(1)}, u32[]{:S(2)}, u32[]{:S(2)}) collective-permute-start(f32[2,8,32,128]{3,2,1,0:T(8,128)S(1)} %bitcast.5), channel_id=1, source_target_pairs={{0,8},{1,9},{2,10},{3,11},{4,12},{5,13},{6,14},{7,15},{8,16},{9,17... | collective-permute-start | bytes 786440 | tf_op jit(solution)/shard_map/ppermute | solution.py:110
  8.0 2.0 %collective-permute-start.4 = (f32[2,5,32,128]{3,2,1,0:T(8,128)S(1)}, f32[2,5,32,128]{3,2,1,0:T(8,128)S(1)}, u32[]{:S(2)}, u32[]{:S(2)}) collective-permute-start(f32[2,5,32,128]{3,2,1,0:T(8,128)S(1)} %get-tuple-element.105), channel_id=1, source_target_pairs={{0,15},{1,8},{2,9},{3,10},{4,11},{5,12},{6,13},{7,14},{8,23},{9,16... | collective-permute-start | bytes 491528 | tf_op jit(solution)/shard_map/ppermute | solution.py:110
  10.1 1.9 %collective-permute-start.3 = (f32[2,5,32,128]{3,2,1,0:T(8,128)S(1)}, f32[2,5,32,128]{3,2,1,0:T(8,128)S(1)}, u32[]{:S(2)}, u32[]{:S(2)}) collective-permute-start(f32[2,5,32,128]{3,2,1,0:T(8,128)S(1)} %get-tuple-element.106), channel_id=1, source_target_pairs={{0,9},{1,10},{2,11},{3,12},{4,13},{5,14},{6,15},{7,8},{8,17},{9,18... | collective-permute-start | bytes 491528 | tf_op jit(solution)/shard_map/ppermute | solution.py:110
  12.0 14.3 %collective-permute-done.got_before_ref = f32[2,13,32,128]{3,2,1,0:T(8,128)S(1)} collective-permute-done((f32[2,13,32,128]{3,2,1,0:T(8,128)S(1)}, f32[2,13,32,128]{3,2,1,0:T(8,128)S(1)}, u32[]{:S(2)}, u32[]{:S(2)}) %collective-permute-start) | collective-permute-done | bytes 426016 | tf_op jit(solution)/shard_map/ppermute | solution.py:557
  26.3 2.3 %collective-permute-done.1.got_after_ref = f32[2,13,32,128]{3,2,1,0:T(8,128)S(1)} collective-permute-done((f32[2,13,32,128]{3,2,1,0:T(8,128)S(1)}, f32[2,13,32,128]{3,2,1,0:T(8,128)S(1)}, u32[]{:S(2)}, u32[]{:S(2)}) %collective-permute-start.1) | collective-permute-done | bytes 426016 | tf_op jit(solution)/shard_map/ppermute | solution.py:561
  28.6 0.8 copy-done.4
  29.4 3.7 %shard_map.46 = (f32[4,2,8,32,128]{4,3,2,1,0:T(8,128)}, f32[2,10,32,128]{3,2,1,0:T(8,128)}, f32[2,10,32,128]{3,2,1,0:T(8,128)}, f32[2,8,16,128]{3,2,1,0:T(8,128)...) custom-call(f32[2]{0:T(128)} %diff_ref.13, ...), custom_call_target="tpu_custom_call" | custom-call | tf_op jit(solution)/shard_map/pallas_call | solution.py:498
  33.1 0.6 copy-done.12
  33.8 0.1 copy-done.11
  33.9 4.8 %shard_map.47 = (f32[2,10,32,128]{3,2,1,0:T(8,128)}, f32[2,10,32,128]{3,2,1,0:T(8,128)}, f32[2,10,32,128]{3,2,1,0:T(8,128)}, f32[2,10,32,128]{3,2,1,0:T(8,128)},...) custom-call(f32[2]{0:T(128)} %diff_ref.13, ...), custom_call_target="tpu_custom_call" | custom-call | tf_op jit(solution)/shard_map/pallas_call | solution.py:301
  38.7 1.0 collective-permute-start.5
  39.7 3.8 %collective-permute-start.6 = (f32[2,5,16,128]{3,2,1,0:T(8,128)}, f32[2,5,16,128]{3,2,1,0:T(8,128)S(1)}, u32[]{:S(2)}, u32[]{:S(2)}) collective-permute-start(f32[2,5,16,128]{3,2,1,0:T(8,128)} %get-tuple-element.64), channel_id=1, source_target_pairs={{1,0},{2,1},{3,2},{4,3},{5,4},{6,5},{7,6},{0,7},{9,8},{10,9},{11,1... | collective-permute-start | bytes 245768 | tf_op jit(solution)/shard_map/ppermute | solution.py:612
  43.4 2.6 %collective-permute-done.5.cbefore_ref = f32[2,5,16,128]{3,2,1,0:T(8,128)S(1)} collective-permute-done((f32[2,5,16,128]{3,2,1,0:T(8,128)}, f32[2,5,16,128]{3,2,1,0:T(8,128)S(1)}, u32[]{:S(2)}, u32[]{:S(2)}) %collective-permute-start.5) | collective-permute-done | bytes 81952 | tf_op jit(solution)/shard_map/ppermute | solution.py:611
  46.1 0.6 copy-done.18
  46.7 4.7 %shard_map.48 = (f32[4,2,8,32,128]{4,3,2,1,0:T(8,128)}, f32[2,10,32,128]{3,2,1,0:T(8,128)}, f32[2,10,32,128]{3,2,1,0:T(8,128)}, f32[2,10,32,128]{3,2,1,0:T(8,128...) custom-call(f32[2]{0:T(128)} %diff_ref.13, f32[4,2,4,16,128]{4,3,2,1,0:T(8,128)} %get-tuple-element.62.cown_ref, ...), custom_call_target="tpu_custom_call" | custom-call | tf_op jit(solution)/shard_map/pallas_call | solution.py:434
  51.5 1.9 %collective-permute-start.7 = (f32[2,10,32,128]{3,2,1,0:T(8,128)}, f32[2,10,32,128]{3,2,1,0:T(8,128)S(1)}, u32[]{:S(2)}, u32[]{:S(2)}) collective-permute-start(f32[2,10,32,128]{3,2,1,0:T(8,128)} %get-tuple-element.73), channel_id=1, source_target_pairs={{0,8},{1,9},{2,10},{3,11},{4,12},{5,13},{6,14},{7,15},{8,16},{9,17... | collective-permute-start | bytes 983048 | tf_op jit(solution)/shard_map/ppermute | solution.py:110
  53.4 0.8 collective-permute-start.10
  54.2 4.0 %collective-permute-start.11 = (f32[2,10,32,128]{3,2,1,0:T(8,128)}, f32[2,10,32,128]{3,2,1,0:T(8,128)S(1)}, u32[]{:S(2)}, u32[]{:S(2)}) collective-permute-start(f32[2,10,32,128]{3,2,1,0:T(8,128)} %get-tuple-element.78), channel_id=1, source_target_pairs={{1,0},{2,1},{3,2},{4,3},{5,4},{6,5},{7,6},{0,7},{9,8},{10,9},{11,1... | collective-permute-start | bytes 983048 | tf_op jit(solution)/shard_map/ppermute | solution.py:637
  58.2 1.9 %collective-permute-start.8 = (f32[2,4,32,128]{3,2,1,0:T(8,128)}, f32[2,4,32,128]{3,2,1,0:T(8,128)S(1)}, u32[]{:S(2)}, u32[]{:S(2)}) collective-permute-start(f32[2,4,32,128]{3,2,1,0:T(8,128)} %get-tuple-element.74), channel_id=1, source_target_pairs={{0,9},{1,10},{2,11},{3,12},{4,13},{5,14},{6,15},{7,8},{8,17},{9,18... | collective-permute-start | bytes 393224 | tf_op jit(solution)/shard_map/ppermute | solution.py:110
  60.1 1.9 %collective-permute-start.9 = (f32[2,4,32,128]{3,2,1,0:T(8,128)}, f32[2,4,32,128]{3,2,1,0:T(8,128)S(1)}, u32[]{:S(2)}, u32[]{:S(2)}) collective-permute-start(f32[2,4,32,128]{3,2,1,0:T(8,128)} %get-tuple-element.75), channel_id=1, source_target_pairs={{0,15},{1,8},{2,9},{3,10},{4,11},{5,12},{6,13},{7,14},{8,23},{9,16... | collective-permute-start | bytes 393224 | tf_op jit(solution)/shard_map/ppermute | solution.py:110
  62.0 10.2 %collective-permute-done.8.bbefore_ref = f32[2,4,32,128]{3,2,1,0:T(8,128)S(1)} collective-permute-done((f32[2,4,32,128]{3,2,1,0:T(8,128)}, f32[2,4,32,128]{3,2,1,0:T(8,128)S(1)}, u32[]{:S(2)}, u32[]{:S(2)}) %collective-permute-start.8) | collective-permute-done | bytes 131104 | tf_op jit(solution)/shard_map/ppermute | solution.py:110
  72.3 1.9 %collective-permute-done.11.after_ref = f32[2,10,32,128]{3,2,1,0:T(8,128)S(1)} collective-permute-done((f32[2,10,32,128]{3,2,1,0:T(8,128)}, f32[2,10,32,128]{3,2,1,0:T(8,128)S(1)}, u32[]{:S(2)}, u32[]{:S(2)}) %collective-permute-start.11) | collective-permute-done | bytes 327712 | tf_op jit(solution)/shard_map/ppermute | solution.py:637
  74.2 0.7 copy-done.10
  74.9 4.8 %shard_map.49 = (f32[2,10,32,128]{3,2,1,0:T(8,128)}, f32[2,10,32,128]{3,2,1,0:T(8,128)}, f32[2,10,32,128]{3,2,1,0:T(8,128)}, f32[2,10,32,128]{3,2,1,0:T(8,128)},...) custom-call(f32[2]{0:T(128)} %diff_ref.13, ...), custom_call_target="tpu_custom_call" | custom-call | tf_op jit(solution)/shard_map/pallas_call | solution.py:301
  79.7 1.4 %collective-permute-start.12 = (f32[2,5,16,128]{3,2,1,0:T(8,128)}, f32[2,5,16,128]{3,2,1,0:T(8,128)S(1)}, u32[]{:S(2)}, u32[]{:S(2)}) collective-permute-start(f32[2,5,16,128]{3,2,1,0:T(8,128)} %get-tuple-element.80), channel_id=1, source_target_pairs={{0,1},{1,2},{2,3},{3,4},{4,5},{5,6},{6,7},{7,0},{8,9},{9,10},{10,1... | collective-permute-start | bytes 245768 | tf_op jit(solution)/shard_map/ppermute | solution.py:611
  81.1 3.4 %collective-permute-start.13 = (f32[2,5,16,128]{3,2,1,0:T(8,128)}, f32[2,5,16,128]{3,2,1,0:T(8,128)S(1)}, u32[]{:S(2)}, u32[]{:S(2)}) collective-permute-start(f32[2,5,16,128]{3,2,1,0:T(8,128)} %get-tuple-element.81), channel_id=1, source_target_pairs={{1,0},{2,1},{3,2},{4,3},{5,4},{6,5},{7,6},{0,7},{9,8},{10,9},{11,1... | collective-permute-start | bytes 245768 | tf_op jit(solution)/shard_map/ppermute | solution.py:612
  84.4 3.1 %collective-permute-done.12.cbefore_ref = f32[2,5,16,128]{3,2,1,0:T(8,128)S(1)} collective-permute-done((f32[2,5,16,128]{3,2,1,0:T(8,128)}, f32[2,5,16,128]{3,2,1,0:T(8,128)S(1)}, u32[]{:S(2)}, u32[]{:S(2)}) %collective-permute-start.12) | collective-permute-done | bytes 81952 | tf_op jit(solution)/shard_map/ppermute | solution.py:611
  87.5 0.6 collective-permute-done.13.cafter_ref
  88.2 0.6 copy-done.21
  88.8 4.7 %shard_map.50 = (f32[4,2,8,32,128]{4,3,2,1,0:T(8,128)}, f32[2,10,32,128]{3,2,1,0:T(8,128)}, f32[2,10,32,128]{3,2,1,0:T(8,128)}, f32[2,10,32,128]{3,2,1,0:T(8,128...) custom-call(f32[2]{0:T(128)} %diff_ref.13, f32[4,2,4,16,128]{4,3,2,1,0:T(8,128)} %get-tuple-element.79.cown_ref, ...), custom_call_target="tpu_custom_call" | custom-call | tf_op jit(solution)/shard_map/pallas_call | solution.py:434
  93.5 2.0 %collective-permute-start.14 = (f32[2,10,32,128]{3,2,1,0:T(8,128)}, f32[2,10,32,128]{3,2,1,0:T(8,128)S(1)}, u32[]{:S(2)}, u32[]{:S(2)}) collective-permute-start(f32[2,10,32,128]{3,2,1,0:T(8,128)} %get-tuple-element.89), channel_id=1, source_target_pairs={{0,8},{1,9},{2,10},{3,11},{4,12},{5,13},{6,14},{7,15},{8,16},{9,17... | collective-permute-start | bytes 983048 | tf_op jit(solution)/shard_map/ppermute | solution.py:110
  95.5 0.8 collective-permute-start.17
  96.3 4.0 %collective-permute-start.18 = (f32[2,10,32,128]{3,2,1,0:T(8,128)}, f32[2,10,32,128]{3,2,1,0:T(8,128)S(1)}, u32[]{:S(2)}, u32[]{:S(2)}) collective-permute-start(f32[2,10,32,128]{3,2,1,0:T(8,128)} %get-tuple-element.94), channel_id=1, source_target_pairs={{1,0},{2,1},{3,2},{4,3},{5,4},{6,5},{7,6},{0,7},{9,8},{10,9},{11,1... | collective-permute-start | bytes 983048 | tf_op jit(solution)/shard_map/ppermute | solution.py:637
  100.3 1.9 %collective-permute-start.15 = (f32[2,4,32,128]{3,2,1,0:T(8,128)}, f32[2,4,32,128]{3,2,1,0:T(8,128)S(1)}, u32[]{:S(2)}, u32[]{:S(2)}) collective-permute-start(f32[2,4,32,128]{3,2,1,0:T(8,128)} %get-tuple-element.90), channel_id=1, source_target_pairs={{0,9},{1,10},{2,11},{3,12},{4,13},{5,14},{6,15},{7,8},{8,17},{9,18... | collective-permute-start | bytes 393224 | tf_op jit(solution)/shard_map/ppermute | solution.py:110
  102.2 1.9 %collective-permute-start.16 = (f32[2,4,32,128]{3,2,1,0:T(8,128)}, f32[2,4,32,128]{3,2,1,0:T(8,128)S(1)}, u32[]{:S(2)}, u32[]{:S(2)}) collective-permute-start(f32[2,4,32,128]{3,2,1,0:T(8,128)} %get-tuple-element.91), channel_id=1, source_target_pairs={{0,15},{1,8},{2,9},{3,10},{4,11},{5,12},{6,13},{7,14},{8,23},{9,16... | collective-permute-start | bytes 393224 | tf_op jit(solution)/shard_map/ppermute | solution.py:110
  104.1 11.7 %collective-permute-done.15.bbefore_ref = f32[2,4,32,128]{3,2,1,0:T(8,128)S(1)} collective-permute-done((f32[2,4,32,128]{3,2,1,0:T(8,128)}, f32[2,4,32,128]{3,2,1,0:T(8,128)S(1)}, u32[]{:S(2)}, u32[]{:S(2)}) %collective-permute-start.15) | collective-permute-done | bytes 131104 | tf_op jit(solution)/shard_map/ppermute | solution.py:110
  115.8 0.6 collective-permute-done.18.after_ref
  116.5 0.1 copy-done.5
  116.7 0.5 copy-done.9
  117.2 4.7 %shard_map.51 = (f32[2,10,32,128]{3,2,1,0:T(8,128)}, f32[2,10,32,128]{3,2,1,0:T(8,128)}, f32[2,10,32,128]{3,2,1,0:T(8,128)}, f32[2,10,32,128]{3,2,1,0:T(8,128)},...) custom-call(f32[2]{0:T(128)} %diff_ref.13, ...), custom_call_target="tpu_custom_call" | custom-call | tf_op jit(solution)/shard_map/pallas_call | solution.py:301
  122.0 1.4 %collective-permute-start.19 = (f32[2,1,16,128]{3,2,1,0:T(8,128)}, f32[2,1,16,128]{3,2,1,0:T(8,128)S(1)}, u32[]{:S(2)}, u32[]{:S(2)}) collective-permute-start(f32[2,1,16,128]{3,2,1,0:T(8,128)} %get-tuple-element.96), channel_id=1, source_target_pairs={{0,1},{1,2},{2,3},{3,4},{4,5},{5,6},{6,7},{7,0},{8,9},{9,10},{10,1... | collective-permute-start | bytes 49160 | tf_op jit(solution)/shard_map/ppermute | solution.py:611
  123.4 3.3 %collective-permute-start.20 = (f32[2,1,16,128]{3,2,1,0:T(8,128)}, f32[2,1,16,128]{3,2,1,0:T(8,128)S(1)}, u32[]{:S(2)}, u32[]{:S(2)}) collective-permute-start(f32[2,1,16,128]{3,2,1,0:T(8,128)} %get-tuple-element.97), channel_id=1, source_target_pairs={{1,0},{2,1},{3,2},{4,3},{5,4},{6,5},{7,6},{0,7},{9,8},{10,9},{11,1... | collective-permute-start | bytes 49160 | tf_op jit(solution)/shard_map/ppermute | solution.py:612
  126.8 1.9 %collective-permute-done.19.cbefore_ref = f32[2,1,16,128]{3,2,1,0:T(8,128)S(1)} collective-permute-done((f32[2,1,16,128]{3,2,1,0:T(8,128)}, f32[2,1,16,128]{3,2,1,0:T(8,128)S(1)}, u32[]{:S(2)}, u32[]{:S(2)}) %collective-permute-start.19) | collective-permute-done | bytes 16416 | tf_op jit(solution)/shard_map/ppermute | solution.py:611
  128.7 0.6 copy-done.22
  129.3 2.9 %shard_map.52 = f32[2,8,32,128]{3,2,1,0:T(8,128)} custom-call(f32[2]{0:T(128)} %diff_ref.13, f32[4,2,4,16,128]{4,3,2,1,0:T(8,128)} %get-tuple-element.95.cown_ref, f32[2,1,16,128]{3,2,1,0:T(8,128)} %copy-done.22, f32[2,1,16,128]{3,2,1,0:T(8,128)} %copy-done.23, f32[2,6,16,128]{3,2,1,0:T(8,128)} %get-tuple-element.98.v1w_ref, ...), custom_call_target="tpu_custom_call" | custom-call | tf_op jit(solution)/shard_map/pallas_call | solution.py:434
  (53 shorter events, 0.5 us)
Async XLA Ops:
  0.0 1.1 copy-start.1
  0.0 1.2 copy-start.2
  1.3 25.0 %collective-permute-start = (f32[2,13,32,128]{3,2,1,0:T(8,128)S(1)}, f32[2,13,32,128]{3,2,1,0:T(8,128)S(1)}, u32[]{:S(2)}, u32[]{:S(2)}) collective-permute-start(f32[2,13,32,128]{3,2,1,0:T(8,128)S(1)} %pad_maximum_fusion), channel_id=1, source_target_pairs={{0,1},{1,2},{2,3},{3,4},{4,5},{5,6},{6,7},{7,0},{8,9},{9,10},{10,1... | collective-permute-start | bytes 1277960 | tf_op jit(solution)/shard_map/ppermute | solution.py:557
  2.8 3.3 %copy-start = (f32[1,2,8,32,128]{4,3,2,1,0:T(8,128)S(1)}, f32[1,2,8,32,128]{4,3,2,1,0:T(8,128)}, u32[]{:S(2)}) copy-start(f32[1,2,8,32,128]{4,3,2,1,0:T(8,128)} %param.4) | copy-start | bytes 786436
  2.9 25.7 %collective-permute-start.1 = (f32[2,13,32,128]{3,2,1,0:T(8,128)S(1)}, f32[2,13,32,128]{3,2,1,0:T(8,128)S(1)}, u32[]{:S(2)}, u32[]{:S(2)}) collective-permute-start(f32[2,13,32,128]{3,2,1,0:T(8,128)S(1)} %pad_maximum_fusion.1), channel_id=1, source_target_pairs={{1,0},{2,1},{3,2},{4,3},{5,4},{6,5},{7,6},{0,7},{9,8},{10,9},{11,1... | collective-permute-start | bytes 1277960 | tf_op jit(solution)/shard_map/ppermute | solution.py:561
  6.1 27.0 %collective-permute-start.2 = (f32[2,8,32,128]{3,2,1,0:T(8,128)S(1)}, f32[2,8,32,128]{3,2,1,0:T(8,128)S(1)}, u32[]{:S(2)}, u32[]{:S(2)}) collective-permute-start(f32[2,8,32,128]{3,2,1,0:T(8,128)S(1)} %bitcast.5), channel_id=1, source_target_pairs={{0,8},{1,9},{2,10},{3,11},{4,12},{5,13},{6,14},{7,15},{8,16},{9,17... | collective-permute-start | bytes 786440 | tf_op jit(solution)/shard_map/ppermute | solution.py:110
  8.0 25.0 %collective-permute-start.4 = (f32[2,5,32,128]{3,2,1,0:T(8,128)S(1)}, f32[2,5,32,128]{3,2,1,0:T(8,128)S(1)}, u32[]{:S(2)}, u32[]{:S(2)}) collective-permute-start(f32[2,5,32,128]{3,2,1,0:T(8,128)S(1)} %get-tuple-element.105), channel_id=1, source_target_pairs={{0,15},{1,8},{2,9},{3,10},{4,11},{5,12},{6,13},{7,14},{8,23},{9,16... | collective-permute-start | bytes 491528 | tf_op jit(solution)/shard_map/ppermute | solution.py:110
  10.1 23.0 %collective-permute-start.3 = (f32[2,5,32,128]{3,2,1,0:T(8,128)S(1)}, f32[2,5,32,128]{3,2,1,0:T(8,128)S(1)}, u32[]{:S(2)}, u32[]{:S(2)}) collective-permute-start(f32[2,5,32,128]{3,2,1,0:T(8,128)S(1)} %get-tuple-element.106), channel_id=1, source_target_pairs={{0,9},{1,10},{2,11},{3,12},{4,13},{5,14},{6,15},{7,8},{8,17},{9,18... | collective-permute-start | bytes 491528 | tf_op jit(solution)/shard_map/ppermute | solution.py:110
  26.3 2.3 %copy-start.3 = (f32[2,13,32,128]{3,2,1,0:T(8,128)}, f32[2,13,32,128]{3,2,1,0:T(8,128)S(1)}, u32[]{:S(2)}) copy-start(f32[2,13,32,128]{3,2,1,0:T(8,128)S(1)} %collective-permute-done.got_before_ref) | copy-start | bytes 1277956
  28.6 0.8 copy-start.4
  33.1 0.7 copy-start.12
  33.1 0.7 copy-start.13
  33.1 0.8 copy-start.11
  38.7 7.4 %collective-permute-start.5 = (f32[2,5,16,128]{3,2,1,0:T(8,128)}, f32[2,5,16,128]{3,2,1,0:T(8,128)S(1)}, u32[]{:S(2)}, u32[]{:S(2)}) collective-permute-start(f32[2,5,16,128]{3,2,1,0:T(8,128)} %get-tuple-element.63), channel_id=1, source_target_pairs={{0,1},{1,2},{2,3},{3,4},{4,5},{5,6},{6,7},{7,0},{8,9},{9,10},{10,1... | collective-permute-start | bytes 245768 | tf_op jit(solution)/shard_map/ppermute | solution.py:611
  39.7 6.4 %collective-permute-start.6 = (f32[2,5,16,128]{3,2,1,0:T(8,128)}, f32[2,5,16,128]{3,2,1,0:T(8,128)S(1)}, u32[]{:S(2)}, u32[]{:S(2)}) collective-permute-start(f32[2,5,16,128]{3,2,1,0:T(8,128)} %get-tuple-element.64), channel_id=1, source_target_pairs={{1,0},{2,1},{3,2},{4,3},{5,4},{6,5},{7,6},{0,7},{9,8},{10,9},{11,1... | collective-permute-start | bytes 245768 | tf_op jit(solution)/shard_map/ppermute | solution.py:612
  46.1 0.6 copy-start.18
  46.1 0.7 copy-start.20
  51.5 20.8 %collective-permute-start.7 = (f32[2,10,32,128]{3,2,1,0:T(8,128)}, f32[2,10,32,128]{3,2,1,0:T(8,128)S(1)}, u32[]{:S(2)}, u32[]{:S(2)}) collective-permute-start(f32[2,10,32,128]{3,2,1,0:T(8,128)} %get-tuple-element.73), channel_id=1, source_target_pairs={{0,8},{1,9},{2,10},{3,11},{4,12},{5,13},{6,14},{7,15},{8,16},{9,17... | collective-permute-start | bytes 983048 | tf_op jit(solution)/shard_map/ppermute | solution.py:110
  53.4 18.9 %collective-permute-start.10 = (f32[2,10,32,128]{3,2,1,0:T(8,128)}, f32[2,10,32,128]{3,2,1,0:T(8,128)S(1)}, u32[]{:S(2)}, u32[]{:S(2)}) collective-permute-start(f32[2,10,32,128]{3,2,1,0:T(8,128)} %get-tuple-element.77), channel_id=1, source_target_pairs={{0,1},{1,2},{2,3},{3,4},{4,5},{5,6},{6,7},{7,0},{8,9},{9,10},{10,1... | collective-permute-start | bytes 983048 | tf_op jit(solution)/shard_map/ppermute | solution.py:636
  54.2 20.0 %collective-permute-start.11 = (f32[2,10,32,128]{3,2,1,0:T(8,128)}, f32[2,10,32,128]{3,2,1,0:T(8,128)S(1)}, u32[]{:S(2)}, u32[]{:S(2)}) collective-permute-start(f32[2,10,32,128]{3,2,1,0:T(8,128)} %get-tuple-element.78), channel_id=1, source_target_pairs={{1,0},{2,1},{3,2},{4,3},{5,4},{6,5},{7,6},{0,7},{9,8},{10,9},{11,1... | collective-permute-start | bytes 983048 | tf_op jit(solution)/shard_map/ppermute | solution.py:637
  58.2 14.1 %collective-permute-start.8 = (f32[2,4,32,128]{3,2,1,0:T(8,128)}, f32[2,4,32,128]{3,2,1,0:T(8,128)S(1)}, u32[]{:S(2)}, u32[]{:S(2)}) collective-permute-start(f32[2,4,32,128]{3,2,1,0:T(8,128)} %get-tuple-element.74), channel_id=1, source_target_pairs={{0,9},{1,10},{2,11},{3,12},{4,13},{5,14},{6,15},{7,8},{8,17},{9,18... | collective-permute-start | bytes 393224 | tf_op jit(solution)/shard_map/ppermute | solution.py:110
  60.1 12.2 %collective-permute-start.9 = (f32[2,4,32,128]{3,2,1,0:T(8,128)}, f32[2,4,32,128]{3,2,1,0:T(8,128)S(1)}, u32[]{:S(2)}, u32[]{:S(2)}) collective-permute-start(f32[2,4,32,128]{3,2,1,0:T(8,128)} %get-tuple-element.75), channel_id=1, source_target_pairs={{0,15},{1,8},{2,9},{3,10},{4,11},{5,12},{6,13},{7,14},{8,23},{9,16... | collective-permute-start | bytes 393224 | tf_op jit(solution)/shard_map/ppermute | solution.py:110
  72.3 1.9 %copy-start.15 = (f32[2,4,32,128]{3,2,1,0:T(8,128)}, f32[2,4,32,128]{3,2,1,0:T(8,128)S(1)}, u32[]{:S(2)}) copy-start(f32[2,4,32,128]{3,2,1,0:T(8,128)S(1)} %collective-permute-done.8.bbefore_ref) | copy-start | bytes 393220
  72.3 1.9 %copy-start.17 = (f32[2,4,32,128]{3,2,1,0:T(8,128)}, f32[2,4,32,128]{3,2,1,0:T(8,128)S(1)}, u32[]{:S(2)}) copy-start(f32[2,4,32,128]{3,2,1,0:T(8,128)S(1)} %collective-permute-done.9.bafter_ref) | copy-start | bytes 393220
  72.3 1.9 %copy-start.6 = (f32[2,10,32,128]{3,2,1,0:T(8,128)}, f32[2,10,32,128]{3,2,1,0:T(8,128)S(1)}, u32[]{:S(2)}) copy-start(f32[2,10,32,128]{3,2,1,0:T(8,128)S(1)} %collective-permute-done.7.centre_ref) | copy-start | bytes 983044
  72.3 1.9 %copy-start.8 = (f32[2,10,32,128]{3,2,1,0:T(8,128)}, f32[2,10,32,128]{3,2,1,0:T(8,128)S(1)}, u32[]{:S(2)}) copy-start(f32[2,10,32,128]{3,2,1,0:T(8,128)S(1)} %collective-permute-done.10.before_ref) | copy-start | bytes 983044
  74.2 0.7 copy-start.10
  79.7 7.9 %collective-permute-start.12 = (f32[2,5,16,128]{3,2,1,0:T(8,128)}, f32[2,5,16,128]{3,2,1,0:T(8,128)S(1)}, u32[]{:S(2)}, u32[]{:S(2)}) collective-permute-start(f32[2,5,16,128]{3,2,1,0:T(8,128)} %get-tuple-element.80), channel_id=1, source_target_pairs={{0,1},{1,2},{2,3},{3,4},{4,5},{5,6},{6,7},{7,0},{8,9},{9,10},{10,1... | collective-permute-start | bytes 245768 | tf_op jit(solution)/shard_map/ppermute | solution.py:611
  81.1 7.1 %collective-permute-start.13 = (f32[2,5,16,128]{3,2,1,0:T(8,128)}, f32[2,5,16,128]{3,2,1,0:T(8,128)S(1)}, u32[]{:S(2)}, u32[]{:S(2)}) collective-permute-start(f32[2,5,16,128]{3,2,1,0:T(8,128)} %get-tuple-element.81), channel_id=1, source_target_pairs={{1,0},{2,1},{3,2},{4,3},{5,4},{6,5},{7,6},{0,7},{9,8},{10,9},{11,1... | collective-permute-start | bytes 245768 | tf_op jit(solution)/shard_map/ppermute | solution.py:612
  87.5 0.6 copy-start.19
  88.1 0.6 copy-start.21
  93.5 22.3 %collective-permute-start.14 = (f32[2,10,32,128]{3,2,1,0:T(8,128)}, f32[2,10,32,128]{3,2,1,0:T(8,128)S(1)}, u32[]{:S(2)}, u32[]{:S(2)}) collective-permute-start(f32[2,10,32,128]{3,2,1,0:T(8,128)} %get-tuple-element.89), channel_id=1, source_target_pairs={{0,8},{1,9},{2,10},{3,11},{4,12},{5,13},{6,14},{7,15},{8,16},{9,17... | collective-permute-start | bytes 983048 | tf_op jit(solution)/shard_map/ppermute | solution.py:110
  95.5 20.3 %collective-permute-start.17 = (f32[2,10,32,128]{3,2,1,0:T(8,128)}, f32[2,10,32,128]{3,2,1,0:T(8,128)S(1)}, u32[]{:S(2)}, u32[]{:S(2)}) collective-permute-start(f32[2,10,32,128]{3,2,1,0:T(8,128)} %get-tuple-element.93), channel_id=1, source_target_pairs={{0,1},{1,2},{2,3},{3,4},{4,5},{5,6},{6,7},{7,0},{8,9},{9,10},{10,1... | collective-permute-start | bytes 983048 | tf_op jit(solution)/shard_map/ppermute | solution.py:636
  96.3 20.2 %collective-permute-start.18 = (f32[2,10,32,128]{3,2,1,0:T(8,128)}, f32[2,10,32,128]{3,2,1,0:T(8,128)S(1)}, u32[]{:S(2)}, u32[]{:S(2)}) collective-permute-start(f32[2,10,32,128]{3,2,1,0:T(8,128)} %get-tuple-element.94), channel_id=1, source_target_pairs={{1,0},{2,1},{3,2},{4,3},{5,4},{6,5},{7,6},{0,7},{9,8},{10,9},{11,1... | collective-permute-start | bytes 983048 | tf_op jit(solution)/shard_map/ppermute | solution.py:637
  100.3 15.5 %collective-permute-start.15 = (f32[2,4,32,128]{3,2,1,0:T(8,128)}, f32[2,4,32,128]{3,2,1,0:T(8,128)S(1)}, u32[]{:S(2)}, u32[]{:S(2)}) collective-permute-start(f32[2,4,32,128]{3,2,1,0:T(8,128)} %get-tuple-element.90), channel_id=1, source_target_pairs={{0,9},{1,10},{2,11},{3,12},{4,13},{5,14},{6,15},{7,8},{8,17},{9,18... | collective-permute-start | bytes 393224 | tf_op jit(solution)/shard_map/ppermute | solution.py:110
  102.2 13.6 %collective-permute-start.16 = (f32[2,4,32,128]{3,2,1,0:T(8,128)}, f32[2,4,32,128]{3,2,1,0:T(8,128)S(1)}, u32[]{:S(2)}, u32[]{:S(2)}) collective-permute-start(f32[2,4,32,128]{3,2,1,0:T(8,128)} %get-tuple-element.91), channel_id=1, source_target_pairs={{0,15},{1,8},{2,9},{3,10},{4,11},{5,12},{6,13},{7,14},{8,23},{9,16... | collective-permute-start | bytes 393224 | tf_op jit(solution)/shard_map/ppermute | solution.py:110
  115.8 0.7 copy-start.14
  115.8 0.7 copy-start.16
  115.8 0.8 copy-start.5
  115.8 0.9 copy-start.7
  116.5 0.7 copy-start.9
  122.0 6.7 %collective-permute-start.19 = (f32[2,1,16,128]{3,2,1,0:T(8,128)}, f32[2,1,16,128]{3,2,1,0:T(8,128)S(1)}, u32[]{:S(2)}, u32[]{:S(2)}) collective-permute-start(f32[2,1,16,128]{3,2,1,0:T(8,128)} %get-tuple-element.96), channel_id=1, source_target_pairs={{0,1},{1,2},{2,3},{3,4},{4,5},{5,6},{6,7},{7,0},{8,9},{9,10},{10,1... | collective-permute-start | bytes 49160 | tf_op jit(solution)/shard_map/ppermute | solution.py:611
  123.4 5.3 %collective-permute-start.20 = (f32[2,1,16,128]{3,2,1,0:T(8,128)}, f32[2,1,16,128]{3,2,1,0:T(8,128)S(1)}, u32[]{:S(2)}, u32[]{:S(2)}) collective-permute-start(f32[2,1,16,128]{3,2,1,0:T(8,128)} %get-tuple-element.97), channel_id=1, source_target_pairs={{1,0},{2,1},{3,2},{4,3},{5,4},{6,5},{7,6},{0,7},{9,8},{10,9},{11,1... | collective-permute-start | bytes 49160 | tf_op jit(solution)/shard_map/ppermute | solution.py:612
  128.7 0.6 copy-start.22
  128.7 0.6 copy-start.23
